TPU v7x, 512 devices: a whole 4x8x8 slice. The times are simulated.
512 devices in a mesh: seq: 32 (over y, x), tensor: 8 (over z), dp: 2 (over core).
Axes of the slice: x: 4, y: 8, z: 8, core: 2. Of those that a mesh axis runs over, the one named last changes fastest.
Arguments:
- x_stream: bfloat16 [32768, 5120], P(('dp', 'seq'), 'tensor'), parts along dimension 0
- bc_stream: bfloat16 [32768, 256], P(('dp', 'seq')), parts along dimension 0, may hold values from -6 to 6
- z_gate: bfloat16 [32768, 5120], P(('dp', 'seq'), 'tensor'), parts along dimension 0
- dt_stream: bfloat16 [80, 32768], P('tensor', ('dp', 'seq')), parts along dimension 1, as said below
- doc_ids: int32 [32768], P(('dp', 'seq')), parts along dimension 0, may hold values from 0 to 7, never falling along the last dimension, each value on 1 to 8192 neighbouring positions
- conv_x: bfloat16 [4, 5120], P(None, 'tensor'), may hold values from -3 to 3
- conv_bc: bfloat16 [4, 256], replicated, may hold values from -3 to 3
- a_log: float32 [80], P('tensor')
- dt_bias: float32 [80], P('tensor'), as said below
- d_skip: float32 [80], P('tensor'), may hold values from 0.5 to 4
- norm_gain: float32 [5120], P('tensor'), may hold values from 0.5 to 1.5
- w_out: bfloat16 [5120, 2560], P('tensor'), may hold values from -0.078125 to 0.078125
Outputs:
- layer_out: bfloat16 [32768, 2560], P(('dp', 'seq'), 'tensor'), parts along dimension 0
There are 2 independent parts, one for each index of `dp`. A program takes and returns all parts, laid end to end along the dimension named above; an argument that names none is the same for every part. Nothing has to cross between parts.
Inputs may be any that keep to these rules, and one draw needn't show every extreme that they name: `doc_ids`: document ids never fall along the tokens; each document has 1 to 8192 tokens and one has exactly 8192. `dt_bias`: step size bias. `dt_stream`: step size logits.
All inputs are finite; a program needn't handle non-finite values.
Results may differ from a plain program's by a relative error of at most 0.017.
Values may be sent and summed in bfloat16 or wider, within the bound.
No kernel may reach another device: no remote copies, remote signals or barrier semaphores. Data moves between devices by JAX's collectives and lax.ppermute only.
A program may use at most 64 MiB of HBM per device.

v0:
```python
import jax
import jax.numpy as jnp
from jax import lax
from jax.sharding import PartitionSpec as P

SPAN = 256


def from_behind(block, axis, distance):
    devices = range(lax.axis_size(axis))
    route = [(i - distance, i) for i in devices if i - distance in devices]
    return lax.ppermute(block, axis, route)


def causal_conv(extended, weights, ext_ids, own_ids, row_count):
    tap_count = weights.shape[0]
    total = jnp.zeros((row_count, extended.shape[1]), jnp.float32)
    for offset in range(tap_count):
        first_row = tap_count - 1 - offset
        window = extended[first_row : first_row + row_count]
        keep_mask = ext_ids[first_row : first_row + row_count] == own_ids
        total = total + jnp.where(
            keep_mask[:, None],
            window.astype(jnp.float32) * weights[offset].astype(jnp.float32),
            0.0,
        )
    return jax.nn.silu(total).astype(jnp.bfloat16)


def pass_state(device_decay, local_final):

    def hand_on(counter, carry_pair):
        passed = from_behind(carry_pair[0].astype(jnp.bfloat16), "seq", 1).astype(jnp.float32)
        return (device_decay[:, None, None] * passed + local_final, passed)

    return lax.fori_loop(
        0, lax.axis_size("seq") - 1, hand_on, (local_final, jnp.zeros_like(local_final))
    )[1]


def local(
    x_stream,
    bc_stream,
    z_gate,
    dt_stream,
    doc_ids,
    conv_x,
    conv_bc,
    a_log,
    dt_bias,
    d_skip,
    norm_gain,
    w_out,
):
    highest = lax.Precision.HIGHEST
    row_count = x_stream.shape[0]
    head_count = dt_stream.shape[0]
    inner_width = x_stream.shape[1]
    head_size = inner_width // head_count
    state_size = bc_stream.shape[1] // 2
    tap_count = conv_x.shape[0]
    blocks = row_count // SPAN
    edge_start = row_count - tap_count + 1
    own_ids = doc_ids.astype(jnp.float32)
    rim_x, rim_bc, rim_ids = from_behind(
        (x_stream[edge_start:], bc_stream[edge_start:], own_ids[edge_start:].astype(jnp.bfloat16)),
        "seq",
        1,
    )
    ext_ids = jnp.concatenate([rim_ids.astype(jnp.float32), own_ids])
    mixed_x = causal_conv(jnp.concatenate([rim_x, x_stream]), conv_x, ext_ids, own_ids, row_count)
    mixed_bc = causal_conv(
        jnp.concatenate([rim_bc, bc_stream]), conv_bc, ext_ids, own_ids, row_count
    )
    prior_id = ext_ids[tap_count - 2]
    step_size = jax.nn.softplus(dt_stream.astype(jnp.float32) + dt_bias[:, None])
    log_rates = -jnp.exp(a_log)[:, None] * step_size
    block_steps = step_size.reshape(head_count, blocks, SPAN)
    cum_rates = jnp.cumsum(log_rates.reshape(head_count, blocks, SPAN), axis=2)
    block_x = mixed_x.reshape(blocks, SPAN, head_count, head_size)
    b_vals = mixed_bc[:, :state_size].reshape(blocks, SPAN, state_size)
    c_vals = mixed_bc[:, state_size:].reshape(blocks, SPAN, state_size)
    c_wide = c_vals.astype(jnp.float32)
    block_ids = own_ids.reshape(blocks, SPAN)
    before = jnp.concatenate([prior_id[None], own_ids[SPAN - 1 :: SPAN][: blocks - 1]])
    carried = block_ids == before[:, None]
    entry_gain = jnp.where(carried[None], jnp.exp(cum_rates), 0.0)
    tail_weight = (
        jnp.where(
            (block_ids == block_ids[:, -1:])[None], jnp.exp(cum_rates[:, :, -1:] - cum_rates), 0.0
        )
        * block_steps
    )
    weighted = block_x.astype(jnp.float32) * jnp.transpose(tail_weight, (1, 2, 0))[..., None]
    block_states = jnp.einsum(
        "cshp,csn->chpn", weighted, b_vals.astype(jnp.float32), precision=highest
    )
    block_decay = jnp.where(carried[:, -1][None], jnp.exp(cum_rates[:, :, -1]), 0.0)
    device_decay = jnp.prod(block_decay, axis=1)
    skip_term = d_skip[None, None, :, None] * block_x.astype(jnp.float32)
    zero_state = jnp.zeros((head_count, head_size, state_size), jnp.float32)

    def advance(carry_state, inputs_now):
        decay_now, fresh_state = inputs_now
        return (decay_now[:, None, None] * carry_state + fresh_state, carry_state)

    local_final, local_entries = lax.scan(advance, zero_state, (block_decay.T, block_states))
    reached = jnp.einsum("ctn,chpn->cthp", c_wide, local_entries, precision=highest)
    lower_mask = jnp.tril(jnp.ones((SPAN, SPAN), jnp.bool_))
    same_doc = (block_ids[:, :, None] == block_ids[:, None, :]) & lower_mask[None]
    spread = cum_rates[:, :, :, None] - cum_rates[:, :, None, :]
    decay_now = jnp.where(same_doc[None], jnp.exp(jnp.minimum(spread, 0.0)), 0.0)
    scores = jnp.einsum("ctn,csn->cts", c_vals, b_vals, preferred_element_type=jnp.float32)
    weights = (scores[None] * decay_now * block_steps[:, :, None, :]).astype(jnp.bfloat16)
    result = (
        jnp.einsum("hcts,cshp->cthp", weights, block_x, preferred_element_type=jnp.float32)
        + reached * jnp.transpose(entry_gain, (1, 2, 0))[..., None]
        + skip_term
    )
    incoming = pass_state(device_decay, local_final)
    prefix = jnp.cumprod(
        jnp.concatenate([jnp.ones((head_count, 1), jnp.float32), block_decay[:, :-1]], axis=1),
        axis=1,
    )
    reach_term = jnp.einsum("ctn,hpn->cthp", c_wide, incoming, precision=highest)
    result = (
        result + reach_term * jnp.transpose(entry_gain * prefix[:, :, None], (1, 2, 0))[..., None]
    )
    y_vals = lax.optimization_barrier(result.reshape(row_count, inner_width).astype(jnp.bfloat16))
    gated = y_vals.astype(jnp.float32) * jax.nn.silu(z_gate.astype(jnp.float32))
    squares = lax.psum(jnp.sum(gated * gated, axis=1), "tensor")
    inv_norm = lax.rsqrt(squares / (inner_width * lax.axis_size("tensor")) + 1e-05)
    normed = (gated * inv_norm[:, None] * norm_gain[None, :]).astype(jnp.bfloat16)
    partial_value = jnp.dot(normed, w_out, preferred_element_type=jnp.float32)
    return lax.psum_scatter(
        partial_value.astype(jnp.bfloat16), "tensor", scatter_dimension=1, tiled=True
    )


def solution(mesh):
    return jax.shard_map(
        local,
        mesh=mesh,
        in_specs=(
            P(("dp", "seq"), "tensor"),
            P(("dp", "seq"), None),
            P(("dp", "seq"), "tensor"),
            P("tensor", ("dp", "seq")),
            P(("dp", "seq")),
            P(None, "tensor"),
            P(),
            P("tensor"),
            P("tensor"),
            P("tensor"),
            P("tensor"),
            P("tensor", None),
        ),
        out_specs=P(("dp", "seq"), "tensor"),
        check_vma=False,
    )
```

profile of v0, /device:TPU:6, one launch (start us, length us, event | category | flops | bytes accessed | tf_op | source)
XLA Modules:
  0.0 555.0 jit_solution(4379225244561466151)
XLA Ops:
  8.0 3.4 collective-permute-start.1
  13.0 3.4 collective-permute-start.2
  17.7 3.4 collective-permute-start.3
  56.9 3.4 multiply_convert_fusion.5
  65.7 6.2 %while.26 = (s32[]{:T(128)}, f32[10,64,128]{2,1,0:T(8,128)}, f32[2,10,64,128]{3,2,1,0:T(8,128)}, f32[2,10]{1,0:T(2,128)S(1)}, f32[2,10,64,128]{3,2,1,0:T(8,128)}, /*index=5*/s32[]{:T(128)}, s32[]{:T(128)}) while((s32[]{:T(128)}, f32[10,64,128]{2,1,0:T(8,128)}, f32[2,10,64,128]{3,2,1,0:T(8,128)}, f32[2,10]{1,0:T(2,128)S(1)}, ...), condition=%wide.region_3.4_spmd.clone, body=%wide.region_2.3_spmd.clone.sunk | while | flops 327683 | bytes 1639128 | solution.py:107
  73.6 3.3 fusion.9
  79.0 356.6 %while.25 = (s32[]{:T(128)}, bf16[10,64,128]{2,1,0:T(8,128)(2,1)}, f32[10,64,128]{2,1,0:T(8,128)}, f32[10]{0:T(128)S(1)}, f32[10,64,128]{2,1,0:T(8,128)}, /*index=5*/s32[]{:T(128)}) while((s32[]{:T(128)}, bf16[10,64,128]{2,1,0:T(8,128)(2,1)}, f32[10,64,128]{2,1,0:T(8,128)}, f32[10]{0:T(128)S(1)}, f32[10,64,128]{2,1,0:T(8,128)}, ...), condition=%wide.region_6.7_spmd, body=%wide.region_5.6_spmd.sunk | while | flops 327682 | bytes 1638549 | solution.py:36
  79.0 3.2 collective-permute-start
  82.2 4.3 collective-permute-done
  88.3 5.2 collective-permute-start
  93.5 3.1 collective-permute-done
  98.5 6.4 %collective-permute-start = (bf16[10,64,128]{2,1,0:T(8,128)(2,1)}, bf16[10,64,128]{2,1,0:T(8,128)(2,1)S(1)}, u32[]{:S(2)}, u32[]{:S(2)}) collective-permute-start(bf16[10,64,128]{2,1,0:T(8,128)(2,1)} %get-tuple-element.219), channel_id=1, source_target_pairs={{0,16},{16,32},{32,48},{48,64},{64,80},{80,96},{96,112},{112,128},... | collective-permute-start | bytes 491528 | tf_op jit(solution)/shard_map/while/body/eval_jaxpr/ppermute | solution.py:12
  109.8 6.4 %collective-permute-start = (bf16[10,64,128]{2,1,0:T(8,128)(2,1)}, bf16[10,64,128]{2,1,0:T(8,128)(2,1)S(1)}, u32[]{:S(2)}, u32[]{:S(2)}) collective-permute-start(bf16[10,64,128]{2,1,0:T(8,128)(2,1)} %get-tuple-element.219), channel_id=1, source_target_pairs={{0,16},{16,32},{32,48},{48,64},{64,80},{80,96},{96,112},{112,128},... | collective-permute-start | bytes 491528 | tf_op jit(solution)/shard_map/while/body/eval_jaxpr/ppermute | solution.py:12
  121.1 6.4 %collective-permute-start = (bf16[10,64,128]{2,1,0:T(8,128)(2,1)}, bf16[10,64,128]{2,1,0:T(8,128)(2,1)S(1)}, u32[]{:S(2)}, u32[]{:S(2)}) collective-permute-start(bf16[10,64,128]{2,1,0:T(8,128)(2,1)} %get-tuple-element.219), channel_id=1, source_target_pairs={{0,16},{16,32},{32,48},{48,64},{64,80},{80,96},{96,112},{112,128},... | collective-permute-start | bytes 491528 | tf_op jit(solution)/shard_map/while/body/eval_jaxpr/ppermute | solution.py:12
  127.5 3.1 collective-permute-done
  132.5 6.4 %collective-permute-start = (bf16[10,64,128]{2,1,0:T(8,128)(2,1)}, bf16[10,64,128]{2,1,0:T(8,128)(2,1)S(1)}, u32[]{:S(2)}, u32[]{:S(2)}) collective-permute-start(bf16[10,64,128]{2,1,0:T(8,128)(2,1)} %get-tuple-element.219), channel_id=1, source_target_pairs={{0,16},{16,32},{32,48},{48,64},{64,80},{80,96},{96,112},{112,128},... | collective-permute-start | bytes 491528 | tf_op jit(solution)/shard_map/while/body/eval_jaxpr/ppermute | solution.py:12
  138.9 3.1 collective-permute-done
  143.8 6.4 %collective-permute-start = (bf16[10,64,128]{2,1,0:T(8,128)(2,1)}, bf16[10,64,128]{2,1,0:T(8,128)(2,1)S(1)}, u32[]{:S(2)}, u32[]{:S(2)}) collective-permute-start(bf16[10,64,128]{2,1,0:T(8,128)(2,1)} %get-tuple-element.219), channel_id=1, source_target_pairs={{0,16},{16,32},{32,48},{48,64},{64,80},{80,96},{96,112},{112,128},... | collective-permute-start | bytes 491528 | tf_op jit(solution)/shard_map/while/body/eval_jaxpr/ppermute | solution.py:12
  150.2 3.5 collective-permute-done
  155.5 6.4 %collective-permute-start = (bf16[10,64,128]{2,1,0:T(8,128)(2,1)}, bf16[10,64,128]{2,1,0:T(8,128)(2,1)S(1)}, u32[]{:S(2)}, u32[]{:S(2)}) collective-permute-start(bf16[10,64,128]{2,1,0:T(8,128)(2,1)} %get-tuple-element.219), channel_id=1, source_target_pairs={{0,16},{16,32},{32,48},{48,64},{64,80},{80,96},{96,112},{112,128},... | collective-permute-start | bytes 491528 | tf_op jit(solution)/shard_map/while/body/eval_jaxpr/ppermute | solution.py:12
  161.9 4.7 collective-permute-done
  168.4 6.4 %collective-permute-start = (bf16[10,64,128]{2,1,0:T(8,128)(2,1)}, bf16[10,64,128]{2,1,0:T(8,128)(2,1)S(1)}, u32[]{:S(2)}, u32[]{:S(2)}) collective-permute-start(bf16[10,64,128]{2,1,0:T(8,128)(2,1)} %get-tuple-element.219), channel_id=1, source_target_pairs={{0,16},{16,32},{32,48},{48,64},{64,80},{80,96},{96,112},{112,128},... | collective-permute-start | bytes 491528 | tf_op jit(solution)/shard_map/while/body/eval_jaxpr/ppermute | solution.py:12
  174.8 4.0 collective-permute-done
  180.6 6.4 %collective-permute-start = (bf16[10,64,128]{2,1,0:T(8,128)(2,1)}, bf16[10,64,128]{2,1,0:T(8,128)(2,1)S(1)}, u32[]{:S(2)}, u32[]{:S(2)}) collective-permute-start(bf16[10,64,128]{2,1,0:T(8,128)(2,1)} %get-tuple-element.219), channel_id=1, source_target_pairs={{0,16},{16,32},{32,48},{48,64},{64,80},{80,96},{96,112},{112,128},... | collective-permute-start | bytes 491528 | tf_op jit(solution)/shard_map/while/body/eval_jaxpr/ppermute | solution.py:12
  187.0 3.2 collective-permute-done
  192.0 6.4 %collective-permute-start = (bf16[10,64,128]{2,1,0:T(8,128)(2,1)}, bf16[10,64,128]{2,1,0:T(8,128)(2,1)S(1)}, u32[]{:S(2)}, u32[]{:S(2)}) collective-permute-start(bf16[10,64,128]{2,1,0:T(8,128)(2,1)} %get-tuple-element.219), channel_id=1, source_target_pairs={{0,16},{16,32},{32,48},{48,64},{64,80},{80,96},{96,112},{112,128},... | collective-permute-start | bytes 491528 | tf_op jit(solution)/shard_map/while/body/eval_jaxpr/ppermute | solution.py:12
  198.4 3.1 collective-permute-done
  203.4 6.4 %collective-permute-start = (bf16[10,64,128]{2,1,0:T(8,128)(2,1)}, bf16[10,64,128]{2,1,0:T(8,128)(2,1)S(1)}, u32[]{:S(2)}, u32[]{:S(2)}) collective-permute-start(bf16[10,64,128]{2,1,0:T(8,128)(2,1)} %get-tuple-element.219), channel_id=1, source_target_pairs={{0,16},{16,32},{32,48},{48,64},{64,80},{80,96},{96,112},{112,128},... | collective-permute-start | bytes 491528 | tf_op jit(solution)/shard_map/while/body/eval_jaxpr/ppermute | solution.py:12
  214.7 6.4 %collective-permute-start = (bf16[10,64,128]{2,1,0:T(8,128)(2,1)}, bf16[10,64,128]{2,1,0:T(8,128)(2,1)S(1)}, u32[]{:S(2)}, u32[]{:S(2)}) collective-permute-start(bf16[10,64,128]{2,1,0:T(8,128)(2,1)} %get-tuple-element.219), channel_id=1, source_target_pairs={{0,16},{16,32},{32,48},{48,64},{64,80},{80,96},{96,112},{112,128},... | collective-permute-start | bytes 491528 | tf_op jit(solution)/shard_map/while/body/eval_jaxpr/ppermute | solution.py:12
  221.1 3.1 collective-permute-done
  226.0 6.4 %collective-permute-start = (bf16[10,64,128]{2,1,0:T(8,128)(2,1)}, bf16[10,64,128]{2,1,0:T(8,128)(2,1)S(1)}, u32[]{:S(2)}, u32[]{:S(2)}) collective-permute-start(bf16[10,64,128]{2,1,0:T(8,128)(2,1)} %get-tuple-element.219), channel_id=1, source_target_pairs={{0,16},{16,32},{32,48},{48,64},{64,80},{80,96},{96,112},{112,128},... | collective-permute-start | bytes 491528 | tf_op jit(solution)/shard_map/while/body/eval_jaxpr/ppermute | solution.py:12
  232.4 3.1 collective-permute-done
  237.4 6.4 %collective-permute-start = (bf16[10,64,128]{2,1,0:T(8,128)(2,1)}, bf16[10,64,128]{2,1,0:T(8,128)(2,1)S(1)}, u32[]{:S(2)}, u32[]{:S(2)}) collective-permute-start(bf16[10,64,128]{2,1,0:T(8,128)(2,1)} %get-tuple-element.219), channel_id=1, source_target_pairs={{0,16},{16,32},{32,48},{48,64},{64,80},{80,96},{96,112},{112,128},... | collective-permute-start | bytes 491528 | tf_op jit(solution)/shard_map/while/body/eval_jaxpr/ppermute | solution.py:12
  248.7 6.4 %collective-permute-start = (bf16[10,64,128]{2,1,0:T(8,128)(2,1)}, bf16[10,64,128]{2,1,0:T(8,128)(2,1)S(1)}, u32[]{:S(2)}, u32[]{:S(2)}) collective-permute-start(bf16[10,64,128]{2,1,0:T(8,128)(2,1)} %get-tuple-element.219), channel_id=1, source_target_pairs={{0,16},{16,32},{32,48},{48,64},{64,80},{80,96},{96,112},{112,128},... | collective-permute-start | bytes 491528 | tf_op jit(solution)/shard_map/while/body/eval_jaxpr/ppermute | solution.py:12
  255.1 3.3 collective-permute-done
  260.2 6.4 %collective-permute-start = (bf16[10,64,128]{2,1,0:T(8,128)(2,1)}, bf16[10,64,128]{2,1,0:T(8,128)(2,1)S(1)}, u32[]{:S(2)}, u32[]{:S(2)}) collective-permute-start(bf16[10,64,128]{2,1,0:T(8,128)(2,1)} %get-tuple-element.219), channel_id=1, source_target_pairs={{0,16},{16,32},{32,48},{48,64},{64,80},{80,96},{96,112},{112,128},... | collective-permute-start | bytes 491528 | tf_op jit(solution)/shard_map/while/body/eval_jaxpr/ppermute | solution.py:12
  266.6 4.5 collective-permute-done
  272.9 6.4 %collective-permute-start = (bf16[10,64,128]{2,1,0:T(8,128)(2,1)}, bf16[10,64,128]{2,1,0:T(8,128)(2,1)S(1)}, u32[]{:S(2)}, u32[]{:S(2)}) collective-permute-start(bf16[10,64,128]{2,1,0:T(8,128)(2,1)} %get-tuple-element.219), channel_id=1, source_target_pairs={{0,16},{16,32},{32,48},{48,64},{64,80},{80,96},{96,112},{112,128},... | collective-permute-start | bytes 491528 | tf_op jit(solution)/shard_map/while/body/eval_jaxpr/ppermute | solution.py:12
  279.3 4.1 collective-permute-done
  285.2 6.4 %collective-permute-start = (bf16[10,64,128]{2,1,0:T(8,128)(2,1)}, bf16[10,64,128]{2,1,0:T(8,128)(2,1)S(1)}, u32[]{:S(2)}, u32[]{:S(2)}) collective-permute-start(bf16[10,64,128]{2,1,0:T(8,128)(2,1)} %get-tuple-element.219), channel_id=1, source_target_pairs={{0,16},{16,32},{32,48},{48,64},{64,80},{80,96},{96,112},{112,128},... | collective-permute-start | bytes 491528 | tf_op jit(solution)/shard_map/while/body/eval_jaxpr/ppermute | solution.py:12
  291.6 3.3 collective-permute-done
  296.7 6.4 %collective-permute-start = (bf16[10,64,128]{2,1,0:T(8,128)(2,1)}, bf16[10,64,128]{2,1,0:T(8,128)(2,1)S(1)}, u32[]{:S(2)}, u32[]{:S(2)}) collective-permute-start(bf16[10,64,128]{2,1,0:T(8,128)(2,1)} %get-tuple-element.219), channel_id=1, source_target_pairs={{0,16},{16,32},{32,48},{48,64},{64,80},{80,96},{96,112},{112,128},... | collective-permute-start | bytes 491528 | tf_op jit(solution)/shard_map/while/body/eval_jaxpr/ppermute | solution.py:12
  303.1 3.1 collective-permute-done
  308.0 6.4 %collective-permute-start = (bf16[10,64,128]{2,1,0:T(8,128)(2,1)}, bf16[10,64,128]{2,1,0:T(8,128)(2,1)S(1)}, u32[]{:S(2)}, u32[]{:S(2)}) collective-permute-start(bf16[10,64,128]{2,1,0:T(8,128)(2,1)} %get-tuple-element.219), channel_id=1, source_target_pairs={{0,16},{16,32},{32,48},{48,64},{64,80},{80,96},{96,112},{112,128},... | collective-permute-start | bytes 491528 | tf_op jit(solution)/shard_map/while/body/eval_jaxpr/ppermute | solution.py:12
  314.4 3.1 collective-permute-done
  319.3 6.4 %collective-permute-start = (bf16[10,64,128]{2,1,0:T(8,128)(2,1)}, bf16[10,64,128]{2,1,0:T(8,128)(2,1)S(1)}, u32[]{:S(2)}, u32[]{:S(2)}) collective-permute-start(bf16[10,64,128]{2,1,0:T(8,128)(2,1)} %get-tuple-element.219), channel_id=1, source_target_pairs={{0,16},{16,32},{32,48},{48,64},{64,80},{80,96},{96,112},{112,128},... | collective-permute-start | bytes 491528 | tf_op jit(solution)/shard_map/while/body/eval_jaxpr/ppermute | solution.py:12
  330.7 6.4 %collective-permute-start = (bf16[10,64,128]{2,1,0:T(8,128)(2,1)}, bf16[10,64,128]{2,1,0:T(8,128)(2,1)S(1)}, u32[]{:S(2)}, u32[]{:S(2)}) collective-permute-start(bf16[10,64,128]{2,1,0:T(8,128)(2,1)} %get-tuple-element.219), channel_id=1, source_target_pairs={{0,16},{16,32},{32,48},{48,64},{64,80},{80,96},{96,112},{112,128},... | collective-permute-start | bytes 491528 | tf_op jit(solution)/shard_map/while/body/eval_jaxpr/ppermute | solution.py:12
  337.1 3.1 collective-permute-done
  342.0 6.4 %collective-permute-start = (bf16[10,64,128]{2,1,0:T(8,128)(2,1)}, bf16[10,64,128]{2,1,0:T(8,128)(2,1)S(1)}, u32[]{:S(2)}, u32[]{:S(2)}) collective-permute-start(bf16[10,64,128]{2,1,0:T(8,128)(2,1)} %get-tuple-element.219), channel_id=1, source_target_pairs={{0,16},{16,32},{32,48},{48,64},{64,80},{80,96},{96,112},{112,128},... | collective-permute-start | bytes 491528 | tf_op jit(solution)/shard_map/while/body/eval_jaxpr/ppermute | solution.py:12
  348.4 3.1 collective-permute-done
  353.3 6.4 %collective-permute-start = (bf16[10,64,128]{2,1,0:T(8,128)(2,1)}, bf16[10,64,128]{2,1,0:T(8,128)(2,1)S(1)}, u32[]{:S(2)}, u32[]{:S(2)}) collective-permute-start(bf16[10,64,128]{2,1,0:T(8,128)(2,1)} %get-tuple-element.219), channel_id=1, source_target_pairs={{0,16},{16,32},{32,48},{48,64},{64,80},{80,96},{96,112},{112,128},... | collective-permute-start | bytes 491528 | tf_op jit(solution)/shard_map/while/body/eval_jaxpr/ppermute | solution.py:12
  364.7 6.4 %collective-permute-start = (bf16[10,64,128]{2,1,0:T(8,128)(2,1)}, bf16[10,64,128]{2,1,0:T(8,128)(2,1)S(1)}, u32[]{:S(2)}, u32[]{:S(2)}) collective-permute-start(bf16[10,64,128]{2,1,0:T(8,128)(2,1)} %get-tuple-element.219), channel_id=1, source_target_pairs={{0,16},{16,32},{32,48},{48,64},{64,80},{80,96},{96,112},{112,128},... | collective-permute-start | bytes 491528 | tf_op jit(solution)/shard_map/while/body/eval_jaxpr/ppermute | solution.py:12
  371.0 4.2 collective-permute-done
  377.0 6.4 %collective-permute-start = (bf16[10,64,128]{2,1,0:T(8,128)(2,1)}, bf16[10,64,128]{2,1,0:T(8,128)(2,1)S(1)}, u32[]{:S(2)}, u32[]{:S(2)}) collective-permute-start(bf16[10,64,128]{2,1,0:T(8,128)(2,1)} %get-tuple-element.219), channel_id=1, source_target_pairs={{0,16},{16,32},{32,48},{48,64},{64,80},{80,96},{96,112},{112,128},... | collective-permute-start | bytes 491528 | tf_op jit(solution)/shard_map/while/body/eval_jaxpr/ppermute | solution.py:12
  383.4 4.5 collective-permute-done
  389.7 6.4 %collective-permute-start = (bf16[10,64,128]{2,1,0:T(8,128)(2,1)}, bf16[10,64,128]{2,1,0:T(8,128)(2,1)S(1)}, u32[]{:S(2)}, u32[]{:S(2)}) collective-permute-start(bf16[10,64,128]{2,1,0:T(8,128)(2,1)} %get-tuple-element.219), channel_id=1, source_target_pairs={{0,16},{16,32},{32,48},{48,64},{64,80},{80,96},{96,112},{112,128},... | collective-permute-start | bytes 491528 | tf_op jit(solution)/shard_map/while/body/eval_jaxpr/ppermute | solution.py:12
  396.1 3.7 collective-permute-done
  401.6 6.4 %collective-permute-start = (bf16[10,64,128]{2,1,0:T(8,128)(2,1)}, bf16[10,64,128]{2,1,0:T(8,128)(2,1)S(1)}, u32[]{:S(2)}, u32[]{:S(2)}) collective-permute-start(bf16[10,64,128]{2,1,0:T(8,128)(2,1)} %get-tuple-element.219), channel_id=1, source_target_pairs={{0,16},{16,32},{32,48},{48,64},{64,80},{80,96},{96,112},{112,128},... | collective-permute-start | bytes 491528 | tf_op jit(solution)/shard_map/while/body/eval_jaxpr/ppermute | solution.py:12
  407.9 3.1 collective-permute-done
  412.9 6.4 %collective-permute-start = (bf16[10,64,128]{2,1,0:T(8,128)(2,1)}, bf16[10,64,128]{2,1,0:T(8,128)(2,1)S(1)}, u32[]{:S(2)}, u32[]{:S(2)}) collective-permute-start(bf16[10,64,128]{2,1,0:T(8,128)(2,1)} %get-tuple-element.219), channel_id=1, source_target_pairs={{0,16},{16,32},{32,48},{48,64},{64,80},{80,96},{96,112},{112,128},... | collective-permute-start | bytes 491528 | tf_op jit(solution)/shard_map/while/body/eval_jaxpr/ppermute | solution.py:12
  424.2 6.4 %collective-permute-start = (bf16[10,64,128]{2,1,0:T(8,128)(2,1)}, bf16[10,64,128]{2,1,0:T(8,128)(2,1)S(1)}, u32[]{:S(2)}, u32[]{:S(2)}) collective-permute-start(bf16[10,64,128]{2,1,0:T(8,128)(2,1)} %get-tuple-element.219), channel_id=1, source_target_pairs={{0,16},{16,32},{32,48},{48,64},{64,80},{80,96},{96,112},{112,128},... | collective-permute-start | bytes 491528 | tf_op jit(solution)/shard_map/while/body/eval_jaxpr/ppermute | solution.py:12
  439.9 23.3 %psum.7 = f32[512]{0:T(512)S(1)} all-reduce(f32[512]{0:T(512)S(1)} %multiply_reduce_fusion), channel_id=1, replica_groups=mesh['seq'=32,'tensor'=8,'dp'=2] {'tensor'}, use_global_device_ids=true, to_apply=%region_9.10 | all-reduce | flops 512 | bytes 4096 | tf_op jit(solution)/shard_map/psum | solution.py:131
  463.3 5.2 convolution_convert_fusion
  468.6 79.6 %reduce-scatter.2.cloned.1.call-done = bf16[512,320]{0,1:T(8,128)(2,1)} async-done(((bf16[512,2560]{0,1:T(8,128)(2,1)}), bf16[512,320]{0,1:T(8,128)(2,1)}) %reduce-scatter.2.cloned.1.call-update) | async-done | bytes 327696 | tf_op jit(solution)/shard_map/reduce_scatter | solution.py:135
  (165 shorter events, 140.8 us)
Async XLA Ops:
  6.5 456.8 %copy-start = (bf16[640,2560]{1,0:T(8,128)(2,1)S(1)}, bf16[640,2560]{1,0:T(8,128)(2,1)}, u32[]{:S(2)}) copy-start(bf16[640,2560]{1,0:T(8,128)(2,1)} %param.27) | copy-start | bytes 9830404
  6.5 17.4 %copy-start.25 = (f32[10]{0:T(128)S(1)}, f32[10]{0:T(128)}, u32[]{:S(2)}) copy-start(f32[10]{0:T(128)} %param.23) | copy-start | bytes 124
  6.5 17.4 %copy-start.17 = (bf16[10,512]{1,0:T(8,128)(2,1)S(1)}, bf16[10,512]{1,0:T(8,128)(2,1)}, u32[]{:S(2)}) copy-start(bf16[10,512]{1,0:T(8,128)(2,1)} %param.19) | copy-start | bytes 30724
  6.5 17.4 %copy-start.23 = (f32[10]{0:T(128)S(1)}, f32[10]{0:T(128)}, u32[]{:S(2)}) copy-start(f32[10]{0:T(128)} %param.24) | copy-start | bytes 124
  6.5 541.6 %reduce-scatter.2.cloned.1.call-start = ((), (), s32[]{:S(2)}) async-start(), calls=%async_computation.1 | async-start | bytes 2949120 | tf_op jit(solution)/shard_map/reduce_scatter | solution.py:135
  7.4 16.5 %copy-start.12 = (f32[512]{0:T(512)}, f32[512]{0:T(512)S(1)}, u32[]{:S(2)}) copy-start(f32[512]{0:T(512)S(1)} %get-tuple-element.122) | copy-start | bytes 6148
  8.0 34.6 %collective-permute-start.1 = (bf16[3]{0:T(256)(128)(2,1)}, bf16[3]{0:T(256)(128)(2,1)}, u32[]{:S(2)}, u32[]{:S(2)}) collective-permute-start(bf16[3]{0:T(256)(128)(2,1)} %slice.99), channel_id=1, source_target_pairs={{0,16},{16,32},{32,48},{48,64},{64,80},{80,96},{96,112},{112,128},... | collective-permute-start | bytes 26 | tf_op jit(solution)/shard_map/ppermute | solution.py:12
  13.0 43.8 %collective-permute-start.2 = (bf16[3,640]{0,1:T(8,128)(2,1)}, bf16[3,640]{0,1:T(8,128)(2,1)}, u32[]{:S(2)}, u32[]{:S(2)}) collective-permute-start(bf16[3,640]{0,1:T(8,128)(2,1)} %copy.46), channel_id=1, source_target_pairs={{0,16},{16,32},{32,48},{48,64},{64,80},{80,96},{96,112},{112,128},... | collective-permute-start | bytes 11528 | tf_op jit(solution)/shard_map/ppermute | solution.py:12
  17.7 36.5 %collective-permute-start.3 = (bf16[3,256]{1,0:T(4,128)(2,1)}, bf16[3,256]{1,0:T(4,128)(2,1)}, u32[]{:S(2)}, u32[]{:S(2)}) collective-permute-start(bf16[3,256]{1,0:T(4,128)(2,1)} %slice.111), channel_id=1, source_target_pairs={{0,16},{16,32},{32,48},{48,64},{64,80},{80,96},{96,112},{112,128},... | collective-permute-start | bytes 4616 | tf_op jit(solution)/shard_map/ppermute | solution.py:12
  26.1 28.0 %copy-start.7 = (bf16[512,256]{1,0:T(8,128)(2,1)S(1)}, bf16[512,256]{1,0:T(8,128)(2,1)}, u32[]{:S(2)}) copy-start(bf16[512,256]{1,0:T(8,128)(2,1)} %param.17) | copy-start | bytes 786436
  32.3 14.4 %copy-start.18 = (f32[10,2,1]{0,1,2:T(2,128)S(1)}, f32[10,2,1]{0,1,2:T(2,128)}, u32[]{:S(2)}) copy-start(f32[10,2,1]{0,1,2:T(2,128)} %copy.56) | copy-start | bytes 244
  46.6 0.8 copy-start.19
  47.4 0.5 copy-start.20
  49.3 7.5 %copy-start.3 = (bf16[512,640]{0,1:T(8,128)(2,1)S(1)}, bf16[512,640]{0,1:T(8,128)(2,1)}, u32[]{:S(2)}) copy-start(bf16[512,640]{0,1:T(8,128)(2,1)} %copy.45) | copy-start | bytes 1966084
  49.3 7.5 %copy-start.13 = (f32[640]{0:T(1024)S(1)}, f32[640]{0:T(1024)}, u32[]{:S(2)}) copy-start(f32[640]{0:T(1024)} %get-tuple-element.80) | copy-start | bytes 7684
  49.3 7.5 %copy-start.14 = (f32[640]{0:T(1024)S(1)}, f32[640]{0:T(1024)}, u32[]{:S(2)}) copy-start(f32[640]{0:T(1024)} %get-tuple-element.81) | copy-start | bytes 7684
  49.3 7.6 %copy-start.15 = (f32[640]{0:T(1024)S(1)}, f32[640]{0:T(1024)}, u32[]{:S(2)}) copy-start(f32[640]{0:T(1024)} %get-tuple-element.82) | copy-start | bytes 7684
  49.3 7.6 %copy-start.16 = (f32[640]{0:T(1024)S(1)}, f32[640]{0:T(1024)}, u32[]{:S(2)}) copy-start(f32[640]{0:T(1024)} %get-tuple-element.83) | copy-start | bytes 7684
  55.8 21.1 %copy-start.5 = (bf16[512,128]{1,0:T(8,128)(2,1)}, bf16[512,128]{1,0:T(8,128)(2,1)S(1)}, u32[]{:S(2)}) copy-start(bf16[512,128]{1,0:T(8,128)(2,1)S(1)} %get-tuple-element.109) | copy-start | bytes 393220
  60.3 5.4 copy-start.21
  65.7 7.9 %copy-start.10 = (pred[2,256,256]{2,1,0:T(8,128)(4,1)S(1)}, pred[2,256,256]{2,1,0:T(8,128)(4,1)}, u32[]{:S(2)}) copy-start(pred[2,256,256]{2,1,0:T(8,128)(4,1)} %compare_and_fusion) | copy-start | bytes 393220
  73.6 3.3 copy-start.1
  73.6 3.3 copy-start.6
  73.6 3.3 copy-start.9
  73.6 3.3 copy-start.22
  77.0 2.0 copy-start.11
  79.0 356.6 %copy-start.8 = (f32[2,256,10]{1,2,0:T(8,128)S(1)}, f32[2,256,10]{1,2,0:T(8,128)}, u32[]{:S(2)}) copy-start(f32[2,256,10]{1,2,0:T(8,128)} %copy.62) | copy-start | bytes 61444
  79.0 7.5 %collective-permute-start = (bf16[10,64,128]{2,1,0:T(8,128)(2,1)}, bf16[10,64,128]{2,1,0:T(8,128)(2,1)S(1)}, u32[]{:S(2)}, u32[]{:S(2)}) collective-permute-start(bf16[10,64,128]{2,1,0:T(8,128)(2,1)} %get-tuple-element.219), channel_id=1, source_target_pairs={{0,16},{16,32},{32,48},{48,64},{64,80},{80,96},{96,112},{112,128},... | collective-permute-start | bytes 491528 | tf_op jit(solution)/shard_map/while/body/eval_jaxpr/ppermute | solution.py:12
  88.3 8.4 %collective-permute-start = (bf16[10,64,128]{2,1,0:T(8,128)(2,1)}, bf16[10,64,128]{2,1,0:T(8,128)(2,1)S(1)}, u32[]{:S(2)}, u32[]{:S(2)}) collective-permute-start(bf16[10,64,128]{2,1,0:T(8,128)(2,1)} %get-tuple-element.219), channel_id=1, source_target_pairs={{0,16},{16,32},{32,48},{48,64},{64,80},{80,96},{96,112},{112,128},... | collective-permute-start | bytes 491528 | tf_op jit(solution)/shard_map/while/body/eval_jaxpr/ppermute | solution.py:12
  98.5 9.5 %collective-permute-start = (bf16[10,64,128]{2,1,0:T(8,128)(2,1)}, bf16[10,64,128]{2,1,0:T(8,128)(2,1)S(1)}, u32[]{:S(2)}, u32[]{:S(2)}) collective-permute-start(bf16[10,64,128]{2,1,0:T(8,128)(2,1)} %get-tuple-element.219), channel_id=1, source_target_pairs={{0,16},{16,32},{32,48},{48,64},{64,80},{80,96},{96,112},{112,128},... | collective-permute-start | bytes 491528 | tf_op jit(solution)/shard_map/while/body/eval_jaxpr/ppermute | solution.py:12
  109.8 9.5 %collective-permute-start = (bf16[10,64,128]{2,1,0:T(8,128)(2,1)}, bf16[10,64,128]{2,1,0:T(8,128)(2,1)S(1)}, u32[]{:S(2)}, u32[]{:S(2)}) collective-permute-start(bf16[10,64,128]{2,1,0:T(8,128)(2,1)} %get-tuple-element.219), channel_id=1, source_target_pairs={{0,16},{16,32},{32,48},{48,64},{64,80},{80,96},{96,112},{112,128},... | collective-permute-start | bytes 491528 | tf_op jit(solution)/shard_map/while/body/eval_jaxpr/ppermute | solution.py:12
  121.1 9.5 %collective-permute-start = (bf16[10,64,128]{2,1,0:T(8,128)(2,1)}, bf16[10,64,128]{2,1,0:T(8,128)(2,1)S(1)}, u32[]{:S(2)}, u32[]{:S(2)}) collective-permute-start(bf16[10,64,128]{2,1,0:T(8,128)(2,1)} %get-tuple-element.219), channel_id=1, source_target_pairs={{0,16},{16,32},{32,48},{48,64},{64,80},{80,96},{96,112},{112,128},... | collective-permute-start | bytes 491528 | tf_op jit(solution)/shard_map/while/body/eval_jaxpr/ppermute | solution.py:12
  132.5 9.5 %collective-permute-start = (bf16[10,64,128]{2,1,0:T(8,128)(2,1)}, bf16[10,64,128]{2,1,0:T(8,128)(2,1)S(1)}, u32[]{:S(2)}, u32[]{:S(2)}) collective-permute-start(bf16[10,64,128]{2,1,0:T(8,128)(2,1)} %get-tuple-element.219), channel_id=1, source_target_pairs={{0,16},{16,32},{32,48},{48,64},{64,80},{80,96},{96,112},{112,128},... | collective-permute-start | bytes 491528 | tf_op jit(solution)/shard_map/while/body/eval_jaxpr/ppermute | solution.py:12
  143.8 9.9 %collective-permute-start = (bf16[10,64,128]{2,1,0:T(8,128)(2,1)}, bf16[10,64,128]{2,1,0:T(8,128)(2,1)S(1)}, u32[]{:S(2)}, u32[]{:S(2)}) collective-permute-start(bf16[10,64,128]{2,1,0:T(8,128)(2,1)} %get-tuple-element.219), channel_id=1, source_target_pairs={{0,16},{16,32},{32,48},{48,64},{64,80},{80,96},{96,112},{112,128},... | collective-permute-start | bytes 491528 | tf_op jit(solution)/shard_map/while/body/eval_jaxpr/ppermute | solution.py:12
  155.5 11.1 %collective-permute-start = (bf16[10,64,128]{2,1,0:T(8,128)(2,1)}, bf16[10,64,128]{2,1,0:T(8,128)(2,1)S(1)}, u32[]{:S(2)}, u32[]{:S(2)}) collective-permute-start(bf16[10,64,128]{2,1,0:T(8,128)(2,1)} %get-tuple-element.219), channel_id=1, source_target_pairs={{0,16},{16,32},{32,48},{48,64},{64,80},{80,96},{96,112},{112,128},... | collective-permute-start | bytes 491528 | tf_op jit(solution)/shard_map/while/body/eval_jaxpr/ppermute | solution.py:12
  168.4 10.4 %collective-permute-start = (bf16[10,64,128]{2,1,0:T(8,128)(2,1)}, bf16[10,64,128]{2,1,0:T(8,128)(2,1)S(1)}, u32[]{:S(2)}, u32[]{:S(2)}) collective-permute-start(bf16[10,64,128]{2,1,0:T(8,128)(2,1)} %get-tuple-element.219), channel_id=1, source_target_pairs={{0,16},{16,32},{32,48},{48,64},{64,80},{80,96},{96,112},{112,128},... | collective-permute-start | bytes 491528 | tf_op jit(solution)/shard_map/while/body/eval_jaxpr/ppermute | solution.py:12
  180.6 9.6 %collective-permute-start = (bf16[10,64,128]{2,1,0:T(8,128)(2,1)}, bf16[10,64,128]{2,1,0:T(8,128)(2,1)S(1)}, u32[]{:S(2)}, u32[]{:S(2)}) collective-permute-start(bf16[10,64,128]{2,1,0:T(8,128)(2,1)} %get-tuple-element.219), channel_id=1, source_target_pairs={{0,16},{16,32},{32,48},{48,64},{64,80},{80,96},{96,112},{112,128},... | collective-permute-start | bytes 491528 | tf_op jit(solution)/shard_map/while/body/eval_jaxpr/ppermute | solution.py:12
  192.0 9.5 %collective-permute-start = (bf16[10,64,128]{2,1,0:T(8,128)(2,1)}, bf16[10,64,128]{2,1,0:T(8,128)(2,1)S(1)}, u32[]{:S(2)}, u32[]{:S(2)}) collective-permute-start(bf16[10,64,128]{2,1,0:T(8,128)(2,1)} %get-tuple-element.219), channel_id=1, source_target_pairs={{0,16},{16,32},{32,48},{48,64},{64,80},{80,96},{96,112},{112,128},... | collective-permute-start | bytes 491528 | tf_op jit(solution)/shard_map/while/body/eval_jaxpr/ppermute | solution.py:12
  203.4 9.5 %collective-permute-start = (bf16[10,64,128]{2,1,0:T(8,128)(2,1)}, bf16[10,64,128]{2,1,0:T(8,128)(2,1)S(1)}, u32[]{:S(2)}, u32[]{:S(2)}) collective-permute-start(bf16[10,64,128]{2,1,0:T(8,128)(2,1)} %get-tuple-element.219), channel_id=1, source_target_pairs={{0,16},{16,32},{32,48},{48,64},{64,80},{80,96},{96,112},{112,128},... | collective-permute-start | bytes 491528 | tf_op jit(solution)/shard_map/while/body/eval_jaxpr/ppermute | solution.py:12
  214.7 9.5 %collective-permute-start = (bf16[10,64,128]{2,1,0:T(8,128)(2,1)}, bf16[10,64,128]{2,1,0:T(8,128)(2,1)S(1)}, u32[]{:S(2)}, u32[]{:S(2)}) collective-permute-start(bf16[10,64,128]{2,1,0:T(8,128)(2,1)} %get-tuple-element.219), channel_id=1, source_target_pairs={{0,16},{16,32},{32,48},{48,64},{64,80},{80,96},{96,112},{112,128},... | collective-permute-start | bytes 491528 | tf_op jit(solution)/shard_map/while/body/eval_jaxpr/ppermute | solution.py:12
  226.0 9.5 %collective-permute-start = (bf16[10,64,128]{2,1,0:T(8,128)(2,1)}, bf16[10,64,128]{2,1,0:T(8,128)(2,1)S(1)}, u32[]{:S(2)}, u32[]{:S(2)}) collective-permute-start(bf16[10,64,128]{2,1,0:T(8,128)(2,1)} %get-tuple-element.219), channel_id=1, source_target_pairs={{0,16},{16,32},{32,48},{48,64},{64,80},{80,96},{96,112},{112,128},... | collective-permute-start | bytes 491528 | tf_op jit(solution)/shard_map/while/body/eval_jaxpr/ppermute | solution.py:12
  237.4 9.5 %collective-permute-start = (bf16[10,64,128]{2,1,0:T(8,128)(2,1)}, bf16[10,64,128]{2,1,0:T(8,128)(2,1)S(1)}, u32[]{:S(2)}, u32[]{:S(2)}) collective-permute-start(bf16[10,64,128]{2,1,0:T(8,128)(2,1)} %get-tuple-element.219), channel_id=1, source_target_pairs={{0,16},{16,32},{32,48},{48,64},{64,80},{80,96},{96,112},{112,128},... | collective-permute-start | bytes 491528 | tf_op jit(solution)/shard_map/while/body/eval_jaxpr/ppermute | solution.py:12
  248.7 9.7 %collective-permute-start = (bf16[10,64,128]{2,1,0:T(8,128)(2,1)}, bf16[10,64,128]{2,1,0:T(8,128)(2,1)S(1)}, u32[]{:S(2)}, u32[]{:S(2)}) collective-permute-start(bf16[10,64,128]{2,1,0:T(8,128)(2,1)} %get-tuple-element.219), channel_id=1, source_target_pairs={{0,16},{16,32},{32,48},{48,64},{64,80},{80,96},{96,112},{112,128},... | collective-permute-start | bytes 491528 | tf_op jit(solution)/shard_map/while/body/eval_jaxpr/ppermute | solution.py:12
  260.2 10.9 %collective-permute-start = (bf16[10,64,128]{2,1,0:T(8,128)(2,1)}, bf16[10,64,128]{2,1,0:T(8,128)(2,1)S(1)}, u32[]{:S(2)}, u32[]{:S(2)}) collective-permute-start(bf16[10,64,128]{2,1,0:T(8,128)(2,1)} %get-tuple-element.219), channel_id=1, source_target_pairs={{0,16},{16,32},{32,48},{48,64},{64,80},{80,96},{96,112},{112,128},... | collective-permute-start | bytes 491528 | tf_op jit(solution)/shard_map/while/body/eval_jaxpr/ppermute | solution.py:12
  272.9 10.5 %collective-permute-start = (bf16[10,64,128]{2,1,0:T(8,128)(2,1)}, bf16[10,64,128]{2,1,0:T(8,128)(2,1)S(1)}, u32[]{:S(2)}, u32[]{:S(2)}) collective-permute-start(bf16[10,64,128]{2,1,0:T(8,128)(2,1)} %get-tuple-element.219), channel_id=1, source_target_pairs={{0,16},{16,32},{32,48},{48,64},{64,80},{80,96},{96,112},{112,128},... | collective-permute-start | bytes 491528 | tf_op jit(solution)/shard_map/while/body/eval_jaxpr/ppermute | solution.py:12
  285.2 9.7 %collective-permute-start = (bf16[10,64,128]{2,1,0:T(8,128)(2,1)}, bf16[10,64,128]{2,1,0:T(8,128)(2,1)S(1)}, u32[]{:S(2)}, u32[]{:S(2)}) collective-permute-start(bf16[10,64,128]{2,1,0:T(8,128)(2,1)} %get-tuple-element.219), channel_id=1, source_target_pairs={{0,16},{16,32},{32,48},{48,64},{64,80},{80,96},{96,112},{112,128},... | collective-permute-start | bytes 491528 | tf_op jit(solution)/shard_map/while/body/eval_jaxpr/ppermute | solution.py:12
  296.7 9.5 %collective-permute-start = (bf16[10,64,128]{2,1,0:T(8,128)(2,1)}, bf16[10,64,128]{2,1,0:T(8,128)(2,1)S(1)}, u32[]{:S(2)}, u32[]{:S(2)}) collective-permute-start(bf16[10,64,128]{2,1,0:T(8,128)(2,1)} %get-tuple-element.219), channel_id=1, source_target_pairs={{0,16},{16,32},{32,48},{48,64},{64,80},{80,96},{96,112},{112,128},... | collective-permute-start | bytes 491528 | tf_op jit(solution)/shard_map/while/body/eval_jaxpr/ppermute | solution.py:12
  308.0 9.5 %collective-permute-start = (bf16[10,64,128]{2,1,0:T(8,128)(2,1)}, bf16[10,64,128]{2,1,0:T(8,128)(2,1)S(1)}, u32[]{:S(2)}, u32[]{:S(2)}) collective-permute-start(bf16[10,64,128]{2,1,0:T(8,128)(2,1)} %get-tuple-element.219), channel_id=1, source_target_pairs={{0,16},{16,32},{32,48},{48,64},{64,80},{80,96},{96,112},{112,128},... | collective-permute-start | bytes 491528 | tf_op jit(solution)/shard_map/while/body/eval_jaxpr/ppermute | solution.py:12
  319.3 9.5 %collective-permute-start = (bf16[10,64,128]{2,1,0:T(8,128)(2,1)}, bf16[10,64,128]{2,1,0:T(8,128)(2,1)S(1)}, u32[]{:S(2)}, u32[]{:S(2)}) collective-permute-start(bf16[10,64,128]{2,1,0:T(8,128)(2,1)} %get-tuple-element.219), channel_id=1, source_target_pairs={{0,16},{16,32},{32,48},{48,64},{64,80},{80,96},{96,112},{112,128},... | collective-permute-start | bytes 491528 | tf_op jit(solution)/shard_map/while/body/eval_jaxpr/ppermute | solution.py:12
  330.7 9.5 %collective-permute-start = (bf16[10,64,128]{2,1,0:T(8,128)(2,1)}, bf16[10,64,128]{2,1,0:T(8,128)(2,1)S(1)}, u32[]{:S(2)}, u32[]{:S(2)}) collective-permute-start(bf16[10,64,128]{2,1,0:T(8,128)(2,1)} %get-tuple-element.219), channel_id=1, source_target_pairs={{0,16},{16,32},{32,48},{48,64},{64,80},{80,96},{96,112},{112,128},... | collective-permute-start | bytes 491528 | tf_op jit(solution)/shard_map/while/body/eval_jaxpr/ppermute | solution.py:12
  342.0 9.5 %collective-permute-start = (bf16[10,64,128]{2,1,0:T(8,128)(2,1)}, bf16[10,64,128]{2,1,0:T(8,128)(2,1)S(1)}, u32[]{:S(2)}, u32[]{:S(2)}) collective-permute-start(bf16[10,64,128]{2,1,0:T(8,128)(2,1)} %get-tuple-element.219), channel_id=1, source_target_pairs={{0,16},{16,32},{32,48},{48,64},{64,80},{80,96},{96,112},{112,128},... | collective-permute-start | bytes 491528 | tf_op jit(solution)/shard_map/while/body/eval_jaxpr/ppermute | solution.py:12
  353.3 9.5 %collective-permute-start = (bf16[10,64,128]{2,1,0:T(8,128)(2,1)}, bf16[10,64,128]{2,1,0:T(8,128)(2,1)S(1)}, u32[]{:S(2)}, u32[]{:S(2)}) collective-permute-start(bf16[10,64,128]{2,1,0:T(8,128)(2,1)} %get-tuple-element.219), channel_id=1, source_target_pairs={{0,16},{16,32},{32,48},{48,64},{64,80},{80,96},{96,112},{112,128},... | collective-permute-start | bytes 491528 | tf_op jit(solution)/shard_map/while/body/eval_jaxpr/ppermute | solution.py:12
  364.7 10.6 %collective-permute-start = (bf16[10,64,128]{2,1,0:T(8,128)(2,1)}, bf16[10,64,128]{2,1,0:T(8,128)(2,1)S(1)}, u32[]{:S(2)}, u32[]{:S(2)}) collective-permute-start(bf16[10,64,128]{2,1,0:T(8,128)(2,1)} %get-tuple-element.219), channel_id=1, source_target_pairs={{0,16},{16,32},{32,48},{48,64},{64,80},{80,96},{96,112},{112,128},... | collective-permute-start | bytes 491528 | tf_op jit(solution)/shard_map/while/body/eval_jaxpr/ppermute | solution.py:12
  377.0 10.8 %collective-permute-start = (bf16[10,64,128]{2,1,0:T(8,128)(2,1)}, bf16[10,64,128]{2,1,0:T(8,128)(2,1)S(1)}, u32[]{:S(2)}, u32[]{:S(2)}) collective-permute-start(bf16[10,64,128]{2,1,0:T(8,128)(2,1)} %get-tuple-element.219), channel_id=1, source_target_pairs={{0,16},{16,32},{32,48},{48,64},{64,80},{80,96},{96,112},{112,128},... | collective-permute-start | bytes 491528 | tf_op jit(solution)/shard_map/while/body/eval_jaxpr/ppermute | solution.py:12
  389.7 10.1 %collective-permute-start = (bf16[10,64,128]{2,1,0:T(8,128)(2,1)}, bf16[10,64,128]{2,1,0:T(8,128)(2,1)S(1)}, u32[]{:S(2)}, u32[]{:S(2)}) collective-permute-start(bf16[10,64,128]{2,1,0:T(8,128)(2,1)} %get-tuple-element.219), channel_id=1, source_target_pairs={{0,16},{16,32},{32,48},{48,64},{64,80},{80,96},{96,112},{112,128},... | collective-permute-start | bytes 491528 | tf_op jit(solution)/shard_map/while/body/eval_jaxpr/ppermute | solution.py:12
  401.6 9.5 %collective-permute-start = (bf16[10,64,128]{2,1,0:T(8,128)(2,1)}, bf16[10,64,128]{2,1,0:T(8,128)(2,1)S(1)}, u32[]{:S(2)}, u32[]{:S(2)}) collective-permute-start(bf16[10,64,128]{2,1,0:T(8,128)(2,1)} %get-tuple-element.219), channel_id=1, source_target_pairs={{0,16},{16,32},{32,48},{48,64},{64,80},{80,96},{96,112},{112,128},... | collective-permute-start | bytes 491528 | tf_op jit(solution)/shard_map/while/body/eval_jaxpr/ppermute | solution.py:12
  412.9 9.5 %collective-permute-start = (bf16[10,64,128]{2,1,0:T(8,128)(2,1)}, bf16[10,64,128]{2,1,0:T(8,128)(2,1)S(1)}, u32[]{:S(2)}, u32[]{:S(2)}) collective-permute-start(bf16[10,64,128]{2,1,0:T(8,128)(2,1)} %get-tuple-element.219), channel_id=1, source_target_pairs={{0,16},{16,32},{32,48},{48,64},{64,80},{80,96},{96,112},{112,128},... | collective-permute-start | bytes 491528 | tf_op jit(solution)/shard_map/while/body/eval_jaxpr/ppermute | solution.py:12
  424.2 9.5 %collective-permute-start = (bf16[10,64,128]{2,1,0:T(8,128)(2,1)}, bf16[10,64,128]{2,1,0:T(8,128)(2,1)S(1)}, u32[]{:S(2)}, u32[]{:S(2)}) collective-permute-start(bf16[10,64,128]{2,1,0:T(8,128)(2,1)} %get-tuple-element.219), channel_id=1, source_target_pairs={{0,16},{16,32},{32,48},{48,64},{64,80},{80,96},{96,112},{112,128},... | collective-permute-start | bytes 491528 | tf_op jit(solution)/shard_map/while/body/eval_jaxpr/ppermute | solution.py:12
  437.7 1.7 copy-start.2
  438.4 24.9 %copy-start.24 = (f32[640]{0:T(1024)S(1)}, f32[640]{0:T(1024)}, u32[]{:S(2)}) copy-start(f32[640]{0:T(1024)} %param.26) | copy-start | bytes 7684
  438.6 0.8 copy-start.4
Sparse Core Ops, SparseCore 0:
  468.7 79.4 reduce-scatter.1
where the time goes:
time: 559 us; the launch traced here: 555 us
  starting transfers between devices  204 us (36%)
  waiting for transfers between devices  186 us (33%)
  other arithmetic  84.4 us (15%)
  local copies, waits for them, and re-layouts  26.8 us (5%)
  blocking collectives  23.3 us (4%)
  matrix products  16.5 us (3%)
  between operations  13.7 us (2%)
    ppermute x34, starting transfers between devices, from_behind(): return lax.ppermute(block, axis, route)  204 us
    ppermute x34, waiting for transfers between devices, from_behind(): return lax.ppermute(block, axis, route)  107 us
    reduce_scatter x1, waiting for transfers between devices, local(): lax.psum_scatter(partial_value.astype(jnp.bfloat16), 'tensor', scatter_di...  79.6 us
    add x31, other arithmetic, hand_on(): return (device_decay[:, None, None] * passed + local_final, passed)  56 us
    psum x1, blocking collectives, local(): squares = lax.psum(jnp.sum(gated * gated, axis=1), 'tensor')  23.3 us
  transfers between devices with their start and end apart: 35, of which 32 were waited for; matrix products, arithmetic and copies ran while one was open for 7% of the time, Pallas kernels for 0%

commit v1 on v0

--- a/solution.py
+++ b/solution.py
@@ -28,14 +28,21 @@
 
 
 def pass_state(device_decay, local_final):
-
-    def hand_on(counter, carry_pair):
-        passed = from_behind(carry_pair[0].astype(jnp.bfloat16), "seq", 1).astype(jnp.float32)
-        return (device_decay[:, None, None] * passed + local_final, passed)
-
-    return lax.fori_loop(
-        0, lax.axis_size("seq") - 1, hand_on, (local_final, jnp.zeros_like(local_final))
-    )[1]
+    shard_count = lax.axis_size("seq")
+    decay, state = device_decay, local_final
+    window = 1
+    while 2 * window < shard_count - 1:
+        prev_decay, prev_state = from_behind((decay, state.astype(jnp.bfloat16)), "seq", window)
+        state = decay[:, None, None] * prev_state.astype(jnp.float32) + state
+        decay = decay * prev_decay
+        window *= 2
+    near_decay, near_state = from_behind((decay, state.astype(jnp.bfloat16)), "seq", 1)
+    if window + 1 < shard_count:
+        far_state = from_behind(state.astype(jnp.bfloat16), "seq", window + 1)
+        return near_decay[:, None, None] * far_state.astype(jnp.float32) + near_state.astype(
+            jnp.float32
+        )
+    return near_state.astype(jnp.float32)
 
 
 def local(

time: 559 us -> 215 us (0.38)
  starting transfers between devices: 204 us -> 69.8 us
  waiting for transfers between devices: 186 us -> 55.6 us
  other arithmetic: 84.4 us -> 21.9 us
  local copies, waits for them, and re-layouts: 26.8 us -> 17.5 us
    ppermute x34 -> x14, starting transfers between devices: 204 us -> 69.8 us  [from_behind(): return lax.ppermute(block, axis, route)]
    ppermute x34 -> x14, waiting for transfers between devices: 107 us -> 15 us  [from_behind(): return lax.ppermute(block, axis, route)]
    add x31 -> x0, other arithmetic: 56 us -> none  [hand_on(): return (device_decay[:, None, None] * passed + local_final, passed)]
    reduce_scatter x1, waiting for transfers between devices: 79.6 us -> 40.6 us  [local(): lax.psum_scatter(partial_value.astype(jnp.bfloat16), 'tensor', scatter_di...]
  transfers between devices with their start and end apart: 35 -> 15, of which waited for: 32 -> 7; matrix products, arithmetic and copies ran while one was open for 7% -> 11% of each run, Pallas kernels for 0% -> 0%
where the time goes in v1:
time: 215 us; the launch traced here: 214 us
  starting transfers between devices  69.8 us (32%)
  waiting for transfers between devices  55.6 us (26%)
  blocking collectives  23.4 us (11%)
  other arithmetic  21.9 us (10%)
  local copies, waits for them, and re-layouts  17.5 us (8%)
  between operations  13.9 us (6%)
  matrix products  11.8 us (5%)
    ppermute x14, starting transfers between devices, from_behind(): return lax.ppermute(block, axis, route)  69.8 us
    reduce_scatter x1, waiting for transfers between devices, local(): lax.psum_scatter(partial_value.astype(jnp.bfloat16), 'tensor', scatter_di...  40.6 us
    psum x1, blocking collectives, local(): squares = lax.psum(jnp.sum(gated * gated, axis=1), 'tensor')  23.4 us
    ppermute x14, waiting for transfers between devices, from_behind(): return lax.ppermute(block, axis, route)  15 us
    convert_element_type x2, other arithmetic, causal_conv(): return jax.nn.silu(total).astype(jnp.bfloat16)  5.65 us
    unnamed x45, local copies, waits for them, and re-layouts  5.38 us
    dot_general x1, matrix products, local(): partial_value = jnp.dot(normed, w_out, preferred_element_type=jnp.float32)  5.24 us
  transfers between devices with their start and end apart: 15, of which 7 were waited for; matrix products, arithmetic and copies ran while one was open for 11% of the time, Pallas kernels for 0%

profile of v1, /device:TPU:6, one launch (start us, length us, event | category | flops | bytes accessed | tf_op | source)
XLA Modules:
  0.0 214.0 jit_solution(12981406027322690598)
XLA Ops:
  6.6 0.8 convert_convert_fusion
  7.5 3.5 %collective-permute-start = (bf16[3]{0:T(256)(128)(2,1)S(1)}, bf16[3]{0:T(256)(128)(2,1)S(1)}, u32[]{:S(2)}, u32[]{:S(2)}) collective-permute-start(bf16[3]{0:T(256)(128)(2,1)S(1)} %slice.99), channel_id=1, source_target_pairs={{0,16},{16,32},{32,48},{48,64},{64,80},{80,96},{96,112},{112,128},... | collective-permute-start | bytes 26 | tf_op jit(solution)/shard_map/ppermute | solution.py:12
  11.1 0.7 slice.101
  11.8 0.8 copy.46
  12.6 3.4 %collective-permute-start.1 = (bf16[3,640]{0,1:T(8,128)(2,1)}, bf16[3,640]{0,1:T(8,128)(2,1)}, u32[]{:S(2)}, u32[]{:S(2)}) collective-permute-start(bf16[3,640]{0,1:T(8,128)(2,1)} %copy.46), channel_id=1, source_target_pairs={{0,16},{16,32},{32,48},{48,64},{64,80},{80,96},{96,112},{112,128},... | collective-permute-start | bytes 11528 | tf_op jit(solution)/shard_map/ppermute | solution.py:12
  16.0 0.7 slice.111
  16.7 3.4 %collective-permute-start.2 = (bf16[3,256]{1,0:T(4,128)(2,1)S(1)}, bf16[3,256]{1,0:T(4,128)(2,1)S(1)}, u32[]{:S(2)}, u32[]{:S(2)}) collective-permute-start(bf16[3,256]{1,0:T(4,128)(2,1)S(1)} %slice.111), channel_id=1, source_target_pairs={{0,16},{16,32},{32,48},{48,64},{64,80},{80,96},{96,112},{112,128},... | collective-permute-start | bytes 4616 | tf_op jit(solution)/shard_map/ppermute | solution.py:12
  20.2 2.2 %copy.45 = bf16[512,640]{0,1:T(8,128)(2,1)} copy(bf16[512,640]{1,0:T(8,128)(2,1)} %param.14) | data formatting | bytes 1310720 | tf_op args[0]
  22.4 0.2 slice_reduce_fusion.1
  22.7 1.2 reduce-window.9
  23.9 0.1 copy.49
  24.6 0.6 convert_reduce_fusion.3
  25.2 0.6 slice.122
  25.8 0.7 pad_maximum_fusion.3
  26.5 0.2 slice_reduce_fusion
  26.7 0.7 fusion.40
  27.6 0.7 multiply_bitcast_fusion
  28.4 0.6 copy.59
  29.0 2.2 %multiply_convert_fusion.7 = bf16[512,256]{1,0:T(8,128)(2,1)S(1)} fusion(bf16[512,256]{1,0:T(8,128)(2,1)} %param.15, bf16[3,256]{1,0:T(4,128)(2,1)S(1)} %collective-permute-done.2, f32[256]{0:T(256)S(1)} %bitcast.69, f32[256]{0:T(256)S(1)} %bitcast.70, f32[256]{0:T(256)S(1)} %bitcast.68, f32[256]{0:T(256)S(1)} %bitcast.67, ...), kind=kLoop, calls=%fused_computation.42 | loop fusion | flops 3801088 | bytes 531968 | tf_op jit(solution)/shard_map/convert_element_type | solution.py:27
  31.2 3.5 %multiply_convert_fusion.5 = bf16[512,640]{0,1:T(8,128)(2,1)} fusion(bf16[512,640]{0,1:T(8,128)(2,1)S(1)} %copy-done.3, bf16[3,640]{0,1:T(8,128)(2,1)} %collective-permute-done.1, f32[640]{0:T(1024)S(1)} %get-tuple-element.55, f32[640]{0:T(1024)} %get-tuple-element.56, f32[640]{0:T(1024)S(1)} %get-tuple-element.54, f32[640]{0:T(1024)S(1)} %get-tuple-element.53, ...), kind=kLoop, calls=%fused_computation.31 | loop fusion | flops 9502720 | bytes 1326848 | tf_op jit(solution)/shard_map/convert_element_type | solution.py:27
  34.7 2.7 %reshape.119 = bf16[2,256,10,64]{1,0,3,2:T(2,128)(2,1)} reshape(bf16[512,640]{0,1:T(8,128)(2,1)} %multiply_convert_fusion.5) | data formatting | bytes 1310720 | tf_op jit(solution)/shard_map/reshape | solution.py:87
  37.4 2.7 %fusion.13 = f32[2,10,64,128]{3,2,1,0:T(8,128)} fusion(bf16[2,256,128,1]{2,1,3,0:T(8,128)(2,1)S(1)} %bitcast.63, f32[2,256,10]{1,2,0:T(8,128)} %copy.59, bf16[2,256,10,64]{1,0,3,2:T(2,128)(2,1)} %reshape.119), kind=kOutput, calls=%fused_computation.24 | convolution fusion | flops 503971840 | bytes 1462272 | tf_op jit(solution)/shard_map/cshp,csn->chpn/dot_general | solution.py:102
  40.1 6.2 %while.13 = (s32[]{:T(128)}, f32[10,64,128]{2,1,0:T(8,128)}, f32[2,10,64,128]{3,2,1,0:T(8,128)}, f32[2,10]{1,0:T(2,128)S(1)}, f32[2,10,64,128]{3,2,1,0:T(8,128)}, /*index=5*/s32[]{:T(128)}, s32[]{:T(128)}) while((s32[]{:T(128)}, f32[10,64,128]{2,1,0:T(8,128)}, f32[2,10,64,128]{3,2,1,0:T(8,128)}, f32[2,10]{1,0:T(2,128)S(1)}, ...), condition=%wide.region_3.4_spmd.clone, body=%wide.region_2.3_spmd.clone.sunk | while | flops 327683 | bytes 1639128 | solution.py:114
  40.1 0.8 bitcast_dynamic-update-slice_fusion.2
  40.9 1.8 bitcast_add_fusion.2
  42.7 1.7 bitcast_dynamic-update-slice_fusion.2
  44.4 1.9 bitcast_add_fusion.2
  46.3 1.7 convert_element_type.132
  48.0 3.1 %collective-permute-start.8 = (bf16[10,64,128]{2,1,0:T(8,128)(2,1)}, bf16[10,64,128]{2,1,0:T(8,128)(2,1)}, u32[]{:S(2)}, u32[]{:S(2)}) collective-permute-start(bf16[10,64,128]{2,1,0:T(8,128)(2,1)} %convert_element_type.132), channel_id=1, source_target_pairs={{0,16},{16,32},{32,48},{48,64},{64,80},{80,96},{96,112},{112,128},... | collective-permute-start | bytes 491528 | tf_op jit(solution)/shard_map/ppermute | solution.py:12
  51.1 1.3 copy.52
  52.5 1.3 copy.54
  53.8 2.2 %copy.64 = bf16[512,640]{0,1:T(8,128)(2,1)} copy(bf16[512,640]{1,0:T(8,128)(2,1)} %param.16) | data formatting | bytes 1310720 | tf_op args[2]
  56.0 1.1 fusion.32
  57.1 4.3 %collective-permute-start.9 = (bf16[10,64,128]{2,1,0:T(8,128)(2,1)S(1)}, bf16[10,64,128]{2,1,0:T(8,128)(2,1)S(1)}, u32[]{:S(2)}, u32[]{:S(2)}) collective-permute-start(bf16[10,64,128]{2,1,0:T(8,128)(2,1)S(1)} %fusion.32), channel_id=1, source_target_pairs={{0,32},{16,48},{32,64},{48,80},{64,96},{80,112},{96,128},{112,144}... | collective-permute-start | bytes 491528 | tf_op jit(solution)/shard_map/ppermute | solution.py:12
  61.5 0.2 compare_and_fusion
  61.6 4.0 %collective-permute-start.3 = (f32[10]{0:T(128)S(1)}, f32[10]{0:T(128)S(1)}, u32[]{:S(2)}, u32[]{:S(2)}) collective-permute-start(f32[10]{0:T(128)S(1)} %copy-done.14), channel_id=1, source_target_pairs={{0,16},{16,32},{32,48},{48,64},{64,80},{80,96},{96,112},{112,128},... | collective-permute-start | bytes 128 | tf_op jit(solution)/shard_map/ppermute | solution.py:12
  65.7 0.7 copy.60
  66.4 0.7 copy.62
  67.2 4.3 %collective-permute-start.4 = (f32[10]{0:T(128)S(1)}, f32[10]{0:T(128)S(1)}, u32[]{:S(2)}, u32[]{:S(2)}) collective-permute-start(f32[10]{0:T(128)S(1)} %mul.318), channel_id=1, source_target_pairs={{0,32},{16,48},{32,64},{48,80},{64,96},{80,112},{96,128},{112,144}... | collective-permute-start | bytes 128 | tf_op jit(solution)/shard_map/ppermute | solution.py:12
  71.4 2.8 %collective-permute-done.4 = f32[10]{0:T(128)S(1)} collective-permute-done((f32[10]{0:T(128)S(1)}, f32[10]{0:T(128)S(1)}, u32[]{:S(2)}, u32[]{:S(2)}) %collective-permute-start.4) | collective-permute-done | bytes 72 | tf_op jit(solution)/shard_map/ppermute | solution.py:12
  74.2 3.5 %collective-permute-start.5 = (f32[10]{0:T(128)S(1)}, f32[10]{0:T(128)S(1)}, u32[]{:S(2)}, u32[]{:S(2)}) collective-permute-start(f32[10]{0:T(128)S(1)} %mul.319), channel_id=1, source_target_pairs={{0,64},{16,80},{32,96},{48,112},{64,128},{80,144},{96,160},{112,17... | collective-permute-start | bytes 128 | tf_op jit(solution)/shard_map/ppermute | solution.py:12
  77.7 1.3 collective-permute-done.5
  79.0 6.4 %collective-permute-start.6 = (f32[10]{0:T(128)S(1)}, f32[10]{0:T(128)S(1)}, u32[]{:S(2)}, u32[]{:S(2)}) collective-permute-start(f32[10]{0:T(128)S(1)} %mul.320), channel_id=1, source_target_pairs={{0,128},{16,144},{32,160},{48,176},{64,192},{80,208},{96,224},{112... | collective-permute-start | bytes 128 | tf_op jit(solution)/shard_map/ppermute | solution.py:12
  85.4 1.3 collective-permute-done.6
  86.6 8.1 %collective-permute-start.7 = (f32[10]{0:T(128)S(1)}, f32[10]{0:T(128)S(1)}, u32[]{:S(2)}, u32[]{:S(2)}) collective-permute-start(f32[10]{0:T(128)S(1)} %mul.321), channel_id=1, source_target_pairs={{0,16},{16,32},{32,48},{48,64},{64,80},{80,96},{96,112},{112,128},... | collective-permute-start | bytes 128 | tf_op jit(solution)/shard_map/ppermute | solution.py:12
  94.7 1.2 fusion.39
  95.9 5.4 %collective-permute-start.10 = (bf16[10,64,128]{2,1,0:T(8,128)(2,1)S(1)}, bf16[10,64,128]{2,1,0:T(8,128)(2,1)S(1)}, u32[]{:S(2)}, u32[]{:S(2)}) collective-permute-start(bf16[10,64,128]{2,1,0:T(8,128)(2,1)S(1)} %get-tuple-element.67), channel_id=1, source_target_pairs={{0,64},{16,80},{32,96},{48,112},{64,128},{80,144},{96,160},{112,17... | collective-permute-start | bytes 491528 | tf_op jit(solution)/shard_map/ppermute | solution.py:12
  101.3 0.2 fusion.42
  101.5 3.6 %collective-permute-done.10 = bf16[10,64,128]{2,1,0:T(8,128)(2,1)S(1)} collective-permute-done((bf16[10,64,128]{2,1,0:T(8,128)(2,1)S(1)}, bf16[10,64,128]{2,1,0:T(8,128)(2,1)S(1)}, u32[]{:S(2)}, u32[]{:S(2)}) %collective-permute-start.10) | collective-permute-done | bytes 163872 | tf_op jit(solution)/shard_map/ppermute | solution.py:12
  105.3 8.3 %collective-permute-start.11 = (bf16[10,64,128]{2,1,0:T(8,128)(2,1)S(1)}, bf16[10,64,128]{2,1,0:T(8,128)(2,1)S(1)}, u32[]{:S(2)}, u32[]{:S(2)}) collective-permute-start(bf16[10,64,128]{2,1,0:T(8,128)(2,1)S(1)} %fusion.33), channel_id=1, source_target_pairs={{0,128},{16,144},{32,160},{48,176},{64,192},{80,208},{96,224},{112... | collective-permute-start | bytes 491528 | tf_op jit(solution)/shard_map/ppermute | solution.py:12
  113.6 2.0 fusion.9
  115.6 1.7 collective-permute-done.11
  117.3 0.1 add_convert_fusion
  117.4 10.2 %collective-permute-start.12 = (bf16[10,64,128]{2,1,0:T(8,128)(2,1)S(1)}, bf16[10,64,128]{2,1,0:T(8,128)(2,1)S(1)}, u32[]{:S(2)}, u32[]{:S(2)}) collective-permute-start(bf16[10,64,128]{2,1,0:T(8,128)(2,1)S(1)} %add_convert_fusion), channel_id=1, source_target_pairs={{0,272},{16,288},{32,304},{48,320},{64,336},{80,352},{96,368},{112... | collective-permute-start | bytes 491528 | tf_op jit(solution)/shard_map/ppermute | solution.py:12
  127.7 1.9 collective-permute-start.13
  129.6 0.9 fusion.11
  130.5 4.3 %collective-permute-done.13 = bf16[10,64,128]{2,1,0:T(8,128)(2,1)S(1)} collective-permute-done((bf16[10,64,128]{2,1,0:T(8,128)(2,1)S(1)}, bf16[10,64,128]{2,1,0:T(8,128)(2,1)S(1)}, u32[]{:S(2)}, u32[]{:S(2)}) %collective-permute-start.13) | collective-permute-done | bytes 163872 | tf_op jit(solution)/shard_map/ppermute | solution.py:12
  134.9 0.8 fusion.12
  135.7 0.7 copy.63
  136.5 0.8 copy-done.4
  137.3 0.5 multiply_reduce_fusion
  137.9 23.4 %psum.7 = f32[512]{0:T(512)S(1)} all-reduce(f32[512]{0:T(512)S(1)} %multiply_reduce_fusion), channel_id=1, replica_groups=mesh['seq'=32,'tensor'=8,'dp'=2] {'tensor'}, use_global_device_ids=true, to_apply=%region_7.8 | all-reduce | flops 512 | bytes 4096 | tf_op jit(solution)/shard_map/psum | solution.py:138
  161.2 5.2 %convolution_convert_fusion = bf16[512,2560]{0,1:T(8,128)(2,1)} fusion(bf16[640,2560]{1,0:T(8,128)(2,1)S(1)} %copy-done, f32[640]{0:T(1024)S(1)} %copy-done.19, f32[512]{0:T(512)S(1)} %add_rsqrt_fusion, bf16[512,640]{0,1:T(8,128)(2,1)} %copy.64, bf16[512,640]{0,1:T(8,128)(2,1)} %bitcast.58), kind=kOutput, calls=%fused_computation.5 | convolution fusion | flops 1682309120 | bytes 7213568 | tf_op jit(solution)/shard_map/dot_general | solution.py:141
  166.5 40.6 %reduce-scatter.2.cloned.1.call-done = bf16[512,320]{0,1:T(8,128)(2,1)} async-done(((bf16[512,2560]{0,1:T(8,128)(2,1)}), bf16[512,320]{0,1:T(8,128)(2,1)}) %reduce-scatter.2.cloned.1.call-update) | async-done | bytes 327696 | tf_op jit(solution)/shard_map/reduce_scatter | solution.py:142
  (90 shorter events, 1.7 us)
Async XLA Ops:
  6.5 154.7 %copy-start = (bf16[640,2560]{1,0:T(8,128)(2,1)S(1)}, bf16[640,2560]{1,0:T(8,128)(2,1)}, u32[]{:S(2)}) copy-start(bf16[640,2560]{1,0:T(8,128)(2,1)} %param.25) | copy-start | bytes 9830404
  6.5 21.8 %copy-start.12 = (s32[512]{0:T(512)S(1)}, s32[512]{0:T(512)}, u32[]{:S(2)}) copy-start(s32[512]{0:T(512)} %param.18) | copy-start | bytes 6148
  6.5 16.0 %copy-start.20 = (f32[10]{0:T(128)S(1)}, f32[10]{0:T(128)}, u32[]{:S(2)}) copy-start(f32[10]{0:T(128)} %param.21) | copy-start | bytes 124
  6.5 16.0 %copy-start.11 = (bf16[10,512]{1,0:T(8,128)(2,1)S(1)}, bf16[10,512]{1,0:T(8,128)(2,1)}, u32[]{:S(2)}) copy-start(bf16[10,512]{1,0:T(8,128)(2,1)} %param.17) | copy-start | bytes 30724
  6.5 16.0 %copy-start.18 = (f32[10]{0:T(128)S(1)}, f32[10]{0:T(128)}, u32[]{:S(2)}) copy-start(f32[10]{0:T(128)} %param.22) | copy-start | bytes 124
  6.5 18.0 %copy-start.10 = (bf16[4,640]{1,0:T(4,128)(2,1)S(1)}, bf16[4,640]{1,0:T(4,128)(2,1)}, u32[]{:S(2)}) copy-start(bf16[4,640]{1,0:T(4,128)(2,1)} %param.19) | copy-start | bytes 15364
  6.6 18.6 %copy-start.13 = (bf16[4,256]{1,0:T(4,128)(2,1)S(1)}, bf16[4,256]{1,0:T(4,128)(2,1)}, u32[]{:S(2)}) copy-start(bf16[4,256]{1,0:T(4,128)(2,1)} %param.20) | copy-start | bytes 6148
  6.6 200.6 %reduce-scatter.2.cloned.1.call-start = ((), (), s32[]{:S(2)}) async-start(), calls=%async_computation.1 | async-start | bytes 2949120 | tf_op jit(solution)/shard_map/reduce_scatter | solution.py:142
  7.5 17.7 %collective-permute-start = (bf16[3]{0:T(256)(128)(2,1)S(1)}, bf16[3]{0:T(256)(128)(2,1)S(1)}, u32[]{:S(2)}, u32[]{:S(2)}) collective-permute-start(bf16[3]{0:T(256)(128)(2,1)S(1)} %slice.99), channel_id=1, source_target_pairs={{0,16},{16,32},{32,48},{48,64},{64,80},{80,96},{96,112},{112,128},... | collective-permute-start | bytes 26 | tf_op jit(solution)/shard_map/ppermute | solution.py:12
  12.6 18.6 %collective-permute-start.1 = (bf16[3,640]{0,1:T(8,128)(2,1)}, bf16[3,640]{0,1:T(8,128)(2,1)}, u32[]{:S(2)}, u32[]{:S(2)}) collective-permute-start(bf16[3,640]{0,1:T(8,128)(2,1)} %copy.46), channel_id=1, source_target_pairs={{0,16},{16,32},{32,48},{48,64},{64,80},{80,96},{96,112},{112,128},... | collective-permute-start | bytes 11528 | tf_op jit(solution)/shard_map/ppermute | solution.py:12
  16.7 12.3 %collective-permute-start.2 = (bf16[3,256]{1,0:T(4,128)(2,1)S(1)}, bf16[3,256]{1,0:T(4,128)(2,1)S(1)}, u32[]{:S(2)}, u32[]{:S(2)}) collective-permute-start(bf16[3,256]{1,0:T(4,128)(2,1)S(1)} %slice.111), channel_id=1, source_target_pairs={{0,16},{16,32},{32,48},{48,64},{64,80},{80,96},{96,112},{112,128},... | collective-permute-start | bytes 4616 | tf_op jit(solution)/shard_map/ppermute | solution.py:12
  24.3 4.7 %copy-start.6 = (f32[10,2,256]{2,1,0:T(2,128)}, f32[10,2,256]{2,1,0:T(2,128)S(1)}, u32[]{:S(2)}) copy-start(f32[10,2,256]{2,1,0:T(2,128)S(1)} %reduce_window_sum.24) | copy-start | bytes 61444
  24.6 4.4 %copy-start.7 = (f32[10,2,256]{2,1,0:T(2,128)}, f32[10,2,256]{2,1,0:T(2,128)S(1)}, u32[]{:S(2)}) copy-start(f32[10,2,256]{2,1,0:T(2,128)S(1)} %mul.308) | copy-start | bytes 61444
  27.4 1.6 copy-start.15
  27.5 3.7 %copy-start.3 = (bf16[512,640]{0,1:T(8,128)(2,1)S(1)}, bf16[512,640]{0,1:T(8,128)(2,1)}, u32[]{:S(2)}) copy-start(bf16[512,640]{0,1:T(8,128)(2,1)} %copy.45) | copy-start | bytes 1966084
  34.7 5.4 %copy-start.16 = (f32[10,2]{0,1:T(2,128)S(1)}, f32[10,2]{0,1:T(2,128)}, u32[]{:S(2)}) copy-start(f32[10,2]{0,1:T(2,128)} %copy-done.15) | copy-start | bytes 244
  46.3 9.7 %copy-start.14 = (f32[10]{0:T(128)S(1)}, f32[10]{0:T(128)}, u32[]{:S(2)}) copy-start(f32[10]{0:T(128)} %get-tuple-element.69) | copy-start | bytes 124
  48.0 8.0 %collective-permute-start.8 = (bf16[10,64,128]{2,1,0:T(8,128)(2,1)}, bf16[10,64,128]{2,1,0:T(8,128)(2,1)}, u32[]{:S(2)}, u32[]{:S(2)}) collective-permute-start(bf16[10,64,128]{2,1,0:T(8,128)(2,1)} %convert_element_type.132), channel_id=1, source_target_pairs={{0,16},{16,32},{32,48},{48,64},{64,80},{80,96},{96,112},{112,128},... | collective-permute-start | bytes 491528 | tf_op jit(solution)/shard_map/ppermute | solution.py:12
  57.1 37.6 %collective-permute-start.9 = (bf16[10,64,128]{2,1,0:T(8,128)(2,1)S(1)}, bf16[10,64,128]{2,1,0:T(8,128)(2,1)S(1)}, u32[]{:S(2)}, u32[]{:S(2)}) collective-permute-start(bf16[10,64,128]{2,1,0:T(8,128)(2,1)S(1)} %fusion.32), channel_id=1, source_target_pairs={{0,32},{16,48},{32,64},{48,80},{64,96},{80,112},{96,128},{112,144}... | collective-permute-start | bytes 491528 | tf_op jit(solution)/shard_map/ppermute | solution.py:12
  61.6 5.5 %collective-permute-start.3 = (f32[10]{0:T(128)S(1)}, f32[10]{0:T(128)S(1)}, u32[]{:S(2)}, u32[]{:S(2)}) collective-permute-start(f32[10]{0:T(128)S(1)} %copy-done.14), channel_id=1, source_target_pairs={{0,16},{16,32},{32,48},{48,64},{64,80},{80,96},{96,112},{112,128},... | collective-permute-start | bytes 128 | tf_op jit(solution)/shard_map/ppermute | solution.py:12
  67.1 46.5 %copy-start.1 = (bf16[2,256,10,64]{1,0,3,2:T(2,128)(2,1)S(1)}, bf16[2,256,10,64]{1,0,3,2:T(2,128)(2,1)}, u32[]{:S(2)}) copy-start(bf16[2,256,10,64]{1,0,3,2:T(2,128)(2,1)} %reshape.119) | copy-start | bytes 1966084
  67.1 46.5 %copy-start.8 = (f32[10,2,256]{2,0,1:T(8,128)S(1)}, f32[10,2,256]{2,0,1:T(8,128)}, u32[]{:S(2)}) copy-start(f32[10,2,256]{2,0,1:T(8,128)} %copy.52) | copy-start | bytes 61444
  67.1 46.5 %copy-start.9 = (f32[10,2,256]{2,0,1:T(8,128)S(1)}, f32[10,2,256]{2,0,1:T(8,128)}, u32[]{:S(2)}) copy-start(f32[10,2,256]{2,0,1:T(8,128)} %copy.54) | copy-start | bytes 61444
  67.2 7.1 %collective-permute-start.4 = (f32[10]{0:T(128)S(1)}, f32[10]{0:T(128)S(1)}, u32[]{:S(2)}, u32[]{:S(2)}) collective-permute-start(f32[10]{0:T(128)S(1)} %mul.318), channel_id=1, source_target_pairs={{0,32},{16,48},{32,64},{48,80},{64,96},{80,112},{96,128},{112,144}... | collective-permute-start | bytes 128 | tf_op jit(solution)/shard_map/ppermute | solution.py:12
  74.2 4.8 %collective-permute-start.5 = (f32[10]{0:T(128)S(1)}, f32[10]{0:T(128)S(1)}, u32[]{:S(2)}, u32[]{:S(2)}) collective-permute-start(f32[10]{0:T(128)S(1)} %mul.319), channel_id=1, source_target_pairs={{0,64},{16,80},{32,96},{48,112},{64,128},{80,144},{96,160},{112,17... | collective-permute-start | bytes 128 | tf_op jit(solution)/shard_map/ppermute | solution.py:12
  79.0 7.6 %collective-permute-start.6 = (f32[10]{0:T(128)S(1)}, f32[10]{0:T(128)S(1)}, u32[]{:S(2)}, u32[]{:S(2)}) collective-permute-start(f32[10]{0:T(128)S(1)} %mul.320), channel_id=1, source_target_pairs={{0,128},{16,144},{32,160},{48,176},{64,192},{80,208},{96,224},{112... | collective-permute-start | bytes 128 | tf_op jit(solution)/shard_map/ppermute | solution.py:12
  86.6 43.9 %collective-permute-start.7 = (f32[10]{0:T(128)S(1)}, f32[10]{0:T(128)S(1)}, u32[]{:S(2)}, u32[]{:S(2)}) collective-permute-start(f32[10]{0:T(128)S(1)} %mul.321), channel_id=1, source_target_pairs={{0,16},{16,32},{32,48},{48,64},{64,80},{80,96},{96,112},{112,128},... | collective-permute-start | bytes 128 | tf_op jit(solution)/shard_map/ppermute | solution.py:12
  95.9 9.2 %collective-permute-start.10 = (bf16[10,64,128]{2,1,0:T(8,128)(2,1)S(1)}, bf16[10,64,128]{2,1,0:T(8,128)(2,1)S(1)}, u32[]{:S(2)}, u32[]{:S(2)}) collective-permute-start(bf16[10,64,128]{2,1,0:T(8,128)(2,1)S(1)} %get-tuple-element.67), channel_id=1, source_target_pairs={{0,64},{16,80},{32,96},{48,112},{64,128},{80,144},{96,160},{112,17... | collective-permute-start | bytes 491528 | tf_op jit(solution)/shard_map/ppermute | solution.py:12
  105.2 24.4 %copy-start.5 = (f32[2,10,64,128]{3,2,1,0:T(8,128)S(1)}, f32[2,10,64,128]{3,2,1,0:T(8,128)}, u32[]{:S(2)}) copy-start(f32[2,10,64,128]{3,2,1,0:T(8,128)} %get-tuple-element.33) | copy-start | bytes 1966084
  105.3 24.4 %copy-start.17 = (f32[10]{0:T(128)S(1)}, f32[10]{0:T(128)}, u32[]{:S(2)}) copy-start(f32[10]{0:T(128)} %param.23) | copy-start | bytes 124
  105.3 12.0 %collective-permute-start.11 = (bf16[10,64,128]{2,1,0:T(8,128)(2,1)S(1)}, bf16[10,64,128]{2,1,0:T(8,128)(2,1)S(1)}, u32[]{:S(2)}, u32[]{:S(2)}) collective-permute-start(bf16[10,64,128]{2,1,0:T(8,128)(2,1)S(1)} %fusion.33), channel_id=1, source_target_pairs={{0,128},{16,144},{32,160},{48,176},{64,192},{80,208},{96,224},{112... | collective-permute-start | bytes 491528 | tf_op jit(solution)/shard_map/ppermute | solution.py:12
  117.4 13.1 %collective-permute-start.12 = (bf16[10,64,128]{2,1,0:T(8,128)(2,1)S(1)}, bf16[10,64,128]{2,1,0:T(8,128)(2,1)S(1)}, u32[]{:S(2)}, u32[]{:S(2)}) collective-permute-start(bf16[10,64,128]{2,1,0:T(8,128)(2,1)S(1)} %add_convert_fusion), channel_id=1, source_target_pairs={{0,272},{16,288},{32,304},{48,320},{64,336},{80,352},{96,368},{112... | collective-permute-start | bytes 491528 | tf_op jit(solution)/shard_map/ppermute | solution.py:12
  127.7 7.2 %collective-permute-start.13 = (bf16[10,64,128]{2,1,0:T(8,128)(2,1)S(1)}, bf16[10,64,128]{2,1,0:T(8,128)(2,1)S(1)}, u32[]{:S(2)}, u32[]{:S(2)}) collective-permute-start(bf16[10,64,128]{2,1,0:T(8,128)(2,1)S(1)} %add_convert_fusion), channel_id=1, source_target_pairs={{0,16},{16,32},{32,48},{48,64},{64,80},{80,96},{96,112},{112,128},... | collective-permute-start | bytes 491528 | tf_op jit(solution)/shard_map/ppermute | solution.py:12
  135.6 1.7 copy-start.2
  136.3 24.9 %copy-start.19 = (f32[640]{0:T(1024)S(1)}, f32[640]{0:T(1024)}, u32[]{:S(2)}) copy-start(f32[640]{0:T(1024)} %param.24) | copy-start | bytes 7684
  136.5 0.8 copy-start.4
Sparse Core Ops, SparseCore 0:
  166.6 40.4 reduce-scatter.1

commit v2 on v1

--- a/solution.py
+++ b/solution.py
@@ -106,12 +106,11 @@
     device_decay = jnp.prod(block_decay, axis=1)
     skip_term = d_skip[None, None, :, None] * block_x.astype(jnp.float32)
     zero_state = jnp.zeros((head_count, head_size, state_size), jnp.float32)
-
-    def advance(carry_state, inputs_now):
-        decay_now, fresh_state = inputs_now
-        return (decay_now[:, None, None] * carry_state + fresh_state, carry_state)
-
-    local_final, local_entries = lax.scan(advance, zero_state, (block_decay.T, block_states))
+    entry_list = [zero_state]
+    for block in range(blocks):
+        entry_list.append(block_decay[:, block, None, None] * entry_list[-1] + block_states[block])
+    local_final = entry_list[-1]
+    local_entries = jnp.stack(entry_list[:-1])
     reached = jnp.einsum("ctn,chpn->cthp", c_wide, local_entries, precision=highest)
     lower_mask = jnp.tril(jnp.ones((SPAN, SPAN), jnp.bool_))
     same_doc = (block_ids[:, :, None] == block_ids[:, None, :]) & lower_mask[None]
@@ -135,13 +134,28 @@
     )
     y_vals = lax.optimization_barrier(result.reshape(row_count, inner_width).astype(jnp.bfloat16))
     gated = y_vals.astype(jnp.float32) * jax.nn.silu(z_gate.astype(jnp.float32))
-    squares = lax.psum(jnp.sum(gated * gated, axis=1), "tensor")
-    inv_norm = lax.rsqrt(squares / (inner_width * lax.axis_size("tensor")) + 1e-05)
-    normed = (gated * inv_norm[:, None] * norm_gain[None, :]).astype(jnp.bfloat16)
-    partial_value = jnp.dot(normed, w_out, preferred_element_type=jnp.float32)
-    return lax.psum_scatter(
-        partial_value.astype(jnp.bfloat16), "tensor", scatter_dimension=1, tiled=True
+    group_count = lax.axis_size("tensor")
+    squares = jnp.sum(gated * gated, axis=1)
+    scaled = (gated * norm_gain[None, :]).astype(jnp.bfloat16)
+    out_width = w_out.shape[1] // group_count
+    partial_value = jnp.einsum(
+        "tc,cgk->gtk",
+        scaled,
+        w_out.reshape(inner_width, group_count, out_width),
+        preferred_element_type=jnp.float32,
+    ).astype(jnp.bfloat16)
+    pad_rows = -(-row_count // out_width)
+    square_rows = jnp.pad(squares, (0, pad_rows * out_width - row_count)).reshape(
+        pad_rows, out_width
     )
+    square_rows = jnp.broadcast_to(
+        square_rows.astype(jnp.bfloat16)[None], (group_count, pad_rows, out_width)
+    )
+    payload = jnp.concatenate([partial_value, square_rows], axis=1)
+    summed = lax.psum_scatter(payload, "tensor", scatter_dimension=0, tiled=True)[0]
+    total_squares = summed[row_count:].reshape(-1)[:row_count].astype(jnp.float32)
+    inv_norm = lax.rsqrt(total_squares / (inner_width * group_count) + 1e-05)
+    return (summed[:row_count].astype(jnp.float32) * inv_norm[:, None]).astype(jnp.bfloat16)
 
 
 def solution(mesh):

time: 215 us -> 203 us (0.944)
  blocking collectives: 23.4 us -> 0 us
  waiting for transfers between devices: 55.6 us -> 72.5 us
  matrix products: 11.8 us -> 8.3 us
  other arithmetic: 21.9 us -> 18.7 us
    psum x1 -> x0, blocking collectives: 23.4 us -> none  [local(): squares = lax.psum(jnp.sum(gated * gated, axis=1), 'tensor')]
    reduce_scatter x1, waiting for transfers between devices: 40.6 us -> 52 us  [local(): lax.psum_scatter(payload, 'tensor', scatter_dimension=0, tiled=True)[0]]
    ppermute x14, waiting for transfers between devices: 15 us -> 20.4 us  [from_behind(): return lax.ppermute(block, axis, route)]
    add x2 -> x1, other arithmetic: 3.69 us -> 0.09 us  [local(): block_decay[:, block, None, None] * entry_list[-1] + block_states[block]]
    convert_element_type x4, other arithmetic: 4.07 us -> 0.5 us  [pass_state(): state.astype(jnp.bfloat16)]
    unnamed x45 -> x50, local copies, waits for them, and re-layouts: 5.38 us -> 8.69 us
    reshape x1, local copies, waits for them, and re-layouts: 2.66 us -> 0.15 us  [local(): block_x = mixed_x.reshape(blocks, SPAN, head_count, head_size)]
    dynamic_update_slice x2 -> x0, other arithmetic: 2.49 us -> none  [local(): lax.scan(advance, zero_state, (block_decay.T, block_states))]
  transfers between devices with their start and end apart: 15 -> 15, of which waited for: 7 -> 9; matrix products, arithmetic and copies ran while one was open for 11% -> 15% of each run, Pallas kernels for 0% -> 0%
where the time goes in v2:
time: 203 us; the launch traced here: 202 us
  waiting for transfers between devices  72.5 us (36%)
  starting transfers between devices  69.2 us (34%)
  local copies, waits for them, and re-layouts  19.2 us (9%)
  other arithmetic  18.7 us (9%)
  between operations  14 us (7%)
  matrix products  8.3 us (4%)
    ppermute x14, starting transfers between devices, from_behind(): return lax.ppermute(block, axis, route)  69.2 us
    reduce_scatter x1, waiting for transfers between devices, local(): lax.psum_scatter(payload, 'tensor', scatter_dimension=0, tiled=True)[0]  52 us
    ppermute x14, waiting for transfers between devices, from_behind(): return lax.ppermute(block, axis, route)  20.4 us
    unnamed x50, local copies, waits for them, and re-layouts  8.69 us
    convert_element_type x2, other arithmetic, causal_conv(): return jax.nn.silu(total).astype(jnp.bfloat16)  4.29 us
  transfers between devices with their start and end apart: 15, of which 9 were waited for; matrix products, arithmetic and copies ran while one was open for 15% of the time, Pallas kernels for 0%

profile of v2, /device:TPU:6, one launch (start us, length us, event | category | flops | bytes accessed | tf_op | source)
XLA Modules:
  0.0 201.9 jit_solution(6905224981948435860)
XLA Ops:
  6.6 0.7 convert_convert_fusion
  7.3 0.6 slice.120
  7.9 3.4 %collective-permute-start = (bf16[3]{0:T(256)(128)(2,1)}, bf16[3]{0:T(256)(128)(2,1)}, u32[]{:S(2)}, u32[]{:S(2)}) collective-permute-start(bf16[3]{0:T(256)(128)(2,1)} %slice.120), channel_id=1, source_target_pairs={{0,16},{16,32},{32,48},{48,64},{64,80},{80,96},{96,112},{112,128},... | collective-permute-start | bytes 26 | tf_op jit(solution)/shard_map/ppermute | solution.py:12
  11.3 0.7 slice.122
  12.1 0.8 copy.51
  12.9 3.4 %collective-permute-start.1 = (bf16[3,640]{0,1:T(8,128)(2,1)}, bf16[3,640]{0,1:T(8,128)(2,1)}, u32[]{:S(2)}, u32[]{:S(2)}) collective-permute-start(bf16[3,640]{0,1:T(8,128)(2,1)} %copy.51), channel_id=1, source_target_pairs={{0,16},{16,32},{32,48},{48,64},{64,80},{80,96},{96,112},{112,128},... | collective-permute-start | bytes 11528 | tf_op jit(solution)/shard_map/ppermute | solution.py:12
  16.3 1.3 slice.132
  17.6 3.4 %collective-permute-start.2 = (bf16[3,256]{1,0:T(4,128)(2,1)}, bf16[3,256]{1,0:T(4,128)(2,1)}, u32[]{:S(2)}, u32[]{:S(2)}) collective-permute-start(bf16[3,256]{1,0:T(4,128)(2,1)} %slice.132), channel_id=1, source_target_pairs={{0,16},{16,32},{32,48},{48,64},{64,80},{80,96},{96,112},{112,128},... | collective-permute-start | bytes 4616 | tf_op jit(solution)/shard_map/ppermute | solution.py:12
  21.0 0.7 slice.144
  21.6 2.3 %copy.50 = bf16[512,640]{0,1:T(8,128)(2,1)} copy(bf16[512,640]{1,0:T(8,128)(2,1)} %param.12) | data formatting | bytes 1310720 | tf_op args[0]
  24.1 1.2 reduce-window.9
  25.8 0.6 copy.57
  26.4 0.7 iota_compare_fusion
  27.0 0.7 slice_reduce_fusion.1
  28.0 0.6 convert_reduce_fusion.3
  28.6 0.6 slice_convert_fusion.3
  29.2 0.6 copy.59
  29.8 2.2 %copy.69 = bf16[512,640]{0,1:T(8,128)(2,1)} copy(bf16[512,640]{1,0:T(8,128)(2,1)} %param.14) | data formatting | bytes 1310720 | tf_op args[2]
  32.0 3.4 %copy.70 = bf16[640,2560]{0,1:T(8,128)(2,1)} copy(bf16[640,2560]{1,0:T(8,128)(2,1)S(1)} %copy-done) | data formatting | bytes 6553600 | tf_op args[11]
  35.5 1.3 slice.143
  36.8 1.4 pad_maximum_fusion.4
  38.2 0.7 broadcast_compare_fusion
  38.9 0.2 slice_reduce_fusion
  39.0 0.8 fusion.45
  40.0 0.6 convert_element_type.144
  40.6 0.8 multiply_bitcast_fusion
  41.5 0.8 slice_compare_fusion.2
  42.3 1.6 multiply_convert_fusion.6
  43.9 2.7 %multiply_convert_fusion.5 = bf16[512,640]{0,1:T(8,128)(2,1)S(1)} fusion(bf16[512,640]{0,1:T(8,128)(2,1)S(1)} %copy-done.3, bf16[3,640]{0,1:T(8,128)(2,1)} %collective-permute-done.1, f32[640]{0:T(1024)S(1)} %copy-done.14, f32[640]{0:T(1024)S(1)} %copy-done.15, f32[640]{0:T(1024)S(1)} %copy-done.13, f32[640]{0:T(1024)S(1)} %copy-done.12, ...), kind=kLoop, calls=%fused_computation.28 | loop fusion | flops 9502720 | bytes 1326848 | tf_op jit(solution)/shard_map/convert_element_type | solution.py:27
  46.8 0.8 fusion.12
  47.8 3.1 %collective-permute-start.8 = (bf16[10,64,128]{2,1,0:T(8,128)(2,1)S(1)}, bf16[10,64,128]{2,1,0:T(8,128)(2,1)S(1)}, u32[]{:S(2)}, u32[]{:S(2)}) collective-permute-start(bf16[10,64,128]{2,1,0:T(8,128)(2,1)S(1)} %get-tuple-element.13), channel_id=1, source_target_pairs={{0,16},{16,32},{32,48},{48,64},{64,80},{80,96},{96,112},{112,128},... | collective-permute-start | bytes 491528 | tf_op jit(solution)/shard_map/ppermute | solution.py:12
  50.9 0.2 compare_and_fusion
  51.1 3.4 %collective-permute-start.3 = (f32[10]{0:T(128)S(1)}, f32[10]{0:T(128)S(1)}, u32[]{:S(2)}, u32[]{:S(2)}) collective-permute-start(f32[10]{0:T(128)S(1)} %get-tuple-element.11), channel_id=1, source_target_pairs={{0,16},{16,32},{32,48},{48,64},{64,80},{80,96},{96,112},{112,128},... | collective-permute-start | bytes 128 | tf_op jit(solution)/shard_map/ppermute | solution.py:12
  54.5 2.0 collective-permute-done.3
  56.5 4.3 %collective-permute-start.4 = (f32[10]{0:T(128)S(1)}, f32[10]{0:T(128)S(1)}, u32[]{:S(2)}, u32[]{:S(2)}) collective-permute-start(f32[10]{0:T(128)S(1)} %mul.335), channel_id=1, source_target_pairs={{0,32},{16,48},{32,64},{48,80},{64,96},{80,112},{96,128},{112,144}... | collective-permute-start | bytes 128 | tf_op jit(solution)/shard_map/ppermute | solution.py:12
  60.8 2.6 %collective-permute-done.4 = f32[10]{0:T(128)S(1)} collective-permute-done((f32[10]{0:T(128)S(1)}, f32[10]{0:T(128)S(1)}, u32[]{:S(2)}, u32[]{:S(2)}) %collective-permute-start.4) | collective-permute-done | bytes 72 | tf_op jit(solution)/shard_map/ppermute | solution.py:12
  63.4 3.5 %collective-permute-start.5 = (f32[10]{0:T(128)S(1)}, f32[10]{0:T(128)S(1)}, u32[]{:S(2)}, u32[]{:S(2)}) collective-permute-start(f32[10]{0:T(128)S(1)} %mul.336), channel_id=1, source_target_pairs={{0,64},{16,80},{32,96},{48,112},{64,128},{80,144},{96,160},{112,17... | collective-permute-start | bytes 128 | tf_op jit(solution)/shard_map/ppermute | solution.py:12
  66.9 1.3 collective-permute-done.5
  68.2 5.7 %collective-permute-start.6 = (f32[10]{0:T(128)S(1)}, f32[10]{0:T(128)S(1)}, u32[]{:S(2)}, u32[]{:S(2)}) collective-permute-start(f32[10]{0:T(128)S(1)} %mul.337), channel_id=1, source_target_pairs={{0,128},{16,144},{32,160},{48,176},{64,192},{80,208},{96,224},{112... | collective-permute-start | bytes 128 | tf_op jit(solution)/shard_map/ppermute | solution.py:12
  73.9 1.3 collective-permute-done.6
  75.2 7.9 %collective-permute-start.7 = (f32[10]{0:T(128)S(1)}, f32[10]{0:T(128)S(1)}, u32[]{:S(2)}, u32[]{:S(2)}) collective-permute-start(f32[10]{0:T(128)S(1)} %mul.338), channel_id=1, source_target_pairs={{0,16},{16,32},{32,48},{48,64},{64,80},{80,96},{96,112},{112,128},... | collective-permute-start | bytes 128 | tf_op jit(solution)/shard_map/ppermute | solution.py:12
  83.2 1.9 collective-permute-start.9
  85.2 0.2 fusion.49
  85.4 6.6 %collective-permute-done.9 = bf16[10,64,128]{2,1,0:T(8,128)(2,1)S(1)} collective-permute-done((bf16[10,64,128]{2,1,0:T(8,128)(2,1)S(1)}, bf16[10,64,128]{2,1,0:T(8,128)(2,1)S(1)}, u32[]{:S(2)}, u32[]{:S(2)}) %collective-permute-start.9) | collective-permute-done | bytes 163872 | tf_op jit(solution)/shard_map/ppermute | solution.py:12
  92.1 5.4 %collective-permute-start.10 = (bf16[10,64,128]{2,1,0:T(8,128)(2,1)S(1)}, bf16[10,64,128]{2,1,0:T(8,128)(2,1)S(1)}, u32[]{:S(2)}, u32[]{:S(2)}) collective-permute-start(bf16[10,64,128]{2,1,0:T(8,128)(2,1)S(1)} %get-tuple-element.9), channel_id=1, source_target_pairs={{0,64},{16,80},{32,96},{48,112},{64,128},{80,144},{96,160},{112,17... | collective-permute-start | bytes 491528 | tf_op jit(solution)/shard_map/ppermute | solution.py:12
  97.5 2.0 fusion.8
  99.5 2.3 %collective-permute-done.10 = bf16[10,64,128]{2,1,0:T(8,128)(2,1)S(1)} collective-permute-done((bf16[10,64,128]{2,1,0:T(8,128)(2,1)S(1)}, bf16[10,64,128]{2,1,0:T(8,128)(2,1)S(1)}, u32[]{:S(2)}, u32[]{:S(2)}) %collective-permute-start.10) | collective-permute-done | bytes 163872 | tf_op jit(solution)/shard_map/ppermute | solution.py:12
  101.9 7.9 %collective-permute-start.11 = (bf16[10,64,128]{2,1,0:T(8,128)(2,1)S(1)}, bf16[10,64,128]{2,1,0:T(8,128)(2,1)S(1)}, u32[]{:S(2)}, u32[]{:S(2)}) collective-permute-start(bf16[10,64,128]{2,1,0:T(8,128)(2,1)S(1)} %fusion.37), channel_id=1, source_target_pairs={{0,128},{16,144},{32,160},{48,176},{64,192},{80,208},{96,224},{112... | collective-permute-start | bytes 491528 | tf_op jit(solution)/shard_map/ppermute | solution.py:12
  109.8 2.7 %collective-permute-done.11 = bf16[10,64,128]{2,1,0:T(8,128)(2,1)S(1)} collective-permute-done((bf16[10,64,128]{2,1,0:T(8,128)(2,1)S(1)}, bf16[10,64,128]{2,1,0:T(8,128)(2,1)S(1)}, u32[]{:S(2)}, u32[]{:S(2)}) %collective-permute-start.11) | collective-permute-done | bytes 163872 | tf_op jit(solution)/shard_map/ppermute | solution.py:12
  112.7 11.0 %collective-permute-start.12 = (bf16[10,64,128]{2,1,0:T(8,128)(2,1)S(1)}, bf16[10,64,128]{2,1,0:T(8,128)(2,1)S(1)}, u32[]{:S(2)}, u32[]{:S(2)}) collective-permute-start(bf16[10,64,128]{2,1,0:T(8,128)(2,1)S(1)} %add_convert_fusion), channel_id=1, source_target_pairs={{0,272},{16,288},{32,304},{48,320},{64,336},{80,352},{96,368},{112... | collective-permute-start | bytes 491528 | tf_op jit(solution)/shard_map/ppermute | solution.py:12
  123.7 5.0 %collective-permute-start.13 = (bf16[10,64,128]{2,1,0:T(8,128)(2,1)S(1)}, bf16[10,64,128]{2,1,0:T(8,128)(2,1)S(1)}, u32[]{:S(2)}, u32[]{:S(2)}) collective-permute-start(bf16[10,64,128]{2,1,0:T(8,128)(2,1)S(1)} %add_convert_fusion), channel_id=1, source_target_pairs={{0,16},{16,32},{32,48},{48,64},{64,80},{80,96},{96,112},{112,128},... | collective-permute-start | bytes 491528 | tf_op jit(solution)/shard_map/ppermute | solution.py:12
  128.7 0.9 fusion.10
  129.6 1.7 collective-permute-done.13
  131.4 0.8 fusion.11
  132.2 0.7 copy.68
  133.0 0.5 multiply_reduce_fusion
  133.6 0.3 copy-done.4
  133.9 0.2 copy.72
  134.1 0.3 copy-done.1
  134.4 3.6 %convert_bitcast_fusion = bf16[8,512,320]{1,2,0:T(8,128)(2,1)S(1)} fusion(bf16[640,8,320]{0,2,1:T(8,128)(2,1)S(1)} %bitcast.70, f32[640]{0:T(1024)S(1)} %copy-done.21, bf16[512,640]{0,1:T(8,128)(2,1)} %copy.69, bf16[512,640]{0,1:T(8,128)(2,1)} %bitcast.72), kind=kOutput, calls=%fused_computation.3 | convolution fusion | flops 1681981440 | bytes 7211520 | tf_op jit(solution)/shard_map/tc,cgk->gtk/dot_general | solution.py:141
  138.1 2.0 %pad_maximum_fusion = bf16[8,514,320]{1,2,0:T(8,128)(2,1)} fusion(bf16[8,2,320]{1,2,0:T(8,128)(2,1)S(1)} %broadcast_in_dim.170, bf16[8,512,320]{1,2,0:T(8,128)(2,1)S(1)} %convert_bitcast_fusion), kind=kLoop, calls=%fused_computation.1 | loop fusion | flops 5263360 | bytes 5263360 | tf_op jit(solution)/shard_map/concatenate | solution.py:154
  140.2 52.0 %reduce-scatter.2.cloned.1.call-done = bf16[1,514,320]{1,2,0:T(8,128)(2,1)} async-done(((bf16[8,514,320]{1,2,0:T(8,128)(2,1)}), bf16[1,514,320]{1,2,0:T(8,128)(2,1)}) %reduce-scatter.2.cloned.1.call-update) | async-done | bytes 328976 | tf_op jit(solution)/shard_map/reduce_scatter | solution.py:155
  192.2 0.9 slice.174
  193.3 1.8 fusion.21
  (95 shorter events, 2.6 us)
Async XLA Ops:
  6.5 17.4 %copy-start.22 = (f32[10]{0:T(128)S(1)}, f32[10]{0:T(128)}, u32[]{:S(2)}) copy-start(f32[10]{0:T(128)} %param.19) | copy-start | bytes 124
  6.5 17.4 %copy-start.16 = (bf16[10,512]{1,0:T(8,128)(2,1)S(1)}, bf16[10,512]{1,0:T(8,128)(2,1)}, u32[]{:S(2)}) copy-start(bf16[10,512]{1,0:T(8,128)(2,1)} %param.15) | copy-start | bytes 30724
  6.5 17.4 %copy-start.19 = (f32[10]{0:T(128)S(1)}, f32[10]{0:T(128)}, u32[]{:S(2)}) copy-start(f32[10]{0:T(128)} %param.20) | copy-start | bytes 124
  6.5 21.4 %copy-start.11 = (bf16[4,640]{1,0:T(4,128)(2,1)S(1)}, bf16[4,640]{1,0:T(4,128)(2,1)}, u32[]{:S(2)}) copy-start(bf16[4,640]{1,0:T(4,128)(2,1)} %param.17) | copy-start | bytes 15364
  6.5 22.1 %copy-start.18 = (bf16[4,256]{1,0:T(4,128)(2,1)S(1)}, bf16[4,256]{1,0:T(4,128)(2,1)}, u32[]{:S(2)}) copy-start(bf16[4,256]{1,0:T(4,128)(2,1)} %param.18) | copy-start | bytes 6148
  6.5 185.6 %reduce-scatter.2.cloned.1.call-start = ((), (), s32[]{:S(2)}) async-start(), calls=%async_computation.1 | async-start | bytes 3686400 | tf_op jit(solution)/shard_map/reduce_scatter | solution.py:155
  7.9 27.5 %collective-permute-start = (bf16[3]{0:T(256)(128)(2,1)}, bf16[3]{0:T(256)(128)(2,1)}, u32[]{:S(2)}, u32[]{:S(2)}) collective-permute-start(bf16[3]{0:T(256)(128)(2,1)} %slice.120), channel_id=1, source_target_pairs={{0,16},{16,32},{32,48},{48,64},{64,80},{80,96},{96,112},{112,128},... | collective-permute-start | bytes 26 | tf_op jit(solution)/shard_map/ppermute | solution.py:12
  12.9 31.0 %collective-permute-start.1 = (bf16[3,640]{0,1:T(8,128)(2,1)}, bf16[3,640]{0,1:T(8,128)(2,1)}, u32[]{:S(2)}, u32[]{:S(2)}) collective-permute-start(bf16[3,640]{0,1:T(8,128)(2,1)} %copy.51), channel_id=1, source_target_pairs={{0,16},{16,32},{32,48},{48,64},{64,80},{80,96},{96,112},{112,128},... | collective-permute-start | bytes 11528 | tf_op jit(solution)/shard_map/ppermute | solution.py:12
  17.6 24.7 %collective-permute-start.2 = (bf16[3,256]{1,0:T(4,128)(2,1)}, bf16[3,256]{1,0:T(4,128)(2,1)}, u32[]{:S(2)}, u32[]{:S(2)}) collective-permute-start(bf16[3,256]{1,0:T(4,128)(2,1)} %slice.132), channel_id=1, source_target_pairs={{0,16},{16,32},{32,48},{48,64},{64,80},{80,96},{96,112},{112,128},... | collective-permute-start | bytes 4616 | tf_op jit(solution)/shard_map/ppermute | solution.py:12
  21.6 10.4 %copy-start = (bf16[640,2560]{1,0:T(8,128)(2,1)S(1)}, bf16[640,2560]{1,0:T(8,128)(2,1)}, u32[]{:S(2)}) copy-start(bf16[640,2560]{1,0:T(8,128)(2,1)} %param.23) | copy-start | bytes 9830404
  25.7 4.2 %copy-start.7 = (f32[10,2,256]{2,1,0:T(2,128)}, f32[10,2,256]{2,1,0:T(2,128)S(1)}, u32[]{:S(2)}) copy-start(f32[10,2,256]{2,1,0:T(2,128)S(1)} %reduce_window_sum.24) | copy-start | bytes 61444
  27.8 2.0 copy-start.17
  28.0 1.9 copy-start.8
  32.0 10.2 %copy-start.5 = (bf16[512,256]{1,0:T(8,128)(2,1)S(1)}, bf16[512,256]{1,0:T(8,128)(2,1)}, u32[]{:S(2)}) copy-start(bf16[512,256]{1,0:T(8,128)(2,1)} %param.13) | copy-start | bytes 786436
  35.4 8.5 %copy-start.3 = (bf16[512,640]{0,1:T(8,128)(2,1)S(1)}, bf16[512,640]{0,1:T(8,128)(2,1)}, u32[]{:S(2)}) copy-start(bf16[512,640]{0,1:T(8,128)(2,1)} %copy.50) | copy-start | bytes 1966084
  35.4 8.5 %copy-start.12 = (f32[640]{0:T(1024)S(1)}, f32[640]{0:T(1024)}, u32[]{:S(2)}) copy-start(f32[640]{0:T(1024)} %get-tuple-element.5) | copy-start | bytes 7684
  35.4 8.5 %copy-start.13 = (f32[640]{0:T(1024)S(1)}, f32[640]{0:T(1024)}, u32[]{:S(2)}) copy-start(f32[640]{0:T(1024)} %get-tuple-element.6) | copy-start | bytes 7684
  35.4 8.5 %copy-start.14 = (f32[640]{0:T(1024)S(1)}, f32[640]{0:T(1024)}, u32[]{:S(2)}) copy-start(f32[640]{0:T(1024)} %get-tuple-element.7) | copy-start | bytes 7684
  35.4 8.5 %copy-start.15 = (f32[640]{0:T(1024)S(1)}, f32[640]{0:T(1024)}, u32[]{:S(2)}) copy-start(f32[640]{0:T(1024)} %get-tuple-element.8) | copy-start | bytes 7684
  46.8 4.1 %copy-start.6 = (pred[256,256]{1,0:T(8,128)(4,1)S(1)}, pred[256,256]{1,0:T(8,128)(4,1)}, u32[]{:S(2)}) copy-start(pred[256,256]{1,0:T(8,128)(4,1)} %iota_compare_fusion) | copy-start | bytes 196612
  47.8 35.3 %collective-permute-start.8 = (bf16[10,64,128]{2,1,0:T(8,128)(2,1)S(1)}, bf16[10,64,128]{2,1,0:T(8,128)(2,1)S(1)}, u32[]{:S(2)}, u32[]{:S(2)}) collective-permute-start(bf16[10,64,128]{2,1,0:T(8,128)(2,1)S(1)} %get-tuple-element.13), channel_id=1, source_target_pairs={{0,16},{16,32},{32,48},{48,64},{64,80},{80,96},{96,112},{112,128},... | collective-permute-start | bytes 491528 | tf_op jit(solution)/shard_map/ppermute | solution.py:12
  51.1 5.4 %collective-permute-start.3 = (f32[10]{0:T(128)S(1)}, f32[10]{0:T(128)S(1)}, u32[]{:S(2)}, u32[]{:S(2)}) collective-permute-start(f32[10]{0:T(128)S(1)} %get-tuple-element.11), channel_id=1, source_target_pairs={{0,16},{16,32},{32,48},{48,64},{64,80},{80,96},{96,112},{112,128},... | collective-permute-start | bytes 128 | tf_op jit(solution)/shard_map/ppermute | solution.py:12
  54.5 43.0 %copy-start.9 = (f32[10,2,256]{2,0,1:T(8,128)S(1)}, f32[10,2,256]{2,0,1:T(8,128)}, u32[]{:S(2)}) copy-start(f32[10,2,256]{2,0,1:T(8,128)} %copy.57) | copy-start | bytes 61444
  54.5 43.0 %copy-start.10 = (f32[10,2,256]{2,0,1:T(8,128)S(1)}, f32[10,2,256]{2,0,1:T(8,128)}, u32[]{:S(2)}) copy-start(f32[10,2,256]{2,0,1:T(8,128)} %copy.59) | copy-start | bytes 61444
  56.5 6.9 %collective-permute-start.4 = (f32[10]{0:T(128)S(1)}, f32[10]{0:T(128)S(1)}, u32[]{:S(2)}, u32[]{:S(2)}) collective-permute-start(f32[10]{0:T(128)S(1)} %mul.335), channel_id=1, source_target_pairs={{0,32},{16,48},{32,64},{48,80},{64,96},{80,112},{96,128},{112,144}... | collective-permute-start | bytes 128 | tf_op jit(solution)/shard_map/ppermute | solution.py:12
  63.4 4.8 %collective-permute-start.5 = (f32[10]{0:T(128)S(1)}, f32[10]{0:T(128)S(1)}, u32[]{:S(2)}, u32[]{:S(2)}) collective-permute-start(f32[10]{0:T(128)S(1)} %mul.336), channel_id=1, source_target_pairs={{0,64},{16,80},{32,96},{48,112},{64,128},{80,144},{96,160},{112,17... | collective-permute-start | bytes 128 | tf_op jit(solution)/shard_map/ppermute | solution.py:12
  68.2 7.0 %collective-permute-start.6 = (f32[10]{0:T(128)S(1)}, f32[10]{0:T(128)S(1)}, u32[]{:S(2)}, u32[]{:S(2)}) collective-permute-start(f32[10]{0:T(128)S(1)} %mul.337), channel_id=1, source_target_pairs={{0,128},{16,144},{32,160},{48,176},{64,192},{80,208},{96,224},{112... | collective-permute-start | bytes 128 | tf_op jit(solution)/shard_map/ppermute | solution.py:12
  75.2 54.4 %collective-permute-start.7 = (f32[10]{0:T(128)S(1)}, f32[10]{0:T(128)S(1)}, u32[]{:S(2)}, u32[]{:S(2)}) collective-permute-start(f32[10]{0:T(128)S(1)} %mul.338), channel_id=1, source_target_pairs={{0,16},{16,32},{32,48},{48,64},{64,80},{80,96},{96,112},{112,128},... | collective-permute-start | bytes 128 | tf_op jit(solution)/shard_map/ppermute | solution.py:12
  83.2 8.7 %collective-permute-start.9 = (bf16[10,64,128]{2,1,0:T(8,128)(2,1)S(1)}, bf16[10,64,128]{2,1,0:T(8,128)(2,1)S(1)}, u32[]{:S(2)}, u32[]{:S(2)}) collective-permute-start(bf16[10,64,128]{2,1,0:T(8,128)(2,1)S(1)} %fusion.36), channel_id=1, source_target_pairs={{0,32},{16,48},{32,64},{48,80},{64,96},{80,112},{96,128},{112,144}... | collective-permute-start | bytes 491528 | tf_op jit(solution)/shard_map/ppermute | solution.py:12
  92.1 9.7 %collective-permute-start.10 = (bf16[10,64,128]{2,1,0:T(8,128)(2,1)S(1)}, bf16[10,64,128]{2,1,0:T(8,128)(2,1)S(1)}, u32[]{:S(2)}, u32[]{:S(2)}) collective-permute-start(bf16[10,64,128]{2,1,0:T(8,128)(2,1)S(1)} %get-tuple-element.9), channel_id=1, source_target_pairs={{0,64},{16,80},{32,96},{48,112},{64,128},{80,144},{96,160},{112,17... | collective-permute-start | bytes 491528 | tf_op jit(solution)/shard_map/ppermute | solution.py:12
  99.5 29.3 %copy-start.20 = (f32[10]{0:T(128)S(1)}, f32[10]{0:T(128)}, u32[]{:S(2)}) copy-start(f32[10]{0:T(128)} %param.21) | copy-start | bytes 124
  101.9 10.7 %collective-permute-start.11 = (bf16[10,64,128]{2,1,0:T(8,128)(2,1)S(1)}, bf16[10,64,128]{2,1,0:T(8,128)(2,1)S(1)}, u32[]{:S(2)}, u32[]{:S(2)}) collective-permute-start(bf16[10,64,128]{2,1,0:T(8,128)(2,1)S(1)} %fusion.37), channel_id=1, source_target_pairs={{0,128},{16,144},{32,160},{48,176},{64,192},{80,208},{96,224},{112... | collective-permute-start | bytes 491528 | tf_op jit(solution)/shard_map/ppermute | solution.py:12
  112.7 16.9 %collective-permute-start.12 = (bf16[10,64,128]{2,1,0:T(8,128)(2,1)S(1)}, bf16[10,64,128]{2,1,0:T(8,128)(2,1)S(1)}, u32[]{:S(2)}, u32[]{:S(2)}) collective-permute-start(bf16[10,64,128]{2,1,0:T(8,128)(2,1)S(1)} %add_convert_fusion), channel_id=1, source_target_pairs={{0,272},{16,288},{32,304},{48,320},{64,336},{80,352},{96,368},{112... | collective-permute-start | bytes 491528 | tf_op jit(solution)/shard_map/ppermute | solution.py:12
  123.7 7.7 %collective-permute-start.13 = (bf16[10,64,128]{2,1,0:T(8,128)(2,1)S(1)}, bf16[10,64,128]{2,1,0:T(8,128)(2,1)S(1)}, u32[]{:S(2)}, u32[]{:S(2)}) collective-permute-start(bf16[10,64,128]{2,1,0:T(8,128)(2,1)S(1)} %add_convert_fusion), channel_id=1, source_target_pairs={{0,16},{16,32},{32,48},{48,64},{64,80},{80,96},{96,112},{112,128},... | collective-permute-start | bytes 491528 | tf_op jit(solution)/shard_map/ppermute | solution.py:12
  131.4 1.7 copy-start.2
  132.2 2.2 %copy-start.1 = (bf16[640,2560]{0,1:T(8,128)(2,1)S(1)}, bf16[640,2560]{0,1:T(8,128)(2,1)}, u32[]{:S(2)}) copy-start(bf16[640,2560]{0,1:T(8,128)(2,1)} %copy.70) | copy-start | bytes 9830404
  132.9 1.5 copy-start.21
  133.0 0.8 copy-start.4
Sparse Core Ops, SparseCore 0:
  140.3 51.8 reduce-scatter.1

commit v3 on v2

--- a/solution.py
+++ b/solution.py
@@ -27,22 +27,34 @@
     return jax.nn.silu(total).astype(jnp.bfloat16)
 
 
+def with_decay(decay, state):
+    high = decay.astype(jnp.bfloat16)
+    low = (decay - high.astype(jnp.float32)).astype(jnp.bfloat16)
+    tail = jnp.broadcast_to(jnp.stack([high, low], 1)[:, :, None], (decay.shape[0], 2, state.shape[2]))
+    return jnp.concatenate([state.astype(jnp.bfloat16), tail], axis=1)
+
+
+def split_decay(packed):
+    decay = packed[:, -2, 0].astype(jnp.float32) + packed[:, -1, 0].astype(jnp.float32)
+    return decay, packed[:, :-2].astype(jnp.float32)
+
+
 def pass_state(device_decay, local_final):
     shard_count = lax.axis_size("seq")
     decay, state = device_decay, local_final
     window = 1
     while 2 * window < shard_count - 1:
-        prev_decay, prev_state = from_behind((decay, state.astype(jnp.bfloat16)), "seq", window)
-        state = decay[:, None, None] * prev_state.astype(jnp.float32) + state
+        prev_decay, prev_state = split_decay(
+            from_behind(with_decay(decay, state), "seq", window)
+        )
+        state = decay[:, None, None] * prev_state + state
         decay = decay * prev_decay
         window *= 2
-    near_decay, near_state = from_behind((decay, state.astype(jnp.bfloat16)), "seq", 1)
+    near_decay, near_state = split_decay(from_behind(with_decay(decay, state), "seq", 1))
     if window + 1 < shard_count:
         far_state = from_behind(state.astype(jnp.bfloat16), "seq", window + 1)
-        return near_decay[:, None, None] * far_state.astype(jnp.float32) + near_state.astype(
-            jnp.float32
-        )
-    return near_state.astype(jnp.float32)
+        return near_decay[:, None, None] * far_state.astype(jnp.float32) + near_state
+    return near_state
 
 
 def local(
@@ -69,11 +81,25 @@
     blocks = row_count // SPAN
     edge_start = row_count - tap_count + 1
     own_ids = doc_ids.astype(jnp.float32)
-    rim_x, rim_bc, rim_ids = from_behind(
-        (x_stream[edge_start:], bc_stream[edge_start:], own_ids[edge_start:].astype(jnp.bfloat16)),
+    x_width = x_stream.shape[1]
+    bc_width = bc_stream.shape[1]
+    rim = from_behind(
+        jnp.concatenate(
+            [
+                x_stream[edge_start:],
+                bc_stream[edge_start:],
+                jnp.broadcast_to(own_ids[edge_start:, None], (tap_count - 1, 128)).astype(
+                    jnp.bfloat16
+                ),
+            ],
+            axis=1,
+        ),
         "seq",
         1,
     )
+    rim_x = rim[:, :x_width]
+    rim_bc = rim[:, x_width : x_width + bc_width]
+    rim_ids = rim[:, x_width + bc_width]
     ext_ids = jnp.concatenate([rim_ids.astype(jnp.float32), own_ids])
     mixed_x = causal_conv(jnp.concatenate([rim_x, x_stream]), conv_x, ext_ids, own_ids, row_count)
     mixed_bc = causal_conv(

time: 203 us -> 169 us (0.83)
  starting transfers between devices: 69.2 us -> 36 us
  waiting for transfers between devices: 72.5 us -> 69.8 us
    ppermute x14 -> x7, starting transfers between devices: 69.2 us -> 36 us  [from_behind(): return lax.ppermute(block, axis, route)]
    ppermute x14 -> x7, waiting for transfers between devices: 20.4 us -> 16.3 us  [from_behind(): return lax.ppermute(block, axis, route)]
    unnamed x50 -> x34, local copies, waits for them, and re-layouts: 8.69 us -> 9.31 us
  transfers between devices with their start and end apart: 15 -> 8, of which waited for: 9 -> 6; matrix products, arithmetic and copies ran while one was open for 15% -> 11% of each run, Pallas kernels for 0% -> 0%
where the time goes in v3:
time: 169 us; the launch traced here: 168 us
  waiting for transfers between devices  69.8 us (41%)
  starting transfers between devices  36 us (21%)
  other arithmetic  19.7 us (12%)
  local copies, waits for them, and re-layouts  19.7 us (12%)
  between operations  13.9 us (8%)
  matrix products  8.98 us (5%)
    reduce_scatter x1, waiting for transfers between devices, local(): lax.psum_scatter(payload, 'tensor', scatter_dimension=0, tiled=True)[0]  53.4 us
    ppermute x7, starting transfers between devices, from_behind(): return lax.ppermute(block, axis, route)  36 us
    ppermute x7, waiting for transfers between devices, from_behind(): return lax.ppermute(block, axis, route)  16.3 us
    unnamed x34, local copies, waits for them, and re-layouts  9.31 us
    convert_element_type x2, other arithmetic, causal_conv(): return jax.nn.silu(total).astype(jnp.bfloat16)  4.74 us
    dot_general x1, matrix products, local(): jnp.einsum('tc,cgk->gtk', scaled, w_out.reshape(inner_width, group_count,...  3.64 us
  transfers between devices with their start and end apart: 8, of which 6 were waited for; matrix products, arithmetic and copies ran while one was open for 11% of the time, Pallas kernels for 0%

profile of v3, /device:TPU:6, one launch (start us, length us, event | category | flops | bytes accessed | tf_op | source)
XLA Modules:
  0.0 168.1 jit_solution(7993374606312006682)
XLA Ops:
  6.5 0.7 fusion.66
  7.3 0.7 slice.177
  8.0 0.7 slice.178
  8.8 0.9 copy.97
  9.7 3.4 %collective-permute-start = (bf16[3,1024]{0,1:T(8,128)(2,1)}, bf16[3,1024]{0,1:T(8,128)(2,1)}, u32[]{:S(2)}, u32[]{:S(2)}) collective-permute-start(bf16[3,1024]{0,1:T(8,128)(2,1)} %copy.97), channel_id=1, source_target_pairs={{0,16},{16,32},{32,48},{48,64},{64,80},{80,96},{96,112},{112,128},... | collective-permute-start | bytes 18440 | tf_op jit(solution)/shard_map/ppermute | solution.py:12
  13.1 0.7 exponential_negate_fusion
  13.8 0.8 broadcast_multiply_fusion
  14.7 1.2 reduce-window.9
  16.1 0.9 convert_reduce_fusion.3
  17.0 1.4 slice_convert_fusion.13
  18.4 0.2 slice_reduce_fusion.1
  18.7 2.2 %copy.96 = bf16[512,640]{0,1:T(8,128)(2,1)} copy(bf16[512,640]{1,0:T(8,128)(2,1)} %param.12) | data formatting | bytes 1310720 | tf_op args[0]
  21.0 0.6 copy.104
  21.9 0.6 copy.106
  22.5 2.2 %copy.122 = bf16[512,640]{0,1:T(8,128)(2,1)} copy(bf16[512,640]{1,0:T(8,128)(2,1)} %param.14) | data formatting | bytes 1310720 | tf_op args[2]
  24.6 3.4 %copy.123 = bf16[640,2560]{0,1:T(8,128)(2,1)} copy(bf16[640,2560]{1,0:T(8,128)(2,1)S(1)} %copy-done) | data formatting | bytes 6553600 | tf_op args[11]
  28.0 0.7 slice_convert_fusion.14
  28.7 0.6 slice.203
  29.3 0.8 pad_maximum_fusion.10
  30.1 0.2 slice_reduce_fusion
  30.8 0.9 slice.233
  31.8 4.0 %multiply_convert_fusion.5 = bf16[512,640]{0,1:T(8,128)(2,1)S(1)} fusion(bf16[512,640]{0,1:T(8,128)(2,1)} %copy.96, bf16[3,640]{0,1:T(8,128)(2,1)S(1)} %slice.233, f32[640]{0:T(1024)S(1)} %get-tuple-element.12, f32[640]{0:T(1024)S(1)} %get-tuple-element.13, f32[640]{0:T(1024)S(1)} %get-tuple-element.11, f32[640]{0:T(1024)S(1)} %get-tuple-element.10, ...), kind=kLoop, calls=%fused_computation.28 | loop fusion | flops 9502720 | bytes 1326848 | tf_op jit(solution)/shard_map/convert_element_type | solution.py:27
  35.7 0.2 reshape.490
  35.9 0.8 slice.238
  36.9 0.8 multiply_convert_fusion.6
  37.8 0.8 fusion.12
  38.6 0.1 fusion.62
  38.8 3.4 %collective-permute-start.1 = (bf16[10,66,128]{2,1,0:T(8,128)(2,1)S(1)}, bf16[10,66,128]{2,1,0:T(8,128)(2,1)S(1)}, u32[]{:S(2)}, u32[]{:S(2)}) collective-permute-start(bf16[10,66,128]{2,1,0:T(8,128)(2,1)S(1)} %pad_maximum_fusion.3), channel_id=1, source_target_pairs={{0,16},{16,32},{32,48},{48,64},{64,80},{80,96},{96,112},{112,128},... | collective-permute-start | bytes 506888 | tf_op jit(solution)/shard_map/ppermute | solution.py:12
  42.2 0.2 compare_and_fusion
  42.5 4.3 %collective-permute-done.1 = bf16[10,66,128]{2,1,0:T(8,128)(2,1)S(1)} collective-permute-done((bf16[10,66,128]{2,1,0:T(8,128)(2,1)S(1)}, bf16[10,66,128]{2,1,0:T(8,128)(2,1)S(1)}, u32[]{:S(2)}, u32[]{:S(2)}) %collective-permute-start.1) | collective-permute-done | bytes 168992 | tf_op jit(solution)/shard_map/ppermute | solution.py:12
  46.8 0.2 multiply_reduce_fusion.3
  47.1 0.1 fusion.36
  47.4 4.3 %collective-permute-start.2 = (bf16[10,66,128]{2,1,0:T(8,128)(2,1)S(1)}, bf16[10,66,128]{2,1,0:T(8,128)(2,1)S(1)}, u32[]{:S(2)}, u32[]{:S(2)}) collective-permute-start(bf16[10,66,128]{2,1,0:T(8,128)(2,1)S(1)} %pad_maximum_fusion.4), channel_id=1, source_target_pairs={{0,32},{16,48},{32,64},{48,80},{64,96},{80,112},{96,128},{112,144}... | collective-permute-start | bytes 506888 | tf_op jit(solution)/shard_map/ppermute | solution.py:12
  51.7 1.0 fusion.67
  52.7 3.6 %collective-permute-done.2 = bf16[10,66,128]{2,1,0:T(8,128)(2,1)S(1)} collective-permute-done((bf16[10,66,128]{2,1,0:T(8,128)(2,1)S(1)}, bf16[10,66,128]{2,1,0:T(8,128)(2,1)S(1)}, u32[]{:S(2)}, u32[]{:S(2)}) %collective-permute-start.2) | collective-permute-done | bytes 168992 | tf_op jit(solution)/shard_map/ppermute | solution.py:12
  56.3 0.2 fusion.58
  56.6 0.2 fusion.57
  56.9 3.5 %collective-permute-start.3 = (bf16[10,66,128]{2,1,0:T(8,128)(2,1)S(1)}, bf16[10,66,128]{2,1,0:T(8,128)(2,1)S(1)}, u32[]{:S(2)}, u32[]{:S(2)}) collective-permute-start(bf16[10,66,128]{2,1,0:T(8,128)(2,1)S(1)} %pad_maximum_fusion.5), channel_id=1, source_target_pairs={{0,64},{16,80},{32,96},{48,112},{64,128},{80,144},{96,160},{112,17... | collective-permute-start | bytes 506888 | tf_op jit(solution)/shard_map/ppermute | solution.py:12
  60.4 2.0 %fusion.8 = f32[2,256,10,64]{1,3,2,0:T(8,128)S(1)} fusion(f32[10,2,256]{2,0,1:T(8,128)S(1)} %copy-done.9, f32[10,2,256]{2,0,1:T(8,128)S(1)} %copy-done.8, f32[2,256,256]{2,1,0:T(8,128)S(1)} %copy-done.5, pred[2,256,256]{2,1,0:T(8,128)(4,1)S(1)} %compare_and_fusion, bf16[2,256,10,64]{1,0,3,2:T(2,128)(2,1)S(1)} %reshape.490), kind=kOutput, calls=%fused_computation.17 | convolution fusion | flops 175636480 | bytes 2662400 | tf_op jit(solution)/shard_map/hcts,cshp->cthp/dot_general | solution.py:148
  62.4 1.0 collective-permute-done.3
  63.4 0.2 multiply_reduce_fusion.1
  63.7 0.1 fusion.37
  63.9 0.1 copy-done.4
  64.1 5.7 %collective-permute-start.4 = (bf16[10,66,128]{2,1,0:T(8,128)(2,1)S(1)}, bf16[10,66,128]{2,1,0:T(8,128)(2,1)S(1)}, u32[]{:S(2)}, u32[]{:S(2)}) collective-permute-start(bf16[10,66,128]{2,1,0:T(8,128)(2,1)S(1)} %pad_maximum_fusion.6), channel_id=1, source_target_pairs={{0,128},{16,144},{32,160},{48,176},{64,192},{80,208},{96,224},{112... | collective-permute-start | bytes 506888 | tf_op jit(solution)/shard_map/ppermute | solution.py:12
  69.9 2.9 %collective-permute-done.4 = bf16[10,66,128]{2,1,0:T(8,128)(2,1)S(1)} collective-permute-done((bf16[10,66,128]{2,1,0:T(8,128)(2,1)S(1)}, bf16[10,66,128]{2,1,0:T(8,128)(2,1)S(1)}, u32[]{:S(2)}, u32[]{:S(2)}) %collective-permute-start.4) | collective-permute-done | bytes 168992 | tf_op jit(solution)/shard_map/ppermute | solution.py:12
  72.8 0.7 copy-done.7
  73.5 0.2 fusion.47
  73.8 1.2 add_convert_fusion
  74.9 13.6 %collective-permute-start.6 = (bf16[10,64,128]{2,1,0:T(8,128)(2,1)S(1)}, bf16[10,64,128]{2,1,0:T(8,128)(2,1)S(1)}, u32[]{:S(2)}, u32[]{:S(2)}) collective-permute-start(bf16[10,64,128]{2,1,0:T(8,128)(2,1)S(1)} %add_convert_fusion), channel_id=1, source_target_pairs={{0,272},{16,288},{32,304},{48,320},{64,336},{80,352},{96,368},{112... | collective-permute-start | bytes 491528 | tf_op jit(solution)/shard_map/ppermute | solution.py:12
  88.6 2.1 %collective-permute-start.5 = (bf16[10,66,128]{2,1,0:T(8,128)(2,1)S(1)}, bf16[10,66,128]{2,1,0:T(8,128)(2,1)S(1)}, u32[]{:S(2)}, u32[]{:S(2)}) collective-permute-start(bf16[10,66,128]{2,1,0:T(8,128)(2,1)S(1)} %pad_maximum_fusion.7), channel_id=1, source_target_pairs={{0,16},{16,32},{32,48},{48,64},{64,80},{80,96},{96,112},{112,128},... | collective-permute-start | bytes 506888 | tf_op jit(solution)/shard_map/ppermute | solution.py:12
  90.7 0.8 fusion.10
  91.5 4.5 %collective-permute-done.5 = bf16[10,66,128]{2,1,0:T(8,128)(2,1)S(1)} collective-permute-done((bf16[10,66,128]{2,1,0:T(8,128)(2,1)S(1)}, bf16[10,66,128]{2,1,0:T(8,128)(2,1)S(1)}, u32[]{:S(2)}, u32[]{:S(2)}) %collective-permute-start.5) | collective-permute-done | bytes 168992 | tf_op jit(solution)/shard_map/ppermute | solution.py:12
  96.0 0.2 fusion.48
  96.2 0.8 fusion.11
  97.0 0.7 copy.121
  97.8 0.5 multiply_reduce_fusion
  98.3 0.3 copy-done.3
  98.7 0.2 copy.125
  98.9 0.3 copy-done.1
  99.2 3.6 %convert_bitcast_fusion = bf16[8,512,320]{1,2,0:T(8,128)(2,1)S(1)} fusion(bf16[640,8,320]{0,2,1:T(8,128)(2,1)S(1)} %bitcast.106, f32[640]{0:T(1024)S(1)} %copy-done.14, bf16[512,640]{0,1:T(8,128)(2,1)} %copy.122, bf16[512,640]{0,1:T(8,128)(2,1)} %bitcast.108), kind=kOutput, calls=%fused_computation.3 | convolution fusion | flops 1681981440 | bytes 7211520 | tf_op jit(solution)/shard_map/tc,cgk->gtk/dot_general | solution.py:167
  102.9 2.0 %pad_maximum_fusion = bf16[8,514,320]{1,2,0:T(8,128)(2,1)} fusion(bf16[8,2,320]{1,2,0:T(8,128)(2,1)S(1)} %broadcast_in_dim.212, bf16[8,512,320]{1,2,0:T(8,128)(2,1)S(1)} %convert_bitcast_fusion), kind=kLoop, calls=%fused_computation.1 | loop fusion | flops 5263360 | bytes 5263360 | tf_op jit(solution)/shard_map/concatenate | solution.py:180
  105.0 53.4 %reduce-scatter.2.cloned.1.call-done = bf16[1,514,320]{1,2,0:T(8,128)(2,1)} async-done(((bf16[8,514,320]{1,2,0:T(8,128)(2,1)}), bf16[1,514,320]{1,2,0:T(8,128)(2,1)}) %reduce-scatter.2.cloned.1.call-update) | async-done | bytes 328976 | tf_op jit(solution)/shard_map/reduce_scatter | solution.py:181
  158.4 0.9 slice.268
  159.5 1.8 %fusion.21 = bf16[512,320]{0,1:T(8,128)(2,1)} fusion(bf16[1,514,320]{1,2,0:T(8,128)(2,1)} %reduce-scatter.2.cloned.1.call-done, f32[512]{0:T(512)S(1)} %add_rsqrt_fusion), kind=kLoop, calls=%fused_computation.38 | loop fusion | flops 491520 | bytes 657408 | tf_op jit(solution)/shard_map/convert_element_type | solution.py:184
  (99 shorter events, 3.4 us)
Async XLA Ops:
  6.5 151.9 %reduce-scatter.2.cloned.1.call-start = ((), (), s32[]{:S(2)}) async-start(), calls=%async_computation.1 | async-start | bytes 3686400 | tf_op jit(solution)/shard_map/reduce_scatter | solution.py:181
  9.7 18.4 %collective-permute-start = (bf16[3,1024]{0,1:T(8,128)(2,1)}, bf16[3,1024]{0,1:T(8,128)(2,1)}, u32[]{:S(2)}, u32[]{:S(2)}) collective-permute-start(bf16[3,1024]{0,1:T(8,128)(2,1)} %copy.97), channel_id=1, source_target_pairs={{0,16},{16,32},{32,48},{48,64},{64,80},{80,96},{96,112},{112,128},... | collective-permute-start | bytes 18440 | tf_op jit(solution)/shard_map/ppermute | solution.py:12
  14.6 10.0 %copy-start = (bf16[640,2560]{1,0:T(8,128)(2,1)S(1)}, bf16[640,2560]{1,0:T(8,128)(2,1)}, u32[]{:S(2)}) copy-start(bf16[640,2560]{1,0:T(8,128)(2,1)} %param.23) | copy-start | bytes 9830404
  24.6 6.1 %copy-start.10 = (s32[512]{0:T(512)S(1)}, s32[512]{0:T(512)}, u32[]{:S(2)}) copy-start(s32[512]{0:T(512)} %param.16) | copy-start | bytes 6148
  31.7 5.1 %copy-start.6 = (bf16[512,256]{1,0:T(8,128)(2,1)S(1)}, bf16[512,256]{1,0:T(8,128)(2,1)}, u32[]{:S(2)}) copy-start(bf16[512,256]{1,0:T(8,128)(2,1)} %param.13) | copy-start | bytes 786436
  31.7 5.1 %copy-start.11 = (f32[1,256]{1,0:T(1,128)S(1)}, f32[1,256]{1,0:T(1,128)}, u32[]{:S(2)}) copy-start(f32[1,256]{1,0:T(1,128)} %get-tuple-element.46) | copy-start | bytes 3076
  31.8 5.1 %copy-start.12 = (f32[1,256]{1,0:T(1,128)S(1)}, f32[1,256]{1,0:T(1,128)}, u32[]{:S(2)}) copy-start(f32[1,256]{1,0:T(1,128)} %get-tuple-element.47) | copy-start | bytes 3076
  38.8 8.0 %collective-permute-start.1 = (bf16[10,66,128]{2,1,0:T(8,128)(2,1)S(1)}, bf16[10,66,128]{2,1,0:T(8,128)(2,1)S(1)}, u32[]{:S(2)}, u32[]{:S(2)}) collective-permute-start(bf16[10,66,128]{2,1,0:T(8,128)(2,1)S(1)} %pad_maximum_fusion.3), channel_id=1, source_target_pairs={{0,16},{16,32},{32,48},{48,64},{64,80},{80,96},{96,112},{112,128},... | collective-permute-start | bytes 506888 | tf_op jit(solution)/shard_map/ppermute | solution.py:12
  47.3 13.0 %copy-start.8 = (f32[10,2,256]{2,0,1:T(8,128)S(1)}, f32[10,2,256]{2,0,1:T(8,128)}, u32[]{:S(2)}) copy-start(f32[10,2,256]{2,0,1:T(8,128)} %copy.104) | copy-start | bytes 61444
  47.3 13.0 %copy-start.9 = (f32[10,2,256]{2,0,1:T(8,128)S(1)}, f32[10,2,256]{2,0,1:T(8,128)}, u32[]{:S(2)}) copy-start(f32[10,2,256]{2,0,1:T(8,128)} %copy.106) | copy-start | bytes 61444
  47.4 8.9 %collective-permute-start.2 = (bf16[10,66,128]{2,1,0:T(8,128)(2,1)S(1)}, bf16[10,66,128]{2,1,0:T(8,128)(2,1)S(1)}, u32[]{:S(2)}, u32[]{:S(2)}) collective-permute-start(bf16[10,66,128]{2,1,0:T(8,128)(2,1)S(1)} %pad_maximum_fusion.4), channel_id=1, source_target_pairs={{0,32},{16,48},{32,64},{48,80},{64,96},{80,112},{96,128},{112,144}... | collective-permute-start | bytes 506888 | tf_op jit(solution)/shard_map/ppermute | solution.py:12
  56.6 3.8 %copy-start.5 = (f32[2,256,256]{2,1,0:T(8,128)S(1)}, f32[2,256,256]{2,1,0:T(8,128)}, u32[]{:S(2)}) copy-start(f32[2,256,256]{2,1,0:T(8,128)} %fusion.67) | copy-start | bytes 1572868
  56.9 6.5 %collective-permute-start.3 = (bf16[10,66,128]{2,1,0:T(8,128)(2,1)S(1)}, bf16[10,66,128]{2,1,0:T(8,128)(2,1)S(1)}, u32[]{:S(2)}, u32[]{:S(2)}) collective-permute-start(bf16[10,66,128]{2,1,0:T(8,128)(2,1)S(1)} %pad_maximum_fusion.5), channel_id=1, source_target_pairs={{0,64},{16,80},{32,96},{48,112},{64,128},{80,144},{96,160},{112,17... | collective-permute-start | bytes 506888 | tf_op jit(solution)/shard_map/ppermute | solution.py:12
  63.4 0.7 copy-start.4
  63.7 27.0 %copy-start.13 = (f32[10]{0:T(128)S(1)}, f32[10]{0:T(128)}, u32[]{:S(2)}) copy-start(f32[10]{0:T(128)} %param.21) | copy-start | bytes 124
  64.1 8.7 %collective-permute-start.4 = (bf16[10,66,128]{2,1,0:T(8,128)(2,1)S(1)}, bf16[10,66,128]{2,1,0:T(8,128)(2,1)S(1)}, u32[]{:S(2)}, u32[]{:S(2)}) collective-permute-start(bf16[10,66,128]{2,1,0:T(8,128)(2,1)S(1)} %pad_maximum_fusion.6), channel_id=1, source_target_pairs={{0,128},{16,144},{32,160},{48,176},{64,192},{80,208},{96,224},{112... | collective-permute-start | bytes 506888 | tf_op jit(solution)/shard_map/ppermute | solution.py:12
  72.8 0.7 copy-start.7
  74.9 21.3 %collective-permute-start.6 = (bf16[10,64,128]{2,1,0:T(8,128)(2,1)S(1)}, bf16[10,64,128]{2,1,0:T(8,128)(2,1)S(1)}, u32[]{:S(2)}, u32[]{:S(2)}) collective-permute-start(bf16[10,64,128]{2,1,0:T(8,128)(2,1)S(1)} %add_convert_fusion), channel_id=1, source_target_pairs={{0,272},{16,288},{32,304},{48,320},{64,336},{80,352},{96,368},{112... | collective-permute-start | bytes 491528 | tf_op jit(solution)/shard_map/ppermute | solution.py:12
  88.6 7.4 %collective-permute-start.5 = (bf16[10,66,128]{2,1,0:T(8,128)(2,1)S(1)}, bf16[10,66,128]{2,1,0:T(8,128)(2,1)S(1)}, u32[]{:S(2)}, u32[]{:S(2)}) collective-permute-start(bf16[10,66,128]{2,1,0:T(8,128)(2,1)S(1)} %pad_maximum_fusion.7), channel_id=1, source_target_pairs={{0,16},{16,32},{32,48},{48,64},{64,80},{80,96},{96,112},{112,128},... | collective-permute-start | bytes 506888 | tf_op jit(solution)/shard_map/ppermute | solution.py:12
  96.2 1.6 copy-start.2
  97.0 2.2 %copy-start.1 = (bf16[640,2560]{0,1:T(8,128)(2,1)S(1)}, bf16[640,2560]{0,1:T(8,128)(2,1)}, u32[]{:S(2)}) copy-start(bf16[640,2560]{0,1:T(8,128)(2,1)} %copy.123) | copy-start | bytes 9830404
  97.7 1.5 copy-start.14
  97.8 0.8 copy-start.3
Sparse Core Ops, SparseCore 0:
  105.1 53.2 reduce-scatter.1

commit v4 on v3

--- a/solution.py
+++ b/solution.py
@@ -71,7 +71,7 @@
     norm_gain,
     w_out,
 ):
-    highest = lax.Precision.HIGHEST
+    highest = lax.Precision.HIGH
     row_count = x_stream.shape[0]
     head_count = dt_stream.shape[0]
     inner_width = x_stream.shape[1]
@@ -164,12 +164,8 @@
     squares = jnp.sum(gated * gated, axis=1)
     scaled = (gated * norm_gain[None, :]).astype(jnp.bfloat16)
     out_width = w_out.shape[1] // group_count
-    partial_value = jnp.einsum(
-        "tc,cgk->gtk",
-        scaled,
-        w_out.reshape(inner_width, group_count, out_width),
-        preferred_element_type=jnp.float32,
-    ).astype(jnp.bfloat16)
+    partial_value = jnp.dot(scaled, w_out, preferred_element_type=jnp.float32).astype(jnp.bfloat16)
+    partial_value = jnp.transpose(partial_value.reshape(row_count, group_count, out_width), (1, 0, 2))
     pad_rows = -(-row_count // out_width)
     square_rows = jnp.pad(squares, (0, pad_rows * out_width - row_count)).reshape(
         pad_rows, out_width

time: 169 us -> 210 us (1.24)
  other arithmetic: 19.7 us -> 41.5 us
  local copies, waits for them, and re-layouts: 19.7 us -> 37.6 us
  matrix products: 8.98 us -> 14.1 us
  waiting for transfers between devices: 69.8 us -> 65.8 us
    convert_element_type x5, other arithmetic: 1.68 us -> 6.55 us  [with_decay(): return jnp.concatenate([state.astype(jnp.bfloat16), tail], axis=1)]
    convert_element_type x0 -> x1, local copies, waits for them, and re-layouts: none -> 4.43 us  [local(): jnp.dot(scaled, w_out, preferred_element_type=jnp.float32)]
    ppermute x7, waiting for transfers between devices: 16.3 us -> 12.1 us  [from_behind(): return lax.ppermute(block, axis, route)]
    reshape x1, local copies, waits for them, and re-layouts: 0.15 us -> 2.69 us  [local(): block_x = mixed_x.reshape(blocks, SPAN, head_count, head_size)]
    another operation x5, local copies, waits for them, and re-layouts: 0.48 us -> 2.84 us  [with_decay(): jnp.stack([high, low], 1)[:, :, None]]
    unnamed x34 -> x71, local copies, waits for them, and re-layouts: 9.31 us -> 9.37 us
  transfers between devices with their start and end apart: 8 -> 8, of which waited for: 6 -> 5; matrix products, arithmetic and copies ran while one was open for 11% -> 13% of each run, Pallas kernels for 0% -> 0%
where the time goes in v4:
time: 210 us; the launch traced here: 208 us
  waiting for transfers between devices  65.8 us (31%)
  other arithmetic  41.5 us (20%)
  local copies, waits for them, and re-layouts  37.6 us (18%)
  starting transfers between devices  35.2 us (17%)
  matrix products  14.1 us (7%)
  between operations  13.9 us (7%)
    reduce_scatter x1, waiting for transfers between devices, local(): lax.psum_scatter(payload, 'tensor', scatter_dimension=0, tiled=True)[0]  53.7 us
    ppermute x7, starting transfers between devices, from_behind(): return lax.ppermute(block, axis, route)  35.1 us
    ppermute x7, waiting for transfers between devices, from_behind(): return lax.ppermute(block, axis, route)  12.1 us
    unnamed x71, local copies, waits for them, and re-layouts  9.37 us
    convert_element_type x5, other arithmetic, with_decay(): return jnp.concatenate([state.astype(jnp.bfloat16), tail], axis=1)  6.55 us
    dot_general x1, matrix products, local(): jnp.dot(scaled, w_out, preferred_element_type=jnp.float32)  5.16 us
    convert_element_type x2, other arithmetic, causal_conv(): return jax.nn.silu(total).astype(jnp.bfloat16)  4.69 us
    convert_element_type x1, local copies, waits for them, and re-layouts, local(): jnp.dot(scaled, w_out, preferred_element_type=jnp.float32)  4.43 us
  transfers between devices with their start and end apart: 8, of which 5 were waited for; matrix products, arithmetic and copies ran while one was open for 13% of the time, Pallas kernels for 0%

profile of v4, /device:TPU:6, one launch (start us, length us, event | category | flops | bytes accessed | tf_op | source)
XLA Modules:
  0.0 208.1 jit_solution(4393731161834379366)
XLA Ops:
  6.5 0.8 slice.178
  7.4 0.8 fusion.64
  8.3 0.7 slice.177
  9.1 0.9 copy.95
  10.0 3.4 %collective-permute-start = (bf16[3,1024]{0,1:T(8,128)(2,1)}, bf16[3,1024]{0,1:T(8,128)(2,1)}, u32[]{:S(2)}, u32[]{:S(2)}) collective-permute-start(bf16[3,1024]{0,1:T(8,128)(2,1)} %copy.95), channel_id=1, source_target_pairs={{0,16},{16,32},{32,48},{48,64},{64,80},{80,96},{96,112},{112,128},... | collective-permute-start | bytes 18440 | tf_op jit(solution)/shard_map/ppermute | solution.py:12
  14.7 1.4 slice_convert_fusion.13
  16.1 1.5 convert_reduce_fusion.3
  17.6 1.4 broadcast_multiply_fusion
  19.1 1.2 reduce-window.9
  20.6 0.7 slice_reduce_fusion.1
  23.1 2.2 %copy.94 = bf16[512,640]{0,1:T(8,128)(2,1)} copy(bf16[512,640]{1,0:T(8,128)(2,1)} %param.12) | data formatting | bytes 1310720 | tf_op args[0]
  25.4 1.4 mul.434
  26.7 1.3 copy.104
  28.1 0.7 copy.106
  28.8 0.8 copy.108
  29.5 2.2 %copy.120 = bf16[512,640]{0,1:T(8,128)(2,1)} copy(bf16[512,640]{1,0:T(8,128)(2,1)} %param.14) | data formatting | bytes 1310720 | tf_op args[2]
  33.0 1.3 pad_maximum_fusion.10
  34.2 1.3 broadcast_compare_fusion
  36.3 0.8 fusion.62
  37.6 0.7 pad_maximum_fusion.9
  38.4 1.3 slice_compare_fusion.2
  40.2 1.3 copy.111
  41.4 1.2 reduce_window.9
  42.6 1.3 copy.117
  43.9 1.5 multiply_bitcast_fusion
  46.0 1.5 slice.238
  47.5 0.9 copy.97
  48.4 1.6 multiply_convert_fusion.7
  50.0 0.9 slice.233
  51.0 3.1 %multiply_convert_fusion.5 = bf16[512,640]{0,1:T(8,128)(2,1)} fusion(bf16[512,640]{0,1:T(8,128)(2,1)S(1)} %copy-done.5, bf16[3,640]{0,1:T(8,128)(2,1)S(1)} %slice.233, f32[640]{0:T(1024)} %get-tuple-element.12, f32[640]{0:T(1024)} %get-tuple-element.13, f32[640]{0:T(1024)} %get-tuple-element.11, f32[640]{0:T(1024)} %get-tuple-element.10, ...), kind=kLoop, calls=%fused_computation.28 | loop fusion | flops 9502720 | bytes 1326848 | tf_op jit(solution)/shard_map/convert_element_type | solution.py:27
  54.1 2.7 %reshape.490 = bf16[2,256,10,64]{1,0,3,2:T(2,128)(2,1)} reshape(bf16[512,640]{0,1:T(8,128)(2,1)} %multiply_convert_fusion.5) | data formatting | bytes 1310720 | tf_op jit(solution)/shard_map/reshape | solution.py:113
  56.8 1.7 fusion.12
  58.5 0.8 copy-done.3
  59.3 0.8 fusion.60
  60.2 0.7 pad_maximum_fusion.3
  60.9 3.4 %collective-permute-start.1 = (bf16[10,66,128]{2,1,0:T(8,128)(2,1)}, bf16[10,66,128]{2,1,0:T(8,128)(2,1)}, u32[]{:S(2)}, u32[]{:S(2)}) collective-permute-start(bf16[10,66,128]{2,1,0:T(8,128)(2,1)} %pad_maximum_fusion.3), channel_id=1, source_target_pairs={{0,16},{16,32},{32,48},{48,64},{64,80},{80,96},{96,112},{112,128},... | collective-permute-start | bytes 506888 | tf_op jit(solution)/shard_map/ppermute | solution.py:12
  64.3 0.8 compare_and_fusion
  65.3 4.0 %collective-permute-done.1 = bf16[10,66,128]{2,1,0:T(8,128)(2,1)} collective-permute-done((bf16[10,66,128]{2,1,0:T(8,128)(2,1)}, bf16[10,66,128]{2,1,0:T(8,128)(2,1)}, u32[]{:S(2)}, u32[]{:S(2)}) %collective-permute-start.1) | collective-permute-done | bytes 168992 | tf_op jit(solution)/shard_map/ppermute | solution.py:12
  69.2 1.4 multiply_reduce_fusion.3
  72.3 1.3 copy.113
  73.6 1.1 fusion.34
  74.7 0.8 broadcast_in_dim.208
  75.5 4.3 %collective-permute-start.2 = (bf16[10,66,128]{2,1,0:T(8,128)(2,1)S(1)}, bf16[10,66,128]{2,1,0:T(8,128)(2,1)S(1)}, u32[]{:S(2)}, u32[]{:S(2)}) collective-permute-start(bf16[10,66,128]{2,1,0:T(8,128)(2,1)S(1)} %pad_maximum_fusion.4), channel_id=1, source_target_pairs={{0,32},{16,48},{32,64},{48,80},{64,96},{80,112},{96,128},{112,144}... | collective-permute-start | bytes 506888 | tf_op jit(solution)/shard_map/ppermute | solution.py:12
  79.9 1.0 fusion.65
  80.9 3.6 %collective-permute-done.2 = bf16[10,66,128]{2,1,0:T(8,128)(2,1)S(1)} collective-permute-done((bf16[10,66,128]{2,1,0:T(8,128)(2,1)S(1)}, bf16[10,66,128]{2,1,0:T(8,128)(2,1)S(1)}, u32[]{:S(2)}, u32[]{:S(2)}) %collective-permute-start.2) | collective-permute-done | bytes 168992 | tf_op jit(solution)/shard_map/ppermute | solution.py:12
  85.4 2.1 fusion.55
  87.6 3.5 %collective-permute-start.3 = (bf16[10,66,128]{2,1,0:T(8,128)(2,1)S(1)}, bf16[10,66,128]{2,1,0:T(8,128)(2,1)S(1)}, u32[]{:S(2)}, u32[]{:S(2)}) collective-permute-start(bf16[10,66,128]{2,1,0:T(8,128)(2,1)S(1)} %pad_maximum_fusion.5), channel_id=1, source_target_pairs={{0,64},{16,80},{32,96},{48,112},{64,128},{80,144},{96,160},{112,17... | collective-permute-start | bytes 506888 | tf_op jit(solution)/shard_map/ppermute | solution.py:12
  91.1 3.7 %fusion.8 = f32[2,256,10,64]{1,3,2,0:T(8,128)} fusion(f32[10,2,256]{2,0,1:T(8,128)} %copy.104, f32[10,2,256]{2,0,1:T(8,128)} %copy.102, f32[2,256,256]{2,1,0:T(8,128)S(1)} %copy-done.9, pred[2,256,256]{2,1,0:T(8,128)(4,1)} %compare_and_fusion, bf16[2,256,10,64]{1,0,3,2:T(2,128)(2,1)S(1)} %copy-done.1), kind=kOutput, calls=%fused_computation.17 | convolution fusion | flops 175636480 | bytes 2662400 | tf_op jit(solution)/shard_map/hcts,cshp->cthp/dot_general | solution.py:148
  95.8 1.2 fusion.35
  97.1 5.7 %collective-permute-start.4 = (bf16[10,66,128]{2,1,0:T(8,128)(2,1)S(1)}, bf16[10,66,128]{2,1,0:T(8,128)(2,1)S(1)}, u32[]{:S(2)}, u32[]{:S(2)}) collective-permute-start(bf16[10,66,128]{2,1,0:T(8,128)(2,1)S(1)} %pad_maximum_fusion.6), channel_id=1, source_target_pairs={{0,128},{16,144},{32,160},{48,176},{64,192},{80,208},{96,224},{112... | collective-permute-start | bytes 506888 | tf_op jit(solution)/shard_map/ppermute | solution.py:12
  102.8 1.8 slice_add_fusion
  104.6 1.2 collective-permute-done.4
  105.9 0.7 copy-done.13
  106.8 1.3 add_convert_fusion
  108.2 12.7 %collective-permute-start.6 = (bf16[10,64,128]{2,1,0:T(8,128)(2,1)S(1)}, bf16[10,64,128]{2,1,0:T(8,128)(2,1)S(1)}, u32[]{:S(2)}, u32[]{:S(2)}) collective-permute-start(bf16[10,64,128]{2,1,0:T(8,128)(2,1)S(1)} %add_convert_fusion), channel_id=1, source_target_pairs={{0,272},{16,288},{32,304},{48,320},{64,336},{80,352},{96,368},{112... | collective-permute-start | bytes 491528 | tf_op jit(solution)/shard_map/ppermute | solution.py:12
  121.0 2.1 %collective-permute-start.5 = (bf16[10,66,128]{2,1,0:T(8,128)(2,1)S(1)}, bf16[10,66,128]{2,1,0:T(8,128)(2,1)S(1)}, u32[]{:S(2)}, u32[]{:S(2)}) collective-permute-start(bf16[10,66,128]{2,1,0:T(8,128)(2,1)S(1)} %pad_maximum_fusion.7), channel_id=1, source_target_pairs={{0,16},{16,32},{32,48},{48,64},{64,80},{80,96},{96,112},{112,128},... | collective-permute-start | bytes 506888 | tf_op jit(solution)/shard_map/ppermute | solution.py:12
  123.2 2.0 fusion.10
  125.2 3.3 %collective-permute-done.5 = bf16[10,66,128]{2,1,0:T(8,128)(2,1)S(1)} collective-permute-done((bf16[10,66,128]{2,1,0:T(8,128)(2,1)S(1)}, bf16[10,66,128]{2,1,0:T(8,128)(2,1)S(1)}, u32[]{:S(2)}, u32[]{:S(2)}) %collective-permute-start.5) | collective-permute-done | bytes 168992 | tf_op jit(solution)/shard_map/ppermute | solution.py:12
  131.2 5.2 %convolution_convert_fusion = bf16[512,2560]{1,0:T(8,128)(2,1)} fusion(bf16[640,2560]{1,0:T(8,128)(2,1)S(1)} %copy-done, f32[640]{0:T(1024)S(1)} %copy-done.33, bf16[512,640]{0,1:T(8,128)(2,1)} %copy.120, bf16[512,640]{0,1:T(8,128)(2,1)} %bitcast.105), kind=kOutput, calls=%fused_computation.1 | convolution fusion | flops 1681981440 | bytes 7211520 | tf_op jit(solution)/shard_map/dot_general | solution.py:167
  136.3 4.4 %copy.121 = bf16[512,2560]{0,1:T(8,128)(2,1)} copy(bf16[512,2560]{1,0:T(8,128)(2,1)} %convolution_convert_fusion) | data formatting | bytes 5242880 | tf_op jit(solution)/shard_map/convert_element_type | solution.py:167
  140.8 3.8 %pad_maximum_fusion = bf16[8,514,320]{1,2,0:T(8,128)(2,1)} fusion(bf16[8,2,320]{1,2,0:T(8,128)(2,1)S(1)} %broadcast_in_dim.212, bf16[8,512,320]{1,2,0:T(8,128)(2,1)} %bitcast.103), kind=kLoop, calls=%fused_computation.2 | loop fusion | flops 5263360 | bytes 5263360 | tf_op jit(solution)/shard_map/concatenate | solution.py:176
  144.6 53.7 %reduce-scatter.2.cloned.1.call-done = bf16[1,514,320]{1,2,0:T(8,128)(2,1)} async-done(((bf16[8,514,320]{1,2,0:T(8,128)(2,1)}), bf16[1,514,320]{1,2,0:T(8,128)(2,1)}) %reduce-scatter.2.cloned.1.call-update) | async-done | bytes 328976 | tf_op jit(solution)/shard_map/reduce_scatter | solution.py:177
  198.4 0.9 slice.268
  199.4 1.8 fusion.19
  (137 shorter events, 14.7 us)
Async XLA Ops:
  6.5 124.6 %copy-start = (bf16[640,2560]{1,0:T(8,128)(2,1)S(1)}, bf16[640,2560]{1,0:T(8,128)(2,1)}, u32[]{:S(2)}) copy-start(bf16[640,2560]{1,0:T(8,128)(2,1)} %param.23) | copy-start | bytes 9830404
  6.5 191.8 %reduce-scatter.2.cloned.1.call-start = ((), (), s32[]{:S(2)}) async-start(), calls=%async_computation.1 | async-start | bytes 3686400 | tf_op jit(solution)/shard_map/reduce_scatter | solution.py:177
  8.2 13.8 %copy-start.17 = (f32[512]{0:T(512)}, f32[512]{0:T(512)S(1)}, u32[]{:S(2)}) copy-start(f32[512]{0:T(512)S(1)} %get-tuple-element.42) | copy-start | bytes 6148
  10.0 21.7 %collective-permute-start = (bf16[3,1024]{0,1:T(8,128)(2,1)}, bf16[3,1024]{0,1:T(8,128)(2,1)}, u32[]{:S(2)}, u32[]{:S(2)}) collective-permute-start(bf16[3,1024]{0,1:T(8,128)(2,1)} %copy.95), channel_id=1, source_target_pairs={{0,16},{16,32},{32,48},{48,64},{64,80},{80,96},{96,112},{112,128},... | collective-permute-start | bytes 18440 | tf_op jit(solution)/shard_map/ppermute | solution.py:12
  21.9 0.6 copy-start.12
  23.1 25.2 %copy-start.10 = (bf16[512,256]{1,0:T(8,128)(2,1)S(1)}, bf16[512,256]{1,0:T(8,128)(2,1)}, u32[]{:S(2)}) copy-start(bf16[512,256]{1,0:T(8,128)(2,1)} %param.13) | copy-start | bytes 786436
  35.5 0.6 copy-start.30
  37.0 0.6 copy-start.18
  39.7 11.3 %copy-start.26 = (pred[512]{0:T(512)(128)(4,1)S(1)}, pred[512]{0:T(512)(128)(4,1)}, u32[]{:S(2)}) copy-start(pred[512]{0:T(512)(128)(4,1)} %get-tuple-element.36) | copy-start | bytes 1540
  45.4 5.6 %copy-start.27 = (pred[512]{0:T(512)(128)(4,1)S(1)}, pred[512]{0:T(512)(128)(4,1)}, u32[]{:S(2)}) copy-start(pred[512]{0:T(512)(128)(4,1)} %get-tuple-element.37) | copy-start | bytes 1540
  48.4 2.6 %copy-start.5 = (bf16[512,640]{0,1:T(8,128)(2,1)S(1)}, bf16[512,640]{0,1:T(8,128)(2,1)}, u32[]{:S(2)}) copy-start(bf16[512,640]{0,1:T(8,128)(2,1)} %copy.94) | copy-start | bytes 1966084
  48.4 2.6 %copy-start.28 = (pred[512]{0:T(512)(128)(4,1)S(1)}, pred[512]{0:T(512)(128)(4,1)}, u32[]{:S(2)}) copy-start(pred[512]{0:T(512)(128)(4,1)} %get-tuple-element.38) | copy-start | bytes 1540
  48.4 2.6 %copy-start.29 = (pred[512]{0:T(512)(128)(4,1)S(1)}, pred[512]{0:T(512)(128)(4,1)}, u32[]{:S(2)}) copy-start(pred[512]{0:T(512)(128)(4,1)} %get-tuple-element.41) | copy-start | bytes 1540
  54.1 5.2 %copy-start.24 = (f32[10]{0:T(128)S(1)}, f32[10]{0:T(128)}, u32[]{:S(2)}) copy-start(f32[10]{0:T(128)} %get-tuple-element.53) | copy-start | bytes 124
  54.1 5.2 %copy-start.31 = (f32[10]{0:T(128)S(1)}, f32[10]{0:T(128)}, u32[]{:S(2)}) copy-start(f32[10]{0:T(128)} %get-tuple-element.52) | copy-start | bytes 124
  56.8 3.4 %copy-start.20 = (bf16[10,2]{1,0:T(8,128)(2,1)S(1)}, bf16[10,2]{1,0:T(8,128)(2,1)}, u32[]{:S(2)}) copy-start(bf16[10,2]{1,0:T(8,128)(2,1)} %copy.111) | copy-start | bytes 124
  56.8 7.5 %copy-start.11 = (pred[256,256]{1,0:T(8,128)(4,1)S(1)}, pred[256,256]{1,0:T(8,128)(4,1)}, u32[]{:S(2)}) copy-start(pred[256,256]{1,0:T(8,128)(4,1)} %iota_compare_fusion) | copy-start | bytes 196612
  56.8 8.4 %copy-start.19 = (f32[10]{0:T(128)S(1)}, f32[10]{0:T(128)}, u32[]{:S(2)}) copy-start(f32[10]{0:T(128)} %copy-done.18) | copy-start | bytes 124
  58.5 0.8 copy-start.3
  60.9 8.3 %collective-permute-start.1 = (bf16[10,66,128]{2,1,0:T(8,128)(2,1)}, bf16[10,66,128]{2,1,0:T(8,128)(2,1)}, u32[]{:S(2)}, u32[]{:S(2)}) collective-permute-start(bf16[10,66,128]{2,1,0:T(8,128)(2,1)} %pad_maximum_fusion.3), channel_id=1, source_target_pairs={{0,16},{16,32},{32,48},{48,64},{64,80},{80,96},{96,112},{112,128},... | collective-permute-start | bytes 506888 | tf_op jit(solution)/shard_map/ppermute | solution.py:12
  71.2 0.5 copy-start.21
  73.6 11.7 %copy-start.22 = (f32[10,1]{0,1:T(1,128)S(1)}, f32[10,1]{0,1:T(1,128)}, u32[]{:S(2)}) copy-start(f32[10,1]{0,1:T(1,128)} %copy-done.21) | copy-start | bytes 124
  75.5 8.9 %collective-permute-start.2 = (bf16[10,66,128]{2,1,0:T(8,128)(2,1)S(1)}, bf16[10,66,128]{2,1,0:T(8,128)(2,1)S(1)}, u32[]{:S(2)}, u32[]{:S(2)}) collective-permute-start(bf16[10,66,128]{2,1,0:T(8,128)(2,1)S(1)} %pad_maximum_fusion.4), channel_id=1, source_target_pairs={{0,32},{16,48},{32,64},{48,80},{64,96},{80,112},{96,128},{112,144}... | collective-permute-start | bytes 506888 | tf_op jit(solution)/shard_map/ppermute | solution.py:12
  84.4 0.7 copy-start.14
  85.4 5.7 %copy-start.1 = (bf16[2,256,10,64]{1,0,3,2:T(2,128)(2,1)S(1)}, bf16[2,256,10,64]{1,0,3,2:T(2,128)(2,1)}, u32[]{:S(2)}) copy-start(bf16[2,256,10,64]{1,0,3,2:T(2,128)(2,1)} %reshape.490) | copy-start | bytes 1966084
  85.4 5.7 %copy-start.9 = (f32[2,256,256]{2,1,0:T(8,128)S(1)}, f32[2,256,256]{2,1,0:T(8,128)}, u32[]{:S(2)}) copy-start(f32[2,256,256]{2,1,0:T(8,128)} %fusion.65) | copy-start | bytes 1572868
  87.6 7.2 %copy-start.16 = (f32[2,256,10]{1,0,2:T(2,128)S(1)}, f32[2,256,10]{1,0,2:T(2,128)}, u32[]{:S(2)}) copy-start(f32[2,256,10]{1,0,2:T(2,128)} %get-tuple-element.32) | copy-start | bytes 61444
  87.6 8.1 %copy-start.23 = (f32[10,1]{0,1:T(1,128)S(1)}, f32[10,1]{0,1:T(1,128)}, u32[]{:S(2)}) copy-start(f32[10,1]{0,1:T(1,128)} %copy-done.21) | copy-start | bytes 124
  87.6 15.2 %copy-start.25 = (f32[10]{0:T(128)S(1)}, f32[10]{0:T(128)}, u32[]{:S(2)}) copy-start(f32[10]{0:T(128)} %get-tuple-element.53) | copy-start | bytes 124
  87.6 7.2 %collective-permute-start.3 = (bf16[10,66,128]{2,1,0:T(8,128)(2,1)S(1)}, bf16[10,66,128]{2,1,0:T(8,128)(2,1)S(1)}, u32[]{:S(2)}, u32[]{:S(2)}) collective-permute-start(bf16[10,66,128]{2,1,0:T(8,128)(2,1)S(1)} %pad_maximum_fusion.5), channel_id=1, source_target_pairs={{0,64},{16,80},{32,96},{48,112},{64,128},{80,144},{96,160},{112,17... | collective-permute-start | bytes 506888 | tf_op jit(solution)/shard_map/ppermute | solution.py:12
  94.8 0.7 copy-start.8
  95.8 27.3 %copy-start.32 = (f32[10]{0:T(128)S(1)}, f32[10]{0:T(128)}, u32[]{:S(2)}) copy-start(f32[10]{0:T(128)} %param.21) | copy-start | bytes 124
  97.1 8.8 %collective-permute-start.4 = (bf16[10,66,128]{2,1,0:T(8,128)(2,1)S(1)}, bf16[10,66,128]{2,1,0:T(8,128)(2,1)S(1)}, u32[]{:S(2)}, u32[]{:S(2)}) collective-permute-start(bf16[10,66,128]{2,1,0:T(8,128)(2,1)S(1)} %pad_maximum_fusion.6), channel_id=1, source_target_pairs={{0,128},{16,144},{32,160},{48,176},{64,192},{80,208},{96,224},{112... | collective-permute-start | bytes 506888 | tf_op jit(solution)/shard_map/ppermute | solution.py:12
  105.9 0.7 copy-start.13
  106.8 16.3 %copy-start.2 = (bf16[2,256,10,64]{1,0,3,2:T(2,128)(2,1)S(1)}, bf16[2,256,10,64]{1,0,3,2:T(2,128)(2,1)}, u32[]{:S(2)}) copy-start(bf16[2,256,10,64]{1,0,3,2:T(2,128)(2,1)} %reshape.490) | copy-start | bytes 1966084
  106.8 16.3 %copy-start.7 = (f32[1,10,64,128]{3,2,1,0:T(8,128)S(1)}, f32[1,10,64,128]{3,2,1,0:T(8,128)}, u32[]{:S(2)}) copy-start(f32[1,10,64,128]{3,2,1,0:T(8,128)} %slice_add_fusion) | copy-start | bytes 983044
  108.2 20.4 %collective-permute-start.6 = (bf16[10,64,128]{2,1,0:T(8,128)(2,1)S(1)}, bf16[10,64,128]{2,1,0:T(8,128)(2,1)S(1)}, u32[]{:S(2)}, u32[]{:S(2)}) collective-permute-start(bf16[10,64,128]{2,1,0:T(8,128)(2,1)S(1)} %add_convert_fusion), channel_id=1, source_target_pairs={{0,272},{16,288},{32,304},{48,320},{64,336},{80,352},{96,368},{112... | collective-permute-start | bytes 491528 | tf_op jit(solution)/shard_map/ppermute | solution.py:12
  121.0 7.4 %collective-permute-start.5 = (bf16[10,66,128]{2,1,0:T(8,128)(2,1)S(1)}, bf16[10,66,128]{2,1,0:T(8,128)(2,1)S(1)}, u32[]{:S(2)}, u32[]{:S(2)}) collective-permute-start(bf16[10,66,128]{2,1,0:T(8,128)(2,1)S(1)} %pad_maximum_fusion.7), channel_id=1, source_target_pairs={{0,16},{16,32},{32,48},{48,64},{64,80},{80,96},{96,112},{112,128},... | collective-permute-start | bytes 506888 | tf_op jit(solution)/shard_map/ppermute | solution.py:12
  123.2 2.0 copy-start.15
  129.2 1.1 copy-start.4
  129.9 1.2 copy-start.33
  130.0 0.8 copy-start.6
Sparse Core Ops, SparseCore 0:
  144.7 53.5 reduce-scatter.1

commit v5 on v3

--- a/solution.py
+++ b/solution.py
@@ -39,22 +39,23 @@
     return decay, packed[:, :-2].astype(jnp.float32)
 
 
-def pass_state(device_decay, local_final):
+def pass_state(device_decay, local_final, passengers):
     shard_count = lax.axis_size("seq")
     decay, state = device_decay, local_final
     window = 1
     while 2 * window < shard_count - 1:
-        prev_decay, prev_state = split_decay(
-            from_behind(with_decay(decay, state), "seq", window)
-        )
+        received = from_behind(with_decay(decay, state), "seq", window)
+        if window == 1:
+            received, passengers = lax.optimization_barrier((received, passengers))
+        prev_decay, prev_state = split_decay(received)
         state = decay[:, None, None] * prev_state + state
         decay = decay * prev_decay
         window *= 2
     near_decay, near_state = split_decay(from_behind(with_decay(decay, state), "seq", 1))
     if window + 1 < shard_count:
         far_state = from_behind(state.astype(jnp.bfloat16), "seq", window + 1)
-        return near_decay[:, None, None] * far_state.astype(jnp.float32) + near_state
-    return near_state
+        return near_decay[:, None, None] * far_state.astype(jnp.float32) + near_state, passengers
+    return near_state, passengers
 
 
 def local(
@@ -149,7 +150,7 @@
         + reached * jnp.transpose(entry_gain, (1, 2, 0))[..., None]
         + skip_term
     )
-    incoming = pass_state(device_decay, local_final)
+    incoming, (z_gate, w_out) = pass_state(device_decay, local_final, (z_gate, w_out))
     prefix = jnp.cumprod(
         jnp.concatenate([jnp.ones((head_count, 1), jnp.float32), block_decay[:, :-1]], axis=1),
         axis=1,

time: 169 us -> 168 us (level)
  waiting for transfers between devices: 69.8 us -> 61.9 us
  starting transfers between devices: 36 us -> 40.7 us
  local copies, waits for them, and re-layouts: 19.7 us -> 16.4 us
  other arithmetic: 19.7 us -> 22.8 us
  matrix products: 8.98 us -> 10.8 us
    unnamed x34 -> x42, local copies, waits for them, and re-layouts: 9.31 us -> 1.53 us
    ppermute x7, waiting for transfers between devices: 16.3 us -> 8.78 us  [from_behind(): return lax.ppermute(block, axis, route)]
    optimization_barrier x0 -> x2, local copies, waits for them, and re-layouts: none -> 6.83 us  [pass_state(): received, passengers = lax.optimization_barrier((received, passengers))]
    ppermute x7, starting transfers between devices: 36 us -> 40.7 us  [from_behind(): return lax.ppermute(block, axis, route)]
    convert_element_type x2, other arithmetic: 4.74 us -> 2.43 us  [causal_conv(): return jax.nn.silu(total).astype(jnp.bfloat16)]
  transfers between devices with their start and end apart: 8 -> 8, of which waited for: 6 -> 4; matrix products, arithmetic and copies ran while one was open for 11% -> 13% of each run, Pallas kernels for 0% -> 0%
where the time goes in v5:
time: 168 us; the launch traced here: 167 us
  waiting for transfers between devices  61.9 us (37%)
  starting transfers between devices  40.7 us (24%)
  other arithmetic  22.8 us (14%)
  local copies, waits for them, and re-layouts  16.4 us (10%)
  between operations  13.9 us (8%)
  matrix products  10.8 us (6%)
    reduce_scatter x1, waiting for transfers between devices, local(): lax.psum_scatter(payload, 'tensor', scatter_dimension=0, tiled=True)[0]  53.1 us
    ppermute x7, starting transfers between devices, from_behind(): return lax.ppermute(block, axis, route)  40.7 us
    ppermute x7, waiting for transfers between devices, from_behind(): return lax.ppermute(block, axis, route)  8.78 us
    optimization_barrier x2, local copies, waits for them, and re-layouts, pass_state(): received, passengers = lax.optimization_barrier((received, passengers))  6.83 us
    dot_general x1, matrix products, local(): jnp.einsum('tc,cgk->gtk', scaled, w_out.reshape(inner_width, group_count,...  3.64 us
  transfers between devices with their start and end apart: 8, of which 4 were waited for; matrix products, arithmetic and copies ran while one was open for 13% of the time, Pallas kernels for 0%

profile of v5, /device:TPU:6, one launch (start us, length us, event | category | flops | bytes accessed | tf_op | source)
XLA Modules:
  0.0 166.6 jit_solution(14074644077616468354)
XLA Ops:
  6.5 0.8 convert_convert_fusion
  7.4 0.7 slice.176
  8.1 0.7 slice.177
  8.9 0.2 copy.96
  9.1 3.4 %collective-permute-start = (bf16[3,1024]{0,1:T(8,128)(2,1)S(1)}, bf16[3,1024]{0,1:T(8,128)(2,1)S(1)}, u32[]{:S(2)}, u32[]{:S(2)}) collective-permute-start(bf16[3,1024]{0,1:T(8,128)(2,1)S(1)} %copy.96), channel_id=1, source_target_pairs={{0,16},{16,32},{32,48},{48,64},{64,80},{80,96},{96,112},{112,128},... | collective-permute-start | bytes 18440 | tf_op jit(solution)/shard_map/ppermute | solution.py:12
  12.5 0.7 exponential_negate_fusion
  13.2 0.8 compare_select_fusion
  14.0 1.2 reduce-window.9
  15.3 0.1 copy.98
  15.5 0.9 convert_reduce_fusion.3
  16.4 0.8 slice_convert_fusion.11
  17.2 0.2 slice_reduce_fusion.1
  17.5 0.3 copy.102
  17.9 0.6 copy.110
  18.6 0.1 copy.105
  18.7 0.6 copy.112
  19.4 0.7 slice.180
  20.0 0.8 pad_maximum_fusion.10
  20.9 0.2 slice_reduce_fusion
  21.3 0.7 multiply_bitcast_fusion
  22.2 1.7 multiply_convert_fusion.5
  23.9 0.2 reshape.497
  24.1 0.8 multiply_convert_fusion.6
  25.1 0.8 fusion.12
  25.9 0.1 fusion.60
  26.1 5.2 %collective-permute-start.1 = (bf16[10,66,128]{2,1,0:T(8,128)(2,1)S(1)}, bf16[10,66,128]{2,1,0:T(8,128)(2,1)S(1)}, u32[]{:S(2)}, u32[]{:S(2)}) collective-permute-start(bf16[10,66,128]{2,1,0:T(8,128)(2,1)S(1)} %pad_maximum_fusion.3), channel_id=1, source_target_pairs={{0,16},{16,32},{32,48},{48,64},{64,80},{80,96},{96,112},{112,128},... | collective-permute-start | bytes 506888 | tf_op jit(solution)/shard_map/ppermute | solution.py:12
  31.3 0.2 compare_and_fusion
  31.5 2.8 %collective-permute-done.1 = bf16[10,66,128]{2,1,0:T(8,128)(2,1)S(1)} collective-permute-done((bf16[10,66,128]{2,1,0:T(8,128)(2,1)S(1)}, bf16[10,66,128]{2,1,0:T(8,128)(2,1)S(1)}, u32[]{:S(2)}, u32[]{:S(2)}) %collective-permute-start.1) | collective-permute-done | bytes 168992 | tf_op jit(solution)/shard_map/ppermute | solution.py:12
  34.3 0.1 fusion.36
  34.4 0.6 multiply_reduce_fusion.3
  35.3 4.1 %collective-permute-start.2 = (bf16[10,66,128]{2,1,0:T(8,128)(2,1)S(1)}, bf16[10,66,128]{2,1,0:T(8,128)(2,1)S(1)}, u32[]{:S(2)}, u32[]{:S(2)}) collective-permute-start(bf16[10,66,128]{2,1,0:T(8,128)(2,1)S(1)} %pad_maximum_fusion.4), channel_id=1, source_target_pairs={{0,32},{16,48},{32,64},{48,80},{64,96},{80,112},{96,128},{112,144}... | collective-permute-start | bytes 506888 | tf_op jit(solution)/shard_map/ppermute | solution.py:12
  39.4 1.0 fusion.65
  40.4 3.8 %collective-permute-done.2 = bf16[10,66,128]{2,1,0:T(8,128)(2,1)S(1)} collective-permute-done((bf16[10,66,128]{2,1,0:T(8,128)(2,1)S(1)}, bf16[10,66,128]{2,1,0:T(8,128)(2,1)S(1)}, u32[]{:S(2)}, u32[]{:S(2)}) %collective-permute-start.2) | collective-permute-done | bytes 168992 | tf_op jit(solution)/shard_map/ppermute | solution.py:12
  44.2 0.2 fusion.57
  44.4 0.6 copy-done.12
  45.1 0.2 fusion.56
  45.4 4.2 %collective-permute-start.3 = (bf16[10,66,128]{2,1,0:T(8,128)(2,1)S(1)}, bf16[10,66,128]{2,1,0:T(8,128)(2,1)}, u32[]{:S(2)}, u32[]{:S(2)}) collective-permute-start(bf16[10,66,128]{2,1,0:T(8,128)(2,1)S(1)} %pad_maximum_fusion.5), channel_id=1, source_target_pairs={{0,64},{16,80},{32,96},{48,112},{64,128},{80,144},{96,160},{112,17... | collective-permute-start | bytes 506888 | tf_op jit(solution)/shard_map/ppermute | solution.py:12
  49.6 2.7 %fusion.8 = f32[2,256,10,64]{1,3,2,0:T(8,128)S(1)} fusion(f32[10,2,256]{2,0,1:T(8,128)} %copy.112, f32[10,2,256]{2,0,1:T(8,128)} %copy.110, f32[2,256,256]{2,1,0:T(8,128)S(1)} %copy-done.6, pred[2,256,256]{2,1,0:T(8,128)(4,1)S(1)} %compare_and_fusion, bf16[2,256,10,64]{1,0,3,2:T(2,128)(2,1)S(1)} %reshape.497), kind=kOutput, calls=%fused_computation.17 | convolution fusion | flops 175636480 | bytes 2662400 | tf_op jit(solution)/shard_map/hcts,cshp->cthp/dot_general | solution.py:149
  52.4 1.0 multiply_reduce_fusion.1
  53.5 1.1 fusion.37
  54.7 6.5 %collective-permute-start.4 = (bf16[10,66,128]{2,1,0:T(8,128)(2,1)S(1)}, bf16[10,66,128]{2,1,0:T(8,128)(2,1)S(1)}, u32[]{:S(2)}, u32[]{:S(2)}) collective-permute-start(bf16[10,66,128]{2,1,0:T(8,128)(2,1)S(1)} %pad_maximum_fusion.6), channel_id=1, source_target_pairs={{0,128},{16,144},{32,160},{48,176},{64,192},{80,208},{96,224},{112... | collective-permute-start | bytes 506888 | tf_op jit(solution)/shard_map/ppermute | solution.py:12
  61.2 0.8 slice_add_fusion
  62.0 2.2 %collective-permute-done.4 = bf16[10,66,128]{2,1,0:T(8,128)(2,1)S(1)} collective-permute-done((bf16[10,66,128]{2,1,0:T(8,128)(2,1)S(1)}, bf16[10,66,128]{2,1,0:T(8,128)(2,1)S(1)}, u32[]{:S(2)}, u32[]{:S(2)}) %collective-permute-start.4) | collective-permute-done | bytes 168992 | tf_op jit(solution)/shard_map/ppermute | solution.py:12
  64.2 0.2 fusion.46
  64.5 1.8 %add_convert_fusion = bf16[10,64,128]{2,1,0:T(8,128)(2,1)} fusion(f32[10,64,128]{2,1,0:T(8,128)S(1)} %get-tuple-element.23, bf16[10,66,128]{2,1,0:T(8,128)(2,1)S(1)} %collective-permute-done.4, f32[10]{0:T(128)S(1)} %get-tuple-element.12, f32[10]{0:T(128)S(1)} %get-tuple-element.11, bf16[10,66,128]{2,1,0:T(8,128)(2,1)} %collective-permute-done.3), kind=kLoop, calls=%fused_computation.58 | loop fusion | flops 573440 | bytes 819280 | tf_op jit(solution)/shard_map/convert_element_type | solution.py:34
  66.2 15.3 %collective-permute-start.6 = (bf16[10,64,128]{2,1,0:T(8,128)(2,1)}, bf16[10,64,128]{2,1,0:T(8,128)(2,1)}, u32[]{:S(2)}, u32[]{:S(2)}) collective-permute-start(bf16[10,64,128]{2,1,0:T(8,128)(2,1)} %add_convert_fusion), channel_id=1, source_target_pairs={{0,272},{16,288},{32,304},{48,320},{64,336},{80,352},{96,368},{112... | collective-permute-start | bytes 491528 | tf_op jit(solution)/shard_map/ppermute | solution.py:12
  81.6 1.6 pad_maximum_fusion.7
  83.2 2.1 %collective-permute-start.5 = (bf16[10,66,128]{2,1,0:T(8,128)(2,1)}, bf16[10,66,128]{2,1,0:T(8,128)(2,1)}, u32[]{:S(2)}, u32[]{:S(2)}) collective-permute-start(bf16[10,66,128]{2,1,0:T(8,128)(2,1)} %pad_maximum_fusion.7), channel_id=1, source_target_pairs={{0,16},{16,32},{32,48},{48,64},{64,80},{80,96},{96,112},{112,128},... | collective-permute-start | bytes 506888 | tf_op jit(solution)/shard_map/ppermute | solution.py:12
  85.3 0.8 fusion.10
  86.2 5.7 %copy.109 = bf16[640,2560]{0,1:T(8,128)(2,1)} copy(bf16[640,2560]{1,0:T(8,128)(2,1)} %param.23) | data formatting | bytes 6553600 | tf_op jit(solution)/shard_map/optimization_barrier | solution.py:49
  91.9 1.1 copy.123
  93.0 1.0 fusion.47
  94.0 1.8 %fusion.11 = bf16[2,256,10,64]{1,3,2,0:T(8,128)(2,1)S(1)} fusion(f32[2,256,10,64]{1,3,2,0:T(8,128)S(1)} %fusion.10, bf16[2,256,128,1]{2,1,3,0:T(8,128)(2,1)S(1)} %bitcast.112, f32[2,256,10]{1,2,0:T(8,128)S(1)} %copy.121, bf16[10,64,128]{2,1,0:T(8,128)(2,1)} %collective-permute-done.6, bf16[10,66,128]{2,1,0:T(8,128)(2,1)} %collective-permute-done.5, ...), kind=kOutput, calls=%fused_computation.20 | convolution fusion | flops 504627200 | bytes 2445352 | tf_op jit(solution)/shard_map/ctn,hpn->cthp/dot_general | solution.py:158
  95.8 0.7 copy.122
  96.5 0.1 copy.131
  96.6 0.5 multiply_reduce_fusion
  97.2 0.3 copy-done.2
  97.6 0.2 copy.125
  97.7 0.3 copy-done
  98.0 3.6 %convert_bitcast_fusion = bf16[8,512,320]{1,2,0:T(8,128)(2,1)S(1)} fusion(bf16[640,8,320]{0,2,1:T(8,128)(2,1)S(1)} %bitcast.106, f32[640]{0:T(1024)S(1)} %copy-done.19, bf16[512,640]{0,1:T(8,128)(2,1)} %copy.123, bf16[512,640]{0,1:T(8,128)(2,1)} %bitcast.108), kind=kOutput, calls=%fused_computation.3 | convolution fusion | flops 1681981440 | bytes 7211520 | tf_op jit(solution)/shard_map/tc,cgk->gtk/dot_general | solution.py:168
  101.7 2.0 %pad_maximum_fusion = bf16[8,514,320]{1,2,0:T(8,128)(2,1)} fusion(bf16[8,2,320]{1,2,0:T(8,128)(2,1)S(1)} %broadcast_in_dim.212, bf16[8,512,320]{1,2,0:T(8,128)(2,1)S(1)} %convert_bitcast_fusion), kind=kLoop, calls=%fused_computation.1 | loop fusion | flops 5263360 | bytes 5263360 | tf_op jit(solution)/shard_map/concatenate | solution.py:181
  103.8 53.1 %reduce-scatter.2.cloned.1.call-done = bf16[1,514,320]{1,2,0:T(8,128)(2,1)} async-done(((bf16[8,514,320]{1,2,0:T(8,128)(2,1)}), bf16[1,514,320]{1,2,0:T(8,128)(2,1)}) %reduce-scatter.2.cloned.1.call-update) | async-done | bytes 328976 | tf_op jit(solution)/shard_map/reduce_scatter | solution.py:182
  156.8 0.9 slice.265
  157.9 1.8 %fusion.21 = bf16[512,320]{0,1:T(8,128)(2,1)} fusion(bf16[1,514,320]{1,2,0:T(8,128)(2,1)} %reduce-scatter.2.cloned.1.call-done, f32[512]{0:T(512)S(1)} %add_rsqrt_fusion), kind=kLoop, calls=%fused_computation.38 | loop fusion | flops 491520 | bytes 657408 | tf_op jit(solution)/shard_map/convert_element_type | solution.py:185
  (109 shorter events, 3.0 us)
Async XLA Ops:
  6.5 11.0 %copy-start.4 = (bf16[512,640]{1,0:T(8,128)(2,1)S(1)}, bf16[512,640]{1,0:T(8,128)(2,1)}, u32[]{:S(2)}) copy-start(bf16[512,640]{1,0:T(8,128)(2,1)} %param.12) | copy-start | bytes 1966084
  6.5 150.3 %reduce-scatter.2.cloned.1.call-start = ((), (), s32[]{:S(2)}) async-start(), calls=%async_computation.1 | async-start | bytes 3686400 | tf_op jit(solution)/shard_map/reduce_scatter | solution.py:182
  8.8 13.2 %copy-start.11 = (s32[512]{0:T(512)S(1)}, s32[512]{0:T(512)}, u32[]{:S(2)}) copy-start(s32[512]{0:T(512)} %param.16) | copy-start | bytes 6148
  9.1 10.3 %collective-permute-start = (bf16[3,1024]{0,1:T(8,128)(2,1)S(1)}, bf16[3,1024]{0,1:T(8,128)(2,1)S(1)}, u32[]{:S(2)}, u32[]{:S(2)}) collective-permute-start(bf16[3,1024]{0,1:T(8,128)(2,1)S(1)} %copy.96), channel_id=1, source_target_pairs={{0,16},{16,32},{32,48},{48,64},{64,80},{80,96},{96,112},{112,128},... | collective-permute-start | bytes 18440 | tf_op jit(solution)/shard_map/ppermute | solution.py:12
  21.2 4.7 %copy-start.16 = (f32[10]{0:T(128)}, f32[10]{0:T(128)S(1)}, u32[]{:S(2)}) copy-start(f32[10]{0:T(128)S(1)} %get-tuple-element.59) | copy-start | bytes 124
  22.2 1.9 %copy-start.7 = (bf16[512,256]{1,0:T(8,128)(2,1)S(1)}, bf16[512,256]{1,0:T(8,128)(2,1)}, u32[]{:S(2)}) copy-start(bf16[512,256]{1,0:T(8,128)(2,1)} %param.13) | copy-start | bytes 786436
  26.1 8.2 %collective-permute-start.1 = (bf16[10,66,128]{2,1,0:T(8,128)(2,1)S(1)}, bf16[10,66,128]{2,1,0:T(8,128)(2,1)S(1)}, u32[]{:S(2)}, u32[]{:S(2)}) collective-permute-start(bf16[10,66,128]{2,1,0:T(8,128)(2,1)S(1)} %pad_maximum_fusion.3), channel_id=1, source_target_pairs={{0,16},{16,32},{32,48},{48,64},{64,80},{80,96},{96,112},{112,128},... | collective-permute-start | bytes 506888 | tf_op jit(solution)/shard_map/ppermute | solution.py:12
  35.1 10.0 %copy-start.14 = (f32[10,1]{0,1:T(1,128)}, f32[10,1]{0,1:T(1,128)S(1)}, u32[]{:S(2)}) copy-start(f32[10,1]{0,1:T(1,128)S(1)} %get-tuple-element.27) | copy-start | bytes 124
  35.3 8.9 %collective-permute-start.2 = (bf16[10,66,128]{2,1,0:T(8,128)(2,1)S(1)}, bf16[10,66,128]{2,1,0:T(8,128)(2,1)S(1)}, u32[]{:S(2)}, u32[]{:S(2)}) collective-permute-start(bf16[10,66,128]{2,1,0:T(8,128)(2,1)S(1)} %pad_maximum_fusion.4), channel_id=1, source_target_pairs={{0,32},{16,48},{32,64},{48,80},{64,96},{80,112},{96,128},{112,144}... | collective-permute-start | bytes 506888 | tf_op jit(solution)/shard_map/ppermute | solution.py:12
  44.4 0.6 copy-start.12
  45.1 4.5 %copy-start.6 = (f32[2,256,256]{2,1,0:T(8,128)S(1)}, f32[2,256,256]{2,1,0:T(8,128)}, u32[]{:S(2)}) copy-start(f32[2,256,256]{2,1,0:T(8,128)} %fusion.65) | copy-start | bytes 1572868
  45.3 7.0 %copy-start.9 = (f32[2,256,10]{1,0,2:T(2,128)S(1)}, f32[2,256,10]{1,0,2:T(2,128)}, u32[]{:S(2)}) copy-start(f32[2,256,10]{1,0,2:T(2,128)} %get-tuple-element.38) | copy-start | bytes 61444
  45.4 7.0 %copy-start.10 = (f32[10,1,1]{2,1,0:T(1,128)S(1)}, f32[10,1,1]{2,1,0:T(1,128)}, u32[]{:S(2)}) copy-start(f32[10,1,1]{2,1,0:T(1,128)} %get-tuple-element.28) | copy-start | bytes 124
  45.4 8.0 %copy-start.13 = (f32[10]{0:T(128)S(1)}, f32[10]{0:T(128)}, u32[]{:S(2)}) copy-start(f32[10]{0:T(128)} %copy-done.12) | copy-start | bytes 124
  45.4 8.0 %copy-start.15 = (f32[10,1]{0,1:T(1,128)S(1)}, f32[10,1]{0,1:T(1,128)}, u32[]{:S(2)}) copy-start(f32[10,1]{0,1:T(1,128)} %copy-done.14) | copy-start | bytes 124
  45.4 15.8 %copy-start.17 = (f32[10]{0:T(128)S(1)}, f32[10]{0:T(128)}, u32[]{:S(2)}) copy-start(f32[10]{0:T(128)} %copy-done.16) | copy-start | bytes 124
  45.4 6.9 %collective-permute-start.3 = (bf16[10,66,128]{2,1,0:T(8,128)(2,1)S(1)}, bf16[10,66,128]{2,1,0:T(8,128)(2,1)}, u32[]{:S(2)}, u32[]{:S(2)}) collective-permute-start(bf16[10,66,128]{2,1,0:T(8,128)(2,1)S(1)} %pad_maximum_fusion.5), channel_id=1, source_target_pairs={{0,64},{16,80},{32,96},{48,112},{64,128},{80,144},{96,160},{112,17... | collective-permute-start | bytes 506888 | tf_op jit(solution)/shard_map/ppermute | solution.py:12
  53.5 31.8 %copy-start.18 = (f32[10]{0:T(128)S(1)}, f32[10]{0:T(128)}, u32[]{:S(2)}) copy-start(f32[10]{0:T(128)} %param.21) | copy-start | bytes 124
  54.7 9.5 %collective-permute-start.4 = (bf16[10,66,128]{2,1,0:T(8,128)(2,1)S(1)}, bf16[10,66,128]{2,1,0:T(8,128)(2,1)S(1)}, u32[]{:S(2)}, u32[]{:S(2)}) collective-permute-start(bf16[10,66,128]{2,1,0:T(8,128)(2,1)S(1)} %pad_maximum_fusion.6), channel_id=1, source_target_pairs={{0,128},{16,144},{32,160},{48,176},{64,192},{80,208},{96,224},{112... | collective-permute-start | bytes 506888 | tf_op jit(solution)/shard_map/ppermute | solution.py:12
  64.5 20.8 %copy-start.3 = (f32[1,10,64,128]{3,2,1,0:T(8,128)S(1)}, f32[1,10,64,128]{3,2,1,0:T(8,128)}, u32[]{:S(2)}) copy-start(f32[1,10,64,128]{3,2,1,0:T(8,128)} %slice_add_fusion) | copy-start | bytes 983044
  66.2 27.7 %collective-permute-start.6 = (bf16[10,64,128]{2,1,0:T(8,128)(2,1)}, bf16[10,64,128]{2,1,0:T(8,128)(2,1)}, u32[]{:S(2)}, u32[]{:S(2)}) collective-permute-start(bf16[10,64,128]{2,1,0:T(8,128)(2,1)} %add_convert_fusion), channel_id=1, source_target_pairs={{0,272},{16,288},{32,304},{48,320},{64,336},{80,352},{96,368},{112... | collective-permute-start | bytes 491528 | tf_op jit(solution)/shard_map/ppermute | solution.py:12
  83.2 9.8 %collective-permute-start.5 = (bf16[10,66,128]{2,1,0:T(8,128)(2,1)}, bf16[10,66,128]{2,1,0:T(8,128)(2,1)}, u32[]{:S(2)}, u32[]{:S(2)}) collective-permute-start(bf16[10,66,128]{2,1,0:T(8,128)(2,1)} %pad_maximum_fusion.7), channel_id=1, source_target_pairs={{0,16},{16,32},{32,48},{48,64},{64,80},{80,96},{96,112},{112,128},... | collective-permute-start | bytes 506888 | tf_op jit(solution)/shard_map/ppermute | solution.py:12
  85.3 0.8 copy-start.8
  86.2 5.7 %copy-start.5 = (bf16[512,640]{1,0:T(8,128)(2,1)S(1)}, bf16[512,640]{1,0:T(8,128)(2,1)}, u32[]{:S(2)}) copy-start(bf16[512,640]{1,0:T(8,128)(2,1)} %param.14) | copy-start | bytes 1966084
  94.0 2.7 %copy-start.1 = (bf16[512,640]{0,1:T(8,128)(2,1)S(1)}, bf16[512,640]{0,1:T(8,128)(2,1)}, u32[]{:S(2)}) copy-start(bf16[512,640]{0,1:T(8,128)(2,1)} %copy.123) | copy-start | bytes 1966084
  95.8 2.2 %copy-start = (bf16[640,2560]{0,1:T(8,128)(2,1)S(1)}, bf16[640,2560]{0,1:T(8,128)(2,1)}, u32[]{:S(2)}) copy-start(bf16[640,2560]{0,1:T(8,128)(2,1)} %copy.109) | copy-start | bytes 9830404
  96.5 1.5 copy-start.19
  96.6 0.8 copy-start.2
Sparse Core Ops, SparseCore 0:
  103.9 52.8 reduce-scatter.1

commit v6 on v5

--- a/solution.py
+++ b/solution.py
@@ -165,21 +165,16 @@
     squares = jnp.sum(gated * gated, axis=1)
     scaled = (gated * norm_gain[None, :]).astype(jnp.bfloat16)
     out_width = w_out.shape[1] // group_count
-    partial_value = jnp.einsum(
-        "tc,cgk->gtk",
-        scaled,
-        w_out.reshape(inner_width, group_count, out_width),
-        preferred_element_type=jnp.float32,
-    ).astype(jnp.bfloat16)
+    partial_value = jnp.dot(scaled, w_out, preferred_element_type=jnp.float32).astype(jnp.bfloat16)
     pad_rows = -(-row_count // out_width)
     square_rows = jnp.pad(squares, (0, pad_rows * out_width - row_count)).reshape(
-        pad_rows, out_width
+        pad_rows, 1, out_width
     )
     square_rows = jnp.broadcast_to(
-        square_rows.astype(jnp.bfloat16)[None], (group_count, pad_rows, out_width)
-    )
-    payload = jnp.concatenate([partial_value, square_rows], axis=1)
-    summed = lax.psum_scatter(payload, "tensor", scatter_dimension=0, tiled=True)[0]
+        square_rows.astype(jnp.bfloat16), (pad_rows, group_count, out_width)
+    ).reshape(pad_rows, group_count * out_width)
+    payload = jnp.concatenate([partial_value, square_rows], axis=0)
+    summed = lax.psum_scatter(payload, "tensor", scatter_dimension=1, tiled=True)
     total_squares = summed[row_count:].reshape(-1)[:row_count].astype(jnp.float32)
     inv_norm = lax.rsqrt(total_squares / (inner_width * group_count) + 1e-05)
     return (summed[:row_count].astype(jnp.float32) * inv_norm[:, None]).astype(jnp.bfloat16)

time: 168 us -> 214 us (1.27)
  local copies, waits for them, and re-layouts: 16.4 us -> 41.3 us
  other arithmetic: 22.8 us -> 43.3 us
  starting transfers between devices: 40.7 us -> 35.8 us
  matrix products: 10.8 us -> 15.7 us
    reduce_scatter x1 -> x0, waiting for transfers between devices: 53.1 us -> none  [local(): lax.psum_scatter(payload, 'tensor', scatter_dimension=0, tiled=True)[0]]
    unnamed x1 -> x2, waiting for transfers between devices: 0.02 us -> 53 us
    unnamed x42 -> x70, local copies, waits for them, and re-layouts: 1.53 us -> 11.4 us
    ppermute x7, starting transfers between devices: 40.7 us -> 35.8 us  [from_behind(): return lax.ppermute(block, axis, route)]
    optimization_barrier x2 -> x1, local copies, waits for them, and re-layouts: 6.83 us -> 2.21 us  [pass_state(): received, passengers = lax.optimization_barrier((received, passengers))]
    convert_element_type x5, other arithmetic: 3.22 us -> 7.2 us  [with_decay(): return jnp.concatenate([state.astype(jnp.bfloat16), tail], axis=1)]
    another operation x5, local copies, waits for them, and re-layouts: 0.66 us -> 4.06 us
    mul x0 -> x2, local copies, waits for them, and re-layouts: none -> 2.7 us  [local(): scores[None] * decay_now * block_steps[:, :, None, :]]
  transfers between devices with their start and end apart: 8 -> 8, of which waited for: 4 -> 5; matrix products, arithmetic and copies ran while one was open for 13% -> 17% of each run, Pallas kernels for 0% -> 0%
where the time goes in v6:
time: 214 us; the launch traced here: 212 us
  waiting for transfers between devices  62 us (29%)
  other arithmetic  43.3 us (20%)
  local copies, waits for them, and re-layouts  41.3 us (19%)
  starting transfers between devices  35.8 us (17%)
  matrix products  15.7 us (7%)
  between operations  13.8 us (6%)
    unnamed x2, waiting for transfers between devices  53 us
    ppermute x7, starting transfers between devices, from_behind(): return lax.ppermute(block, axis, route)  35.8 us
    unnamed x70, local copies, waits for them, and re-layouts  11.4 us
    ppermute x7, waiting for transfers between devices, from_behind(): return lax.ppermute(block, axis, route)  8.99 us
    convert_element_type x5, other arithmetic, with_decay(): return jnp.concatenate([state.astype(jnp.bfloat16), tail], axis=1)  7.2 us
    convert_element_type x2, other arithmetic, causal_conv(): return jax.nn.silu(total).astype(jnp.bfloat16)  4.68 us
  transfers between devices with their start and end apart: 8, of which 5 were waited for; matrix products, arithmetic and copies ran while one was open for 17% of the time, Pallas kernels for 0%

profile of v6, /device:TPU:6, one launch (start us, length us, event | category | flops | bytes accessed | tf_op | source)
XLA Modules:
  0.0 211.9 jit_solution(13616975715503045496)
XLA Ops:
  6.5 0.8 slice.176
  7.4 0.8 convert_convert_fusion
  9.1 0.9 copy.119
  10.0 3.4 %collective-permute-start = (bf16[3,1024]{0,1:T(8,128)(2,1)}, bf16[3,1024]{0,1:T(8,128)(2,1)}, u32[]{:S(2)}, u32[]{:S(2)}) collective-permute-start(bf16[3,1024]{0,1:T(8,128)(2,1)} %copy.119), channel_id=1, source_target_pairs={{0,16},{16,32},{32,48},{48,64},{64,80},{80,96},{96,112},{112,128},... | collective-permute-start | bytes 18440 | tf_op jit(solution)/shard_map/ppermute | solution.py:12
  14.7 1.4 slice_convert_fusion.11
  16.1 1.5 convert_reduce_fusion.3
  17.6 1.4 compare_select_fusion
  19.0 1.2 reduce-window.9
  22.5 1.4 copy.125
  23.9 1.3 reduce_window_sum.24
  25.2 0.8 slice.246
  26.0 1.3 copy.126
  27.3 2.2 %copy.118 = bf16[512,640]{0,1:T(8,128)(2,1)} copy(bf16[512,640]{1,0:T(8,128)(2,1)} %param.12) | data formatting | bytes 1310720 | tf_op args[0]
  29.5 1.4 mul.434
  31.5 0.8 copy.132
  32.3 1.3 copy.128
  34.9 1.4 pad_maximum_fusion.10
  36.3 1.3 broadcast_compare_fusion
  38.3 0.7 fusion.59
  40.4 1.3 slice_compare_fusion.2
  42.2 1.3 copy.135
  43.5 1.2 reduce_window.9
  44.8 1.3 copy.141
  46.1 1.4 multiply_bitcast_fusion
  48.2 1.5 slice.236
  49.7 0.9 copy.121
  50.6 1.6 multiply_convert_fusion.8
  52.2 0.9 slice.231
  53.2 3.1 %multiply_convert_fusion.5 = bf16[512,640]{0,1:T(8,128)(2,1)} fusion(bf16[512,640]{0,1:T(8,128)(2,1)S(1)} %copy-done.4, bf16[3,640]{0,1:T(8,128)(2,1)S(1)} %slice.231, f32[640]{0:T(1024)} %get-tuple-element.18, f32[640]{0:T(1024)} %get-tuple-element.19, f32[640]{0:T(1024)} %get-tuple-element.17, f32[640]{0:T(1024)} %get-tuple-element.16, ...), kind=kLoop, calls=%fused_computation.28 | loop fusion | flops 9502720 | bytes 1326848 | tf_op jit(solution)/shard_map/convert_element_type | solution.py:27
  56.3 2.7 %reshape.487 = bf16[2,256,10,64]{1,0,3,2:T(2,128)(2,1)} reshape(bf16[512,640]{0,1:T(8,128)(2,1)} %multiply_convert_fusion.5) | data formatting | bytes 1310720 | tf_op jit(solution)/shard_map/reshape | solution.py:114
  59.0 1.9 fusion.12
  60.9 0.8 copy-done.3
  61.8 0.8 fusion.57
  63.4 3.4 %collective-permute-start.1 = (bf16[10,66,128]{2,1,0:T(8,128)(2,1)}, bf16[10,66,128]{2,1,0:T(8,128)(2,1)}, u32[]{:S(2)}, u32[]{:S(2)}) collective-permute-start(bf16[10,66,128]{2,1,0:T(8,128)(2,1)} %pad_maximum_fusion.3), channel_id=1, source_target_pairs={{0,16},{16,32},{32,48},{48,64},{64,80},{80,96},{96,112},{112,128},... | collective-permute-start | bytes 506888 | tf_op jit(solution)/shard_map/ppermute | solution.py:12
  66.8 0.8 compare_and_fusion
  67.7 4.0 %collective-permute-done.1 = bf16[10,66,128]{2,1,0:T(8,128)(2,1)} collective-permute-done((bf16[10,66,128]{2,1,0:T(8,128)(2,1)}, bf16[10,66,128]{2,1,0:T(8,128)(2,1)}, u32[]{:S(2)}, u32[]{:S(2)}) %collective-permute-start.1) | collective-permute-done | bytes 168992 | tf_op jit(solution)/shard_map/ppermute | solution.py:12
  71.7 1.5 multiply_reduce_fusion.3
  74.9 1.3 copy.137
  76.1 1.1 fusion.33
  77.3 0.7 broadcast_in_dim.207
  78.1 4.3 %collective-permute-start.2 = (bf16[10,66,128]{2,1,0:T(8,128)(2,1)S(1)}, bf16[10,66,128]{2,1,0:T(8,128)(2,1)S(1)}, u32[]{:S(2)}, u32[]{:S(2)}) collective-permute-start(bf16[10,66,128]{2,1,0:T(8,128)(2,1)S(1)} %pad_maximum_fusion.4), channel_id=1, source_target_pairs={{0,32},{16,48},{32,64},{48,80},{64,96},{80,112},{96,128},{112,144}... | collective-permute-start | bytes 506888 | tf_op jit(solution)/shard_map/ppermute | solution.py:12
  82.4 1.0 fusion.62
  83.4 3.6 %collective-permute-done.2 = bf16[10,66,128]{2,1,0:T(8,128)(2,1)S(1)} collective-permute-done((bf16[10,66,128]{2,1,0:T(8,128)(2,1)S(1)}, bf16[10,66,128]{2,1,0:T(8,128)(2,1)S(1)}, u32[]{:S(2)}, u32[]{:S(2)}) %collective-permute-start.2) | collective-permute-done | bytes 168992 | tf_op jit(solution)/shard_map/ppermute | solution.py:12
  88.0 2.1 fusion.53
  90.2 3.5 %collective-permute-start.3 = (bf16[10,66,128]{2,1,0:T(8,128)(2,1)S(1)}, bf16[10,66,128]{2,1,0:T(8,128)(2,1)S(1)}, u32[]{:S(2)}, u32[]{:S(2)}) collective-permute-start(bf16[10,66,128]{2,1,0:T(8,128)(2,1)S(1)} %pad_maximum_fusion.5), channel_id=1, source_target_pairs={{0,64},{16,80},{32,96},{48,112},{64,128},{80,144},{96,160},{112,17... | collective-permute-start | bytes 506888 | tf_op jit(solution)/shard_map/ppermute | solution.py:12
  93.7 3.7 %fusion.8 = f32[2,256,10,64]{1,3,2,0:T(8,128)} fusion(f32[10,2,256]{2,0,1:T(8,128)} %copy.128, f32[10,2,256]{2,0,1:T(8,128)} %copy.126, f32[2,256,256]{2,1,0:T(8,128)S(1)} %copy-done.9, pred[2,256,256]{2,1,0:T(8,128)(4,1)} %compare_and_fusion, bf16[2,256,10,64]{1,0,3,2:T(2,128)(2,1)S(1)} %copy-done.1), kind=kOutput, calls=%fused_computation.17 | convolution fusion | flops 175636480 | bytes 2662400 | tf_op jit(solution)/shard_map/hcts,cshp->cthp/dot_general | solution.py:149
  98.4 1.2 fusion.34
  99.7 5.7 %collective-permute-start.4 = (bf16[10,66,128]{2,1,0:T(8,128)(2,1)S(1)}, bf16[10,66,128]{2,1,0:T(8,128)(2,1)S(1)}, u32[]{:S(2)}, u32[]{:S(2)}) collective-permute-start(bf16[10,66,128]{2,1,0:T(8,128)(2,1)S(1)} %pad_maximum_fusion.6), channel_id=1, source_target_pairs={{0,128},{16,144},{32,160},{48,176},{64,192},{80,208},{96,224},{112... | collective-permute-start | bytes 506888 | tf_op jit(solution)/shard_map/ppermute | solution.py:12
  105.4 1.8 slice_add_fusion
  107.2 1.2 collective-permute-done.4
  109.4 2.0 add_convert_fusion
  111.4 13.4 %collective-permute-start.6 = (bf16[10,64,128]{2,1,0:T(8,128)(2,1)}, bf16[10,64,128]{2,1,0:T(8,128)(2,1)}, u32[]{:S(2)}, u32[]{:S(2)}) collective-permute-start(bf16[10,64,128]{2,1,0:T(8,128)(2,1)} %add_convert_fusion), channel_id=1, source_target_pairs={{0,272},{16,288},{32,304},{48,320},{64,336},{80,352},{96,368},{112... | collective-permute-start | bytes 491528 | tf_op jit(solution)/shard_map/ppermute | solution.py:12
  124.8 1.6 pad_maximum_fusion.7
  126.4 2.1 collective-permute-start.5
  128.5 3.2 %fusion.10 = f32[2,256,10,64]{1,3,2,0:T(8,128)} fusion(f32[2,256,10,64]{1,3,2,0:T(8,128)} %fusion.8, bf16[2,256,128,1]{2,1,3,0:T(8,128)(2,1)S(1)} %bitcast.102, f32[10]{0:T(128)S(1)} %copy-done.31, f32[2,256,10]{1,2,0:T(8,128)S(1)} %copy.134, f32[1,10,64,128]{3,2,1,0:T(8,128)S(1)} %copy-done.7, bf16[2,256,10,64]{1,0,3,2:T(2,128)(2,1)S(1)} %copy-done.2), kind=kOutput, calls=%fused_computation.19 | convolution fusion | flops 504954880 | bytes 3756072 | tf_op jit(solution)/shard_map/ctn,chpn->cthp/dot_general | solution.py:141
  131.8 2.2 %copy.144 = bf16[512,640]{0,1:T(8,128)(2,1)} copy(bf16[512,640]{1,0:T(8,128)(2,1)} %param.14) | data formatting | bytes 1310720 | tf_op jit(solution)/shard_map/optimization_barrier | solution.py:49
  134.1 1.0 fusion.44
  135.1 2.2 %fusion.11 = bf16[2,256,10,64]{1,3,2,0:T(8,128)(2,1)S(1)} fusion(f32[2,256,10,64]{1,3,2,0:T(8,128)} %fusion.10, bf16[2,256,128,1]{2,1,3,0:T(8,128)(2,1)S(1)} %bitcast.103, f32[2,256,10]{1,2,0:T(8,128)S(1)} %copy.142, bf16[10,64,128]{2,1,0:T(8,128)(2,1)} %collective-permute-done.6, bf16[10,66,128]{2,1,0:T(8,128)(2,1)} %collective-permute-done.5, ...), kind=kOutput, calls=%fused_computation.20 | convolution fusion | flops 504627200 | bytes 2445352 | tf_op jit(solution)/shard_map/ctn,hpn->cthp/dot_general | solution.py:158
  139.2 3.7 %convolution_convert_fusion = bf16[512,2560]{1,0:T(8,128)(2,1)S(1)} fusion(bf16[640,2560]{1,0:T(8,128)(2,1)S(1)} %copy-done, f32[640]{0:T(1024)S(1)} %copy-done.32, bf16[512,640]{0,1:T(8,128)(2,1)} %copy.144, bf16[512,640]{0,1:T(8,128)(2,1)} %bitcast.99), kind=kOutput, calls=%fused_computation.1 | convolution fusion | flops 1681981440 | bytes 7211520 | tf_op jit(solution)/shard_map/dot_general | solution.py:168
  142.9 1.7 pad_maximum_fusion
  144.6 4.6 %copy.148 = bf16[514,2560]{0,1:T(8,128)(2,1)} copy(bf16[514,2560]{1,0:T(8,128)(2,1)} %pad_maximum_fusion) | data formatting | bytes 5263360
  149.3 53.0 %reduce-scatter.4.cloned.1.call-done = bf16[320,514]{1,0:T(8,128)(2,1)} async-done(((bf16[2560,514]{1,0:T(8,128)(2,1)}), bf16[320,514]{1,0:T(8,128)(2,1)}) %reduce-scatter.4.cloned.1.call-update) | async-done | bytes 328976
  202.2 0.9 slice.263
  203.3 1.8 multiply_convert_fusion.7
  (135 shorter events, 17.7 us)
Async XLA Ops:
  6.5 132.7 %copy-start = (bf16[640,2560]{1,0:T(8,128)(2,1)S(1)}, bf16[640,2560]{1,0:T(8,128)(2,1)}, u32[]{:S(2)}) copy-start(bf16[640,2560]{1,0:T(8,128)(2,1)} %param.23) | copy-start | bytes 9830404
  6.5 195.7 %reduce-scatter.4.cloned.1.call-start = ((), (), s32[]{:S(2)}) async-start(), calls=%async_computation.1 | async-start | bytes 3686400
  8.2 15.6 %copy-start.16 = (f32[512]{0:T(512)}, f32[512]{0:T(512)S(1)}, u32[]{:S(2)}) copy-start(f32[512]{0:T(512)S(1)} %get-tuple-element.53) | copy-start | bytes 6148
  10.0 23.6 %collective-permute-start = (bf16[3,1024]{0,1:T(8,128)(2,1)}, bf16[3,1024]{0,1:T(8,128)(2,1)}, u32[]{:S(2)}, u32[]{:S(2)}) collective-permute-start(bf16[3,1024]{0,1:T(8,128)(2,1)} %copy.119), channel_id=1, source_target_pairs={{0,16},{16,32},{32,48},{48,64},{64,80},{80,96},{96,112},{112,128},... | collective-permute-start | bytes 18440 | tf_op jit(solution)/shard_map/ppermute | solution.py:12
  21.1 29.5 %copy-start.10 = (bf16[512,256]{1,0:T(8,128)(2,1)S(1)}, bf16[512,256]{1,0:T(8,128)(2,1)}, u32[]{:S(2)}) copy-start(bf16[512,256]{1,0:T(8,128)(2,1)} %param.13) | copy-start | bytes 786436
  37.5 0.6 copy-start.29
  39.0 0.6 copy-start.17
  41.7 11.5 %copy-start.25 = (pred[512]{0:T(512)(128)(4,1)S(1)}, pred[512]{0:T(512)(128)(4,1)}, u32[]{:S(2)}) copy-start(pred[512]{0:T(512)(128)(4,1)} %get-tuple-element.42) | copy-start | bytes 1540
  47.6 5.6 %copy-start.26 = (pred[512]{0:T(512)(128)(4,1)S(1)}, pred[512]{0:T(512)(128)(4,1)}, u32[]{:S(2)}) copy-start(pred[512]{0:T(512)(128)(4,1)} %get-tuple-element.43) | copy-start | bytes 1540
  50.6 2.6 %copy-start.4 = (bf16[512,640]{0,1:T(8,128)(2,1)S(1)}, bf16[512,640]{0,1:T(8,128)(2,1)}, u32[]{:S(2)}) copy-start(bf16[512,640]{0,1:T(8,128)(2,1)} %copy.118) | copy-start | bytes 1966084
  50.6 2.6 %copy-start.27 = (pred[512]{0:T(512)(128)(4,1)S(1)}, pred[512]{0:T(512)(128)(4,1)}, u32[]{:S(2)}) copy-start(pred[512]{0:T(512)(128)(4,1)} %get-tuple-element.44) | copy-start | bytes 1540
  50.6 2.6 %copy-start.28 = (pred[512]{0:T(512)(128)(4,1)S(1)}, pred[512]{0:T(512)(128)(4,1)}, u32[]{:S(2)}) copy-start(pred[512]{0:T(512)(128)(4,1)} %get-tuple-element.47) | copy-start | bytes 1540
  56.3 5.5 %copy-start.23 = (f32[10]{0:T(128)S(1)}, f32[10]{0:T(128)}, u32[]{:S(2)}) copy-start(f32[10]{0:T(128)} %get-tuple-element.60) | copy-start | bytes 124
  56.3 5.5 %copy-start.30 = (f32[10]{0:T(128)S(1)}, f32[10]{0:T(128)}, u32[]{:S(2)}) copy-start(f32[10]{0:T(128)} %get-tuple-element.59) | copy-start | bytes 124
  59.0 3.6 %copy-start.19 = (bf16[10,2]{1,0:T(8,128)(2,1)S(1)}, bf16[10,2]{1,0:T(8,128)(2,1)}, u32[]{:S(2)}) copy-start(bf16[10,2]{1,0:T(8,128)(2,1)} %copy.135) | copy-start | bytes 124
  59.0 7.8 %copy-start.11 = (pred[256,256]{1,0:T(8,128)(4,1)S(1)}, pred[256,256]{1,0:T(8,128)(4,1)}, u32[]{:S(2)}) copy-start(pred[256,256]{1,0:T(8,128)(4,1)} %iota_compare_fusion) | copy-start | bytes 196612
  59.0 8.6 %copy-start.18 = (f32[10]{0:T(128)S(1)}, f32[10]{0:T(128)}, u32[]{:S(2)}) copy-start(f32[10]{0:T(128)} %copy-done.17) | copy-start | bytes 124
  60.9 0.8 copy-start.3
  63.4 8.3 %collective-permute-start.1 = (bf16[10,66,128]{2,1,0:T(8,128)(2,1)}, bf16[10,66,128]{2,1,0:T(8,128)(2,1)}, u32[]{:S(2)}, u32[]{:S(2)}) collective-permute-start(bf16[10,66,128]{2,1,0:T(8,128)(2,1)} %pad_maximum_fusion.3), channel_id=1, source_target_pairs={{0,16},{16,32},{32,48},{48,64},{64,80},{80,96},{96,112},{112,128},... | collective-permute-start | bytes 506888 | tf_op jit(solution)/shard_map/ppermute | solution.py:12
  73.8 0.5 copy-start.20
  76.1 11.7 %copy-start.21 = (f32[10,1]{0,1:T(1,128)S(1)}, f32[10,1]{0,1:T(1,128)}, u32[]{:S(2)}) copy-start(f32[10,1]{0,1:T(1,128)} %copy-done.20) | copy-start | bytes 124
  78.1 8.9 %collective-permute-start.2 = (bf16[10,66,128]{2,1,0:T(8,128)(2,1)S(1)}, bf16[10,66,128]{2,1,0:T(8,128)(2,1)S(1)}, u32[]{:S(2)}, u32[]{:S(2)}) collective-permute-start(bf16[10,66,128]{2,1,0:T(8,128)(2,1)S(1)} %pad_maximum_fusion.4), channel_id=1, source_target_pairs={{0,32},{16,48},{32,64},{48,80},{64,96},{80,112},{96,128},{112,144}... | collective-permute-start | bytes 506888 | tf_op jit(solution)/shard_map/ppermute | solution.py:12
  87.0 0.7 copy-start.13
  88.0 5.7 %copy-start.1 = (bf16[2,256,10,64]{1,0,3,2:T(2,128)(2,1)S(1)}, bf16[2,256,10,64]{1,0,3,2:T(2,128)(2,1)}, u32[]{:S(2)}) copy-start(bf16[2,256,10,64]{1,0,3,2:T(2,128)(2,1)} %reshape.487) | copy-start | bytes 1966084
  88.0 5.7 %copy-start.9 = (f32[2,256,256]{2,1,0:T(8,128)S(1)}, f32[2,256,256]{2,1,0:T(8,128)}, u32[]{:S(2)}) copy-start(f32[2,256,256]{2,1,0:T(8,128)} %fusion.62) | copy-start | bytes 1572868
  90.1 7.2 %copy-start.15 = (f32[2,256,10]{1,0,2:T(2,128)S(1)}, f32[2,256,10]{1,0,2:T(2,128)}, u32[]{:S(2)}) copy-start(f32[2,256,10]{1,0,2:T(2,128)} %get-tuple-element.38) | copy-start | bytes 61444
  90.2 8.1 %copy-start.22 = (f32[10,1]{0,1:T(1,128)S(1)}, f32[10,1]{0,1:T(1,128)}, u32[]{:S(2)}) copy-start(f32[10,1]{0,1:T(1,128)} %copy-done.20) | copy-start | bytes 124
  90.2 15.2 %copy-start.24 = (f32[10]{0:T(128)S(1)}, f32[10]{0:T(128)}, u32[]{:S(2)}) copy-start(f32[10]{0:T(128)} %get-tuple-element.60) | copy-start | bytes 124
  90.2 7.2 %collective-permute-start.3 = (bf16[10,66,128]{2,1,0:T(8,128)(2,1)S(1)}, bf16[10,66,128]{2,1,0:T(8,128)(2,1)S(1)}, u32[]{:S(2)}, u32[]{:S(2)}) collective-permute-start(bf16[10,66,128]{2,1,0:T(8,128)(2,1)S(1)} %pad_maximum_fusion.5), channel_id=1, source_target_pairs={{0,64},{16,80},{32,96},{48,112},{64,128},{80,144},{96,160},{112,17... | collective-permute-start | bytes 506888 | tf_op jit(solution)/shard_map/ppermute | solution.py:12
  97.4 0.7 copy-start.8
  98.4 30.1 %copy-start.31 = (f32[10]{0:T(128)S(1)}, f32[10]{0:T(128)}, u32[]{:S(2)}) copy-start(f32[10]{0:T(128)} %param.21) | copy-start | bytes 124
  99.7 8.8 %collective-permute-start.4 = (bf16[10,66,128]{2,1,0:T(8,128)(2,1)S(1)}, bf16[10,66,128]{2,1,0:T(8,128)(2,1)S(1)}, u32[]{:S(2)}, u32[]{:S(2)}) collective-permute-start(bf16[10,66,128]{2,1,0:T(8,128)(2,1)S(1)} %pad_maximum_fusion.6), channel_id=1, source_target_pairs={{0,128},{16,144},{32,160},{48,176},{64,192},{80,208},{96,224},{112... | collective-permute-start | bytes 506888 | tf_op jit(solution)/shard_map/ppermute | solution.py:12
  108.4 0.7 copy-start.12
  109.4 19.2 %copy-start.2 = (bf16[2,256,10,64]{1,0,3,2:T(2,128)(2,1)S(1)}, bf16[2,256,10,64]{1,0,3,2:T(2,128)(2,1)}, u32[]{:S(2)}) copy-start(bf16[2,256,10,64]{1,0,3,2:T(2,128)(2,1)} %reshape.487) | copy-start | bytes 1966084
  109.4 19.2 %copy-start.7 = (f32[1,10,64,128]{3,2,1,0:T(8,128)S(1)}, f32[1,10,64,128]{3,2,1,0:T(8,128)}, u32[]{:S(2)}) copy-start(f32[1,10,64,128]{3,2,1,0:T(8,128)} %slice_add_fusion) | copy-start | bytes 983044
  111.4 23.7 %collective-permute-start.6 = (bf16[10,64,128]{2,1,0:T(8,128)(2,1)}, bf16[10,64,128]{2,1,0:T(8,128)(2,1)}, u32[]{:S(2)}, u32[]{:S(2)}) collective-permute-start(bf16[10,64,128]{2,1,0:T(8,128)(2,1)} %add_convert_fusion), channel_id=1, source_target_pairs={{0,272},{16,288},{32,304},{48,320},{64,336},{80,352},{96,368},{112... | collective-permute-start | bytes 491528 | tf_op jit(solution)/shard_map/ppermute | solution.py:12
  126.4 7.7 %collective-permute-start.5 = (bf16[10,66,128]{2,1,0:T(8,128)(2,1)}, bf16[10,66,128]{2,1,0:T(8,128)(2,1)}, u32[]{:S(2)}, u32[]{:S(2)}) collective-permute-start(bf16[10,66,128]{2,1,0:T(8,128)(2,1)} %pad_maximum_fusion.7), channel_id=1, source_target_pairs={{0,16},{16,32},{32,48},{48,64},{64,80},{80,96},{96,112},{112,128},... | collective-permute-start | bytes 506888 | tf_op jit(solution)/shard_map/ppermute | solution.py:12
  128.5 3.2 %copy-start.14 = (f32[2,256,10]{1,0,2:T(2,128)S(1)}, f32[2,256,10]{1,0,2:T(2,128)}, u32[]{:S(2)}) copy-start(f32[2,256,10]{1,0,2:T(2,128)} %get-tuple-element.37) | copy-start | bytes 61444
  137.4 1.1 copy-start.5
  138.1 1.2 copy-start.32
  138.2 0.8 copy-start.6
Sparse Core Ops, SparseCore 0:
  149.4 52.7 reduce-scatter.3

commit v7 on v5

--- a/solution.py
+++ b/solution.py
@@ -43,7 +43,7 @@
     shard_count = lax.axis_size("seq")
     decay, state = device_decay, local_final
     window = 1
-    while 2 * window < shard_count - 1:
+    while 4 * window < shard_count - 1:
         received = from_behind(with_decay(decay, state), "seq", window)
         if window == 1:
             received, passengers = lax.optimization_barrier((received, passengers))
@@ -51,11 +51,18 @@
         state = decay[:, None, None] * prev_state + state
         decay = decay * prev_decay
         window *= 2
-    near_decay, near_state = split_decay(from_behind(with_decay(decay, state), "seq", 1))
-    if window + 1 < shard_count:
-        far_state = from_behind(state.astype(jnp.bfloat16), "seq", window + 1)
-        return near_decay[:, None, None] * far_state.astype(jnp.float32) + near_state, passengers
-    return near_state, passengers
+    packed = with_decay(decay, state)
+    part_count = -(-(shard_count - 1) // window)
+    parts = [
+        split_decay(from_behind(packed, "seq", 1 + part * window)) for part in range(part_count)
+    ]
+    if not parts:
+        return jnp.zeros_like(local_final), passengers
+    incoming_decay, incoming = parts[0]
+    for part_decay, part_state in parts[1:]:
+        incoming = incoming_decay[:, None, None] * part_state + incoming
+        incoming_decay = incoming_decay * part_decay
+    return incoming, passengers
 
 
 def local(

time: 168 us -> 171 us (1.018)
  waiting for transfers between devices: 61.9 us -> 70.8 us
  starting transfers between devices: 40.7 us -> 36.4 us
    ppermute x7 -> x8, waiting for transfers between devices: 8.78 us -> 15.5 us  [from_behind(): return lax.ppermute(block, axis, route)]
    ppermute x7 -> x8, starting transfers between devices: 40.7 us -> 36.3 us  [from_behind(): return lax.ppermute(block, axis, route)]
    reduce_scatter x1, waiting for transfers between devices: 53.1 us -> 55.3 us  [local(): lax.psum_scatter(payload, 'tensor', scatter_dimension=0, tiled=True)[0]]
  transfers between devices with their start and end apart: 8 -> 9, of which waited for: 4 -> 6; matrix products, arithmetic and copies ran while one was open for 13% -> 12% of each run, Pallas kernels for 0% -> 0%
where the time goes in v7:
time: 171 us; the launch traced here: 170 us
  waiting for transfers between devices  70.8 us (41%)
  starting transfers between devices  36.4 us (21%)
  other arithmetic  21.4 us (13%)
  local copies, waits for them, and re-layouts  16.3 us (10%)
  between operations  13.8 us (8%)
  matrix products  11 us (6%)
    reduce_scatter x1, waiting for transfers between devices, local(): lax.psum_scatter(payload, 'tensor', scatter_dimension=0, tiled=True)[0]  55.3 us
    ppermute x8, starting transfers between devices, from_behind(): return lax.ppermute(block, axis, route)  36.3 us
    ppermute x8, waiting for transfers between devices, from_behind(): return lax.ppermute(block, axis, route)  15.5 us
    optimization_barrier x2, local copies, waits for them, and re-layouts, pass_state(): received, passengers = lax.optimization_barrier((received, passengers))  6.83 us
    dot_general x1, matrix products, local(): jnp.einsum('tc,cgk->gtk', scaled, w_out.reshape(inner_width, group_count,...  3.64 us
  transfers between devices with their start and end apart: 9, of which 6 were waited for; matrix products, arithmetic and copies ran while one was open for 12% of the time, Pallas kernels for 0%

profile of v7, /device:TPU:6, one launch (start us, length us, event | category | flops | bytes accessed | tf_op | source)
XLA Modules:
  0.0 169.7 jit_solution(18099339738011623799)
XLA Ops:
  6.5 0.8 convert_convert_fusion
  7.4 0.7 slice.188
  8.1 0.7 slice.189
  8.8 0.2 copy.93
  9.1 3.4 %collective-permute-start = (bf16[3,1024]{0,1:T(8,128)(2,1)S(1)}, bf16[3,1024]{0,1:T(8,128)(2,1)S(1)}, u32[]{:S(2)}, u32[]{:S(2)}) collective-permute-start(bf16[3,1024]{0,1:T(8,128)(2,1)S(1)} %copy.93), channel_id=1, source_target_pairs={{0,16},{16,32},{32,48},{48,64},{64,80},{80,96},{96,112},{112,128},... | collective-permute-start | bytes 18440 | tf_op jit(solution)/shard_map/ppermute | solution.py:12
  12.5 0.7 exponential_negate_fusion
  13.2 0.8 compare_select_fusion
  14.0 1.2 reduce-window.9
  15.5 0.9 convert_reduce_fusion.3
  16.4 0.8 slice_convert_fusion.13
  17.2 0.2 compare_and_fusion
  17.4 0.2 slice_reduce_fusion.1
  17.7 0.3 copy.99
  18.1 0.6 copy.107
  18.9 0.6 copy.109
  19.5 0.6 slice.192
  20.1 0.8 pad_maximum_fusion.9
  20.9 0.2 slice_reduce_fusion
  21.4 0.7 multiply_bitcast_fusion
  22.2 1.7 multiply_convert_fusion.5
  23.9 0.2 reshape.390
  24.2 0.8 multiply_convert_fusion.6
  25.1 0.8 fusion.12
  25.9 0.1 fusion.72
  26.1 5.0 %collective-permute-start.1 = (bf16[10,66,128]{2,1,0:T(8,128)(2,1)S(1)}, bf16[10,66,128]{2,1,0:T(8,128)(2,1)S(1)}, u32[]{:S(2)}, u32[]{:S(2)}) collective-permute-start(bf16[10,66,128]{2,1,0:T(8,128)(2,1)S(1)} %pad_maximum_fusion.3), channel_id=1, source_target_pairs={{0,16},{16,32},{32,48},{48,64},{64,80},{80,96},{96,112},{112,128},... | collective-permute-start | bytes 506888 | tf_op jit(solution)/shard_map/ppermute | solution.py:12
  31.1 1.0 fusion.77
  32.2 2.0 %collective-permute-done.1 = bf16[10,66,128]{2,1,0:T(8,128)(2,1)S(1)} collective-permute-done((bf16[10,66,128]{2,1,0:T(8,128)(2,1)S(1)}, bf16[10,66,128]{2,1,0:T(8,128)(2,1)S(1)}, u32[]{:S(2)}, u32[]{:S(2)}) %collective-permute-start.1) | collective-permute-done | bytes 168992 | tf_op jit(solution)/shard_map/ppermute | solution.py:12
  34.2 0.2 fusion.71
  34.7 0.7 pad_maximum_fusion.4
  35.4 4.4 %collective-permute-start.2 = (bf16[10,66,128]{2,1,0:T(8,128)(2,1)}, bf16[10,66,128]{2,1,0:T(8,128)(2,1)}, u32[]{:S(2)}, u32[]{:S(2)}) collective-permute-start(bf16[10,66,128]{2,1,0:T(8,128)(2,1)} %pad_maximum_fusion.4), channel_id=1, source_target_pairs={{0,32},{16,48},{32,64},{48,80},{64,96},{80,112},{96,128},{112,144}... | collective-permute-start | bytes 506888 | tf_op jit(solution)/shard_map/ppermute | solution.py:12
  39.8 2.9 %fusion.8 = f32[2,256,10,64]{1,3,2,0:T(8,128)S(1)} fusion(f32[10,2,256]{2,0,1:T(8,128)} %copy.109, f32[10,2,256]{2,0,1:T(8,128)} %copy.107, f32[2,256,256]{2,1,0:T(8,128)} %fusion.77, pred[2,256,256]{2,1,0:T(8,128)(4,1)S(1)} %compare_and_fusion, bf16[2,256,10,64]{1,0,3,2:T(2,128)(2,1)S(1)} %reshape.390), kind=kOutput, calls=%fused_computation.17 | convolution fusion | flops 175636480 | bytes 2662400 | tf_op jit(solution)/shard_map/hcts,cshp->cthp/dot_general | solution.py:156
  42.9 1.9 %collective-permute-done.2 = bf16[10,66,128]{2,1,0:T(8,128)(2,1)} collective-permute-done((bf16[10,66,128]{2,1,0:T(8,128)(2,1)}, bf16[10,66,128]{2,1,0:T(8,128)(2,1)}, u32[]{:S(2)}, u32[]{:S(2)}) %collective-permute-start.2) | collective-permute-done | bytes 168992 | tf_op jit(solution)/shard_map/ppermute | solution.py:12
  44.8 1.0 multiply_reduce_fusion.1
  45.9 1.1 fusion.68
  47.1 3.5 %collective-permute-start.3 = (bf16[10,66,128]{2,1,0:T(8,128)(2,1)S(1)}, bf16[10,66,128]{2,1,0:T(8,128)(2,1)S(1)}, u32[]{:S(2)}, u32[]{:S(2)}) collective-permute-start(bf16[10,66,128]{2,1,0:T(8,128)(2,1)S(1)} %pad_maximum_fusion.5), channel_id=1, source_target_pairs={{0,64},{16,80},{32,96},{48,112},{64,128},{80,144},{96,160},{112,17... | collective-permute-start | bytes 506888 | tf_op jit(solution)/shard_map/ppermute | solution.py:12
  50.6 0.8 slice_add_fusion
  51.4 2.2 %collective-permute-done.3 = bf16[10,66,128]{2,1,0:T(8,128)(2,1)S(1)} collective-permute-done((bf16[10,66,128]{2,1,0:T(8,128)(2,1)S(1)}, bf16[10,66,128]{2,1,0:T(8,128)(2,1)S(1)}, u32[]{:S(2)}, u32[]{:S(2)}) %collective-permute-start.3) | collective-permute-done | bytes 168992 | tf_op jit(solution)/shard_map/ppermute | solution.py:12
  53.6 0.7 copy-done.7
  54.3 0.2 fusion.59
  54.5 1.2 add_convert_fusion
  55.9 0.7 pad_maximum_fusion.6
  56.6 8.3 %collective-permute-start.4 = (bf16[10,66,128]{2,1,0:T(8,128)(2,1)}, bf16[10,66,128]{2,1,0:T(8,128)(2,1)}, u32[]{:S(2)}, u32[]{:S(2)}) collective-permute-start(bf16[10,66,128]{2,1,0:T(8,128)(2,1)} %pad_maximum_fusion.6), channel_id=1, source_target_pairs={{0,16},{16,32},{32,48},{48,64},{64,80},{80,96},{96,112},{112,128},... | collective-permute-start | bytes 506888 | tf_op jit(solution)/shard_map/ppermute | solution.py:12
  64.9 8.6 %collective-permute-start.5 = (bf16[10,66,128]{2,1,0:T(8,128)(2,1)}, bf16[10,66,128]{2,1,0:T(8,128)(2,1)}, u32[]{:S(2)}, u32[]{:S(2)}) collective-permute-start(bf16[10,66,128]{2,1,0:T(8,128)(2,1)} %pad_maximum_fusion.6), channel_id=1, source_target_pairs={{0,144},{16,160},{32,176},{48,192},{64,208},{80,224},{96,240},{112... | collective-permute-start | bytes 506888 | tf_op jit(solution)/shard_map/ppermute | solution.py:12
  73.4 0.8 fusion.10
  74.3 5.7 %copy.106 = bf16[640,2560]{0,1:T(8,128)(2,1)} copy(bf16[640,2560]{1,0:T(8,128)(2,1)} %param.23) | data formatting | bytes 6553600 | tf_op jit(solution)/shard_map/optimization_barrier | solution.py:49
  80.0 1.1 copy.119
  81.1 1.7 %collective-permute-start.6 = (bf16[10,66,128]{2,1,0:T(8,128)(2,1)}, bf16[10,66,128]{2,1,0:T(8,128)(2,1)S(1)}, u32[]{:S(2)}, u32[]{:S(2)}) collective-permute-start(bf16[10,66,128]{2,1,0:T(8,128)(2,1)} %pad_maximum_fusion.6), channel_id=1, source_target_pairs={{0,272},{16,288},{32,304},{48,320},{64,336},{80,352},{96,368},{112... | collective-permute-start | bytes 506888 | tf_op jit(solution)/shard_map/ppermute | solution.py:12
  82.8 1.5 collective-permute-start.7
  84.3 0.8 fusion.55
  85.2 0.2 reduce.13
  85.3 6.8 %collective-permute-done.6 = bf16[10,66,128]{2,1,0:T(8,128)(2,1)S(1)} collective-permute-done((bf16[10,66,128]{2,1,0:T(8,128)(2,1)}, bf16[10,66,128]{2,1,0:T(8,128)(2,1)S(1)}, u32[]{:S(2)}, u32[]{:S(2)}) %collective-permute-start.6) | collective-permute-done | bytes 168992 | tf_op jit(solution)/shard_map/ppermute | solution.py:12
  92.2 0.2 fusion.60
  92.3 2.5 %collective-permute-done.7 = bf16[10,66,128]{2,1,0:T(8,128)(2,1)S(1)} collective-permute-done((bf16[10,66,128]{2,1,0:T(8,128)(2,1)}, bf16[10,66,128]{2,1,0:T(8,128)(2,1)S(1)}, u32[]{:S(2)}, u32[]{:S(2)}) %collective-permute-start.7) | collective-permute-done | bytes 168992 | tf_op jit(solution)/shard_map/ppermute | solution.py:12
  94.8 1.8 %fusion.11 = bf16[2,256,10,64]{1,3,2,0:T(8,128)(2,1)S(1)} fusion(f32[2,256,10,64]{1,3,2,0:T(8,128)S(1)} %fusion.10, bf16[2,256,128,1]{2,1,3,0:T(8,128)(2,1)S(1)} %bitcast.115, f32[2,256,10]{1,2,0:T(8,128)S(1)} %copy.117, bf16[10,66,128]{2,1,0:T(8,128)(2,1)} %collective-permute-done.4, bf16[10,66,128]{2,1,0:T(8,128)(2,1)} %collective-permute-done.5, ...), kind=kOutput, calls=%fused_computation.20 | convolution fusion | flops 505118720 | bytes 2786816 | tf_op jit(solution)/shard_map/ctn,hpn->cthp/dot_general | solution.py:165
  96.7 0.7 copy.118
  97.5 0.5 multiply_reduce_fusion
  98.0 0.3 copy-done.2
  98.4 0.2 copy.121
  98.6 0.3 copy-done
  98.8 3.6 %convert_bitcast_fusion = bf16[8,512,320]{1,2,0:T(8,128)(2,1)S(1)} fusion(bf16[640,8,320]{0,2,1:T(8,128)(2,1)S(1)} %bitcast.109, f32[640]{0:T(1024)S(1)} %copy-done.12, bf16[512,640]{0,1:T(8,128)(2,1)} %copy.119, bf16[512,640]{0,1:T(8,128)(2,1)} %bitcast.111), kind=kOutput, calls=%fused_computation.3 | convolution fusion | flops 1681981440 | bytes 7211520 | tf_op jit(solution)/shard_map/tc,cgk->gtk/dot_general | solution.py:175
  102.6 2.0 %pad_maximum_fusion = bf16[8,514,320]{1,2,0:T(8,128)(2,1)} fusion(bf16[8,2,320]{1,2,0:T(8,128)(2,1)S(1)} %broadcast_in_dim.206, bf16[8,512,320]{1,2,0:T(8,128)(2,1)S(1)} %convert_bitcast_fusion), kind=kLoop, calls=%fused_computation.1 | loop fusion | flops 5263360 | bytes 5263360 | tf_op jit(solution)/shard_map/concatenate | solution.py:188
  104.6 55.3 %reduce-scatter.2.cloned.1.call-done = bf16[1,514,320]{1,2,0:T(8,128)(2,1)} async-done(((bf16[8,514,320]{1,2,0:T(8,128)(2,1)}), bf16[1,514,320]{1,2,0:T(8,128)(2,1)}) %reduce-scatter.2.cloned.1.call-update) | async-done | bytes 328976 | tf_op jit(solution)/shard_map/reduce_scatter | solution.py:189
  160.0 0.9 slice.285
  161.0 1.8 %fusion.21 = bf16[512,320]{0,1:T(8,128)(2,1)} fusion(bf16[1,514,320]{1,2,0:T(8,128)(2,1)} %reduce-scatter.2.cloned.1.call-done, f32[512]{0:T(512)S(1)} %add_rsqrt_fusion), kind=kLoop, calls=%fused_computation.38 | loop fusion | flops 491520 | bytes 657408 | tf_op jit(solution)/shard_map/convert_element_type | solution.py:192
  (91 shorter events, 3.1 us)
Async XLA Ops:
  6.5 11.2 %copy-start.4 = (bf16[512,640]{1,0:T(8,128)(2,1)S(1)}, bf16[512,640]{1,0:T(8,128)(2,1)}, u32[]{:S(2)}) copy-start(bf16[512,640]{1,0:T(8,128)(2,1)} %param.12) | copy-start | bytes 1966084
  6.5 153.4 %reduce-scatter.2.cloned.1.call-start = ((), (), s32[]{:S(2)}) async-start(), calls=%async_computation.1 | async-start | bytes 3686400 | tf_op jit(solution)/shard_map/reduce_scatter | solution.py:189
  9.1 13.1 %copy-start.10 = (s32[512]{0:T(512)S(1)}, s32[512]{0:T(512)}, u32[]{:S(2)}) copy-start(s32[512]{0:T(512)} %param.16) | copy-start | bytes 6148
  9.1 10.4 %collective-permute-start = (bf16[3,1024]{0,1:T(8,128)(2,1)S(1)}, bf16[3,1024]{0,1:T(8,128)(2,1)S(1)}, u32[]{:S(2)}, u32[]{:S(2)}) collective-permute-start(bf16[3,1024]{0,1:T(8,128)(2,1)S(1)} %copy.93), channel_id=1, source_target_pairs={{0,16},{16,32},{32,48},{48,64},{64,80},{80,96},{96,112},{112,128},... | collective-permute-start | bytes 18440 | tf_op jit(solution)/shard_map/ppermute | solution.py:12
  22.2 1.9 %copy-start.6 = (bf16[512,256]{1,0:T(8,128)(2,1)S(1)}, bf16[512,256]{1,0:T(8,128)(2,1)}, u32[]{:S(2)}) copy-start(bf16[512,256]{1,0:T(8,128)(2,1)} %param.13) | copy-start | bytes 786436
  26.1 8.1 %collective-permute-start.1 = (bf16[10,66,128]{2,1,0:T(8,128)(2,1)S(1)}, bf16[10,66,128]{2,1,0:T(8,128)(2,1)S(1)}, u32[]{:S(2)}, u32[]{:S(2)}) collective-permute-start(bf16[10,66,128]{2,1,0:T(8,128)(2,1)S(1)} %pad_maximum_fusion.3), channel_id=1, source_target_pairs={{0,16},{16,32},{32,48},{48,64},{64,80},{80,96},{96,112},{112,128},... | collective-permute-start | bytes 506888 | tf_op jit(solution)/shard_map/ppermute | solution.py:12
  35.4 7.5 %copy-start.9 = (f32[2,256,10]{1,0,2:T(2,128)S(1)}, f32[2,256,10]{1,0,2:T(2,128)}, u32[]{:S(2)}) copy-start(f32[2,256,10]{1,0,2:T(2,128)} %get-tuple-element.35) | copy-start | bytes 61444
  35.4 7.5 %copy-start.8 = (f32[2,256,10]{1,0,2:T(2,128)S(1)}, f32[2,256,10]{1,0,2:T(2,128)}, u32[]{:S(2)}) copy-start(f32[2,256,10]{1,0,2:T(2,128)} %get-tuple-element.34) | copy-start | bytes 61444
  35.4 9.4 %collective-permute-start.2 = (bf16[10,66,128]{2,1,0:T(8,128)(2,1)}, bf16[10,66,128]{2,1,0:T(8,128)(2,1)}, u32[]{:S(2)}, u32[]{:S(2)}) collective-permute-start(bf16[10,66,128]{2,1,0:T(8,128)(2,1)} %pad_maximum_fusion.4), channel_id=1, source_target_pairs={{0,32},{16,48},{32,64},{48,80},{64,96},{80,112},{96,128},{112,144}... | collective-permute-start | bytes 506888 | tf_op jit(solution)/shard_map/ppermute | solution.py:12
  46.9 26.5 %copy-start.11 = (f32[10]{0:T(128)S(1)}, f32[10]{0:T(128)}, u32[]{:S(2)}) copy-start(f32[10]{0:T(128)} %param.21) | copy-start | bytes 124
  47.1 6.5 %collective-permute-start.3 = (bf16[10,66,128]{2,1,0:T(8,128)(2,1)S(1)}, bf16[10,66,128]{2,1,0:T(8,128)(2,1)S(1)}, u32[]{:S(2)}, u32[]{:S(2)}) collective-permute-start(bf16[10,66,128]{2,1,0:T(8,128)(2,1)S(1)} %pad_maximum_fusion.5), channel_id=1, source_target_pairs={{0,64},{16,80},{32,96},{48,112},{64,128},{80,144},{96,160},{112,17... | collective-permute-start | bytes 506888 | tf_op jit(solution)/shard_map/ppermute | solution.py:12
  53.6 0.7 copy-start.7
  54.5 18.9 %copy-start.3 = (f32[1,10,64,128]{3,2,1,0:T(8,128)S(1)}, f32[1,10,64,128]{3,2,1,0:T(8,128)}, u32[]{:S(2)}) copy-start(f32[1,10,64,128]{3,2,1,0:T(8,128)} %slice_add_fusion) | copy-start | bytes 983044
  56.6 27.7 %collective-permute-start.4 = (bf16[10,66,128]{2,1,0:T(8,128)(2,1)}, bf16[10,66,128]{2,1,0:T(8,128)(2,1)}, u32[]{:S(2)}, u32[]{:S(2)}) collective-permute-start(bf16[10,66,128]{2,1,0:T(8,128)(2,1)} %pad_maximum_fusion.6), channel_id=1, source_target_pairs={{0,16},{16,32},{32,48},{48,64},{64,80},{80,96},{96,112},{112,128},... | collective-permute-start | bytes 506888 | tf_op jit(solution)/shard_map/ppermute | solution.py:12
  64.9 19.5 %collective-permute-start.5 = (bf16[10,66,128]{2,1,0:T(8,128)(2,1)}, bf16[10,66,128]{2,1,0:T(8,128)(2,1)}, u32[]{:S(2)}, u32[]{:S(2)}) collective-permute-start(bf16[10,66,128]{2,1,0:T(8,128)(2,1)} %pad_maximum_fusion.6), channel_id=1, source_target_pairs={{0,144},{16,160},{32,176},{48,192},{64,208},{80,224},{96,240},{112... | collective-permute-start | bytes 506888 | tf_op jit(solution)/shard_map/ppermute | solution.py:12
  74.2 5.7 %copy-start.5 = (bf16[512,640]{1,0:T(8,128)(2,1)S(1)}, bf16[512,640]{1,0:T(8,128)(2,1)}, u32[]{:S(2)}) copy-start(bf16[512,640]{1,0:T(8,128)(2,1)} %param.14) | copy-start | bytes 1966084
  81.1 11.1 %collective-permute-start.6 = (bf16[10,66,128]{2,1,0:T(8,128)(2,1)}, bf16[10,66,128]{2,1,0:T(8,128)(2,1)S(1)}, u32[]{:S(2)}, u32[]{:S(2)}) collective-permute-start(bf16[10,66,128]{2,1,0:T(8,128)(2,1)} %pad_maximum_fusion.6), channel_id=1, source_target_pairs={{0,272},{16,288},{32,304},{48,320},{64,336},{80,352},{96,368},{112... | collective-permute-start | bytes 506888 | tf_op jit(solution)/shard_map/ppermute | solution.py:12
  82.8 12.0 %collective-permute-start.7 = (bf16[10,66,128]{2,1,0:T(8,128)(2,1)}, bf16[10,66,128]{2,1,0:T(8,128)(2,1)S(1)}, u32[]{:S(2)}, u32[]{:S(2)}) collective-permute-start(bf16[10,66,128]{2,1,0:T(8,128)(2,1)} %pad_maximum_fusion.6), channel_id=1, source_target_pairs={{0,400},{16,416},{32,432},{48,448},{64,464},{80,480},{96,496},{1,4... | collective-permute-start | bytes 506888 | tf_op jit(solution)/shard_map/ppermute | solution.py:12
  94.8 2.6 %copy-start.1 = (bf16[512,640]{0,1:T(8,128)(2,1)S(1)}, bf16[512,640]{0,1:T(8,128)(2,1)}, u32[]{:S(2)}) copy-start(bf16[512,640]{0,1:T(8,128)(2,1)} %copy.119) | copy-start | bytes 1966084
  96.6 2.2 %copy-start = (bf16[640,2560]{0,1:T(8,128)(2,1)S(1)}, bf16[640,2560]{0,1:T(8,128)(2,1)}, u32[]{:S(2)}) copy-start(bf16[640,2560]{0,1:T(8,128)(2,1)} %copy.106) | copy-start | bytes 9830404
  97.3 1.5 copy-start.12
  97.5 0.8 copy-start.2
Sparse Core Ops, SparseCore 0:
  104.7 55.1 reduce-scatter.1

commit v8 on v7

--- a/solution.py
+++ b/solution.py
@@ -28,15 +28,23 @@
 
 
 def with_decay(decay, state):
+    head_count = state.shape[0]
     high = decay.astype(jnp.bfloat16)
     low = (decay - high.astype(jnp.float32)).astype(jnp.bfloat16)
-    tail = jnp.broadcast_to(jnp.stack([high, low], 1)[:, :, None], (decay.shape[0], 2, state.shape[2]))
-    return jnp.concatenate([state.astype(jnp.bfloat16), tail], axis=1)
-
-
-def split_decay(packed):
-    decay = packed[:, -2, 0].astype(jnp.float32) + packed[:, -1, 0].astype(jnp.float32)
-    return decay, packed[:, :-2].astype(jnp.float32)
+    tail_rows = -(-head_count // 16) * 16
+    tail = jnp.pad(
+        jnp.stack([high, low], 1), ((0, tail_rows - head_count), (0, state.shape[2] - 2))
+    )
+    flat = state.astype(jnp.bfloat16).reshape(head_count * state.shape[1], state.shape[2])
+    return jnp.concatenate([flat, tail], axis=0)
+
+
+def split_decay(packed, head_count, head_size):
+    rows = head_count * head_size
+    decay = packed[rows : rows + head_count, 0].astype(jnp.float32) + packed[
+        rows : rows + head_count, 1
+    ].astype(jnp.float32)
+    return decay, packed[:rows].astype(jnp.float32).reshape(head_count, head_size, -1)
 
 
 def pass_state(device_decay, local_final, passengers):
@@ -47,14 +55,15 @@
         received = from_behind(with_decay(decay, state), "seq", window)
         if window == 1:
             received, passengers = lax.optimization_barrier((received, passengers))
-        prev_decay, prev_state = split_decay(received)
+        prev_decay, prev_state = split_decay(received, *state.shape[:2])
         state = decay[:, None, None] * prev_state + state
         decay = decay * prev_decay
         window *= 2
     packed = with_decay(decay, state)
     part_count = -(-(shard_count - 1) // window)
     parts = [
-        split_decay(from_behind(packed, "seq", 1 + part * window)) for part in range(part_count)
+        split_decay(from_behind(packed, "seq", 1 + part * window), *state.shape[:2])
+        for part in range(part_count)
     ]
     if not parts:
         return jnp.zeros_like(local_final), passengers

time: 171 us -> 164 us (0.959)
  other arithmetic: 21.4 us -> 17.9 us
  waiting for transfers between devices: 70.8 us -> 67.3 us
    ppermute x8, waiting for transfers between devices: 15.5 us -> 8.9 us  [from_behind(): return lax.ppermute(block, axis, route)]
    reduce_scatter x1, waiting for transfers between devices: 55.3 us -> 58.4 us  [local(): lax.psum_scatter(payload, 'tensor', scatter_dimension=0, tiled=True)[0]]
    convert_element_type x4, other arithmetic: 2.56 us -> 0.28 us  [with_decay(): state.astype(jnp.bfloat16)]
  transfers between devices with their start and end apart: 9 -> 9, of which waited for: 6 -> 4; matrix products, arithmetic and copies ran while one was open for 12% -> 13% of each run, Pallas kernels for 0% -> 0%
where the time goes in v8:
time: 164 us
  waiting for transfers between devices  67.3 us (41%)
  starting transfers between devices  37.1 us (23%)
  other arithmetic  17.9 us (11%)
  local copies, waits for them, and re-layouts  16.5 us (10%)
  between operations  13.9 us (8%)
  matrix products  10.9 us (7%)
    reduce_scatter x1, waiting for transfers between devices, local(): lax.psum_scatter(payload, 'tensor', scatter_dimension=0, tiled=True)[0]  58.4 us
    ppermute x8, starting transfers between devices, from_behind(): return lax.ppermute(block, axis, route)  37.1 us
    ppermute x8, waiting for transfers between devices, from_behind(): return lax.ppermute(block, axis, route)  8.9 us
    optimization_barrier x2, local copies, waits for them, and re-layouts, pass_state(): received, passengers = lax.optimization_barrier((received, passengers))  6.78 us
    dot_general x1, matrix products, local(): jnp.einsum('tc,cgk->gtk', scaled, w_out.reshape(inner_width, group_count,...  3.64 us
  transfers between devices with their start and end apart: 9, of which 4 were waited for; matrix products, arithmetic and copies ran while one was open for 13% of the time, Pallas kernels for 0%

profile of v8, /device:TPU:6, one launch (start us, length us, event | category | flops | bytes accessed | tf_op | source)
XLA Modules:
  0.0 163.5 jit_solution(255943608108102915)
XLA Ops:
  6.5 0.8 convert_convert_fusion
  7.4 0.7 slice.188
  8.1 0.7 slice.189
  8.9 0.2 copy.87
  9.1 3.4 %collective-permute-start = (bf16[3,1024]{0,1:T(8,128)(2,1)S(1)}, bf16[3,1024]{0,1:T(8,128)(2,1)S(1)}, u32[]{:S(2)}, u32[]{:S(2)}) collective-permute-start(bf16[3,1024]{0,1:T(8,128)(2,1)S(1)} %copy.87), channel_id=1, source_target_pairs={{0,16},{16,32},{32,48},{48,64},{64,80},{80,96},{96,112},{112,128},... | collective-permute-start | bytes 18440 | tf_op jit(solution)/shard_map/ppermute | solution.py:12
  12.5 0.7 exponential_negate_fusion
  13.2 0.8 compare_select_fusion
  14.0 1.2 reduce-window.9
  15.3 0.1 copy.89
  15.5 0.9 convert_reduce_fusion.3
  16.4 0.8 slice_convert_fusion.3
  17.2 0.2 slice_reduce_fusion.1
  17.4 0.1 slice.194
  17.5 0.3 copy.93
  17.9 0.6 copy.102
  18.5 0.1 copy.92
  18.6 0.1 copy.96
  18.7 0.6 copy.104
  19.4 0.6 slice.192
  20.0 0.8 pad_maximum_fusion.9
  20.8 0.2 slice_reduce_fusion
  21.1 0.1 copy.108
  21.2 0.7 multiply_bitcast_fusion
  22.1 1.7 %multiply_convert_fusion.5 = bf16[512,640]{0,1:T(8,128)(2,1)S(1)} fusion(bf16[512,640]{0,1:T(8,128)(2,1)S(1)} %copy.93, bf16[3,640]{0,1:T(8,128)(2,1)S(1)} %slice.253, f32[640]{0:T(1024)S(1)} %get-tuple-element.13, f32[640]{0:T(1024)S(1)} %get-tuple-element.14, f32[640]{0:T(1024)S(1)} %get-tuple-element.12, f32[640]{0:T(1024)S(1)} %get-tuple-element.11, ...), kind=kLoop, calls=%fused_computation.28 | loop fusion | flops 9502720 | bytes 1326848 | tf_op jit(solution)/shard_map/convert_element_type | solution.py:27
  23.8 0.2 reshape.310
  24.0 0.8 multiply_convert_fusion.6
  24.8 0.8 fusion.12
  25.6 0.8 broadcast_add_fusion
  26.4 0.2 copy.100
  26.6 0.2 copy.99
  27.2 5.1 %collective-permute-start.1 = (bf16[656,128]{0,1:T(8,128)(2,1)S(1)}, bf16[656,128]{0,1:T(8,128)(2,1)S(1)}, u32[]{:S(2)}, u32[]{:S(2)}) collective-permute-start(bf16[656,128]{0,1:T(8,128)(2,1)S(1)} %pad_maximum_fusion.3), channel_id=1, source_target_pairs={{0,16},{16,32},{32,48},{48,64},{64,80},{80,96},{96,112},{112,128},... | collective-permute-start | bytes 503816 | tf_op jit(solution)/shard_map/ppermute | solution.py:12
  32.3 0.2 compare_and_fusion
  32.6 3.0 %collective-permute-done.1 = bf16[656,128]{0,1:T(8,128)(2,1)S(1)} collective-permute-done((bf16[656,128]{0,1:T(8,128)(2,1)S(1)}, bf16[656,128]{0,1:T(8,128)(2,1)S(1)}, u32[]{:S(2)}, u32[]{:S(2)}) %collective-permute-start.1) | collective-permute-done | bytes 167968 | tf_op jit(solution)/shard_map/ppermute | solution.py:12
  35.7 4.2 %collective-permute-start.2 = (bf16[656,128]{0,1:T(8,128)(2,1)S(1)}, bf16[656,128]{0,1:T(8,128)(2,1)S(1)}, u32[]{:S(2)}, u32[]{:S(2)}) collective-permute-start(bf16[656,128]{0,1:T(8,128)(2,1)S(1)} %pad_maximum_fusion.4), channel_id=1, source_target_pairs={{0,32},{16,48},{32,64},{48,80},{64,96},{80,112},{96,128},{112,144}... | collective-permute-start | bytes 503816 | tf_op jit(solution)/shard_map/ppermute | solution.py:12
  39.9 1.0 fusion.82
  40.9 3.9 %collective-permute-done.2 = bf16[656,128]{0,1:T(8,128)(2,1)S(1)} collective-permute-done((bf16[656,128]{0,1:T(8,128)(2,1)S(1)}, bf16[656,128]{0,1:T(8,128)(2,1)S(1)}, u32[]{:S(2)}, u32[]{:S(2)}) %collective-permute-start.2) | collective-permute-done | bytes 167968 | tf_op jit(solution)/shard_map/ppermute | solution.py:12
  45.1 3.6 %collective-permute-start.3 = (bf16[656,128]{0,1:T(8,128)(2,1)S(1)}, bf16[656,128]{0,1:T(8,128)(2,1)S(1)}, u32[]{:S(2)}, u32[]{:S(2)}) collective-permute-start(bf16[656,128]{0,1:T(8,128)(2,1)S(1)} %pad_maximum_fusion.5), channel_id=1, source_target_pairs={{0,64},{16,80},{32,96},{48,112},{64,128},{80,144},{96,160},{112,17... | collective-permute-start | bytes 503816 | tf_op jit(solution)/shard_map/ppermute | solution.py:12
  48.7 2.9 %fusion.8 = f32[2,256,10,64]{1,3,2,0:T(8,128)S(1)} fusion(f32[10,2,256]{2,0,1:T(8,128)} %copy.104, f32[10,2,256]{2,0,1:T(8,128)} %copy.102, f32[2,256,256]{2,1,0:T(8,128)} %fusion.82, pred[2,256,256]{2,1,0:T(8,128)(4,1)S(1)} %compare_and_fusion, bf16[2,256,10,64]{1,0,3,2:T(2,128)(2,1)S(1)} %reshape.310), kind=kOutput, calls=%fused_computation.17 | convolution fusion | flops 175636480 | bytes 2662400 | tf_op jit(solution)/shard_map/hcts,cshp->cthp/dot_general | solution.py:165
  51.9 0.1 add_convert_fusion
  52.0 0.7 pad_maximum_fusion.6
  52.7 8.3 %collective-permute-start.4 = (bf16[656,128]{0,1:T(8,128)(2,1)}, bf16[656,128]{0,1:T(8,128)(2,1)}, u32[]{:S(2)}, u32[]{:S(2)}) collective-permute-start(bf16[656,128]{0,1:T(8,128)(2,1)} %pad_maximum_fusion.6), channel_id=1, source_target_pairs={{0,16},{16,32},{32,48},{48,64},{64,80},{80,96},{96,112},{112,128},... | collective-permute-start | bytes 503816 | tf_op jit(solution)/shard_map/ppermute | solution.py:12
  61.0 8.6 %collective-permute-start.5 = (bf16[656,128]{0,1:T(8,128)(2,1)}, bf16[656,128]{0,1:T(8,128)(2,1)}, u32[]{:S(2)}, u32[]{:S(2)}) collective-permute-start(bf16[656,128]{0,1:T(8,128)(2,1)} %pad_maximum_fusion.6), channel_id=1, source_target_pairs={{0,144},{16,160},{32,176},{48,192},{64,208},{80,224},{96,240},{112... | collective-permute-start | bytes 503816 | tf_op jit(solution)/shard_map/ppermute | solution.py:12
  69.6 2.4 %collective-permute-start.6 = (bf16[656,128]{0,1:T(8,128)(2,1)}, bf16[656,128]{0,1:T(8,128)(2,1)}, u32[]{:S(2)}, u32[]{:S(2)}) collective-permute-start(bf16[656,128]{0,1:T(8,128)(2,1)} %pad_maximum_fusion.6), channel_id=1, source_target_pairs={{0,272},{16,288},{32,304},{48,320},{64,336},{80,352},{96,368},{112... | collective-permute-start | bytes 503816 | tf_op jit(solution)/shard_map/ppermute | solution.py:12
  72.0 1.8 %fusion.10 = f32[2,256,10,64]{1,3,2,0:T(8,128)S(1)} fusion(f32[2,256,10,64]{1,3,2,0:T(8,128)S(1)} %fusion.8, bf16[2,256,128,1]{2,1,3,0:T(8,128)(2,1)S(1)} %bitcast.95, f32[10]{0:T(128)S(1)} %copy-done.9, f32[2,256,10]{1,2,0:T(8,128)S(1)} %copy.106, f32[1,10,64,128]{3,2,1,0:T(8,128)} %get-tuple-element.30, bf16[2,256,10,64]{1,0,3,2:T(2,128)(2,1)S(1)} %reshape.310), kind=kOutput, calls=%fused_computation.19 | convolution fusion | flops 504954880 | bytes 3756072 | tf_op jit(solution)/shard_map/ctn,chpn->cthp/dot_general | solution.py:157
  73.8 5.7 %copy.101 = bf16[640,2560]{0,1:T(8,128)(2,1)} copy(bf16[640,2560]{1,0:T(8,128)(2,1)} %param.23) | data formatting | bytes 6553600 | tf_op jit(solution)/shard_map/optimization_barrier | solution.py:57
  79.5 1.1 copy.111
  80.6 1.5 collective-permute-start.7
  82.1 0.8 fusion.56
  83.3 2.1 %collective-permute-done.7 = bf16[656,128]{0,1:T(8,128)(2,1)S(1)} collective-permute-done((bf16[656,128]{0,1:T(8,128)(2,1)}, bf16[656,128]{0,1:T(8,128)(2,1)S(1)}, u32[]{:S(2)}, u32[]{:S(2)}) %collective-permute-start.7) | collective-permute-done | bytes 167968 | tf_op jit(solution)/shard_map/ppermute | solution.py:12
  85.4 1.2 add_add_fusion
  86.5 0.2 copy.107
  86.7 0.7 fusion.11
  87.4 0.7 copy.110
  88.1 0.1 copy.119
  88.3 0.5 multiply_reduce_fusion
  88.8 0.3 copy-done.2
  89.2 0.2 copy.113
  89.3 0.3 copy-done
  89.6 3.6 %convert_bitcast_fusion = bf16[8,512,320]{1,2,0:T(8,128)(2,1)S(1)} fusion(bf16[640,8,320]{0,2,1:T(8,128)(2,1)S(1)} %bitcast.90, f32[640]{0:T(1024)S(1)} %copy-done.10, bf16[512,640]{0,1:T(8,128)(2,1)} %copy.111, bf16[512,640]{0,1:T(8,128)(2,1)} %bitcast.92), kind=kOutput, calls=%fused_computation.3 | convolution fusion | flops 1681981440 | bytes 7211520 | tf_op jit(solution)/shard_map/tc,cgk->gtk/dot_general | solution.py:184
  93.4 2.0 %pad_maximum_fusion = bf16[8,514,320]{1,2,0:T(8,128)(2,1)} fusion(bf16[8,2,320]{1,2,0:T(8,128)(2,1)S(1)} %broadcast_in_dim.178, bf16[8,512,320]{1,2,0:T(8,128)(2,1)S(1)} %convert_bitcast_fusion), kind=kLoop, calls=%fused_computation.1 | loop fusion | flops 5263360 | bytes 5263360 | tf_op jit(solution)/shard_map/concatenate | solution.py:197
  95.4 58.4 %reduce-scatter.2.cloned.1.call-done = bf16[1,514,320]{1,2,0:T(8,128)(2,1)} async-done(((bf16[8,514,320]{1,2,0:T(8,128)(2,1)}), bf16[1,514,320]{1,2,0:T(8,128)(2,1)}) %reduce-scatter.2.cloned.1.call-update) | async-done | bytes 328976 | tf_op jit(solution)/shard_map/reduce_scatter | solution.py:198
  153.8 0.9 slice.285
  154.8 0.1 reshape.315
  154.9 1.8 %fusion.21 = bf16[512,320]{0,1:T(8,128)(2,1)} fusion(bf16[1,514,320]{1,2,0:T(8,128)(2,1)} %reduce-scatter.2.cloned.1.call-done, f32[512]{0:T(512)S(1)} %add_rsqrt_fusion), kind=kLoop, calls=%fused_computation.38 | loop fusion | flops 491520 | bytes 657408 | tf_op jit(solution)/shard_map/convert_element_type | solution.py:201
  (96 shorter events, 2.9 us)
Async XLA Ops:
  6.5 11.0 %copy-start.3 = (bf16[512,640]{1,0:T(8,128)(2,1)S(1)}, bf16[512,640]{1,0:T(8,128)(2,1)}, u32[]{:S(2)}) copy-start(bf16[512,640]{1,0:T(8,128)(2,1)} %param.12) | copy-start | bytes 1966084
  6.5 147.3 %reduce-scatter.2.cloned.1.call-start = ((), (), s32[]{:S(2)}) async-start(), calls=%async_computation.1 | async-start | bytes 3686400 | tf_op jit(solution)/shard_map/reduce_scatter | solution.py:198
  8.8 13.1 %copy-start.8 = (s32[512]{0:T(512)S(1)}, s32[512]{0:T(512)}, u32[]{:S(2)}) copy-start(s32[512]{0:T(512)} %param.16) | copy-start | bytes 6148
  9.1 10.3 %collective-permute-start = (bf16[3,1024]{0,1:T(8,128)(2,1)S(1)}, bf16[3,1024]{0,1:T(8,128)(2,1)S(1)}, u32[]{:S(2)}, u32[]{:S(2)}) collective-permute-start(bf16[3,1024]{0,1:T(8,128)(2,1)S(1)} %copy.87), channel_id=1, source_target_pairs={{0,16},{16,32},{32,48},{48,64},{64,80},{80,96},{96,112},{112,128},... | collective-permute-start | bytes 18440 | tf_op jit(solution)/shard_map/ppermute | solution.py:12
  22.1 1.9 %copy-start.5 = (bf16[512,256]{1,0:T(8,128)(2,1)S(1)}, bf16[512,256]{1,0:T(8,128)(2,1)}, u32[]{:S(2)}) copy-start(bf16[512,256]{1,0:T(8,128)(2,1)} %param.13) | copy-start | bytes 786436
  27.2 8.4 %collective-permute-start.1 = (bf16[656,128]{0,1:T(8,128)(2,1)S(1)}, bf16[656,128]{0,1:T(8,128)(2,1)S(1)}, u32[]{:S(2)}, u32[]{:S(2)}) collective-permute-start(bf16[656,128]{0,1:T(8,128)(2,1)S(1)} %pad_maximum_fusion.3), channel_id=1, source_target_pairs={{0,16},{16,32},{32,48},{48,64},{64,80},{80,96},{96,112},{112,128},... | collective-permute-start | bytes 503816 | tf_op jit(solution)/shard_map/ppermute | solution.py:12
  35.7 9.1 %collective-permute-start.2 = (bf16[656,128]{0,1:T(8,128)(2,1)S(1)}, bf16[656,128]{0,1:T(8,128)(2,1)S(1)}, u32[]{:S(2)}, u32[]{:S(2)}) collective-permute-start(bf16[656,128]{0,1:T(8,128)(2,1)S(1)} %pad_maximum_fusion.4), channel_id=1, source_target_pairs={{0,32},{16,48},{32,64},{48,80},{64,96},{80,112},{96,128},{112,144}... | collective-permute-start | bytes 503816 | tf_op jit(solution)/shard_map/ppermute | solution.py:12
  45.1 6.6 %copy-start.7 = (f32[2,256,10]{1,0,2:T(2,128)S(1)}, f32[2,256,10]{1,0,2:T(2,128)}, u32[]{:S(2)}) copy-start(f32[2,256,10]{1,0,2:T(2,128)} %get-tuple-element.38) | copy-start | bytes 61444
  45.1 6.6 %copy-start.6 = (f32[2,256,10]{1,0,2:T(2,128)S(1)}, f32[2,256,10]{1,0,2:T(2,128)}, u32[]{:S(2)}) copy-start(f32[2,256,10]{1,0,2:T(2,128)} %get-tuple-element.37) | copy-start | bytes 61444
  45.1 6.8 %collective-permute-start.3 = (bf16[656,128]{0,1:T(8,128)(2,1)S(1)}, bf16[656,128]{0,1:T(8,128)(2,1)S(1)}, u32[]{:S(2)}, u32[]{:S(2)}) collective-permute-start(bf16[656,128]{0,1:T(8,128)(2,1)S(1)} %pad_maximum_fusion.5), channel_id=1, source_target_pairs={{0,64},{16,80},{32,96},{48,112},{64,128},{80,144},{96,160},{112,17... | collective-permute-start | bytes 503816 | tf_op jit(solution)/shard_map/ppermute | solution.py:12
  51.7 20.3 %copy-start.9 = (f32[10]{0:T(128)S(1)}, f32[10]{0:T(128)}, u32[]{:S(2)}) copy-start(f32[10]{0:T(128)} %param.21) | copy-start | bytes 124
  52.7 29.3 %collective-permute-start.4 = (bf16[656,128]{0,1:T(8,128)(2,1)}, bf16[656,128]{0,1:T(8,128)(2,1)}, u32[]{:S(2)}, u32[]{:S(2)}) collective-permute-start(bf16[656,128]{0,1:T(8,128)(2,1)} %pad_maximum_fusion.6), channel_id=1, source_target_pairs={{0,16},{16,32},{32,48},{48,64},{64,80},{80,96},{96,112},{112,128},... | collective-permute-start | bytes 503816 | tf_op jit(solution)/shard_map/ppermute | solution.py:12
  61.0 21.1 %collective-permute-start.5 = (bf16[656,128]{0,1:T(8,128)(2,1)}, bf16[656,128]{0,1:T(8,128)(2,1)}, u32[]{:S(2)}, u32[]{:S(2)}) collective-permute-start(bf16[656,128]{0,1:T(8,128)(2,1)} %pad_maximum_fusion.6), channel_id=1, source_target_pairs={{0,144},{16,160},{32,176},{48,192},{64,208},{80,224},{96,240},{112... | collective-permute-start | bytes 503816 | tf_op jit(solution)/shard_map/ppermute | solution.py:12
  69.6 12.5 %collective-permute-start.6 = (bf16[656,128]{0,1:T(8,128)(2,1)}, bf16[656,128]{0,1:T(8,128)(2,1)}, u32[]{:S(2)}, u32[]{:S(2)}) collective-permute-start(bf16[656,128]{0,1:T(8,128)(2,1)} %pad_maximum_fusion.6), channel_id=1, source_target_pairs={{0,272},{16,288},{32,304},{48,320},{64,336},{80,352},{96,368},{112... | collective-permute-start | bytes 503816 | tf_op jit(solution)/shard_map/ppermute | solution.py:12
  73.8 5.7 %copy-start.4 = (bf16[512,640]{1,0:T(8,128)(2,1)S(1)}, bf16[512,640]{1,0:T(8,128)(2,1)}, u32[]{:S(2)}) copy-start(bf16[512,640]{1,0:T(8,128)(2,1)} %param.14) | copy-start | bytes 1966084
  80.6 4.8 %collective-permute-start.7 = (bf16[656,128]{0,1:T(8,128)(2,1)}, bf16[656,128]{0,1:T(8,128)(2,1)S(1)}, u32[]{:S(2)}, u32[]{:S(2)}) collective-permute-start(bf16[656,128]{0,1:T(8,128)(2,1)} %pad_maximum_fusion.6), channel_id=1, source_target_pairs={{0,400},{16,416},{32,432},{48,448},{64,464},{80,480},{96,496},{1,4... | collective-permute-start | bytes 503816 | tf_op jit(solution)/shard_map/ppermute | solution.py:12
  86.7 1.6 copy-start.1
  87.4 2.2 %copy-start = (bf16[640,2560]{0,1:T(8,128)(2,1)S(1)}, bf16[640,2560]{0,1:T(8,128)(2,1)}, u32[]{:S(2)}) copy-start(bf16[640,2560]{0,1:T(8,128)(2,1)} %copy.101) | copy-start | bytes 9830404
  88.1 1.5 copy-start.10
  88.3 0.8 copy-start.2
Sparse Core Ops, SparseCore 0:
  95.6 58.2 reduce-scatter.1

commit v9 on v8

--- a/solution.py
+++ b/solution.py
@@ -47,14 +47,17 @@
     return decay, packed[:rows].astype(jnp.float32).reshape(head_count, head_size, -1)
 
 
-def pass_state(device_decay, local_final, passengers):
+def pass_state(device_decay, local_final, passengers, prepare):
     shard_count = lax.axis_size("seq")
     decay, state = device_decay, local_final
     window = 1
     while 4 * window < shard_count - 1:
-        received = from_behind(with_decay(decay, state), "seq", window)
+        sent = with_decay(decay, state)
         if window == 1:
-            received, passengers = lax.optimization_barrier((received, passengers))
+            sent, passengers = lax.optimization_barrier((sent, passengers))
+        received = from_behind(sent, "seq", window)
+        if window == 1:
+            received, passengers = lax.optimization_barrier((received, prepare(passengers)))
         prev_decay, prev_state = split_decay(received, *state.shape[:2])
         state = decay[:, None, None] * prev_state + state
         decay = decay * prev_decay
@@ -166,7 +169,12 @@
         + reached * jnp.transpose(entry_gain, (1, 2, 0))[..., None]
         + skip_term
     )
-    incoming, (z_gate, w_out) = pass_state(device_decay, local_final, (z_gate, w_out))
+    incoming, (z_gate, w_rows) = pass_state(
+        device_decay,
+        local_final,
+        (z_gate, w_out),
+        lambda pair: (pair[0], jnp.transpose(pair[1])),
+    )
     prefix = jnp.cumprod(
         jnp.concatenate([jnp.ones((head_count, 1), jnp.float32), block_decay[:, :-1]], axis=1),
         axis=1,
@@ -180,11 +188,11 @@
     group_count = lax.axis_size("tensor")
     squares = jnp.sum(gated * gated, axis=1)
     scaled = (gated * norm_gain[None, :]).astype(jnp.bfloat16)
-    out_width = w_out.shape[1] // group_count
+    out_width = w_rows.shape[0] // group_count
     partial_value = jnp.einsum(
-        "tc,cgk->gtk",
+        "tc,gkc->gtk",
         scaled,
-        w_out.reshape(inner_width, group_count, out_width),
+        w_rows.reshape(group_count, out_width, inner_width),
         preferred_element_type=jnp.float32,
     ).astype(jnp.bfloat16)
     pad_rows = -(-row_count // out_width)

time: 164 us -> 160 us (0.976)
  starting transfers between devices: 37.1 us -> 34.2 us
  waiting for transfers between devices: 67.3 us -> 64.8 us
    ppermute x8, starting transfers between devices: 37.1 us -> 34.1 us  [from_behind(): return lax.ppermute(block, axis, route)]
  transfers between devices with their start and end apart: 9 -> 9, of which waited for: 4 -> 4; matrix products, arithmetic and copies ran while one was open for 13% -> 14% of each run, Pallas kernels for 0% -> 0%
where the time goes in v9:
time: 160 us; the launch traced here: 159 us
  waiting for transfers between devices  64.8 us (40%)
  starting transfers between devices  34.2 us (21%)
  other arithmetic  17.9 us (11%)
  local copies, waits for them, and re-layouts  17.6 us (11%)
  between operations  13.9 us (9%)
  matrix products  10.9 us (7%)
    reduce_scatter x1, waiting for transfers between devices, local(): lax.psum_scatter(payload, 'tensor', scatter_dimension=0, tiled=True)[0]  57 us
    ppermute x8, starting transfers between devices, from_behind(): return lax.ppermute(block, axis, route)  34.1 us
    ppermute x8, waiting for transfers between devices, from_behind(): return lax.ppermute(block, axis, route)  7.78 us
    optimization_barrier x1, local copies, waits for them, and re-layouts, pass_state(): sent, passengers = lax.optimization_barrier((sent, passengers))  5.66 us
    dot_general x1, matrix products, local(): jnp.einsum('tc,gkc->gtk', scaled, w_rows.reshape(group_count, out_width,...  3.64 us
  transfers between devices with their start and end apart: 9, of which 4 were waited for; matrix products, arithmetic and copies ran while one was open for 14% of the time, Pallas kernels for 0%

profile of v9, /device:TPU:6, one launch (start us, length us, event | category | flops | bytes accessed | tf_op | source)
XLA Modules:
  0.0 159.2 jit_solution(14970940284646401335)
XLA Ops:
  6.5 0.8 slice.189
  7.3 0.7 convert_convert_fusion
  8.1 0.7 slice.188
  8.9 0.2 copy.87
  9.1 3.4 %collective-permute-start = (bf16[3,1024]{0,1:T(8,128)(2,1)S(1)}, bf16[3,1024]{0,1:T(8,128)(2,1)S(1)}, u32[]{:S(2)}, u32[]{:S(2)}) collective-permute-start(bf16[3,1024]{0,1:T(8,128)(2,1)S(1)} %copy.87), channel_id=1, source_target_pairs={{0,16},{16,32},{32,48},{48,64},{64,80},{80,96},{96,112},{112,128},... | collective-permute-start | bytes 18440 | tf_op jit(solution)/shard_map/ppermute | solution.py:12
  12.5 0.7 exponential_negate_fusion
  13.2 0.8 slice_convert_fusion.3
  14.1 0.9 convert_reduce_fusion.3
  14.9 0.8 compare_select_fusion
  15.8 1.2 reduce-window.9
  17.0 0.1 copy.89
  17.3 0.2 slice_reduce_fusion.1
  17.5 0.1 slice.194
  17.7 0.6 copy.102
  18.3 0.2 copy.93
  18.6 0.1 copy.92
  18.7 0.1 copy.96
  18.8 0.6 copy.104
  19.4 0.6 slice.192
  20.0 0.8 pad_maximum_fusion.9
  20.8 0.2 slice_reduce_fusion
  21.3 0.1 copy.108
  21.7 0.7 multiply_bitcast_fusion
  22.5 0.8 multiply_convert_fusion.6
  23.3 1.7 %multiply_convert_fusion.5 = bf16[512,640]{0,1:T(8,128)(2,1)S(1)} fusion(bf16[512,640]{0,1:T(8,128)(2,1)S(1)} %copy.93, bf16[3,640]{0,1:T(8,128)(2,1)S(1)} %slice.253, f32[640]{0:T(1024)S(1)} %get-tuple-element.19, f32[640]{0:T(1024)S(1)} %get-tuple-element.20, f32[640]{0:T(1024)S(1)} %get-tuple-element.18, f32[640]{0:T(1024)S(1)} %get-tuple-element.17, ...), kind=kLoop, calls=%fused_computation.28 | loop fusion | flops 9502720 | bytes 1326848 | tf_op jit(solution)/shard_map/convert_element_type | solution.py:27
  25.0 0.2 reshape.310
  25.1 0.8 fusion.12
  25.9 0.8 broadcast_add_fusion
  26.8 0.2 copy.100
  26.9 0.2 copy.99
  27.2 5.1 %collective-permute-start.1 = (bf16[656,128]{0,1:T(8,128)(2,1)S(1)}, bf16[656,128]{0,1:T(8,128)(2,1)S(1)}, u32[]{:S(2)}, u32[]{:S(2)}) collective-permute-start(bf16[656,128]{0,1:T(8,128)(2,1)S(1)} %pad_maximum_fusion.3), channel_id=1, source_target_pairs={{0,16},{16,32},{32,48},{48,64},{64,80},{80,96},{96,112},{112,128},... | collective-permute-start | bytes 503816 | tf_op jit(solution)/shard_map/ppermute | solution.py:12
  32.3 0.2 compare_and_fusion
  32.6 5.7 %copy.101 = bf16[640,2560]{0,1:T(8,128)(2,1)} copy(bf16[640,2560]{1,0:T(8,128)(2,1)} %param.23) | data formatting | bytes 6553600 | tf_op jit(solution)/shard_map/optimization_barrier | solution.py:57
  38.4 2.3 %collective-permute-start.2 = (bf16[656,128]{0,1:T(8,128)(2,1)S(1)}, bf16[656,128]{0,1:T(8,128)(2,1)S(1)}, u32[]{:S(2)}, u32[]{:S(2)}) collective-permute-start(bf16[656,128]{0,1:T(8,128)(2,1)S(1)} %pad_maximum_fusion.4), channel_id=1, source_target_pairs={{0,32},{16,48},{32,64},{48,80},{64,96},{80,112},{96,128},{112,144}... | collective-permute-start | bytes 503816 | tf_op jit(solution)/shard_map/ppermute | solution.py:12
  40.7 1.1 fusion.82
  41.8 5.7 %collective-permute-done.2 = bf16[656,128]{0,1:T(8,128)(2,1)S(1)} collective-permute-done((bf16[656,128]{0,1:T(8,128)(2,1)S(1)}, bf16[656,128]{0,1:T(8,128)(2,1)S(1)}, u32[]{:S(2)}, u32[]{:S(2)}) %collective-permute-start.2) | collective-permute-done | bytes 167968 | tf_op jit(solution)/shard_map/ppermute | solution.py:12
  47.8 3.6 %collective-permute-start.3 = (bf16[656,128]{0,1:T(8,128)(2,1)S(1)}, bf16[656,128]{0,1:T(8,128)(2,1)S(1)}, u32[]{:S(2)}, u32[]{:S(2)}) collective-permute-start(bf16[656,128]{0,1:T(8,128)(2,1)S(1)} %pad_maximum_fusion.5), channel_id=1, source_target_pairs={{0,64},{16,80},{32,96},{48,112},{64,128},{80,144},{96,160},{112,17... | collective-permute-start | bytes 503816 | tf_op jit(solution)/shard_map/ppermute | solution.py:12
  51.4 2.9 %fusion.8 = f32[2,256,10,64]{1,3,2,0:T(8,128)S(1)} fusion(f32[10,2,256]{2,0,1:T(8,128)} %copy.104, f32[10,2,256]{2,0,1:T(8,128)} %copy.102, f32[2,256,256]{2,1,0:T(8,128)} %fusion.82, pred[2,256,256]{2,1,0:T(8,128)(4,1)S(1)} %compare_and_fusion, bf16[2,256,10,64]{1,0,3,2:T(2,128)(2,1)S(1)} %reshape.310), kind=kOutput, calls=%fused_computation.17 | convolution fusion | flops 175636480 | bytes 2662400 | tf_op jit(solution)/shard_map/hcts,cshp->cthp/dot_general | solution.py:168
  54.6 0.1 add_convert_fusion
  54.7 0.7 pad_maximum_fusion.6
  55.4 12.7 %collective-permute-start.6 = (bf16[656,128]{0,1:T(8,128)(2,1)}, bf16[656,128]{0,1:T(8,128)(2,1)}, u32[]{:S(2)}, u32[]{:S(2)}) collective-permute-start(bf16[656,128]{0,1:T(8,128)(2,1)} %pad_maximum_fusion.6), channel_id=1, source_target_pairs={{0,272},{16,288},{32,304},{48,320},{64,336},{80,352},{96,368},{112... | collective-permute-start | bytes 503816 | tf_op jit(solution)/shard_map/ppermute | solution.py:12
  68.1 3.6 %collective-permute-start.5 = (bf16[656,128]{0,1:T(8,128)(2,1)}, bf16[656,128]{0,1:T(8,128)(2,1)}, u32[]{:S(2)}, u32[]{:S(2)}) collective-permute-start(bf16[656,128]{0,1:T(8,128)(2,1)} %pad_maximum_fusion.6), channel_id=1, source_target_pairs={{0,144},{16,160},{32,176},{48,192},{64,208},{80,224},{96,240},{112... | collective-permute-start | bytes 503816 | tf_op jit(solution)/shard_map/ppermute | solution.py:12
  71.8 1.9 %collective-permute-start.4 = (bf16[656,128]{0,1:T(8,128)(2,1)}, bf16[656,128]{0,1:T(8,128)(2,1)}, u32[]{:S(2)}, u32[]{:S(2)}) collective-permute-start(bf16[656,128]{0,1:T(8,128)(2,1)} %pad_maximum_fusion.6), channel_id=1, source_target_pairs={{0,16},{16,32},{32,48},{48,64},{64,80},{80,96},{96,112},{112,128},... | collective-permute-start | bytes 503816 | tf_op jit(solution)/shard_map/ppermute | solution.py:12
  73.7 1.8 %fusion.10 = f32[2,256,10,64]{1,3,2,0:T(8,128)S(1)} fusion(f32[2,256,10,64]{1,3,2,0:T(8,128)S(1)} %fusion.8, bf16[2,256,128,1]{2,1,3,0:T(8,128)(2,1)S(1)} %bitcast.96, f32[10]{0:T(128)S(1)} %copy-done.8, f32[2,256,10]{1,2,0:T(8,128)S(1)} %copy.106, f32[1,10,64,128]{3,2,1,0:T(8,128)} %get-tuple-element.36, bf16[2,256,10,64]{1,0,3,2:T(2,128)(2,1)S(1)} %reshape.310), kind=kOutput, calls=%fused_computation.19 | convolution fusion | flops 504954880 | bytes 3756072 | tf_op jit(solution)/shard_map/ctn,chpn->cthp/dot_general | solution.py:160
  75.5 2.2 %copy.111 = bf16[512,640]{0,1:T(8,128)(2,1)} copy(bf16[512,640]{1,0:T(8,128)(2,1)} %param.14) | data formatting | bytes 1310720 | tf_op jit(solution)/shard_map/optimization_barrier | solution.py:60
  77.6 1.5 collective-permute-start.7
  79.1 0.5 collective-permute-done.4
  79.6 0.8 fusion.56
  80.8 1.6 %collective-permute-done.7 = bf16[656,128]{0,1:T(8,128)(2,1)S(1)} collective-permute-done((bf16[656,128]{0,1:T(8,128)(2,1)}, bf16[656,128]{0,1:T(8,128)(2,1)S(1)}, u32[]{:S(2)}, u32[]{:S(2)}) %collective-permute-start.7) | collective-permute-done | bytes 167968 | tf_op jit(solution)/shard_map/ppermute | solution.py:12
  82.4 1.2 add_add_fusion
  83.6 0.2 copy.107
  83.8 0.7 fusion.11
  84.5 0.7 copy.110
  85.2 0.1 copy.119
  85.3 0.5 multiply_reduce_fusion
  85.9 0.3 copy-done.2
  86.2 0.2 copy.113
  86.4 0.3 copy-done
  86.7 3.6 %convert_bitcast_fusion = bf16[8,512,320]{1,2,0:T(8,128)(2,1)S(1)} fusion(bf16[8,320,640]{2,1,0:T(8,128)(2,1)S(1)} %bitcast.91, f32[640]{0:T(1024)S(1)} %copy-done.9, bf16[512,640]{0,1:T(8,128)(2,1)} %copy.111, bf16[512,640]{0,1:T(8,128)(2,1)} %bitcast.93), kind=kOutput, calls=%fused_computation.3 | convolution fusion | flops 1681981440 | bytes 7211520 | tf_op jit(solution)/shard_map/tc,gkc->gtk/dot_general | solution.py:192
  90.5 2.0 %pad_maximum_fusion = bf16[8,514,320]{1,2,0:T(8,128)(2,1)} fusion(bf16[8,2,320]{1,2,0:T(8,128)(2,1)S(1)} %broadcast_in_dim.178, bf16[8,512,320]{1,2,0:T(8,128)(2,1)S(1)} %convert_bitcast_fusion), kind=kLoop, calls=%fused_computation.1 | loop fusion | flops 5263360 | bytes 5263360 | tf_op jit(solution)/shard_map/concatenate | solution.py:205
  92.5 57.0 %reduce-scatter.2.cloned.1.call-done = bf16[1,514,320]{1,2,0:T(8,128)(2,1)} async-done(((bf16[8,514,320]{1,2,0:T(8,128)(2,1)}), bf16[1,514,320]{1,2,0:T(8,128)(2,1)}) %reduce-scatter.2.cloned.1.call-update) | async-done | bytes 328976 | tf_op jit(solution)/shard_map/reduce_scatter | solution.py:206
  149.5 0.9 slice.285
  150.5 0.1 reshape.315
  150.6 1.8 %fusion.21 = bf16[512,320]{0,1:T(8,128)(2,1)} fusion(bf16[1,514,320]{1,2,0:T(8,128)(2,1)} %reduce-scatter.2.cloned.1.call-done, f32[512]{0:T(512)S(1)} %add_rsqrt_fusion), kind=kLoop, calls=%fused_computation.38 | loop fusion | flops 491520 | bytes 657408 | tf_op jit(solution)/shard_map/convert_element_type | solution.py:209
  (94 shorter events, 2.9 us)
Async XLA Ops:
  6.5 14.7 %copy-start.7 = (s32[512]{0:T(512)S(1)}, s32[512]{0:T(512)}, u32[]{:S(2)}) copy-start(s32[512]{0:T(512)} %param.16) | copy-start | bytes 6148
  6.5 11.8 %copy-start.3 = (bf16[512,640]{1,0:T(8,128)(2,1)S(1)}, bf16[512,640]{1,0:T(8,128)(2,1)}, u32[]{:S(2)}) copy-start(bf16[512,640]{1,0:T(8,128)(2,1)} %param.12) | copy-start | bytes 1966084
  6.5 143.0 %reduce-scatter.2.cloned.1.call-start = ((), (), s32[]{:S(2)}) async-start(), calls=%async_computation.1 | async-start | bytes 3686400 | tf_op jit(solution)/shard_map/reduce_scatter | solution.py:206
  9.1 10.3 %collective-permute-start = (bf16[3,1024]{0,1:T(8,128)(2,1)S(1)}, bf16[3,1024]{0,1:T(8,128)(2,1)S(1)}, u32[]{:S(2)}, u32[]{:S(2)}) collective-permute-start(bf16[3,1024]{0,1:T(8,128)(2,1)S(1)} %copy.87), channel_id=1, source_target_pairs={{0,16},{16,32},{32,48},{48,64},{64,80},{80,96},{96,112},{112,128},... | collective-permute-start | bytes 18440 | tf_op jit(solution)/shard_map/ppermute | solution.py:12
  12.5 10.0 %copy-start.4 = (bf16[512,256]{1,0:T(8,128)(2,1)S(1)}, bf16[512,256]{1,0:T(8,128)(2,1)}, u32[]{:S(2)}) copy-start(bf16[512,256]{1,0:T(8,128)(2,1)} %param.13) | copy-start | bytes 786436
  27.2 11.1 %collective-permute-start.1 = (bf16[656,128]{0,1:T(8,128)(2,1)S(1)}, bf16[656,128]{0,1:T(8,128)(2,1)S(1)}, u32[]{:S(2)}, u32[]{:S(2)}) collective-permute-start(bf16[656,128]{0,1:T(8,128)(2,1)S(1)} %pad_maximum_fusion.3), channel_id=1, source_target_pairs={{0,16},{16,32},{32,48},{48,64},{64,80},{80,96},{96,112},{112,128},... | collective-permute-start | bytes 503816 | tf_op jit(solution)/shard_map/ppermute | solution.py:12
  38.4 9.1 %collective-permute-start.2 = (bf16[656,128]{0,1:T(8,128)(2,1)S(1)}, bf16[656,128]{0,1:T(8,128)(2,1)S(1)}, u32[]{:S(2)}, u32[]{:S(2)}) collective-permute-start(bf16[656,128]{0,1:T(8,128)(2,1)S(1)} %pad_maximum_fusion.4), channel_id=1, source_target_pairs={{0,32},{16,48},{32,64},{48,80},{64,96},{80,112},{96,128},{112,144}... | collective-permute-start | bytes 503816 | tf_op jit(solution)/shard_map/ppermute | solution.py:12
  47.8 6.6 %copy-start.6 = (f32[2,256,10]{1,0,2:T(2,128)S(1)}, f32[2,256,10]{1,0,2:T(2,128)}, u32[]{:S(2)}) copy-start(f32[2,256,10]{1,0,2:T(2,128)} %get-tuple-element.43) | copy-start | bytes 61444
  47.8 6.6 %copy-start.5 = (f32[2,256,10]{1,0,2:T(2,128)S(1)}, f32[2,256,10]{1,0,2:T(2,128)}, u32[]{:S(2)}) copy-start(f32[2,256,10]{1,0,2:T(2,128)} %get-tuple-element.44) | copy-start | bytes 61444
  47.8 6.8 %collective-permute-start.3 = (bf16[656,128]{0,1:T(8,128)(2,1)S(1)}, bf16[656,128]{0,1:T(8,128)(2,1)S(1)}, u32[]{:S(2)}, u32[]{:S(2)}) collective-permute-start(bf16[656,128]{0,1:T(8,128)(2,1)S(1)} %pad_maximum_fusion.5), channel_id=1, source_target_pairs={{0,64},{16,80},{32,96},{48,112},{64,128},{80,144},{96,160},{112,17... | collective-permute-start | bytes 503816 | tf_op jit(solution)/shard_map/ppermute | solution.py:12
  54.4 19.3 %copy-start.8 = (f32[10]{0:T(128)S(1)}, f32[10]{0:T(128)}, u32[]{:S(2)}) copy-start(f32[10]{0:T(128)} %param.21) | copy-start | bytes 124
  55.4 23.7 %collective-permute-start.6 = (bf16[656,128]{0,1:T(8,128)(2,1)}, bf16[656,128]{0,1:T(8,128)(2,1)}, u32[]{:S(2)}, u32[]{:S(2)}) collective-permute-start(bf16[656,128]{0,1:T(8,128)(2,1)} %pad_maximum_fusion.6), channel_id=1, source_target_pairs={{0,272},{16,288},{32,304},{48,320},{64,336},{80,352},{96,368},{112... | collective-permute-start | bytes 503816 | tf_op jit(solution)/shard_map/ppermute | solution.py:12
  68.1 11.0 %collective-permute-start.5 = (bf16[656,128]{0,1:T(8,128)(2,1)}, bf16[656,128]{0,1:T(8,128)(2,1)}, u32[]{:S(2)}, u32[]{:S(2)}) collective-permute-start(bf16[656,128]{0,1:T(8,128)(2,1)} %pad_maximum_fusion.6), channel_id=1, source_target_pairs={{0,144},{16,160},{32,176},{48,192},{64,208},{80,224},{96,240},{112... | collective-permute-start | bytes 503816 | tf_op jit(solution)/shard_map/ppermute | solution.py:12
  71.8 7.9 %collective-permute-start.4 = (bf16[656,128]{0,1:T(8,128)(2,1)}, bf16[656,128]{0,1:T(8,128)(2,1)}, u32[]{:S(2)}, u32[]{:S(2)}) collective-permute-start(bf16[656,128]{0,1:T(8,128)(2,1)} %pad_maximum_fusion.6), channel_id=1, source_target_pairs={{0,16},{16,32},{32,48},{48,64},{64,80},{80,96},{96,112},{112,128},... | collective-permute-start | bytes 503816 | tf_op jit(solution)/shard_map/ppermute | solution.py:12
  77.6 4.8 %collective-permute-start.7 = (bf16[656,128]{0,1:T(8,128)(2,1)}, bf16[656,128]{0,1:T(8,128)(2,1)S(1)}, u32[]{:S(2)}, u32[]{:S(2)}) collective-permute-start(bf16[656,128]{0,1:T(8,128)(2,1)} %pad_maximum_fusion.6), channel_id=1, source_target_pairs={{0,400},{16,416},{32,432},{48,448},{64,464},{80,480},{96,496},{1,4... | collective-permute-start | bytes 503816 | tf_op jit(solution)/shard_map/ppermute | solution.py:12
  83.8 1.6 copy-start.1
  84.5 2.2 %copy-start = (bf16[640,2560]{0,1:T(8,128)(2,1)S(1)}, bf16[640,2560]{0,1:T(8,128)(2,1)}, u32[]{:S(2)}) copy-start(bf16[640,2560]{0,1:T(8,128)(2,1)} %copy.101) | copy-start | bytes 9830404
  85.2 1.5 copy-start.9
  85.3 0.8 copy-start.2
Sparse Core Ops, SparseCore 0:
  92.6 56.8 reduce-scatter.1

commit v10 on v9

--- a/solution.py
+++ b/solution.py
@@ -169,11 +169,11 @@
         + reached * jnp.transpose(entry_gain, (1, 2, 0))[..., None]
         + skip_term
     )
-    incoming, (z_gate, w_rows) = pass_state(
+    incoming, (gate_silu, w_rows) = pass_state(
         device_decay,
         local_final,
         (z_gate, w_out),
-        lambda pair: (pair[0], jnp.transpose(pair[1])),
+        lambda pair: (jax.nn.silu(pair[0].astype(jnp.float32)), jnp.transpose(pair[1])),
     )
     prefix = jnp.cumprod(
         jnp.concatenate([jnp.ones((head_count, 1), jnp.float32), block_decay[:, :-1]], axis=1),
@@ -184,7 +184,7 @@
         result + reach_term * jnp.transpose(entry_gain * prefix[:, :, None], (1, 2, 0))[..., None]
     )
     y_vals = lax.optimization_barrier(result.reshape(row_count, inner_width).astype(jnp.bfloat16))
-    gated = y_vals.astype(jnp.float32) * jax.nn.silu(z_gate.astype(jnp.float32))
+    gated = y_vals.astype(jnp.float32) * gate_silu
     group_count = lax.axis_size("tensor")
     squares = jnp.sum(gated * gated, axis=1)
     scaled = (gated * norm_gain[None, :]).astype(jnp.bfloat16)

time: 160 us -> 159 us (level)
  starting transfers between devices: 34.2 us -> 29.4 us
  matrix products: 10.9 us -> 13.2 us
    ppermute x8, starting transfers between devices: 34.1 us -> 29.4 us  [from_behind(): return lax.ppermute(block, axis, route)]
    optimization_barrier x1 -> x0, local copies, waits for them, and re-layouts: 2.17 us -> none  [pass_state(): lax.optimization_barrier((received, prepare(passengers)))]
    optimization_barrier x1 -> x2, local copies, waits for them, and re-layouts: 5.66 us -> 6.96 us  [pass_state(): sent, passengers = lax.optimization_barrier((sent, passengers))]
  transfers between devices with their start and end apart: 9 -> 9, of which waited for: 4 -> 5; matrix products, arithmetic and copies ran while one was open for 14% -> 14% of each run, Pallas kernels for 0% -> 0%
where the time goes in v10:
time: 159 us; the launch traced here: 158 us
  waiting for transfers between devices  65.9 us (41%)
  starting transfers between devices  29.4 us (18%)
  other arithmetic  18.5 us (12%)
  local copies, waits for them, and re-layouts  17.1 us (11%)
  between operations  13.9 us (9%)
  matrix products  13.2 us (8%)
    reduce_scatter x1, waiting for transfers between devices, local(): lax.psum_scatter(payload, 'tensor', scatter_dimension=0, tiled=True)[0]  56.9 us
    ppermute x8, starting transfers between devices, from_behind(): return lax.ppermute(block, axis, route)  29.4 us
    ppermute x8, waiting for transfers between devices, from_behind(): return lax.ppermute(block, axis, route)  9.03 us
    optimization_barrier x2, local copies, waits for them, and re-layouts, pass_state(): sent, passengers = lax.optimization_barrier((sent, passengers))  6.96 us
    dot_general x1, matrix products, local(): jnp.einsum('tc,gkc->gtk', scaled, w_rows.reshape(group_count, out_width,...  4.21 us
    dot_general x1, matrix products, local(): jnp.einsum('hcts,cshp->cthp', weights, block_x, preferred_element_type=jn...  3.71 us
  transfers between devices with their start and end apart: 9, of which 5 were waited for; matrix products, arithmetic and copies ran while one was open for 14% of the time, Pallas kernels for 0%

profile of v10, /device:TPU:6, one launch (start us, length us, event | category | flops | bytes accessed | tf_op | source)
XLA Modules:
  0.0 158.0 jit_solution(16642724755755989016)
XLA Ops:
  6.5 0.8 slice.189
  7.3 0.7 convert_convert_fusion
  8.1 0.7 slice.188
  8.9 0.2 copy.87
  9.1 3.4 %collective-permute-start = (bf16[3,1024]{0,1:T(8,128)(2,1)S(1)}, bf16[3,1024]{0,1:T(8,128)(2,1)S(1)}, u32[]{:S(2)}, u32[]{:S(2)}) collective-permute-start(bf16[3,1024]{0,1:T(8,128)(2,1)S(1)} %copy.87), channel_id=1, source_target_pairs={{0,16},{16,32},{32,48},{48,64},{64,80},{80,96},{96,112},{112,128},... | collective-permute-start | bytes 18440 | tf_op jit(solution)/shard_map/ppermute | solution.py:12
  12.5 0.7 exponential_negate_fusion
  13.2 0.8 slice_convert_fusion.3
  14.0 0.9 convert_reduce_fusion.3
  14.9 0.8 compare_select_fusion
  15.8 1.2 reduce-window.9
  17.0 0.1 copy.89
  17.2 0.9 compare_and_fusion
  18.1 0.2 slice_reduce_fusion.1
  18.3 0.1 slice.194
  18.5 0.3 copy.93
  18.8 0.1 copy.92
  18.9 0.1 copy.96
  19.0 0.6 copy.105
  19.6 0.6 slice.192
  20.2 0.8 pad_maximum_fusion.9
  21.0 0.2 slice_reduce_fusion
  21.5 0.1 copy.109
  22.0 0.6 multiply_bitcast_fusion
  22.8 0.8 multiply_convert_fusion.6
  23.6 1.6 %multiply_convert_fusion.5 = bf16[512,640]{0,1:T(8,128)(2,1)S(1)} fusion(bf16[512,640]{0,1:T(8,128)(2,1)S(1)} %copy.93, bf16[3,640]{0,1:T(8,128)(2,1)S(1)} %slice.253, f32[640]{0:T(1024)S(1)} %get-tuple-element.19, f32[640]{0:T(1024)S(1)} %get-tuple-element.20, f32[640]{0:T(1024)S(1)} %get-tuple-element.18, f32[640]{0:T(1024)S(1)} %get-tuple-element.17, ...), kind=kLoop, calls=%fused_computation.28 | loop fusion | flops 9502720 | bytes 1326848 | tf_op jit(solution)/shard_map/convert_element_type | solution.py:27
  25.3 0.2 reshape.310
  25.4 0.8 fusion.12
  26.2 0.8 broadcast_add_fusion
  27.0 0.2 copy.100
  27.2 0.2 copy.99
  27.4 0.7 pad_maximum_fusion.3
  28.1 4.9 %collective-permute-start.1 = (bf16[656,128]{0,1:T(8,128)(2,1)}, bf16[656,128]{0,1:T(8,128)(2,1)S(1)}, u32[]{:S(2)}, u32[]{:S(2)}) collective-permute-start(bf16[656,128]{0,1:T(8,128)(2,1)} %pad_maximum_fusion.3), channel_id=1, source_target_pairs={{0,16},{16,32},{32,48},{48,64},{64,80},{80,96},{96,112},{112,128},... | collective-permute-start | bytes 503816 | tf_op jit(solution)/shard_map/ppermute | solution.py:12
  33.0 1.3 copy.101
  34.4 5.6 %copy.102 = bf16[640,2560]{0,1:T(8,128)(2,1)} copy(bf16[640,2560]{1,0:T(8,128)(2,1)} %param.23) | data formatting | bytes 6553600 | tf_op jit(solution)/shard_map/optimization_barrier | solution.py:57
  40.0 0.3 convert_multiply_fusion
  40.5 2.5 %collective-permute-start.2 = (bf16[656,128]{0,1:T(8,128)(2,1)S(1)}, bf16[656,128]{0,1:T(8,128)(2,1)S(1)}, u32[]{:S(2)}, u32[]{:S(2)}) collective-permute-start(bf16[656,128]{0,1:T(8,128)(2,1)S(1)} %pad_maximum_fusion.4), channel_id=1, source_target_pairs={{0,32},{16,48},{32,64},{48,80},{64,96},{80,112},{96,128},{112,144}... | collective-permute-start | bytes 503816 | tf_op jit(solution)/shard_map/ppermute | solution.py:12
  43.0 1.0 fusion.79
  44.1 5.5 %collective-permute-done.2 = bf16[656,128]{0,1:T(8,128)(2,1)S(1)} collective-permute-done((bf16[656,128]{0,1:T(8,128)(2,1)S(1)}, bf16[656,128]{0,1:T(8,128)(2,1)S(1)}, u32[]{:S(2)}, u32[]{:S(2)}) %collective-permute-start.2) | collective-permute-done | bytes 167968 | tf_op jit(solution)/shard_map/ppermute | solution.py:12
  49.9 3.5 %collective-permute-start.3 = (bf16[656,128]{0,1:T(8,128)(2,1)S(1)}, bf16[656,128]{0,1:T(8,128)(2,1)S(1)}, u32[]{:S(2)}, u32[]{:S(2)}) collective-permute-start(bf16[656,128]{0,1:T(8,128)(2,1)S(1)} %pad_maximum_fusion.5), channel_id=1, source_target_pairs={{0,64},{16,80},{32,96},{48,112},{64,128},{80,144},{96,160},{112,17... | collective-permute-start | bytes 503816 | tf_op jit(solution)/shard_map/ppermute | solution.py:12
  53.4 3.7 %fusion.8 = f32[2,256,10,64]{1,3,2,0:T(8,128)} fusion(f32[10,2,256]{2,0,1:T(8,128)S(1)} %copy-done.7, f32[10,2,256]{2,0,1:T(8,128)S(1)} %copy.103, f32[2,256,256]{2,1,0:T(8,128)} %fusion.79, pred[2,256,256]{2,1,0:T(8,128)(4,1)} %compare_and_fusion, bf16[2,256,10,64]{1,0,3,2:T(2,128)(2,1)S(1)} %reshape.310), kind=kOutput, calls=%fused_computation.17 | convolution fusion | flops 175636480 | bytes 2662400 | tf_op jit(solution)/shard_map/hcts,cshp->cthp/dot_general | solution.py:168
  57.3 0.1 add_convert_fusion
  57.4 0.7 pad_maximum_fusion.6
  58.2 10.1 %collective-permute-start.6 = (bf16[656,128]{0,1:T(8,128)(2,1)}, bf16[656,128]{0,1:T(8,128)(2,1)S(1)}, u32[]{:S(2)}, u32[]{:S(2)}) collective-permute-start(bf16[656,128]{0,1:T(8,128)(2,1)} %pad_maximum_fusion.6), channel_id=1, source_target_pairs={{0,272},{16,288},{32,304},{48,320},{64,336},{80,352},{96,368},{112... | collective-permute-start | bytes 503816 | tf_op jit(solution)/shard_map/ppermute | solution.py:12
  68.3 1.6 %collective-permute-start.5 = (bf16[656,128]{0,1:T(8,128)(2,1)}, bf16[656,128]{0,1:T(8,128)(2,1)S(1)}, u32[]{:S(2)}, u32[]{:S(2)}) collective-permute-start(bf16[656,128]{0,1:T(8,128)(2,1)} %pad_maximum_fusion.6), channel_id=1, source_target_pairs={{0,144},{16,160},{32,176},{48,192},{64,208},{80,224},{96,240},{112... | collective-permute-start | bytes 503816 | tf_op jit(solution)/shard_map/ppermute | solution.py:12
  69.9 1.9 %collective-permute-start.4 = (bf16[656,128]{0,1:T(8,128)(2,1)}, bf16[656,128]{0,1:T(8,128)(2,1)S(1)}, u32[]{:S(2)}, u32[]{:S(2)}) collective-permute-start(bf16[656,128]{0,1:T(8,128)(2,1)} %pad_maximum_fusion.6), channel_id=1, source_target_pairs={{0,16},{16,32},{32,48},{48,64},{64,80},{80,96},{96,112},{112,128},... | collective-permute-start | bytes 503816 | tf_op jit(solution)/shard_map/ppermute | solution.py:12
  71.8 1.8 %fusion.10 = f32[2,256,10,64]{1,3,2,0:T(8,128)S(1)} fusion(f32[2,256,10,64]{1,3,2,0:T(8,128)S(1)} %copy-done, bf16[2,256,128,1]{2,1,3,0:T(8,128)(2,1)S(1)} %bitcast.96, f32[10]{0:T(128)S(1)} %copy-done.9, f32[2,256,10]{1,2,0:T(8,128)S(1)} %copy.107, f32[1,10,64,128]{3,2,1,0:T(8,128)} %get-tuple-element.36, bf16[2,256,10,64]{1,0,3,2:T(2,128)(2,1)S(1)} %reshape.310), kind=kOutput, calls=%fused_computation.19 | convolution fusion | flops 504954880 | bytes 3756072 | tf_op jit(solution)/shard_map/ctn,chpn->cthp/dot_general | solution.py:160
  73.6 1.5 collective-permute-start.7
  75.1 1.0 collective-permute-done.6
  76.1 1.5 collective-permute-done.4
  77.7 0.7 copy-done.5
  78.8 1.0 collective-permute-done.7
  79.8 1.2 add_add_fusion
  80.9 0.9 copy.108
  81.8 1.7 %fusion.11 = bf16[2,256,10,64]{1,3,2,0:T(8,128)(2,1)S(1)} fusion(f32[2,256,10,64]{1,3,2,0:T(8,128)S(1)} %fusion.10, bf16[2,256,128,1]{2,1,3,0:T(8,128)(2,1)S(1)} %bitcast.97, f32[10,64,128,1]{2,1,0,3:T(8,128)} %bitcast.98, f32[2,256,10]{1,2,0:T(8,128)S(1)} %copy.110), kind=kOutput, calls=%fused_computation.20 | convolution fusion | flops 504299520 | bytes 2445312 | tf_op jit(solution)/shard_map/ctn,hpn->cthp/dot_general | solution.py:182
  83.5 0.7 copy.111
  84.2 0.1 copy.119
  84.3 0.3 multiply_reduce_fusion
  84.7 0.2 copy.113
  84.8 0.2 copy-done.10
  85.0 4.2 %convert_bitcast_fusion = bf16[8,512,320]{1,2,0:T(8,128)(2,1)S(1)} fusion(bf16[8,320,640]{2,1,0:T(8,128)(2,1)} %bitcast.91, f32[512,640]{0,1:T(8,128)S(1)} %convert_multiply_fusion, bf16[512,640]{0,1:T(8,128)(2,1)S(1)} %bitcast.93, f32[640]{0:T(1024)S(1)} %copy-done.10), kind=kOutput, calls=%fused_computation.3 | convolution fusion | flops 1680343040 | bytes 7866880 | tf_op jit(solution)/shard_map/tc,gkc->gtk/dot_general | solution.py:192
  89.3 2.0 %pad_maximum_fusion = bf16[8,514,320]{1,2,0:T(8,128)(2,1)} fusion(bf16[8,2,320]{1,2,0:T(8,128)(2,1)S(1)} %broadcast_in_dim.178, bf16[8,512,320]{1,2,0:T(8,128)(2,1)S(1)} %convert_bitcast_fusion), kind=kLoop, calls=%fused_computation.1 | loop fusion | flops 5263360 | bytes 5263360 | tf_op jit(solution)/shard_map/concatenate | solution.py:205
  91.4 56.9 %reduce-scatter.2.cloned.1.call-done = bf16[1,514,320]{1,2,0:T(8,128)(2,1)} async-done(((bf16[8,514,320]{1,2,0:T(8,128)(2,1)}), bf16[1,514,320]{1,2,0:T(8,128)(2,1)}) %reduce-scatter.2.cloned.1.call-update) | async-done | bytes 328976 | tf_op jit(solution)/shard_map/reduce_scatter | solution.py:206
  148.3 0.9 slice.285
  149.3 1.8 %fusion.20 = bf16[512,320]{0,1:T(8,128)(2,1)} fusion(bf16[1,514,320]{1,2,0:T(8,128)(2,1)} %reduce-scatter.2.cloned.1.call-done, f32[512]{0:T(512)S(1)} %add_rsqrt_fusion), kind=kLoop, calls=%fused_computation.38 | loop fusion | flops 491520 | bytes 657408 | tf_op jit(solution)/shard_map/convert_element_type | solution.py:209
  (97 shorter events, 2.9 us)
Async XLA Ops:
  6.5 12.0 %copy-start.1 = (bf16[512,640]{1,0:T(8,128)(2,1)S(1)}, bf16[512,640]{1,0:T(8,128)(2,1)}, u32[]{:S(2)}) copy-start(bf16[512,640]{1,0:T(8,128)(2,1)} %param.12) | copy-start | bytes 1966084
  6.5 141.7 %reduce-scatter.2.cloned.1.call-start = ((), (), s32[]{:S(2)}) async-start(), calls=%async_computation.1 | async-start | bytes 3686400 | tf_op jit(solution)/shard_map/reduce_scatter | solution.py:206
  8.8 12.6 %copy-start.8 = (s32[512]{0:T(512)S(1)}, s32[512]{0:T(512)}, u32[]{:S(2)}) copy-start(s32[512]{0:T(512)} %param.16) | copy-start | bytes 6148
  9.1 10.6 %collective-permute-start = (bf16[3,1024]{0,1:T(8,128)(2,1)S(1)}, bf16[3,1024]{0,1:T(8,128)(2,1)S(1)}, u32[]{:S(2)}, u32[]{:S(2)}) collective-permute-start(bf16[3,1024]{0,1:T(8,128)(2,1)S(1)} %copy.87), channel_id=1, source_target_pairs={{0,16},{16,32},{32,48},{48,64},{64,80},{80,96},{96,112},{112,128},... | collective-permute-start | bytes 18440 | tf_op jit(solution)/shard_map/ppermute | solution.py:12
  15.7 7.0 %copy-start.2 = (bf16[512,256]{1,0:T(8,128)(2,1)S(1)}, bf16[512,256]{1,0:T(8,128)(2,1)}, u32[]{:S(2)}) copy-start(bf16[512,256]{1,0:T(8,128)(2,1)} %param.13) | copy-start | bytes 786436
  28.1 12.2 %collective-permute-start.1 = (bf16[656,128]{0,1:T(8,128)(2,1)}, bf16[656,128]{0,1:T(8,128)(2,1)S(1)}, u32[]{:S(2)}, u32[]{:S(2)}) collective-permute-start(bf16[656,128]{0,1:T(8,128)(2,1)} %pad_maximum_fusion.3), channel_id=1, source_target_pairs={{0,16},{16,32},{32,48},{48,64},{64,80},{80,96},{96,112},{112,128},... | collective-permute-start | bytes 503816 | tf_op jit(solution)/shard_map/ppermute | solution.py:12
  40.5 12.9 %copy-start.7 = (f32[10,2,256]{2,0,1:T(8,128)S(1)}, f32[10,2,256]{2,0,1:T(8,128)}, u32[]{:S(2)}) copy-start(f32[10,2,256]{2,0,1:T(8,128)} %copy.105) | copy-start | bytes 61444
  40.5 9.1 %collective-permute-start.2 = (bf16[656,128]{0,1:T(8,128)(2,1)S(1)}, bf16[656,128]{0,1:T(8,128)(2,1)S(1)}, u32[]{:S(2)}, u32[]{:S(2)}) collective-permute-start(bf16[656,128]{0,1:T(8,128)(2,1)S(1)} %pad_maximum_fusion.4), channel_id=1, source_target_pairs={{0,32},{16,48},{32,64},{48,80},{64,96},{80,112},{96,128},{112,144}... | collective-permute-start | bytes 503816 | tf_op jit(solution)/shard_map/ppermute | solution.py:12
  49.9 7.2 %copy-start.6 = (f32[2,256,10]{1,0,2:T(2,128)S(1)}, f32[2,256,10]{1,0,2:T(2,128)}, u32[]{:S(2)}) copy-start(f32[2,256,10]{1,0,2:T(2,128)} %get-tuple-element.44) | copy-start | bytes 61444
  49.9 7.4 %collective-permute-start.3 = (bf16[656,128]{0,1:T(8,128)(2,1)S(1)}, bf16[656,128]{0,1:T(8,128)(2,1)S(1)}, u32[]{:S(2)}, u32[]{:S(2)}) collective-permute-start(bf16[656,128]{0,1:T(8,128)(2,1)S(1)} %pad_maximum_fusion.5), channel_id=1, source_target_pairs={{0,64},{16,80},{32,96},{48,112},{64,128},{80,144},{96,160},{112,17... | collective-permute-start | bytes 503816 | tf_op jit(solution)/shard_map/ppermute | solution.py:12
  57.1 14.7 %copy-start.9 = (f32[10]{0:T(128)S(1)}, f32[10]{0:T(128)}, u32[]{:S(2)}) copy-start(f32[10]{0:T(128)} %param.21) | copy-start | bytes 124
  57.3 14.5 %copy-start = (f32[2,256,10,64]{1,3,2,0:T(8,128)S(1)}, f32[2,256,10,64]{1,3,2,0:T(8,128)}, u32[]{:S(2)}) copy-start(f32[2,256,10,64]{1,3,2,0:T(8,128)} %fusion.8) | copy-start | bytes 3932164
  58.2 18.0 %collective-permute-start.6 = (bf16[656,128]{0,1:T(8,128)(2,1)}, bf16[656,128]{0,1:T(8,128)(2,1)S(1)}, u32[]{:S(2)}, u32[]{:S(2)}) collective-permute-start(bf16[656,128]{0,1:T(8,128)(2,1)} %pad_maximum_fusion.6), channel_id=1, source_target_pairs={{0,272},{16,288},{32,304},{48,320},{64,336},{80,352},{96,368},{112... | collective-permute-start | bytes 503816 | tf_op jit(solution)/shard_map/ppermute | solution.py:12
  68.3 7.8 %collective-permute-start.5 = (bf16[656,128]{0,1:T(8,128)(2,1)}, bf16[656,128]{0,1:T(8,128)(2,1)S(1)}, u32[]{:S(2)}, u32[]{:S(2)}) collective-permute-start(bf16[656,128]{0,1:T(8,128)(2,1)} %pad_maximum_fusion.6), channel_id=1, source_target_pairs={{0,144},{16,160},{32,176},{48,192},{64,208},{80,224},{96,240},{112... | collective-permute-start | bytes 503816 | tf_op jit(solution)/shard_map/ppermute | solution.py:12
  69.9 7.8 %collective-permute-start.4 = (bf16[656,128]{0,1:T(8,128)(2,1)}, bf16[656,128]{0,1:T(8,128)(2,1)S(1)}, u32[]{:S(2)}, u32[]{:S(2)}) collective-permute-start(bf16[656,128]{0,1:T(8,128)(2,1)} %pad_maximum_fusion.6), channel_id=1, source_target_pairs={{0,16},{16,32},{32,48},{48,64},{64,80},{80,96},{96,112},{112,128},... | collective-permute-start | bytes 503816 | tf_op jit(solution)/shard_map/ppermute | solution.py:12
  73.6 6.2 %collective-permute-start.7 = (bf16[656,128]{0,1:T(8,128)(2,1)}, bf16[656,128]{0,1:T(8,128)(2,1)S(1)}, u32[]{:S(2)}, u32[]{:S(2)}) collective-permute-start(bf16[656,128]{0,1:T(8,128)(2,1)} %pad_maximum_fusion.6), channel_id=1, source_target_pairs={{0,400},{16,416},{32,432},{48,448},{64,464},{80,480},{96,496},{1,4... | collective-permute-start | bytes 503816 | tf_op jit(solution)/shard_map/ppermute | solution.py:12
  76.1 1.5 copy-start.3
  76.1 1.5 copy-start.4
  77.6 0.7 copy-start.5
  84.3 0.7 copy-start.10
Sparse Core Ops, SparseCore 0:
  91.5 56.7 reduce-scatter.1

commit v11 on v10

--- a/solution.py
+++ b/solution.py
@@ -195,18 +195,14 @@
         w_rows.reshape(group_count, out_width, inner_width),
         preferred_element_type=jnp.float32,
     ).astype(jnp.bfloat16)
-    pad_rows = -(-row_count // out_width)
-    square_rows = jnp.pad(squares, (0, pad_rows * out_width - row_count)).reshape(
-        pad_rows, out_width
-    )
-    square_rows = jnp.broadcast_to(
-        square_rows.astype(jnp.bfloat16)[None], (group_count, pad_rows, out_width)
-    )
-    payload = jnp.concatenate([partial_value, square_rows], axis=1)
+    square_column = jnp.broadcast_to(
+        squares.astype(jnp.bfloat16)[None, :, None], (group_count, row_count, 1)
+    )
+    payload = jnp.concatenate([partial_value, square_column], axis=2)
     summed = lax.psum_scatter(payload, "tensor", scatter_dimension=0, tiled=True)[0]
-    total_squares = summed[row_count:].reshape(-1)[:row_count].astype(jnp.float32)
+    total_squares = summed[:, out_width].astype(jnp.float32)
     inv_norm = lax.rsqrt(total_squares / (inner_width * group_count) + 1e-05)
-    return (summed[:row_count].astype(jnp.float32) * inv_norm[:, None]).astype(jnp.bfloat16)
+    return (summed[:, :out_width].astype(jnp.float32) * inv_norm[:, None]).astype(jnp.bfloat16)
 
 
 def solution(mesh):

time: 159 us -> 156 us (0.981)
  matrix products: 13.2 us -> 10.4 us
  other arithmetic: 18.5 us -> 20.8 us
  waiting for transfers between devices: 65.9 us -> 63.8 us
    reduce_scatter x1, waiting for transfers between devices: 56.9 us -> 54 us  [local(): lax.psum_scatter(payload, 'tensor', scatter_dimension=0, tiled=True)[0]]
    dot_general x1, matrix products: 4.21 us -> 2.34 us  [local(): jnp.einsum('tc,gkc->gtk', scaled, w_rows.reshape(group_count, out_width,...]
  transfers between devices with their start and end apart: 9 -> 9, of which waited for: 5 -> 5; matrix products, arithmetic and copies ran while one was open for 14% -> 13% of each run, Pallas kernels for 0% -> 0%
where the time goes in v11:
time: 156 us; the launch traced here: 155 us
  waiting for transfers between devices  63.8 us (41%)
  starting transfers between devices  30.6 us (20%)
  other arithmetic  20.8 us (13%)
  local copies, waits for them, and re-layouts  15.9 us (10%)
  between operations  13.8 us (9%)
  matrix products  10.4 us (7%)
    reduce_scatter x1, waiting for transfers between devices, local(): lax.psum_scatter(payload, 'tensor', scatter_dimension=0, tiled=True)[0]  54 us
    ppermute x8, starting transfers between devices, from_behind(): return lax.ppermute(block, axis, route)  30.6 us
    ppermute x8, waiting for transfers between devices, from_behind(): return lax.ppermute(block, axis, route)  9.78 us
    optimization_barrier x2, local copies, waits for them, and re-layouts, pass_state(): sent, passengers = lax.optimization_barrier((sent, passengers))  5.88 us
    dot_general x1, matrix products, local(): jnp.einsum('hcts,cshp->cthp', weights, block_x, preferred_element_type=jn...  3.6 us
  transfers between devices with their start and end apart: 9, of which 5 were waited for; matrix products, arithmetic and copies ran while one was open for 13% of the time, Pallas kernels for 0%

profile of v11, /device:TPU:6, one launch (start us, length us, event | category | flops | bytes accessed | tf_op | source)
XLA Modules:
  0.0 155.4 jit_solution(17775358860460944842)
XLA Ops:
  6.5 0.8 slice.184
  7.3 0.7 convert_convert_fusion
  8.1 0.7 slice.183
  8.9 0.2 copy.83
  9.1 3.4 %collective-permute-start = (bf16[3,1024]{0,1:T(8,128)(2,1)S(1)}, bf16[3,1024]{0,1:T(8,128)(2,1)S(1)}, u32[]{:S(2)}, u32[]{:S(2)}) collective-permute-start(bf16[3,1024]{0,1:T(8,128)(2,1)S(1)} %copy.83), channel_id=1, source_target_pairs={{0,16},{16,32},{32,48},{48,64},{64,80},{80,96},{96,112},{112,128},... | collective-permute-start | bytes 18440 | tf_op jit(solution)/shard_map/ppermute | solution.py:12
  12.5 0.7 exponential_negate_fusion
  13.2 0.8 slice_convert_fusion.4
  14.0 0.9 convert_reduce_fusion.3
  14.9 0.8 compare_select_fusion
  15.8 1.2 reduce-window.9
  17.0 0.1 copy.85
  17.2 0.8 compare_and_fusion
  18.1 0.2 slice_reduce_fusion.1
  18.3 0.1 slice.189
  18.5 0.3 copy.89
  18.8 0.1 copy.88
  18.9 0.1 copy.92
  19.0 0.6 copy.101
  19.6 0.6 slice.187
  20.2 0.8 pad_maximum_fusion.9
  21.0 0.2 slice_reduce_fusion
  21.5 0.1 copy.105
  22.2 0.8 multiply_convert_fusion.7
  23.1 1.7 %multiply_convert_fusion.5 = bf16[512,640]{0,1:T(8,128)(2,1)S(1)} fusion(bf16[512,640]{0,1:T(8,128)(2,1)S(1)} %copy.89, bf16[3,640]{0,1:T(8,128)(2,1)S(1)} %slice.247, f32[640]{0:T(1024)S(1)} %get-tuple-element.19, f32[640]{0:T(1024)S(1)} %get-tuple-element.20, f32[640]{0:T(1024)S(1)} %get-tuple-element.18, f32[640]{0:T(1024)S(1)} %get-tuple-element.17, ...), kind=kLoop, calls=%fused_computation.28 | loop fusion | flops 9502720 | bytes 1326848 | tf_op jit(solution)/shard_map/convert_element_type | solution.py:27
  24.7 0.2 reshape.299
  24.9 0.8 fusion.12
  25.7 0.8 broadcast_add_fusion
  26.5 0.2 copy.96
  26.7 0.2 copy.95
  26.9 0.7 pad_maximum_fusion.3
  27.6 4.9 %collective-permute-start.1 = (bf16[656,128]{0,1:T(8,128)(2,1)}, bf16[656,128]{0,1:T(8,128)(2,1)S(1)}, u32[]{:S(2)}, u32[]{:S(2)}) collective-permute-start(bf16[656,128]{0,1:T(8,128)(2,1)} %pad_maximum_fusion.3), channel_id=1, source_target_pairs={{0,16},{16,32},{32,48},{48,64},{64,80},{80,96},{96,112},{112,128},... | collective-permute-start | bytes 503816 | tf_op jit(solution)/shard_map/ppermute | solution.py:12
  32.5 0.3 copy.97
  32.8 5.6 %copy.98 = bf16[640,2560]{0,1:T(8,128)(2,1)} copy(bf16[640,2560]{1,0:T(8,128)(2,1)} %param.23) | data formatting | bytes 6553600 | tf_op jit(solution)/shard_map/optimization_barrier | solution.py:57
  38.4 0.3 convert_multiply_fusion
  38.9 2.5 %collective-permute-start.2 = (bf16[656,128]{0,1:T(8,128)(2,1)S(1)}, bf16[656,128]{0,1:T(8,128)(2,1)S(1)}, u32[]{:S(2)}, u32[]{:S(2)}) collective-permute-start(bf16[656,128]{0,1:T(8,128)(2,1)S(1)} %pad_maximum_fusion.4), channel_id=1, source_target_pairs={{0,32},{16,48},{32,64},{48,80},{64,96},{80,112},{96,128},{112,144}... | collective-permute-start | bytes 503816 | tf_op jit(solution)/shard_map/ppermute | solution.py:12
  41.4 0.2 fusion.81
  41.7 6.3 %collective-permute-done.2 = bf16[656,128]{0,1:T(8,128)(2,1)S(1)} collective-permute-done((bf16[656,128]{0,1:T(8,128)(2,1)S(1)}, bf16[656,128]{0,1:T(8,128)(2,1)S(1)}, u32[]{:S(2)}, u32[]{:S(2)}) %collective-permute-start.2) | collective-permute-done | bytes 167968 | tf_op jit(solution)/shard_map/ppermute | solution.py:12
  48.3 0.7 pad_maximum_fusion.5
  49.0 4.2 %collective-permute-start.3 = (bf16[656,128]{0,1:T(8,128)(2,1)}, bf16[656,128]{0,1:T(8,128)(2,1)}, u32[]{:S(2)}, u32[]{:S(2)}) collective-permute-start(bf16[656,128]{0,1:T(8,128)(2,1)} %pad_maximum_fusion.5), channel_id=1, source_target_pairs={{0,64},{16,80},{32,96},{48,112},{64,128},{80,144},{96,160},{112,17... | collective-permute-start | bytes 503816 | tf_op jit(solution)/shard_map/ppermute | solution.py:12
  53.2 3.6 %fusion.8 = f32[2,256,10,64]{1,3,2,0:T(8,128)} fusion(f32[10,2,256]{2,0,1:T(8,128)} %copy.101, f32[10,2,256]{2,0,1:T(8,128)S(1)} %copy.99, f32[2,256,256]{2,1,0:T(8,128)S(1)} %fusion.81, pred[2,256,256]{2,1,0:T(8,128)(4,1)} %compare_and_fusion, bf16[2,256,10,64]{1,0,3,2:T(2,128)(2,1)S(1)} %reshape.299), kind=kOutput, calls=%fused_computation.17 | convolution fusion | flops 175636480 | bytes 2662400 | tf_op jit(solution)/shard_map/hcts,cshp->cthp/dot_general | solution.py:168
  56.9 0.8 fusion.72
  57.7 1.0 add_convert_fusion
  58.8 0.7 pad_maximum_fusion.6
  59.5 10.9 %collective-permute-start.6 = (bf16[656,128]{0,1:T(8,128)(2,1)}, bf16[656,128]{0,1:T(8,128)(2,1)S(1)}, u32[]{:S(2)}, u32[]{:S(2)}) collective-permute-start(bf16[656,128]{0,1:T(8,128)(2,1)} %pad_maximum_fusion.6), channel_id=1, source_target_pairs={{0,272},{16,288},{32,304},{48,320},{64,336},{80,352},{96,368},{112... | collective-permute-start | bytes 503816 | tf_op jit(solution)/shard_map/ppermute | solution.py:12
  70.4 1.3 collective-permute-start.5
  71.7 1.9 %collective-permute-start.4 = (bf16[656,128]{0,1:T(8,128)(2,1)}, bf16[656,128]{0,1:T(8,128)(2,1)S(1)}, u32[]{:S(2)}, u32[]{:S(2)}) collective-permute-start(bf16[656,128]{0,1:T(8,128)(2,1)} %pad_maximum_fusion.6), channel_id=1, source_target_pairs={{0,16},{16,32},{32,48},{48,64},{64,80},{80,96},{96,112},{112,128},... | collective-permute-start | bytes 503816 | tf_op jit(solution)/shard_map/ppermute | solution.py:12
  73.7 1.8 %fusion.10 = f32[2,256,10,64]{1,3,2,0:T(8,128)S(1)} fusion(f32[2,256,10,64]{1,3,2,0:T(8,128)S(1)} %copy-done.1, bf16[2,256,128,1]{2,1,3,0:T(8,128)(2,1)S(1)} %bitcast.93, f32[10]{0:T(128)S(1)} %copy-done.9, f32[2,256,10]{1,2,0:T(8,128)S(1)} %copy.103, f32[1,10,64,128]{3,2,1,0:T(8,128)} %get-tuple-element.36, bf16[2,256,10,64]{1,0,3,2:T(2,128)(2,1)S(1)} %reshape.299), kind=kOutput, calls=%fused_computation.19 | convolution fusion | flops 504954880 | bytes 3756072 | tf_op jit(solution)/shard_map/ctn,chpn->cthp/dot_general | solution.py:160
  75.5 1.5 collective-permute-start.7
  76.9 1.4 collective-permute-done.6
  78.4 1.1 collective-permute-done.4
  79.5 0.7 copy-done.7
  80.6 0.9 collective-permute-done.7
  81.5 1.2 add_add_fusion
  82.7 0.9 copy.104
  83.6 1.7 %fusion.11 = bf16[2,256,10,64]{1,3,2,0:T(8,128)(2,1)S(1)} fusion(f32[2,256,10,64]{1,3,2,0:T(8,128)S(1)} %fusion.10, bf16[2,256,128,1]{2,1,3,0:T(8,128)(2,1)S(1)} %bitcast.94, f32[10,64,128,1]{2,1,0,3:T(8,128)} %bitcast.95, f32[2,256,10]{1,2,0:T(8,128)S(1)} %copy.106), kind=kOutput, calls=%fused_computation.20 | convolution fusion | flops 504299520 | bytes 2445312 | tf_op jit(solution)/shard_map/ctn,hpn->cthp/dot_general | solution.py:182
  85.3 0.7 copy.107
  86.0 0.1 copy.113
  86.1 0.3 multiply_reduce_fusion
  86.4 1.5 copy-done
  87.9 2.3 %convert_bitcast_fusion = bf16[8,512,320]{1,2,0:T(8,128)(2,1)S(1)} fusion(bf16[8,320,640]{2,1,0:T(8,128)(2,1)S(1)} %bitcast.88, f32[512,640]{0,1:T(8,128)S(1)} %convert_multiply_fusion, bf16[512,640]{0,1:T(8,128)(2,1)S(1)} %bitcast.90, f32[640]{0:T(1024)S(1)} %copy-done.10), kind=kOutput, calls=%fused_computation.3 | convolution fusion | flops 1680343040 | bytes 7866880 | tf_op jit(solution)/shard_map/tc,gkc->gtk/dot_general | solution.py:192
  90.3 1.7 %pad_maximum_fusion = bf16[8,512,321]{1,2,0:T(8,128)(2,1)} fusion(bf16[8,512,1]{1,2,0:T(2,128)(2,1)S(1)} %broadcast_in_dim.178, bf16[8,512,320]{1,2,0:T(8,128)(2,1)S(1)} %convert_bitcast_fusion), kind=kLoop, calls=%fused_computation.1 | loop fusion | flops 5259264 | bytes 5259264 | tf_op jit(solution)/shard_map/concatenate | solution.py:201
  92.0 54.0 %reduce-scatter.2.cloned.1.call-done = bf16[1,512,321]{1,2,0:T(8,128)(2,1)} async-done(((bf16[8,512,321]{1,2,0:T(8,128)(2,1)}), bf16[1,512,321]{1,2,0:T(8,128)(2,1)}) %reduce-scatter.2.cloned.1.call-update) | async-done | bytes 328720 | tf_op jit(solution)/shard_map/reduce_scatter | solution.py:202
  146.1 0.7 fusion.53
  146.8 1.8 %multiply_convert_fusion.6 = bf16[512,320]{0,1:T(8,128)(2,1)} fusion(bf16[512,321]{0,1:T(8,128)(2,1)} %bitcast.101, f32[512]{0:T(512)S(1)} %bitcast.103), kind=kLoop, calls=%fused_computation.37 | loop fusion | flops 491520 | bytes 657408 | tf_op jit(solution)/shard_map/convert_element_type | solution.py:205
  (91 shorter events, 2.7 us)
Async XLA Ops:
  6.5 12.0 %copy-start.2 = (bf16[512,640]{1,0:T(8,128)(2,1)S(1)}, bf16[512,640]{1,0:T(8,128)(2,1)}, u32[]{:S(2)}) copy-start(bf16[512,640]{1,0:T(8,128)(2,1)} %param.12) | copy-start | bytes 1966084
  6.5 139.5 %reduce-scatter.2.cloned.1.call-start = ((), (), s32[]{:S(2)}) async-start(), calls=%async_computation.1 | async-start | bytes 3022848 | tf_op jit(solution)/shard_map/reduce_scatter | solution.py:202
  8.8 12.5 %copy-start.8 = (s32[512]{0:T(512)S(1)}, s32[512]{0:T(512)}, u32[]{:S(2)}) copy-start(s32[512]{0:T(512)} %param.16) | copy-start | bytes 6148
  9.1 10.5 %collective-permute-start = (bf16[3,1024]{0,1:T(8,128)(2,1)S(1)}, bf16[3,1024]{0,1:T(8,128)(2,1)S(1)}, u32[]{:S(2)}, u32[]{:S(2)}) collective-permute-start(bf16[3,1024]{0,1:T(8,128)(2,1)S(1)} %copy.83), channel_id=1, source_target_pairs={{0,16},{16,32},{32,48},{48,64},{64,80},{80,96},{96,112},{112,128},... | collective-permute-start | bytes 18440 | tf_op jit(solution)/shard_map/ppermute | solution.py:12
  15.7 6.5 %copy-start.4 = (bf16[512,256]{1,0:T(8,128)(2,1)S(1)}, bf16[512,256]{1,0:T(8,128)(2,1)}, u32[]{:S(2)}) copy-start(bf16[512,256]{1,0:T(8,128)(2,1)} %param.13) | copy-start | bytes 786436
  26.5 6.0 %copy-start.3 = (bf16[512,640]{1,0:T(8,128)(2,1)S(1)}, bf16[512,640]{1,0:T(8,128)(2,1)}, u32[]{:S(2)}) copy-start(bf16[512,640]{1,0:T(8,128)(2,1)} %param.14) | copy-start | bytes 1966084
  27.6 11.2 %collective-permute-start.1 = (bf16[656,128]{0,1:T(8,128)(2,1)}, bf16[656,128]{0,1:T(8,128)(2,1)S(1)}, u32[]{:S(2)}, u32[]{:S(2)}) collective-permute-start(bf16[656,128]{0,1:T(8,128)(2,1)} %pad_maximum_fusion.3), channel_id=1, source_target_pairs={{0,16},{16,32},{32,48},{48,64},{64,80},{80,96},{96,112},{112,128},... | collective-permute-start | bytes 503816 | tf_op jit(solution)/shard_map/ppermute | solution.py:12
  38.9 9.1 %collective-permute-start.2 = (bf16[656,128]{0,1:T(8,128)(2,1)S(1)}, bf16[656,128]{0,1:T(8,128)(2,1)S(1)}, u32[]{:S(2)}, u32[]{:S(2)}) collective-permute-start(bf16[656,128]{0,1:T(8,128)(2,1)S(1)} %pad_maximum_fusion.4), channel_id=1, source_target_pairs={{0,32},{16,48},{32,64},{48,80},{64,96},{80,112},{96,128},{112,144}... | collective-permute-start | bytes 503816 | tf_op jit(solution)/shard_map/ppermute | solution.py:12
  49.0 8.0 %collective-permute-start.3 = (bf16[656,128]{0,1:T(8,128)(2,1)}, bf16[656,128]{0,1:T(8,128)(2,1)}, u32[]{:S(2)}, u32[]{:S(2)}) collective-permute-start(bf16[656,128]{0,1:T(8,128)(2,1)} %pad_maximum_fusion.5), channel_id=1, source_target_pairs={{0,64},{16,80},{32,96},{48,112},{64,128},{80,144},{96,160},{112,17... | collective-permute-start | bytes 503816 | tf_op jit(solution)/shard_map/ppermute | solution.py:12
  56.8 16.9 %copy-start.9 = (f32[10]{0:T(128)S(1)}, f32[10]{0:T(128)}, u32[]{:S(2)}) copy-start(f32[10]{0:T(128)} %param.21) | copy-start | bytes 124
  56.9 16.7 %copy-start.1 = (f32[2,256,10,64]{1,3,2,0:T(8,128)S(1)}, f32[2,256,10,64]{1,3,2,0:T(8,128)}, u32[]{:S(2)}) copy-start(f32[2,256,10,64]{1,3,2,0:T(8,128)} %fusion.8) | copy-start | bytes 3932164
  59.5 18.9 %collective-permute-start.6 = (bf16[656,128]{0,1:T(8,128)(2,1)}, bf16[656,128]{0,1:T(8,128)(2,1)S(1)}, u32[]{:S(2)}, u32[]{:S(2)}) collective-permute-start(bf16[656,128]{0,1:T(8,128)(2,1)} %pad_maximum_fusion.6), channel_id=1, source_target_pairs={{0,272},{16,288},{32,304},{48,320},{64,336},{80,352},{96,368},{112... | collective-permute-start | bytes 503816 | tf_op jit(solution)/shard_map/ppermute | solution.py:12
  70.4 8.0 %collective-permute-start.5 = (bf16[656,128]{0,1:T(8,128)(2,1)}, bf16[656,128]{0,1:T(8,128)(2,1)S(1)}, u32[]{:S(2)}, u32[]{:S(2)}) collective-permute-start(bf16[656,128]{0,1:T(8,128)(2,1)} %pad_maximum_fusion.6), channel_id=1, source_target_pairs={{0,144},{16,160},{32,176},{48,192},{64,208},{80,224},{96,240},{112... | collective-permute-start | bytes 503816 | tf_op jit(solution)/shard_map/ppermute | solution.py:12
  71.7 7.8 %collective-permute-start.4 = (bf16[656,128]{0,1:T(8,128)(2,1)}, bf16[656,128]{0,1:T(8,128)(2,1)S(1)}, u32[]{:S(2)}, u32[]{:S(2)}) collective-permute-start(bf16[656,128]{0,1:T(8,128)(2,1)} %pad_maximum_fusion.6), channel_id=1, source_target_pairs={{0,16},{16,32},{32,48},{48,64},{64,80},{80,96},{96,112},{112,128},... | collective-permute-start | bytes 503816 | tf_op jit(solution)/shard_map/ppermute | solution.py:12
  75.5 6.1 %collective-permute-start.7 = (bf16[656,128]{0,1:T(8,128)(2,1)}, bf16[656,128]{0,1:T(8,128)(2,1)S(1)}, u32[]{:S(2)}, u32[]{:S(2)}) collective-permute-start(bf16[656,128]{0,1:T(8,128)(2,1)} %pad_maximum_fusion.6), channel_id=1, source_target_pairs={{0,400},{16,416},{32,432},{48,448},{64,464},{80,480},{96,496},{1,4... | collective-permute-start | bytes 503816 | tf_op jit(solution)/shard_map/ppermute | solution.py:12
  78.4 1.1 copy-start.5
  78.4 1.1 copy-start.6
  79.5 0.7 copy-start.7
  86.0 1.9 %copy-start = (bf16[640,2560]{0,1:T(8,128)(2,1)S(1)}, bf16[640,2560]{0,1:T(8,128)(2,1)}, u32[]{:S(2)}) copy-start(bf16[640,2560]{0,1:T(8,128)(2,1)} %copy.98) | copy-start | bytes 9830404
  86.1 1.8 %copy-start.10 = (f32[640]{0:T(1024)S(1)}, f32[640]{0:T(1024)}, u32[]{:S(2)}) copy-start(f32[640]{0:T(1024)} %param.22) | copy-start | bytes 7684
Sparse Core Ops, SparseCore 0:
  92.2 53.8 reduce-scatter.1

commit v12 on v11

--- a/solution.py
+++ b/solution.py
@@ -183,7 +183,7 @@
     result = (
         result + reach_term * jnp.transpose(entry_gain * prefix[:, :, None], (1, 2, 0))[..., None]
     )
-    y_vals = lax.optimization_barrier(result.reshape(row_count, inner_width).astype(jnp.bfloat16))
+    y_vals = result.reshape(row_count, inner_width).astype(jnp.bfloat16)
     gated = y_vals.astype(jnp.float32) * gate_silu
     group_count = lax.axis_size("tensor")
     squares = jnp.sum(gated * gated, axis=1)

time: 156 us -> 155 us (level)
  no operation moved by 1% of the time
where the time goes in v12:
time: 155 us; the launch traced here: 154 us
  waiting for transfers between devices  63.9 us (41%)
  starting transfers between devices  30.6 us (20%)
  other arithmetic  20.9 us (13%)
  local copies, waits for them, and re-layouts  15.4 us (10%)
  between operations  13.8 us (9%)
  matrix products  9.49 us (6%)
    reduce_scatter x1, waiting for transfers between devices, local(): lax.psum_scatter(payload, 'tensor', scatter_dimension=0, tiled=True)[0]  54.1 us
    ppermute x8, starting transfers between devices, from_behind(): return lax.ppermute(block, axis, route)  30.6 us
    ppermute x8, waiting for transfers between devices, from_behind(): return lax.ppermute(block, axis, route)  9.77 us
    optimization_barrier x2, local copies, waits for them, and re-layouts, pass_state(): sent, passengers = lax.optimization_barrier((sent, passengers))  5.88 us
    dot_general x1, matrix products, local(): jnp.einsum('hcts,cshp->cthp', weights, block_x, preferred_element_type=jn...  3.6 us
  transfers between devices with their start and end apart: 9, of which 5 were waited for; matrix products, arithmetic and copies ran while one was open for 13% of the time, Pallas kernels for 0%

profile of v12, /device:TPU:6, one launch (start us, length us, event | category | flops | bytes accessed | tf_op | source)
XLA Modules:
  0.0 154.1 jit_solution(17693693053150564788)
XLA Ops:
  6.5 0.8 slice.184
  7.3 0.7 fusion.83
  8.1 0.7 slice.183
  8.9 0.2 copy.83
  9.1 3.4 %collective-permute-start = (bf16[3,1024]{0,1:T(8,128)(2,1)S(1)}, bf16[3,1024]{0,1:T(8,128)(2,1)S(1)}, u32[]{:S(2)}, u32[]{:S(2)}) collective-permute-start(bf16[3,1024]{0,1:T(8,128)(2,1)S(1)} %copy.83), channel_id=1, source_target_pairs={{0,16},{16,32},{32,48},{48,64},{64,80},{80,96},{96,112},{112,128},... | collective-permute-start | bytes 18440 | tf_op jit(solution)/shard_map/ppermute | solution.py:12
  12.5 0.7 exponential_negate_fusion
  13.2 0.8 slice_convert_fusion.4
  14.0 0.9 convert_reduce_fusion.3
  14.9 0.8 broadcast_multiply_fusion
  15.8 1.2 reduce-window.9
  17.0 0.1 copy.85
  17.2 0.8 compare_and_fusion
  18.1 0.2 slice_reduce_fusion.1
  18.3 0.1 slice.189
  18.5 0.3 copy.89
  18.8 0.6 copy.101
  19.4 0.1 copy.88
  19.5 0.1 copy.92
  19.6 0.6 slice.187
  20.2 0.8 pad_maximum_fusion.9
  21.0 0.2 slice_reduce_fusion
  21.5 0.1 copy.105
  22.3 0.8 multiply_convert_fusion.7
  23.1 1.7 %multiply_convert_fusion.5 = bf16[512,640]{0,1:T(8,128)(2,1)S(1)} fusion(bf16[512,640]{0,1:T(8,128)(2,1)S(1)} %copy.89, bf16[3,640]{0,1:T(8,128)(2,1)S(1)} %slice.247, f32[640]{0:T(1024)S(1)} %get-tuple-element.19, f32[640]{0:T(1024)S(1)} %get-tuple-element.20, f32[640]{0:T(1024)S(1)} %get-tuple-element.18, f32[640]{0:T(1024)S(1)} %get-tuple-element.17, ...), kind=kLoop, calls=%fused_computation.28 | loop fusion | flops 9502720 | bytes 1326848 | tf_op jit(solution)/shard_map/convert_element_type | solution.py:27
  24.7 0.2 reshape.301
  24.9 0.8 fusion.13
  25.7 0.8 fusion.81
  26.5 0.2 copy.95
  26.7 0.2 copy.96
  26.9 0.7 pad_maximum_fusion.3
  27.6 4.9 %collective-permute-start.1 = (bf16[656,128]{0,1:T(8,128)(2,1)}, bf16[656,128]{0,1:T(8,128)(2,1)S(1)}, u32[]{:S(2)}, u32[]{:S(2)}) collective-permute-start(bf16[656,128]{0,1:T(8,128)(2,1)} %pad_maximum_fusion.3), channel_id=1, source_target_pairs={{0,16},{16,32},{32,48},{48,64},{64,80},{80,96},{96,112},{112,128},... | collective-permute-start | bytes 503816 | tf_op jit(solution)/shard_map/ppermute | solution.py:12
  32.5 0.3 copy.97
  32.8 5.6 %copy.98 = bf16[640,2560]{0,1:T(8,128)(2,1)} copy(bf16[640,2560]{1,0:T(8,128)(2,1)} %param.23) | data formatting | bytes 6553600 | tf_op jit(solution)/shard_map/optimization_barrier | solution.py:57
  38.4 0.3 convert_multiply_fusion
  38.9 2.5 %collective-permute-start.2 = (bf16[656,128]{0,1:T(8,128)(2,1)S(1)}, bf16[656,128]{0,1:T(8,128)(2,1)S(1)}, u32[]{:S(2)}, u32[]{:S(2)}) collective-permute-start(bf16[656,128]{0,1:T(8,128)(2,1)S(1)} %pad_maximum_fusion.4), channel_id=1, source_target_pairs={{0,32},{16,48},{32,64},{48,80},{64,96},{80,112},{96,128},{112,144}... | collective-permute-start | bytes 503816 | tf_op jit(solution)/shard_map/ppermute | solution.py:12
  41.5 0.2 fusion.85
  41.7 6.3 %collective-permute-done.2 = bf16[656,128]{0,1:T(8,128)(2,1)S(1)} collective-permute-done((bf16[656,128]{0,1:T(8,128)(2,1)S(1)}, bf16[656,128]{0,1:T(8,128)(2,1)S(1)}, u32[]{:S(2)}, u32[]{:S(2)}) %collective-permute-start.2) | collective-permute-done | bytes 167968 | tf_op jit(solution)/shard_map/ppermute | solution.py:12
  48.3 0.7 pad_maximum_fusion.5
  49.0 4.2 %collective-permute-start.3 = (bf16[656,128]{0,1:T(8,128)(2,1)}, bf16[656,128]{0,1:T(8,128)(2,1)}, u32[]{:S(2)}, u32[]{:S(2)}) collective-permute-start(bf16[656,128]{0,1:T(8,128)(2,1)} %pad_maximum_fusion.5), channel_id=1, source_target_pairs={{0,64},{16,80},{32,96},{48,112},{64,128},{80,144},{96,160},{112,17... | collective-permute-start | bytes 503816 | tf_op jit(solution)/shard_map/ppermute | solution.py:12
  53.2 3.6 %fusion.8 = f32[2,256,10,64]{1,3,2,0:T(8,128)} fusion(f32[10,2,256]{2,0,1:T(8,128)} %copy.101, f32[10,2,256]{2,0,1:T(8,128)S(1)} %copy.99, f32[2,256,256]{2,1,0:T(8,128)S(1)} %fusion.85, pred[2,256,256]{2,1,0:T(8,128)(4,1)} %compare_and_fusion, bf16[2,256,10,64]{1,0,3,2:T(2,128)(2,1)S(1)} %reshape.301), kind=kOutput, calls=%fused_computation.17 | convolution fusion | flops 175636480 | bytes 2662400 | tf_op jit(solution)/shard_map/hcts,cshp->cthp/dot_general | solution.py:168
  56.9 0.8 fusion.74
  57.7 1.0 add_convert_fusion
  58.8 0.7 pad_maximum_fusion.6
  59.5 10.9 %collective-permute-start.6 = (bf16[656,128]{0,1:T(8,128)(2,1)}, bf16[656,128]{0,1:T(8,128)(2,1)S(1)}, u32[]{:S(2)}, u32[]{:S(2)}) collective-permute-start(bf16[656,128]{0,1:T(8,128)(2,1)} %pad_maximum_fusion.6), channel_id=1, source_target_pairs={{0,272},{16,288},{32,304},{48,320},{64,336},{80,352},{96,368},{112... | collective-permute-start | bytes 503816 | tf_op jit(solution)/shard_map/ppermute | solution.py:12
  70.4 1.3 collective-permute-start.5
  71.7 1.9 %collective-permute-start.4 = (bf16[656,128]{0,1:T(8,128)(2,1)}, bf16[656,128]{0,1:T(8,128)(2,1)S(1)}, u32[]{:S(2)}, u32[]{:S(2)}) collective-permute-start(bf16[656,128]{0,1:T(8,128)(2,1)} %pad_maximum_fusion.6), channel_id=1, source_target_pairs={{0,16},{16,32},{32,48},{48,64},{64,80},{80,96},{96,112},{112,128},... | collective-permute-start | bytes 503816 | tf_op jit(solution)/shard_map/ppermute | solution.py:12
  73.7 1.8 %fusion.10 = f32[2,256,10,64]{1,3,2,0:T(8,128)S(1)} fusion(f32[2,256,10,64]{1,3,2,0:T(8,128)S(1)} %copy-done.1, bf16[2,256,128,1]{2,1,3,0:T(8,128)(2,1)S(1)} %bitcast.93, f32[10]{0:T(128)S(1)} %copy-done.9, f32[2,256,10]{1,2,0:T(8,128)S(1)} %copy.103, f32[1,10,64,128]{3,2,1,0:T(8,128)} %get-tuple-element.37, bf16[2,256,10,64]{1,0,3,2:T(2,128)(2,1)S(1)} %reshape.301), kind=kOutput, calls=%fused_computation.19 | convolution fusion | flops 504954880 | bytes 3756072 | tf_op jit(solution)/shard_map/ctn,chpn->cthp/dot_general | solution.py:160
  75.5 1.5 collective-permute-start.7
  76.9 1.4 collective-permute-done.6
  78.4 1.1 collective-permute-done.4
  79.5 0.7 copy-done.7
  80.6 0.9 collective-permute-done.7
  81.5 1.2 add_add_fusion
  82.7 0.2 copy.104
  82.9 0.7 fusion.12
  83.6 1.0 copy.107
  84.7 0.1 copy.113
  84.8 0.4 multiply_reduce_fusion
  85.2 1.4 copy-done
  86.6 2.4 %convert_bitcast_fusion = bf16[8,512,320]{1,2,0:T(8,128)(2,1)S(1)} fusion(bf16[8,320,640]{2,1,0:T(8,128)(2,1)S(1)} %bitcast.91, f32[640]{0:T(1024)S(1)} %copy-done.10, f32[512,640]{0,1:T(8,128)S(1)} %bitcast.89, f32[512,640]{0,1:T(8,128)S(1)} %convert_multiply_fusion), kind=kOutput, calls=%fused_computation.3 | convolution fusion | flops 1680015360 | bytes 8522240 | tf_op jit(solution)/shard_map/tc,gkc->gtk/dot_general | solution.py:192
  89.0 1.7 %pad_maximum_fusion = bf16[8,512,321]{1,2,0:T(8,128)(2,1)} fusion(bf16[8,512,1]{1,2,0:T(2,128)(2,1)S(1)} %broadcast_in_dim.178, bf16[8,512,320]{1,2,0:T(8,128)(2,1)S(1)} %convert_bitcast_fusion), kind=kLoop, calls=%fused_computation.1 | loop fusion | flops 5259264 | bytes 5259264 | tf_op jit(solution)/shard_map/concatenate | solution.py:201
  90.7 54.1 %reduce-scatter.2.cloned.1.call-done = bf16[1,512,321]{1,2,0:T(8,128)(2,1)} async-done(((bf16[8,512,321]{1,2,0:T(8,128)(2,1)}), bf16[1,512,321]{1,2,0:T(8,128)(2,1)}) %reduce-scatter.2.cloned.1.call-update) | async-done | bytes 328720 | tf_op jit(solution)/shard_map/reduce_scatter | solution.py:202
  144.8 0.7 fusion.55
  145.5 1.8 %multiply_convert_fusion.6 = bf16[512,320]{0,1:T(8,128)(2,1)} fusion(bf16[512,321]{0,1:T(8,128)(2,1)} %bitcast.101, f32[512]{0:T(512)S(1)} %bitcast.103), kind=kLoop, calls=%fused_computation.37 | loop fusion | flops 491520 | bytes 657408 | tf_op jit(solution)/shard_map/convert_element_type | solution.py:205
  (91 shorter events, 2.7 us)
Async XLA Ops:
  6.5 12.0 %copy-start.2 = (bf16[512,640]{1,0:T(8,128)(2,1)S(1)}, bf16[512,640]{1,0:T(8,128)(2,1)}, u32[]{:S(2)}) copy-start(bf16[512,640]{1,0:T(8,128)(2,1)} %param.12) | copy-start | bytes 1966084
  6.5 138.2 %reduce-scatter.2.cloned.1.call-start = ((), (), s32[]{:S(2)}) async-start(), calls=%async_computation.1 | async-start | bytes 3022848 | tf_op jit(solution)/shard_map/reduce_scatter | solution.py:202
  8.8 12.6 %copy-start.8 = (s32[512]{0:T(512)S(1)}, s32[512]{0:T(512)}, u32[]{:S(2)}) copy-start(s32[512]{0:T(512)} %param.16) | copy-start | bytes 6148
  9.1 10.5 %collective-permute-start = (bf16[3,1024]{0,1:T(8,128)(2,1)S(1)}, bf16[3,1024]{0,1:T(8,128)(2,1)S(1)}, u32[]{:S(2)}, u32[]{:S(2)}) collective-permute-start(bf16[3,1024]{0,1:T(8,128)(2,1)S(1)} %copy.83), channel_id=1, source_target_pairs={{0,16},{16,32},{32,48},{48,64},{64,80},{80,96},{96,112},{112,128},... | collective-permute-start | bytes 18440 | tf_op jit(solution)/shard_map/ppermute | solution.py:12
  15.8 6.5 %copy-start.4 = (bf16[512,256]{1,0:T(8,128)(2,1)S(1)}, bf16[512,256]{1,0:T(8,128)(2,1)}, u32[]{:S(2)}) copy-start(bf16[512,256]{1,0:T(8,128)(2,1)} %param.13) | copy-start | bytes 786436
  26.5 6.0 %copy-start.3 = (bf16[512,640]{1,0:T(8,128)(2,1)S(1)}, bf16[512,640]{1,0:T(8,128)(2,1)}, u32[]{:S(2)}) copy-start(bf16[512,640]{1,0:T(8,128)(2,1)} %param.14) | copy-start | bytes 1966084
  27.6 11.1 %collective-permute-start.1 = (bf16[656,128]{0,1:T(8,128)(2,1)}, bf16[656,128]{0,1:T(8,128)(2,1)S(1)}, u32[]{:S(2)}, u32[]{:S(2)}) collective-permute-start(bf16[656,128]{0,1:T(8,128)(2,1)} %pad_maximum_fusion.3), channel_id=1, source_target_pairs={{0,16},{16,32},{32,48},{48,64},{64,80},{80,96},{96,112},{112,128},... | collective-permute-start | bytes 503816 | tf_op jit(solution)/shard_map/ppermute | solution.py:12
  38.9 9.1 %collective-permute-start.2 = (bf16[656,128]{0,1:T(8,128)(2,1)S(1)}, bf16[656,128]{0,1:T(8,128)(2,1)S(1)}, u32[]{:S(2)}, u32[]{:S(2)}) collective-permute-start(bf16[656,128]{0,1:T(8,128)(2,1)S(1)} %pad_maximum_fusion.4), channel_id=1, source_target_pairs={{0,32},{16,48},{32,64},{48,80},{64,96},{80,112},{96,128},{112,144}... | collective-permute-start | bytes 503816 | tf_op jit(solution)/shard_map/ppermute | solution.py:12
  49.0 8.0 %collective-permute-start.3 = (bf16[656,128]{0,1:T(8,128)(2,1)}, bf16[656,128]{0,1:T(8,128)(2,1)}, u32[]{:S(2)}, u32[]{:S(2)}) collective-permute-start(bf16[656,128]{0,1:T(8,128)(2,1)} %pad_maximum_fusion.5), channel_id=1, source_target_pairs={{0,64},{16,80},{32,96},{48,112},{64,128},{80,144},{96,160},{112,17... | collective-permute-start | bytes 503816 | tf_op jit(solution)/shard_map/ppermute | solution.py:12
  56.8 16.9 %copy-start.9 = (f32[10]{0:T(128)S(1)}, f32[10]{0:T(128)}, u32[]{:S(2)}) copy-start(f32[10]{0:T(128)} %param.21) | copy-start | bytes 124
  56.9 16.7 %copy-start.1 = (f32[2,256,10,64]{1,3,2,0:T(8,128)S(1)}, f32[2,256,10,64]{1,3,2,0:T(8,128)}, u32[]{:S(2)}) copy-start(f32[2,256,10,64]{1,3,2,0:T(8,128)} %fusion.8) | copy-start | bytes 3932164
  59.5 18.9 %collective-permute-start.6 = (bf16[656,128]{0,1:T(8,128)(2,1)}, bf16[656,128]{0,1:T(8,128)(2,1)S(1)}, u32[]{:S(2)}, u32[]{:S(2)}) collective-permute-start(bf16[656,128]{0,1:T(8,128)(2,1)} %pad_maximum_fusion.6), channel_id=1, source_target_pairs={{0,272},{16,288},{32,304},{48,320},{64,336},{80,352},{96,368},{112... | collective-permute-start | bytes 503816 | tf_op jit(solution)/shard_map/ppermute | solution.py:12
  70.4 8.0 %collective-permute-start.5 = (bf16[656,128]{0,1:T(8,128)(2,1)}, bf16[656,128]{0,1:T(8,128)(2,1)S(1)}, u32[]{:S(2)}, u32[]{:S(2)}) collective-permute-start(bf16[656,128]{0,1:T(8,128)(2,1)} %pad_maximum_fusion.6), channel_id=1, source_target_pairs={{0,144},{16,160},{32,176},{48,192},{64,208},{80,224},{96,240},{112... | collective-permute-start | bytes 503816 | tf_op jit(solution)/shard_map/ppermute | solution.py:12
  71.7 7.8 %collective-permute-start.4 = (bf16[656,128]{0,1:T(8,128)(2,1)}, bf16[656,128]{0,1:T(8,128)(2,1)S(1)}, u32[]{:S(2)}, u32[]{:S(2)}) collective-permute-start(bf16[656,128]{0,1:T(8,128)(2,1)} %pad_maximum_fusion.6), channel_id=1, source_target_pairs={{0,16},{16,32},{32,48},{48,64},{64,80},{80,96},{96,112},{112,128},... | collective-permute-start | bytes 503816 | tf_op jit(solution)/shard_map/ppermute | solution.py:12
  75.5 6.1 %collective-permute-start.7 = (bf16[656,128]{0,1:T(8,128)(2,1)}, bf16[656,128]{0,1:T(8,128)(2,1)S(1)}, u32[]{:S(2)}, u32[]{:S(2)}) collective-permute-start(bf16[656,128]{0,1:T(8,128)(2,1)} %pad_maximum_fusion.6), channel_id=1, source_target_pairs={{0,400},{16,416},{32,432},{48,448},{64,464},{80,480},{96,496},{1,4... | collective-permute-start | bytes 503816 | tf_op jit(solution)/shard_map/ppermute | solution.py:12
  78.4 1.1 copy-start.5
  78.4 1.1 copy-start.6
  79.5 0.7 copy-start.7
  84.6 1.9 %copy-start = (bf16[640,2560]{0,1:T(8,128)(2,1)S(1)}, bf16[640,2560]{0,1:T(8,128)(2,1)}, u32[]{:S(2)}) copy-start(bf16[640,2560]{0,1:T(8,128)(2,1)} %copy.98) | copy-start | bytes 9830404
  84.8 1.8 %copy-start.10 = (f32[640]{0:T(1024)S(1)}, f32[640]{0:T(1024)}, u32[]{:S(2)}) copy-start(f32[640]{0:T(1024)} %param.22) | copy-start | bytes 7684
Sparse Core Ops, SparseCore 0:
  90.8 53.8 reduce-scatter.1

commit v13 on v12

--- a/solution.py
+++ b/solution.py
@@ -53,11 +53,13 @@
     window = 1
     while 4 * window < shard_count - 1:
         sent = with_decay(decay, state)
-        if window == 1:
+        if window in prepare:
             sent, passengers = lax.optimization_barrier((sent, passengers))
         received = from_behind(sent, "seq", window)
-        if window == 1:
-            received, passengers = lax.optimization_barrier((received, prepare(passengers)))
+        if window in prepare:
+            received, passengers = lax.optimization_barrier(
+                (received, prepare[window](passengers))
+            )
         prev_decay, prev_state = split_decay(received, *state.shape[:2])
         state = decay[:, None, None] * prev_state + state
         decay = decay * prev_decay
@@ -173,7 +175,10 @@
         device_decay,
         local_final,
         (z_gate, w_out),
-        lambda pair: (jax.nn.silu(pair[0].astype(jnp.float32)), jnp.transpose(pair[1])),
+        {
+            1: lambda pair: (jax.nn.silu(pair[0].astype(jnp.float32)), pair[1]),
+            2: lambda pair: (pair[0], jnp.transpose(pair[1])),
+        },
     )
     prefix = jnp.cumprod(
         jnp.concatenate([jnp.ones((head_count, 1), jnp.float32), block_decay[:, :-1]], axis=1),

time: 155 us -> 157 us (1.013)
  starting transfers between devices: 30.6 us -> 35.8 us
  waiting for transfers between devices: 63.9 us -> 59.1 us
    ppermute x8, starting transfers between devices: 30.6 us -> 35.8 us  [from_behind(): return lax.ppermute(block, axis, route)]
    ppermute x8, waiting for transfers between devices: 9.77 us -> 5.48 us  [from_behind(): return lax.ppermute(block, axis, route)]
  transfers between devices with their start and end apart: 9 -> 9, of which waited for: 5 -> 3; matrix products, arithmetic and copies ran while one was open for 13% -> 13% of each run, Pallas kernels for 0% -> 0%
where the time goes in v13:
time: 157 us; the launch traced here: 156 us
  waiting for transfers between devices  59.1 us (38%)
  starting transfers between devices  35.8 us (23%)
  other arithmetic  21.5 us (14%)
  local copies, waits for them, and re-layouts  15.9 us (10%)
  between operations  13.9 us (9%)
  matrix products  9.49 us (6%)
    reduce_scatter x1, waiting for transfers between devices, local(): lax.psum_scatter(payload, 'tensor', scatter_dimension=0, tiled=True)[0]  53.6 us
    ppermute x8, starting transfers between devices, from_behind(): return lax.ppermute(block, axis, route)  35.8 us
    optimization_barrier x2, local copies, waits for them, and re-layouts, pass_state(): sent, passengers = lax.optimization_barrier((sent, passengers))  5.9 us
    ppermute x8, waiting for transfers between devices, from_behind(): return lax.ppermute(block, axis, route)  5.48 us
    dot_general x1, matrix products, local(): jnp.einsum('hcts,cshp->cthp', weights, block_x, preferred_element_type=jn...  3.6 us
  transfers between devices with their start and end apart: 9, of which 3 were waited for; matrix products, arithmetic and copies ran while one was open for 13% of the time, Pallas kernels for 0%

profile of v13, /device:TPU:6, one launch (start us, length us, event | category | flops | bytes accessed | tf_op | source)
XLA Modules:
  0.0 155.6 jit_solution(16898643213677909832)
XLA Ops:
  6.5 0.8 slice.184
  7.3 0.7 fusion.82
  8.1 0.7 slice.183
  8.9 0.2 copy.83
  9.1 3.4 %collective-permute-start = (bf16[3,1024]{0,1:T(8,128)(2,1)S(1)}, bf16[3,1024]{0,1:T(8,128)(2,1)S(1)}, u32[]{:S(2)}, u32[]{:S(2)}) collective-permute-start(bf16[3,1024]{0,1:T(8,128)(2,1)S(1)} %copy.83), channel_id=1, source_target_pairs={{0,16},{16,32},{32,48},{48,64},{64,80},{80,96},{96,112},{112,128},... | collective-permute-start | bytes 18440 | tf_op jit(solution)/shard_map/ppermute | solution.py:12
  12.5 0.7 exponential_negate_fusion
  13.2 0.8 slice_convert_fusion.4
  14.0 0.9 convert_reduce_fusion.3
  14.9 0.8 broadcast_multiply_fusion
  15.8 1.2 reduce-window.9
  17.0 0.1 copy.85
  17.2 0.8 compare_and_fusion
  18.1 0.2 slice_reduce_fusion.1
  18.3 0.1 slice.189
  18.5 0.3 copy.89
  18.8 0.6 copy.101
  19.4 0.1 copy.88
  19.5 0.1 copy.92
  19.6 0.6 slice.187
  20.2 0.8 pad_maximum_fusion.9
  21.0 0.2 slice_reduce_fusion
  21.5 0.1 copy.105
  22.2 0.8 multiply_convert_fusion.7
  23.1 1.7 %multiply_convert_fusion.5 = bf16[512,640]{0,1:T(8,128)(2,1)S(1)} fusion(bf16[512,640]{0,1:T(8,128)(2,1)S(1)} %copy.89, bf16[3,640]{0,1:T(8,128)(2,1)S(1)} %slice.247, f32[640]{0:T(1024)S(1)} %get-tuple-element.31, f32[640]{0:T(1024)S(1)} %get-tuple-element.32, f32[640]{0:T(1024)S(1)} %get-tuple-element.30, f32[640]{0:T(1024)S(1)} %get-tuple-element.29, ...), kind=kLoop, calls=%fused_computation.28 | loop fusion | flops 9502720 | bytes 1326848 | tf_op jit(solution)/shard_map/convert_element_type | solution.py:27
  24.7 0.2 reshape.301
  24.9 0.8 fusion.13
  25.7 0.8 fusion.80
  26.5 0.2 copy.95
  26.7 0.2 copy.96
  26.9 0.7 pad_maximum_fusion.3
  27.6 4.9 %collective-permute-start.1 = (bf16[656,128]{0,1:T(8,128)(2,1)}, bf16[656,128]{0,1:T(8,128)(2,1)S(1)}, u32[]{:S(2)}, u32[]{:S(2)}) collective-permute-start(bf16[656,128]{0,1:T(8,128)(2,1)} %pad_maximum_fusion.3), channel_id=1, source_target_pairs={{0,16},{16,32},{32,48},{48,64},{64,80},{80,96},{96,112},{112,128},... | collective-permute-start | bytes 503816 | tf_op jit(solution)/shard_map/ppermute | solution.py:12
  32.5 0.3 copy.97
  32.8 0.3 convert_multiply_fusion
  33.1 3.0 %collective-permute-done.1 = bf16[656,128]{0,1:T(8,128)(2,1)S(1)} collective-permute-done((bf16[656,128]{0,1:T(8,128)(2,1)}, bf16[656,128]{0,1:T(8,128)(2,1)S(1)}, u32[]{:S(2)}, u32[]{:S(2)}) %collective-permute-start.1) | collective-permute-done | bytes 167968 | tf_op jit(solution)/shard_map/ppermute | solution.py:12
  36.2 0.4 copy-done.10
  36.6 0.7 pad_maximum_fusion.4
  37.3 4.3 %collective-permute-start.2 = (bf16[656,128]{0,1:T(8,128)(2,1)}, bf16[656,128]{0,1:T(8,128)(2,1)S(1)}, u32[]{:S(2)}, u32[]{:S(2)}) collective-permute-start(bf16[656,128]{0,1:T(8,128)(2,1)} %pad_maximum_fusion.4), channel_id=1, source_target_pairs={{0,32},{16,48},{32,64},{48,80},{64,96},{80,112},{96,128},{112,144}... | collective-permute-start | bytes 503816 | tf_op jit(solution)/shard_map/ppermute | solution.py:12
  41.6 0.2 fusion.84
  41.9 5.6 %copy.98 = bf16[640,2560]{0,1:T(8,128)(2,1)} copy(bf16[640,2560]{1,0:T(8,128)(2,1)} %param.23) | data formatting | bytes 6553600 | tf_op jit(solution)/shard_map/optimization_barrier | solution.py:57
  47.8 0.7 pad_maximum_fusion.5
  48.5 4.2 %collective-permute-start.3 = (bf16[656,128]{0,1:T(8,128)(2,1)}, bf16[656,128]{0,1:T(8,128)(2,1)}, u32[]{:S(2)}, u32[]{:S(2)}) collective-permute-start(bf16[656,128]{0,1:T(8,128)(2,1)} %pad_maximum_fusion.5), channel_id=1, source_target_pairs={{0,64},{16,80},{32,96},{48,112},{64,128},{80,144},{96,160},{112,17... | collective-permute-start | bytes 503816 | tf_op jit(solution)/shard_map/ppermute | solution.py:12
  52.7 3.6 %fusion.8 = f32[2,256,10,64]{1,3,2,0:T(8,128)} fusion(f32[10,2,256]{2,0,1:T(8,128)S(1)} %copy-done.8, f32[10,2,256]{2,0,1:T(8,128)S(1)} %copy.99, f32[2,256,256]{2,1,0:T(8,128)S(1)} %fusion.84, pred[2,256,256]{2,1,0:T(8,128)(4,1)} %compare_and_fusion, bf16[2,256,10,64]{1,0,3,2:T(2,128)(2,1)S(1)} %reshape.301), kind=kOutput, calls=%fused_computation.17 | convolution fusion | flops 175636480 | bytes 2662400 | tf_op jit(solution)/shard_map/hcts,cshp->cthp/dot_general | solution.py:170
  56.4 0.8 fusion.73
  57.2 1.0 add_convert_fusion
  58.3 0.7 pad_maximum_fusion.6
  59.0 12.7 %collective-permute-start.6 = (bf16[656,128]{0,1:T(8,128)(2,1)}, bf16[656,128]{0,1:T(8,128)(2,1)S(1)}, u32[]{:S(2)}, u32[]{:S(2)}) collective-permute-start(bf16[656,128]{0,1:T(8,128)(2,1)} %pad_maximum_fusion.6), channel_id=1, source_target_pairs={{0,272},{16,288},{32,304},{48,320},{64,336},{80,352},{96,368},{112... | collective-permute-start | bytes 503816 | tf_op jit(solution)/shard_map/ppermute | solution.py:12
  71.7 3.0 %collective-permute-start.5 = (bf16[656,128]{0,1:T(8,128)(2,1)}, bf16[656,128]{0,1:T(8,128)(2,1)S(1)}, u32[]{:S(2)}, u32[]{:S(2)}) collective-permute-start(bf16[656,128]{0,1:T(8,128)(2,1)} %pad_maximum_fusion.6), channel_id=1, source_target_pairs={{0,144},{16,160},{32,176},{48,192},{64,208},{80,224},{96,240},{112... | collective-permute-start | bytes 503816 | tf_op jit(solution)/shard_map/ppermute | solution.py:12
  74.7 1.9 %collective-permute-start.4 = (bf16[656,128]{0,1:T(8,128)(2,1)}, bf16[656,128]{0,1:T(8,128)(2,1)S(1)}, u32[]{:S(2)}, u32[]{:S(2)}) collective-permute-start(bf16[656,128]{0,1:T(8,128)(2,1)} %pad_maximum_fusion.6), channel_id=1, source_target_pairs={{0,16},{16,32},{32,48},{48,64},{64,80},{80,96},{96,112},{112,128},... | collective-permute-start | bytes 503816 | tf_op jit(solution)/shard_map/ppermute | solution.py:12
  76.6 1.8 %fusion.10 = f32[2,256,10,64]{1,3,2,0:T(8,128)S(1)} fusion(f32[2,256,10,64]{1,3,2,0:T(8,128)S(1)} %copy-done.1, bf16[2,256,128,1]{2,1,3,0:T(8,128)(2,1)S(1)} %bitcast.93, f32[10]{0:T(128)S(1)} %copy-done.12, f32[2,256,10]{1,2,0:T(8,128)S(1)} %copy.103, f32[1,10,64,128]{3,2,1,0:T(8,128)} %get-tuple-element.49, bf16[2,256,10,64]{1,0,3,2:T(2,128)(2,1)S(1)} %reshape.301), kind=kOutput, calls=%fused_computation.19 | convolution fusion | flops 504954880 | bytes 3756072 | tf_op jit(solution)/shard_map/ctn,chpn->cthp/dot_general | solution.py:162
  78.4 1.5 collective-permute-start.7
  79.9 2.5 %collective-permute-done.4 = bf16[656,128]{0,1:T(8,128)(2,1)S(1)} collective-permute-done((bf16[656,128]{0,1:T(8,128)(2,1)}, bf16[656,128]{0,1:T(8,128)(2,1)S(1)}, u32[]{:S(2)}, u32[]{:S(2)}) %collective-permute-start.4) | collective-permute-done | bytes 167968 | tf_op jit(solution)/shard_map/ppermute | solution.py:12
  82.5 0.7 copy-done.7
  83.5 1.2 add_add_fusion
  84.7 0.2 copy.104
  84.9 0.7 fusion.12
  85.6 1.0 copy.107
  86.7 0.1 copy.113
  86.8 0.4 multiply_reduce_fusion
  87.2 1.4 copy-done
  88.6 2.4 %convert_bitcast_fusion = bf16[8,512,320]{1,2,0:T(8,128)(2,1)S(1)} fusion(bf16[8,320,640]{2,1,0:T(8,128)(2,1)S(1)} %bitcast.91, f32[640]{0:T(1024)S(1)} %copy-done.13, f32[512,640]{0,1:T(8,128)S(1)} %bitcast.89, f32[512,640]{0,1:T(8,128)S(1)} %convert_multiply_fusion), kind=kOutput, calls=%fused_computation.3 | convolution fusion | flops 1680015360 | bytes 8522240 | tf_op jit(solution)/shard_map/tc,gkc->gtk/dot_general | solution.py:197
  91.0 1.7 %pad_maximum_fusion = bf16[8,512,321]{1,2,0:T(8,128)(2,1)} fusion(bf16[8,512,1]{1,2,0:T(2,128)(2,1)S(1)} %broadcast_in_dim.178, bf16[8,512,320]{1,2,0:T(8,128)(2,1)S(1)} %convert_bitcast_fusion), kind=kLoop, calls=%fused_computation.1 | loop fusion | flops 5259264 | bytes 5259264 | tf_op jit(solution)/shard_map/concatenate | solution.py:206
  92.7 53.6 %reduce-scatter.2.cloned.1.call-done = bf16[1,512,321]{1,2,0:T(8,128)(2,1)} async-done(((bf16[8,512,321]{1,2,0:T(8,128)(2,1)}), bf16[1,512,321]{1,2,0:T(8,128)(2,1)}) %reduce-scatter.2.cloned.1.call-update) | async-done | bytes 328720 | tf_op jit(solution)/shard_map/reduce_scatter | solution.py:207
  146.3 0.7 fusion.55
  147.0 1.8 %multiply_convert_fusion.6 = bf16[512,320]{0,1:T(8,128)(2,1)} fusion(bf16[512,321]{0,1:T(8,128)(2,1)} %bitcast.101, f32[512]{0:T(512)S(1)} %bitcast.103), kind=kLoop, calls=%fused_computation.37 | loop fusion | flops 491520 | bytes 657408 | tf_op jit(solution)/shard_map/convert_element_type | solution.py:210
  (97 shorter events, 2.7 us)
Async XLA Ops:
  6.5 12.0 %copy-start.2 = (bf16[512,640]{1,0:T(8,128)(2,1)S(1)}, bf16[512,640]{1,0:T(8,128)(2,1)}, u32[]{:S(2)}) copy-start(bf16[512,640]{1,0:T(8,128)(2,1)} %param.12) | copy-start | bytes 1966084
  6.5 139.8 %reduce-scatter.2.cloned.1.call-start = ((), (), s32[]{:S(2)}) async-start(), calls=%async_computation.1 | async-start | bytes 3022848 | tf_op jit(solution)/shard_map/reduce_scatter | solution.py:207
  8.8 12.5 %copy-start.9 = (s32[512]{0:T(512)S(1)}, s32[512]{0:T(512)}, u32[]{:S(2)}) copy-start(s32[512]{0:T(512)} %param.16) | copy-start | bytes 6148
  9.1 10.5 %collective-permute-start = (bf16[3,1024]{0,1:T(8,128)(2,1)S(1)}, bf16[3,1024]{0,1:T(8,128)(2,1)S(1)}, u32[]{:S(2)}, u32[]{:S(2)}) collective-permute-start(bf16[3,1024]{0,1:T(8,128)(2,1)S(1)} %copy.83), channel_id=1, source_target_pairs={{0,16},{16,32},{32,48},{48,64},{64,80},{80,96},{96,112},{112,128},... | collective-permute-start | bytes 18440 | tf_op jit(solution)/shard_map/ppermute | solution.py:12
  15.8 6.5 %copy-start.4 = (bf16[512,256]{1,0:T(8,128)(2,1)S(1)}, bf16[512,256]{1,0:T(8,128)(2,1)}, u32[]{:S(2)}) copy-start(bf16[512,256]{1,0:T(8,128)(2,1)} %param.13) | copy-start | bytes 786436
  26.5 6.0 %copy-start.3 = (bf16[512,640]{1,0:T(8,128)(2,1)S(1)}, bf16[512,640]{1,0:T(8,128)(2,1)}, u32[]{:S(2)}) copy-start(bf16[512,640]{1,0:T(8,128)(2,1)} %param.14) | copy-start | bytes 1966084
  27.6 8.5 %collective-permute-start.1 = (bf16[656,128]{0,1:T(8,128)(2,1)}, bf16[656,128]{0,1:T(8,128)(2,1)S(1)}, u32[]{:S(2)}, u32[]{:S(2)}) collective-permute-start(bf16[656,128]{0,1:T(8,128)(2,1)} %pad_maximum_fusion.3), channel_id=1, source_target_pairs={{0,16},{16,32},{32,48},{48,64},{64,80},{80,96},{96,112},{112,128},... | collective-permute-start | bytes 503816 | tf_op jit(solution)/shard_map/ppermute | solution.py:12
  36.1 0.5 copy-start.10
  37.3 10.2 %collective-permute-start.2 = (bf16[656,128]{0,1:T(8,128)(2,1)}, bf16[656,128]{0,1:T(8,128)(2,1)S(1)}, u32[]{:S(2)}, u32[]{:S(2)}) collective-permute-start(bf16[656,128]{0,1:T(8,128)(2,1)} %pad_maximum_fusion.4), channel_id=1, source_target_pairs={{0,32},{16,48},{32,64},{48,80},{64,96},{80,112},{96,128},{112,144}... | collective-permute-start | bytes 503816 | tf_op jit(solution)/shard_map/ppermute | solution.py:12
  41.8 5.7 %copy-start.11 = (f32[10,1]{0,1:T(1,128)S(1)}, f32[10,1]{0,1:T(1,128)}, u32[]{:S(2)}) copy-start(f32[10,1]{0,1:T(1,128)} %copy-done.10) | copy-start | bytes 124
  41.8 10.8 %copy-start.8 = (f32[10,2,256]{2,0,1:T(8,128)S(1)}, f32[10,2,256]{2,0,1:T(8,128)}, u32[]{:S(2)}) copy-start(f32[10,2,256]{2,0,1:T(8,128)} %copy.101) | copy-start | bytes 61444
  48.5 7.9 %collective-permute-start.3 = (bf16[656,128]{0,1:T(8,128)(2,1)}, bf16[656,128]{0,1:T(8,128)(2,1)}, u32[]{:S(2)}, u32[]{:S(2)}) collective-permute-start(bf16[656,128]{0,1:T(8,128)(2,1)} %pad_maximum_fusion.5), channel_id=1, source_target_pairs={{0,64},{16,80},{32,96},{48,112},{64,128},{80,144},{96,160},{112,17... | collective-permute-start | bytes 503816 | tf_op jit(solution)/shard_map/ppermute | solution.py:12
  56.3 20.3 %copy-start.12 = (f32[10]{0:T(128)S(1)}, f32[10]{0:T(128)}, u32[]{:S(2)}) copy-start(f32[10]{0:T(128)} %param.21) | copy-start | bytes 124
  56.4 20.2 %copy-start.1 = (f32[2,256,10,64]{1,3,2,0:T(8,128)S(1)}, f32[2,256,10,64]{1,3,2,0:T(8,128)}, u32[]{:S(2)}) copy-start(f32[2,256,10,64]{1,3,2,0:T(8,128)} %fusion.8) | copy-start | bytes 3932164
  59.0 20.9 %collective-permute-start.6 = (bf16[656,128]{0,1:T(8,128)(2,1)}, bf16[656,128]{0,1:T(8,128)(2,1)S(1)}, u32[]{:S(2)}, u32[]{:S(2)}) collective-permute-start(bf16[656,128]{0,1:T(8,128)(2,1)} %pad_maximum_fusion.6), channel_id=1, source_target_pairs={{0,272},{16,288},{32,304},{48,320},{64,336},{80,352},{96,368},{112... | collective-permute-start | bytes 503816 | tf_op jit(solution)/shard_map/ppermute | solution.py:12
  71.7 8.2 %collective-permute-start.5 = (bf16[656,128]{0,1:T(8,128)(2,1)}, bf16[656,128]{0,1:T(8,128)(2,1)S(1)}, u32[]{:S(2)}, u32[]{:S(2)}) collective-permute-start(bf16[656,128]{0,1:T(8,128)(2,1)} %pad_maximum_fusion.6), channel_id=1, source_target_pairs={{0,144},{16,160},{32,176},{48,192},{64,208},{80,224},{96,240},{112... | collective-permute-start | bytes 503816 | tf_op jit(solution)/shard_map/ppermute | solution.py:12
  74.7 7.8 %collective-permute-start.4 = (bf16[656,128]{0,1:T(8,128)(2,1)}, bf16[656,128]{0,1:T(8,128)(2,1)S(1)}, u32[]{:S(2)}, u32[]{:S(2)}) collective-permute-start(bf16[656,128]{0,1:T(8,128)(2,1)} %pad_maximum_fusion.6), channel_id=1, source_target_pairs={{0,16},{16,32},{32,48},{48,64},{64,80},{80,96},{96,112},{112,128},... | collective-permute-start | bytes 503816 | tf_op jit(solution)/shard_map/ppermute | solution.py:12
  78.4 5.1 %collective-permute-start.7 = (bf16[656,128]{0,1:T(8,128)(2,1)}, bf16[656,128]{0,1:T(8,128)(2,1)S(1)}, u32[]{:S(2)}, u32[]{:S(2)}) collective-permute-start(bf16[656,128]{0,1:T(8,128)(2,1)} %pad_maximum_fusion.6), channel_id=1, source_target_pairs={{0,400},{16,416},{32,432},{48,448},{64,464},{80,480},{96,496},{1,4... | collective-permute-start | bytes 503816 | tf_op jit(solution)/shard_map/ppermute | solution.py:12
  79.9 2.5 %copy-start.5 = (bf16[656,128]{0,1:T(8,128)(2,1)}, bf16[656,128]{0,1:T(8,128)(2,1)S(1)}, u32[]{:S(2)}) copy-start(bf16[656,128]{0,1:T(8,128)(2,1)S(1)} %collective-permute-done.6) | copy-start | bytes 503812
  79.9 2.5 %copy-start.6 = (bf16[656,128]{0,1:T(8,128)(2,1)}, bf16[656,128]{0,1:T(8,128)(2,1)S(1)}, u32[]{:S(2)}) copy-start(bf16[656,128]{0,1:T(8,128)(2,1)S(1)} %collective-permute-done.5) | copy-start | bytes 503812
  82.4 0.7 copy-start.7
  86.7 1.9 %copy-start = (bf16[640,2560]{0,1:T(8,128)(2,1)S(1)}, bf16[640,2560]{0,1:T(8,128)(2,1)}, u32[]{:S(2)}) copy-start(bf16[640,2560]{0,1:T(8,128)(2,1)} %copy.98) | copy-start | bytes 9830404
  86.8 1.8 %copy-start.13 = (f32[640]{0:T(1024)S(1)}, f32[640]{0:T(1024)}, u32[]{:S(2)}) copy-start(f32[640]{0:T(1024)} %param.22) | copy-start | bytes 7684
Sparse Core Ops, SparseCore 0:
  92.9 53.4 reduce-scatter.1

commit v14 on v12

--- a/solution.py
+++ b/solution.py
@@ -129,7 +129,13 @@
     step_size = jax.nn.softplus(dt_stream.astype(jnp.float32) + dt_bias[:, None])
     log_rates = -jnp.exp(a_log)[:, None] * step_size
     block_steps = step_size.reshape(head_count, blocks, SPAN)
-    cum_rates = jnp.cumsum(log_rates.reshape(head_count, blocks, SPAN), axis=2)
+    running = jnp.triu(jnp.ones((SPAN, SPAN), jnp.float32))
+    cum_rates = jnp.einsum(
+        "hcs,su->hcu",
+        log_rates.reshape(head_count, blocks, SPAN),
+        running,
+        precision=lax.Precision.HIGHEST,
+    )
     block_x = mixed_x.reshape(blocks, SPAN, head_count, head_size)
     b_vals = mixed_bc[:, :state_size].reshape(blocks, SPAN, state_size)
     c_vals = mixed_bc[:, state_size:].reshape(blocks, SPAN, state_size)

time: 155 us -> 154 us (level)
  other arithmetic: 20.9 us -> 17.2 us
  starting transfers between devices: 30.6 us -> 33.7 us
    ppermute x8, starting transfers between devices: 30.6 us -> 33.7 us  [from_behind(): return lax.ppermute(block, axis, route)]
  transfers between devices with their start and end apart: 9 -> 9, of which waited for: 5 -> 5; matrix products, arithmetic and copies ran while one was open for 13% -> 11% of each run, Pallas kernels for 0% -> 0%
where the time goes in v14:
time: 154 us; the launch traced here: 153 us
  waiting for transfers between devices  64.4 us (42%)
  starting transfers between devices  33.7 us (22%)
  other arithmetic  17.2 us (11%)
  local copies, waits for them, and re-layouts  14.4 us (9%)
  between operations  13.9 us (9%)
  matrix products  9.02 us (6%)
    reduce_scatter x1, waiting for transfers between devices, local(): lax.psum_scatter(payload, 'tensor', scatter_dimension=0, tiled=True)[0]  53.5 us
    ppermute x8, starting transfers between devices, from_behind(): return lax.ppermute(block, axis, route)  33.7 us
    ppermute x8, waiting for transfers between devices, from_behind(): return lax.ppermute(block, axis, route)  10.8 us
    optimization_barrier x2, local copies, waits for them, and re-layouts, pass_state(): sent, passengers = lax.optimization_barrier((sent, passengers))  5.91 us
  transfers between devices with their start and end apart: 9, of which 5 were waited for; matrix products, arithmetic and copies ran while one was open for 11% of the time, Pallas kernels for 0%

profile of v14, /device:TPU:6, one launch (start us, length us, event | category | flops | bytes accessed | tf_op | source)
XLA Modules:
  0.0 152.5 jit_solution(10479864770480788947)
XLA Ops:
  6.5 0.8 slice.178
  7.3 0.7 fusion.91
  8.0 0.1 slice.179
  8.1 0.7 slice.177
  8.9 0.2 copy.56
  9.1 3.4 %collective-permute-start = (bf16[3,1024]{0,1:T(8,128)(2,1)S(1)}, bf16[3,1024]{0,1:T(8,128)(2,1)S(1)}, u32[]{:S(2)}, u32[]{:S(2)}) collective-permute-start(bf16[3,1024]{0,1:T(8,128)(2,1)S(1)} %copy.56), channel_id=1, source_target_pairs={{0,16},{16,32},{32,48},{48,64},{64,80},{80,96},{96,112},{112,128},... | collective-permute-start | bytes 18440 | tf_op jit(solution)/shard_map/ppermute | solution.py:12
  12.5 0.7 exponential_negate_fusion
  13.2 0.8 slice_convert_fusion.4
  14.0 0.9 convert_reduce_fusion.3
  14.9 0.8 broadcast_multiply_fusion.1
  15.8 0.3 fusion.29
  16.1 0.2 slice_reduce_fusion
  16.3 0.8 compare_and_fusion
  17.1 0.2 slice_reduce_fusion.2
  17.3 0.1 slice.183
  17.4 0.3 copy.58
  17.6 1.4 collective-permute-done
  19.0 0.6 slice.181
  19.6 0.8 pad_maximum_fusion.9
  20.3 0.1 broadcast_compare_fusion
  20.4 0.2 slice_reduce_fusion.1
  20.6 0.1 fusion.88
  20.8 0.1 slice_compare_fusion.2
  21.3 0.1 copy.62
  21.4 0.8 multiply_convert_fusion.7
  22.2 1.7 %multiply_convert_fusion.5 = bf16[512,640]{0,1:T(8,128)(2,1)S(1)} fusion(bf16[512,640]{0,1:T(8,128)(2,1)S(1)} %copy.58, bf16[3,640]{0,1:T(8,128)(2,1)S(1)} %slice.237, f32[640]{0:T(1024)S(1)} %get-tuple-element.19, f32[640]{0:T(1024)S(1)} %get-tuple-element.20, f32[640]{0:T(1024)S(1)} %get-tuple-element.18, f32[640]{0:T(1024)S(1)} %get-tuple-element.17, ...), kind=kLoop, calls=%fused_computation.28 | loop fusion | flops 9502720 | bytes 1326848 | tf_op jit(solution)/shard_map/convert_element_type | solution.py:27
  23.9 0.2 reshape.271
  24.1 0.1 multiply_bitcast_fusion
  24.1 0.8 fusion.13
  24.9 0.8 fusion.89
  25.8 0.2 copy.63
  25.9 0.2 copy.64
  26.2 0.7 pad_maximum_fusion.3
  26.9 5.5 %collective-permute-start.1 = (bf16[656,128]{0,1:T(8,128)(2,1)}, bf16[656,128]{0,1:T(8,128)(2,1)S(1)}, u32[]{:S(2)}, u32[]{:S(2)}) collective-permute-start(bf16[656,128]{0,1:T(8,128)(2,1)} %pad_maximum_fusion.3), channel_id=1, source_target_pairs={{0,16},{16,32},{32,48},{48,64},{64,80},{80,96},{96,112},{112,128},... | collective-permute-start | bytes 503816 | tf_op jit(solution)/shard_map/ppermute | solution.py:12
  32.4 0.3 copy.65
  32.6 0.3 convert_multiply_fusion
  33.0 5.7 %copy.66 = bf16[640,2560]{0,1:T(8,128)(2,1)} copy(bf16[640,2560]{1,0:T(8,128)(2,1)} %param.23) | data formatting | bytes 6553600 | tf_op jit(solution)/shard_map/optimization_barrier | solution.py:57
  38.7 0.2 fusion.92
  39.0 2.2 %collective-permute-start.2 = (bf16[656,128]{0,1:T(8,128)(2,1)S(1)}, bf16[656,128]{0,1:T(8,128)(2,1)S(1)}, u32[]{:S(2)}, u32[]{:S(2)}) collective-permute-start(bf16[656,128]{0,1:T(8,128)(2,1)S(1)} %pad_maximum_fusion.4), channel_id=1, source_target_pairs={{0,32},{16,48},{32,64},{48,80},{64,96},{80,112},{96,128},{112,144}... | collective-permute-start | bytes 503816 | tf_op jit(solution)/shard_map/ppermute | solution.py:12
  41.3 2.8 %fusion.8 = f32[2,256,10,64]{1,3,2,0:T(8,128)} fusion(f32[10,2,256]{2,0,1:T(8,128)S(1)} %get-tuple-element.46, f32[10,2,256]{2,0,1:T(8,128)S(1)} %fusion.29, f32[2,256,256]{2,1,0:T(8,128)S(1)} %fusion.92, pred[2,256,256]{2,1,0:T(8,128)(4,1)S(1)} %copy-done.8, bf16[2,256,10,64]{1,0,3,2:T(2,128)(2,1)S(1)} %reshape.271), kind=kOutput, calls=%fused_computation.17 | convolution fusion | flops 175636480 | bytes 2662400 | tf_op jit(solution)/shard_map/hcts,cshp->cthp/dot_general | solution.py:174
  44.1 4.0 %collective-permute-done.2 = bf16[656,128]{0,1:T(8,128)(2,1)S(1)} collective-permute-done((bf16[656,128]{0,1:T(8,128)(2,1)S(1)}, bf16[656,128]{0,1:T(8,128)(2,1)S(1)}, u32[]{:S(2)}, u32[]{:S(2)}) %collective-permute-start.2) | collective-permute-done | bytes 167968 | tf_op jit(solution)/shard_map/ppermute | solution.py:12
  48.4 3.5 %collective-permute-start.3 = (bf16[656,128]{0,1:T(8,128)(2,1)S(1)}, bf16[656,128]{0,1:T(8,128)(2,1)S(1)}, u32[]{:S(2)}, u32[]{:S(2)}) collective-permute-start(bf16[656,128]{0,1:T(8,128)(2,1)S(1)} %pad_maximum_fusion.5), channel_id=1, source_target_pairs={{0,64},{16,80},{32,96},{48,112},{64,128},{80,144},{96,160},{112,17... | collective-permute-start | bytes 503816 | tf_op jit(solution)/shard_map/ppermute | solution.py:12
  52.1 2.9 %collective-permute-done.3 = bf16[656,128]{0,1:T(8,128)(2,1)S(1)} collective-permute-done((bf16[656,128]{0,1:T(8,128)(2,1)S(1)}, bf16[656,128]{0,1:T(8,128)(2,1)S(1)}, u32[]{:S(2)}, u32[]{:S(2)}) %collective-permute-start.3) | collective-permute-done | bytes 167968 | tf_op jit(solution)/shard_map/ppermute | solution.py:12
  55.1 0.1 add_convert_fusion
  55.2 0.7 pad_maximum_fusion.6
  55.9 11.7 %collective-permute-start.6 = (bf16[656,128]{0,1:T(8,128)(2,1)}, bf16[656,128]{0,1:T(8,128)(2,1)S(1)}, u32[]{:S(2)}, u32[]{:S(2)}) collective-permute-start(bf16[656,128]{0,1:T(8,128)(2,1)} %pad_maximum_fusion.6), channel_id=1, source_target_pairs={{0,272},{16,288},{32,304},{48,320},{64,336},{80,352},{96,368},{112... | collective-permute-start | bytes 503816 | tf_op jit(solution)/shard_map/ppermute | solution.py:12
  67.6 4.0 %collective-permute-start.5 = (bf16[656,128]{0,1:T(8,128)(2,1)}, bf16[656,128]{0,1:T(8,128)(2,1)S(1)}, u32[]{:S(2)}, u32[]{:S(2)}) collective-permute-start(bf16[656,128]{0,1:T(8,128)(2,1)} %pad_maximum_fusion.6), channel_id=1, source_target_pairs={{0,144},{16,160},{32,176},{48,192},{64,208},{80,224},{96,240},{112... | collective-permute-start | bytes 503816 | tf_op jit(solution)/shard_map/ppermute | solution.py:12
  71.6 1.9 %collective-permute-start.4 = (bf16[656,128]{0,1:T(8,128)(2,1)}, bf16[656,128]{0,1:T(8,128)(2,1)S(1)}, u32[]{:S(2)}, u32[]{:S(2)}) collective-permute-start(bf16[656,128]{0,1:T(8,128)(2,1)} %pad_maximum_fusion.6), channel_id=1, source_target_pairs={{0,16},{16,32},{32,48},{48,64},{64,80},{80,96},{96,112},{112,128},... | collective-permute-start | bytes 503816 | tf_op jit(solution)/shard_map/ppermute | solution.py:12
  73.6 1.8 %fusion.10 = f32[2,256,10,64]{1,3,2,0:T(8,128)S(1)} fusion(f32[2,256,10,64]{1,3,2,0:T(8,128)S(1)} %copy-done.1, bf16[2,256,128,1]{2,1,3,0:T(8,128)(2,1)S(1)} %bitcast.92, f32[10]{0:T(128)S(1)} %copy-done.10, f32[2,256,10]{1,2,0:T(8,128)S(1)} %get-tuple-element.22, f32[1,10,64,128]{3,2,1,0:T(8,128)} %get-tuple-element.39, ...), kind=kOutput, calls=%fused_computation.19 | convolution fusion | flops 504954880 | bytes 3756072 | tf_op jit(solution)/shard_map/ctn,chpn->cthp/dot_general | solution.py:166
  75.3 1.5 collective-permute-start.7
  76.9 2.5 %collective-permute-done.4 = bf16[656,128]{0,1:T(8,128)(2,1)S(1)} collective-permute-done((bf16[656,128]{0,1:T(8,128)(2,1)}, bf16[656,128]{0,1:T(8,128)(2,1)S(1)}, u32[]{:S(2)}, u32[]{:S(2)}) %collective-permute-start.4) | collective-permute-done | bytes 167968 | tf_op jit(solution)/shard_map/ppermute | solution.py:12
  79.4 0.7 copy-done.7
  80.5 1.2 add_add_fusion
  81.7 0.2 copy.69
  81.8 0.7 fusion.12
  82.6 1.0 copy.70
  83.6 0.1 copy.76
  83.7 0.4 multiply_reduce_fusion
  84.1 1.4 copy-done
  85.5 2.4 %convert_bitcast_fusion = bf16[8,512,320]{1,2,0:T(8,128)(2,1)S(1)} fusion(bf16[8,320,640]{2,1,0:T(8,128)(2,1)S(1)} %bitcast.90, f32[640]{0:T(1024)S(1)} %copy-done.11, f32[512,640]{0,1:T(8,128)S(1)} %bitcast.88, f32[512,640]{0,1:T(8,128)S(1)} %convert_multiply_fusion), kind=kOutput, calls=%fused_computation.3 | convolution fusion | flops 1680015360 | bytes 8522240 | tf_op jit(solution)/shard_map/tc,gkc->gtk/dot_general | solution.py:198
  87.9 1.7 %pad_maximum_fusion = bf16[8,512,321]{1,2,0:T(8,128)(2,1)} fusion(bf16[8,512,1]{1,2,0:T(2,128)(2,1)S(1)} %broadcast_in_dim.187, bf16[8,512,320]{1,2,0:T(8,128)(2,1)S(1)} %convert_bitcast_fusion), kind=kLoop, calls=%fused_computation.1 | loop fusion | flops 5259264 | bytes 5259264 | tf_op jit(solution)/shard_map/concatenate | solution.py:207
  89.7 53.5 %reduce-scatter.2.cloned.1.call-done = bf16[1,512,321]{1,2,0:T(8,128)(2,1)} async-done(((bf16[8,512,321]{1,2,0:T(8,128)(2,1)}), bf16[1,512,321]{1,2,0:T(8,128)(2,1)}) %reduce-scatter.2.cloned.1.call-update) | async-done | bytes 328720 | tf_op jit(solution)/shard_map/reduce_scatter | solution.py:208
  143.2 0.7 fusion.61
  143.9 1.8 %multiply_convert_fusion.6 = bf16[512,320]{0,1:T(8,128)(2,1)} fusion(bf16[512,321]{0,1:T(8,128)(2,1)} %bitcast.100, f32[512]{0:T(512)S(1)} %bitcast.101), kind=kLoop, calls=%fused_computation.37 | loop fusion | flops 491520 | bytes 657408 | tf_op jit(solution)/shard_map/convert_element_type | solution.py:211
  (78 shorter events, 1.9 us)
Async XLA Ops:
  6.5 14.3 %copy-start.9 = (s32[512]{0:T(512)S(1)}, s32[512]{0:T(512)}, u32[]{:S(2)}) copy-start(s32[512]{0:T(512)} %param.16) | copy-start | bytes 6148
  6.5 10.8 %copy-start.2 = (bf16[512,640]{1,0:T(8,128)(2,1)S(1)}, bf16[512,640]{1,0:T(8,128)(2,1)}, u32[]{:S(2)}) copy-start(bf16[512,640]{1,0:T(8,128)(2,1)} %param.12) | copy-start | bytes 1966084
  6.5 136.7 %reduce-scatter.2.cloned.1.call-start = ((), (), s32[]{:S(2)}) async-start(), calls=%async_computation.1 | async-start | bytes 3022848 | tf_op jit(solution)/shard_map/reduce_scatter | solution.py:208
  8.9 12.5 %copy-start.4 = (bf16[512,256]{1,0:T(8,128)(2,1)S(1)}, bf16[512,256]{1,0:T(8,128)(2,1)}, u32[]{:S(2)}) copy-start(bf16[512,256]{1,0:T(8,128)(2,1)} %param.13) | copy-start | bytes 786436
  9.1 9.9 %collective-permute-start = (bf16[3,1024]{0,1:T(8,128)(2,1)S(1)}, bf16[3,1024]{0,1:T(8,128)(2,1)S(1)}, u32[]{:S(2)}, u32[]{:S(2)}) collective-permute-start(bf16[3,1024]{0,1:T(8,128)(2,1)S(1)} %copy.56), channel_id=1, source_target_pairs={{0,16},{16,32},{32,48},{48,64},{64,80},{80,96},{96,112},{112,128},... | collective-permute-start | bytes 18440 | tf_op jit(solution)/shard_map/ppermute | solution.py:12
  25.8 6.6 %copy-start.3 = (bf16[512,640]{1,0:T(8,128)(2,1)S(1)}, bf16[512,640]{1,0:T(8,128)(2,1)}, u32[]{:S(2)}) copy-start(bf16[512,640]{1,0:T(8,128)(2,1)} %param.14) | copy-start | bytes 1966084
  26.9 12.0 %collective-permute-start.1 = (bf16[656,128]{0,1:T(8,128)(2,1)}, bf16[656,128]{0,1:T(8,128)(2,1)S(1)}, u32[]{:S(2)}, u32[]{:S(2)}) collective-permute-start(bf16[656,128]{0,1:T(8,128)(2,1)} %pad_maximum_fusion.3), channel_id=1, source_target_pairs={{0,16},{16,32},{32,48},{48,64},{64,80},{80,96},{96,112},{112,128},... | collective-permute-start | bytes 503816 | tf_op jit(solution)/shard_map/ppermute | solution.py:12
  38.7 2.6 %copy-start.8 = (pred[2,256,256]{2,1,0:T(8,128)(4,1)S(1)}, pred[2,256,256]{2,1,0:T(8,128)(4,1)}, u32[]{:S(2)}) copy-start(pred[2,256,256]{2,1,0:T(8,128)(4,1)} %compare_and_fusion) | copy-start | bytes 393220
  39.0 9.1 %collective-permute-start.2 = (bf16[656,128]{0,1:T(8,128)(2,1)S(1)}, bf16[656,128]{0,1:T(8,128)(2,1)S(1)}, u32[]{:S(2)}, u32[]{:S(2)}) collective-permute-start(bf16[656,128]{0,1:T(8,128)(2,1)S(1)} %pad_maximum_fusion.4), channel_id=1, source_target_pairs={{0,32},{16,48},{32,64},{48,80},{64,96},{80,112},{96,128},{112,144}... | collective-permute-start | bytes 503816 | tf_op jit(solution)/shard_map/ppermute | solution.py:12
  48.3 25.3 %copy-start.10 = (f32[10]{0:T(128)S(1)}, f32[10]{0:T(128)}, u32[]{:S(2)}) copy-start(f32[10]{0:T(128)} %param.21) | copy-start | bytes 124
  48.4 6.7 %collective-permute-start.3 = (bf16[656,128]{0,1:T(8,128)(2,1)S(1)}, bf16[656,128]{0,1:T(8,128)(2,1)S(1)}, u32[]{:S(2)}, u32[]{:S(2)}) collective-permute-start(bf16[656,128]{0,1:T(8,128)(2,1)S(1)} %pad_maximum_fusion.5), channel_id=1, source_target_pairs={{0,64},{16,80},{32,96},{48,112},{64,128},{80,144},{96,160},{112,17... | collective-permute-start | bytes 503816 | tf_op jit(solution)/shard_map/ppermute | solution.py:12
  52.1 21.4 %copy-start.1 = (f32[2,256,10,64]{1,3,2,0:T(8,128)S(1)}, f32[2,256,10,64]{1,3,2,0:T(8,128)}, u32[]{:S(2)}) copy-start(f32[2,256,10,64]{1,3,2,0:T(8,128)} %fusion.8) | copy-start | bytes 3932164
  55.9 20.9 %collective-permute-start.6 = (bf16[656,128]{0,1:T(8,128)(2,1)}, bf16[656,128]{0,1:T(8,128)(2,1)S(1)}, u32[]{:S(2)}, u32[]{:S(2)}) collective-permute-start(bf16[656,128]{0,1:T(8,128)(2,1)} %pad_maximum_fusion.6), channel_id=1, source_target_pairs={{0,272},{16,288},{32,304},{48,320},{64,336},{80,352},{96,368},{112... | collective-permute-start | bytes 503816 | tf_op jit(solution)/shard_map/ppermute | solution.py:12
  67.6 9.3 %collective-permute-start.5 = (bf16[656,128]{0,1:T(8,128)(2,1)}, bf16[656,128]{0,1:T(8,128)(2,1)S(1)}, u32[]{:S(2)}, u32[]{:S(2)}) collective-permute-start(bf16[656,128]{0,1:T(8,128)(2,1)} %pad_maximum_fusion.6), channel_id=1, source_target_pairs={{0,144},{16,160},{32,176},{48,192},{64,208},{80,224},{96,240},{112... | collective-permute-start | bytes 503816 | tf_op jit(solution)/shard_map/ppermute | solution.py:12
  71.6 7.8 %collective-permute-start.4 = (bf16[656,128]{0,1:T(8,128)(2,1)}, bf16[656,128]{0,1:T(8,128)(2,1)S(1)}, u32[]{:S(2)}, u32[]{:S(2)}) collective-permute-start(bf16[656,128]{0,1:T(8,128)(2,1)} %pad_maximum_fusion.6), channel_id=1, source_target_pairs={{0,16},{16,32},{32,48},{48,64},{64,80},{80,96},{96,112},{112,128},... | collective-permute-start | bytes 503816 | tf_op jit(solution)/shard_map/ppermute | solution.py:12
  75.3 5.1 %collective-permute-start.7 = (bf16[656,128]{0,1:T(8,128)(2,1)}, bf16[656,128]{0,1:T(8,128)(2,1)S(1)}, u32[]{:S(2)}, u32[]{:S(2)}) collective-permute-start(bf16[656,128]{0,1:T(8,128)(2,1)} %pad_maximum_fusion.6), channel_id=1, source_target_pairs={{0,400},{16,416},{32,432},{48,448},{64,464},{80,480},{96,496},{1,4... | collective-permute-start | bytes 503816 | tf_op jit(solution)/shard_map/ppermute | solution.py:12
  76.8 2.5 %copy-start.5 = (bf16[656,128]{0,1:T(8,128)(2,1)}, bf16[656,128]{0,1:T(8,128)(2,1)S(1)}, u32[]{:S(2)}) copy-start(bf16[656,128]{0,1:T(8,128)(2,1)S(1)} %collective-permute-done.6) | copy-start | bytes 503812
  76.9 2.5 %copy-start.6 = (bf16[656,128]{0,1:T(8,128)(2,1)}, bf16[656,128]{0,1:T(8,128)(2,1)S(1)}, u32[]{:S(2)}) copy-start(bf16[656,128]{0,1:T(8,128)(2,1)S(1)} %collective-permute-done.5) | copy-start | bytes 503812
  79.4 0.7 copy-start.7
  83.6 1.9 %copy-start = (bf16[640,2560]{0,1:T(8,128)(2,1)S(1)}, bf16[640,2560]{0,1:T(8,128)(2,1)}, u32[]{:S(2)}) copy-start(bf16[640,2560]{0,1:T(8,128)(2,1)} %copy.66) | copy-start | bytes 9830404
  83.7 1.8 %copy-start.11 = (f32[640]{0:T(1024)S(1)}, f32[640]{0:T(1024)}, u32[]{:S(2)}) copy-start(f32[640]{0:T(1024)} %param.22) | copy-start | bytes 7684
Sparse Core Ops, SparseCore 0:
  89.8 53.3 reduce-scatter.1

commit v15 on v14

--- a/solution.py
+++ b/solution.py
@@ -181,10 +181,10 @@
         (z_gate, w_out),
         lambda pair: (jax.nn.silu(pair[0].astype(jnp.float32)), jnp.transpose(pair[1])),
     )
-    prefix = jnp.cumprod(
-        jnp.concatenate([jnp.ones((head_count, 1), jnp.float32), block_decay[:, :-1]], axis=1),
-        axis=1,
-    )
+    prefix_list = [jnp.ones((head_count,), jnp.float32)]
+    for block in range(blocks - 1):
+        prefix_list.append(prefix_list[-1] * block_decay[:, block])
+    prefix = jnp.stack(prefix_list, axis=1)
     reach_term = jnp.einsum("ctn,hpn->cthp", c_wide, incoming, precision=highest)
     result = (
         result + reach_term * jnp.transpose(entry_gain * prefix[:, :, None], (1, 2, 0))[..., None]

time: 154 us -> 153 us (level)
  no operation moved by 1% of the time
where the time goes in v15:
time: 153 us
  waiting for transfers between devices  64.3 us (42%)
  starting transfers between devices  33.7 us (22%)
  other arithmetic  17.2 us (11%)
  local copies, waits for them, and re-layouts  14.4 us (9%)
  between operations  13.9 us (9%)
  matrix products  9.04 us (6%)
    reduce_scatter x1, waiting for transfers between devices, local(): lax.psum_scatter(payload, 'tensor', scatter_dimension=0, tiled=True)[0]  53.5 us
    ppermute x8, starting transfers between devices, from_behind(): return lax.ppermute(block, axis, route)  33.7 us
    ppermute x8, waiting for transfers between devices, from_behind(): return lax.ppermute(block, axis, route)  10.8 us
    optimization_barrier x2, local copies, waits for them, and re-layouts, pass_state(): sent, passengers = lax.optimization_barrier((sent, passengers))  5.89 us
  transfers between devices with their start and end apart: 9, of which 5 were waited for; matrix products, arithmetic and copies ran while one was open for 11% of the time, Pallas kernels for 0%

profile of v15, /device:TPU:6, one launch (start us, length us, event | category | flops | bytes accessed | tf_op | source)
XLA Modules:
  0.0 152.5 jit_solution(17824002789908750573)
XLA Ops:
  6.5 0.8 slice.178
  7.3 0.7 fusion.91
  8.1 0.7 slice.177
  8.9 0.2 copy.56
  9.1 3.4 %collective-permute-start = (bf16[3,1024]{0,1:T(8,128)(2,1)S(1)}, bf16[3,1024]{0,1:T(8,128)(2,1)S(1)}, u32[]{:S(2)}, u32[]{:S(2)}) collective-permute-start(bf16[3,1024]{0,1:T(8,128)(2,1)S(1)} %copy.56), channel_id=1, source_target_pairs={{0,16},{16,32},{32,48},{48,64},{64,80},{80,96},{96,112},{112,128},... | collective-permute-start | bytes 18440 | tf_op jit(solution)/shard_map/ppermute | solution.py:12
  12.5 0.7 exponential_negate_fusion
  13.2 0.8 slice_convert_fusion.4
  14.0 0.9 convert_reduce_fusion.3
  14.9 0.8 broadcast_multiply_fusion.1
  15.8 0.3 fusion.29
  16.1 0.2 slice_reduce_fusion
  16.3 0.8 compare_and_fusion
  17.1 0.2 slice_reduce_fusion.2
  17.3 0.1 slice.183
  17.4 0.3 copy.58
  17.7 1.3 collective-permute-done
  19.0 0.6 slice.181
  19.6 0.8 pad_maximum_fusion.9
  20.3 0.1 broadcast_compare_fusion
  20.4 0.2 slice_reduce_fusion.1
  20.6 0.1 fusion.88
  20.8 0.1 slice_compare_fusion.2
  21.3 0.1 copy.62
  21.4 0.8 multiply_convert_fusion.7
  22.2 1.7 %multiply_convert_fusion.5 = bf16[512,640]{0,1:T(8,128)(2,1)S(1)} fusion(bf16[512,640]{0,1:T(8,128)(2,1)S(1)} %copy.58, bf16[3,640]{0,1:T(8,128)(2,1)S(1)} %slice.237, f32[640]{0:T(1024)S(1)} %get-tuple-element.19, f32[640]{0:T(1024)S(1)} %get-tuple-element.20, f32[640]{0:T(1024)S(1)} %get-tuple-element.18, f32[640]{0:T(1024)S(1)} %get-tuple-element.17, ...), kind=kLoop, calls=%fused_computation.28 | loop fusion | flops 9502720 | bytes 1326848 | tf_op jit(solution)/shard_map/convert_element_type | solution.py:27
  23.9 0.2 reshape.269
  24.1 0.1 multiply_bitcast_fusion
  24.1 0.8 fusion.13
  24.9 0.8 fusion.89
  25.8 0.2 copy.63
  25.9 0.2 copy.64
  26.2 0.7 pad_maximum_fusion.3
  26.9 5.5 %collective-permute-start.1 = (bf16[656,128]{0,1:T(8,128)(2,1)}, bf16[656,128]{0,1:T(8,128)(2,1)S(1)}, u32[]{:S(2)}, u32[]{:S(2)}) collective-permute-start(bf16[656,128]{0,1:T(8,128)(2,1)} %pad_maximum_fusion.3), channel_id=1, source_target_pairs={{0,16},{16,32},{32,48},{48,64},{64,80},{80,96},{96,112},{112,128},... | collective-permute-start | bytes 503816 | tf_op jit(solution)/shard_map/ppermute | solution.py:12
  32.4 0.3 copy.65
  32.6 0.3 convert_multiply_fusion
  33.0 5.6 %copy.66 = bf16[640,2560]{0,1:T(8,128)(2,1)} copy(bf16[640,2560]{1,0:T(8,128)(2,1)} %param.23) | data formatting | bytes 6553600 | tf_op jit(solution)/shard_map/optimization_barrier | solution.py:57
  38.6 0.2 fusion.92
  39.0 2.2 %collective-permute-start.2 = (bf16[656,128]{0,1:T(8,128)(2,1)S(1)}, bf16[656,128]{0,1:T(8,128)(2,1)S(1)}, u32[]{:S(2)}, u32[]{:S(2)}) collective-permute-start(bf16[656,128]{0,1:T(8,128)(2,1)S(1)} %pad_maximum_fusion.4), channel_id=1, source_target_pairs={{0,32},{16,48},{32,64},{48,80},{64,96},{80,112},{96,128},{112,144}... | collective-permute-start | bytes 503816 | tf_op jit(solution)/shard_map/ppermute | solution.py:12
  41.2 2.8 %fusion.8 = f32[2,256,10,64]{1,3,2,0:T(8,128)} fusion(f32[10,2,256]{2,0,1:T(8,128)S(1)} %get-tuple-element.46, f32[10,2,256]{2,0,1:T(8,128)S(1)} %fusion.29, f32[2,256,256]{2,1,0:T(8,128)S(1)} %fusion.92, pred[2,256,256]{2,1,0:T(8,128)(4,1)S(1)} %copy-done.8, bf16[2,256,10,64]{1,0,3,2:T(2,128)(2,1)S(1)} %reshape.269), kind=kOutput, calls=%fused_computation.17 | convolution fusion | flops 175636480 | bytes 2662400 | tf_op jit(solution)/shard_map/hcts,cshp->cthp/dot_general | solution.py:174
  44.0 4.0 %collective-permute-done.2 = bf16[656,128]{0,1:T(8,128)(2,1)S(1)} collective-permute-done((bf16[656,128]{0,1:T(8,128)(2,1)S(1)}, bf16[656,128]{0,1:T(8,128)(2,1)S(1)}, u32[]{:S(2)}, u32[]{:S(2)}) %collective-permute-start.2) | collective-permute-done | bytes 167968 | tf_op jit(solution)/shard_map/ppermute | solution.py:12
  48.3 0.1 fusion.45
  48.4 3.5 %collective-permute-start.3 = (bf16[656,128]{0,1:T(8,128)(2,1)S(1)}, bf16[656,128]{0,1:T(8,128)(2,1)S(1)}, u32[]{:S(2)}, u32[]{:S(2)}) collective-permute-start(bf16[656,128]{0,1:T(8,128)(2,1)S(1)} %pad_maximum_fusion.5), channel_id=1, source_target_pairs={{0,64},{16,80},{32,96},{48,112},{64,128},{80,144},{96,160},{112,17... | collective-permute-start | bytes 503816 | tf_op jit(solution)/shard_map/ppermute | solution.py:12
  52.1 2.9 %collective-permute-done.3 = bf16[656,128]{0,1:T(8,128)(2,1)S(1)} collective-permute-done((bf16[656,128]{0,1:T(8,128)(2,1)S(1)}, bf16[656,128]{0,1:T(8,128)(2,1)S(1)}, u32[]{:S(2)}, u32[]{:S(2)}) %collective-permute-start.3) | collective-permute-done | bytes 167968 | tf_op jit(solution)/shard_map/ppermute | solution.py:12
  55.1 0.1 add_convert_fusion
  55.2 0.7 pad_maximum_fusion.6
  55.9 11.7 %collective-permute-start.6 = (bf16[656,128]{0,1:T(8,128)(2,1)}, bf16[656,128]{0,1:T(8,128)(2,1)S(1)}, u32[]{:S(2)}, u32[]{:S(2)}) collective-permute-start(bf16[656,128]{0,1:T(8,128)(2,1)} %pad_maximum_fusion.6), channel_id=1, source_target_pairs={{0,272},{16,288},{32,304},{48,320},{64,336},{80,352},{96,368},{112... | collective-permute-start | bytes 503816 | tf_op jit(solution)/shard_map/ppermute | solution.py:12
  67.6 4.1 %collective-permute-start.5 = (bf16[656,128]{0,1:T(8,128)(2,1)}, bf16[656,128]{0,1:T(8,128)(2,1)S(1)}, u32[]{:S(2)}, u32[]{:S(2)}) collective-permute-start(bf16[656,128]{0,1:T(8,128)(2,1)} %pad_maximum_fusion.6), channel_id=1, source_target_pairs={{0,144},{16,160},{32,176},{48,192},{64,208},{80,224},{96,240},{112... | collective-permute-start | bytes 503816 | tf_op jit(solution)/shard_map/ppermute | solution.py:12
  71.6 1.9 %collective-permute-start.4 = (bf16[656,128]{0,1:T(8,128)(2,1)}, bf16[656,128]{0,1:T(8,128)(2,1)S(1)}, u32[]{:S(2)}, u32[]{:S(2)}) collective-permute-start(bf16[656,128]{0,1:T(8,128)(2,1)} %pad_maximum_fusion.6), channel_id=1, source_target_pairs={{0,16},{16,32},{32,48},{48,64},{64,80},{80,96},{96,112},{112,128},... | collective-permute-start | bytes 503816 | tf_op jit(solution)/shard_map/ppermute | solution.py:12
  73.6 1.8 %fusion.10 = f32[2,256,10,64]{1,3,2,0:T(8,128)S(1)} fusion(f32[2,256,10,64]{1,3,2,0:T(8,128)S(1)} %copy-done.1, bf16[2,256,128,1]{2,1,3,0:T(8,128)(2,1)S(1)} %bitcast.93, f32[10]{0:T(128)S(1)} %copy-done.10, f32[2,256,10]{1,2,0:T(8,128)S(1)} %get-tuple-element.22, f32[1,10,64,128]{3,2,1,0:T(8,128)} %get-tuple-element.39, ...), kind=kOutput, calls=%fused_computation.19 | convolution fusion | flops 504954880 | bytes 3756072 | tf_op jit(solution)/shard_map/ctn,chpn->cthp/dot_general | solution.py:166
  75.4 1.5 collective-permute-start.7
  76.9 2.5 %collective-permute-done.4 = bf16[656,128]{0,1:T(8,128)(2,1)S(1)} collective-permute-done((bf16[656,128]{0,1:T(8,128)(2,1)}, bf16[656,128]{0,1:T(8,128)(2,1)S(1)}, u32[]{:S(2)}, u32[]{:S(2)}) %collective-permute-start.4) | collective-permute-done | bytes 167968 | tf_op jit(solution)/shard_map/ppermute | solution.py:12
  79.4 0.7 copy-done.7
  80.5 1.2 add_add_fusion
  81.7 0.2 copy.69
  81.9 0.7 fusion.12
  82.6 1.0 copy.70
  83.7 0.1 copy.76
  83.8 0.4 multiply_reduce_fusion
  84.2 1.4 copy-done
  85.6 2.4 %convert_bitcast_fusion = bf16[8,512,320]{1,2,0:T(8,128)(2,1)S(1)} fusion(bf16[8,320,640]{2,1,0:T(8,128)(2,1)S(1)} %bitcast.91, f32[640]{0:T(1024)S(1)} %copy-done.11, f32[512,640]{0,1:T(8,128)S(1)} %bitcast.89, f32[512,640]{0,1:T(8,128)S(1)} %convert_multiply_fusion), kind=kOutput, calls=%fused_computation.3 | convolution fusion | flops 1680015360 | bytes 8522240 | tf_op jit(solution)/shard_map/tc,gkc->gtk/dot_general | solution.py:198
  88.0 1.7 %pad_maximum_fusion = bf16[8,512,321]{1,2,0:T(8,128)(2,1)} fusion(bf16[8,512,1]{1,2,0:T(2,128)(2,1)S(1)} %broadcast_in_dim.187, bf16[8,512,320]{1,2,0:T(8,128)(2,1)S(1)} %convert_bitcast_fusion), kind=kLoop, calls=%fused_computation.1 | loop fusion | flops 5259264 | bytes 5259264 | tf_op jit(solution)/shard_map/concatenate | solution.py:207
  89.7 53.5 %reduce-scatter.2.cloned.1.call-done = bf16[1,512,321]{1,2,0:T(8,128)(2,1)} async-done(((bf16[8,512,321]{1,2,0:T(8,128)(2,1)}), bf16[1,512,321]{1,2,0:T(8,128)(2,1)}) %reduce-scatter.2.cloned.1.call-update) | async-done | bytes 328720 | tf_op jit(solution)/shard_map/reduce_scatter | solution.py:208
  143.2 0.7 fusion.61
  143.9 1.8 %multiply_convert_fusion.6 = bf16[512,320]{0,1:T(8,128)(2,1)} fusion(bf16[512,321]{0,1:T(8,128)(2,1)} %bitcast.101, f32[512]{0:T(512)S(1)} %bitcast.102), kind=kLoop, calls=%fused_computation.37 | loop fusion | flops 491520 | bytes 657408 | tf_op jit(solution)/shard_map/convert_element_type | solution.py:211
  (78 shorter events, 1.9 us)
Async XLA Ops:
  6.5 14.3 %copy-start.9 = (s32[512]{0:T(512)S(1)}, s32[512]{0:T(512)}, u32[]{:S(2)}) copy-start(s32[512]{0:T(512)} %param.16) | copy-start | bytes 6148
  6.5 10.8 %copy-start.2 = (bf16[512,640]{1,0:T(8,128)(2,1)S(1)}, bf16[512,640]{1,0:T(8,128)(2,1)}, u32[]{:S(2)}) copy-start(bf16[512,640]{1,0:T(8,128)(2,1)} %param.12) | copy-start | bytes 1966084
  6.5 136.7 %reduce-scatter.2.cloned.1.call-start = ((), (), s32[]{:S(2)}) async-start(), calls=%async_computation.1 | async-start | bytes 3022848 | tf_op jit(solution)/shard_map/reduce_scatter | solution.py:208
  8.9 12.5 %copy-start.4 = (bf16[512,256]{1,0:T(8,128)(2,1)S(1)}, bf16[512,256]{1,0:T(8,128)(2,1)}, u32[]{:S(2)}) copy-start(bf16[512,256]{1,0:T(8,128)(2,1)} %param.13) | copy-start | bytes 786436
  9.1 9.9 %collective-permute-start = (bf16[3,1024]{0,1:T(8,128)(2,1)S(1)}, bf16[3,1024]{0,1:T(8,128)(2,1)S(1)}, u32[]{:S(2)}, u32[]{:S(2)}) collective-permute-start(bf16[3,1024]{0,1:T(8,128)(2,1)S(1)} %copy.56), channel_id=1, source_target_pairs={{0,16},{16,32},{32,48},{48,64},{64,80},{80,96},{96,112},{112,128},... | collective-permute-start | bytes 18440 | tf_op jit(solution)/shard_map/ppermute | solution.py:12
  25.8 6.6 %copy-start.3 = (bf16[512,640]{1,0:T(8,128)(2,1)S(1)}, bf16[512,640]{1,0:T(8,128)(2,1)}, u32[]{:S(2)}) copy-start(bf16[512,640]{1,0:T(8,128)(2,1)} %param.14) | copy-start | bytes 1966084
  26.9 12.0 %collective-permute-start.1 = (bf16[656,128]{0,1:T(8,128)(2,1)}, bf16[656,128]{0,1:T(8,128)(2,1)S(1)}, u32[]{:S(2)}, u32[]{:S(2)}) collective-permute-start(bf16[656,128]{0,1:T(8,128)(2,1)} %pad_maximum_fusion.3), channel_id=1, source_target_pairs={{0,16},{16,32},{32,48},{48,64},{64,80},{80,96},{96,112},{112,128},... | collective-permute-start | bytes 503816 | tf_op jit(solution)/shard_map/ppermute | solution.py:12
  38.6 2.6 %copy-start.8 = (pred[2,256,256]{2,1,0:T(8,128)(4,1)S(1)}, pred[2,256,256]{2,1,0:T(8,128)(4,1)}, u32[]{:S(2)}) copy-start(pred[2,256,256]{2,1,0:T(8,128)(4,1)} %compare_and_fusion) | copy-start | bytes 393220
  39.0 9.1 %collective-permute-start.2 = (bf16[656,128]{0,1:T(8,128)(2,1)S(1)}, bf16[656,128]{0,1:T(8,128)(2,1)S(1)}, u32[]{:S(2)}, u32[]{:S(2)}) collective-permute-start(bf16[656,128]{0,1:T(8,128)(2,1)S(1)} %pad_maximum_fusion.4), channel_id=1, source_target_pairs={{0,32},{16,48},{32,64},{48,80},{64,96},{80,112},{96,128},{112,144}... | collective-permute-start | bytes 503816 | tf_op jit(solution)/shard_map/ppermute | solution.py:12
  48.3 25.3 %copy-start.10 = (f32[10]{0:T(128)S(1)}, f32[10]{0:T(128)}, u32[]{:S(2)}) copy-start(f32[10]{0:T(128)} %param.21) | copy-start | bytes 124
  48.4 6.7 %collective-permute-start.3 = (bf16[656,128]{0,1:T(8,128)(2,1)S(1)}, bf16[656,128]{0,1:T(8,128)(2,1)S(1)}, u32[]{:S(2)}, u32[]{:S(2)}) collective-permute-start(bf16[656,128]{0,1:T(8,128)(2,1)S(1)} %pad_maximum_fusion.5), channel_id=1, source_target_pairs={{0,64},{16,80},{32,96},{48,112},{64,128},{80,144},{96,160},{112,17... | collective-permute-start | bytes 503816 | tf_op jit(solution)/shard_map/ppermute | solution.py:12
  52.1 21.5 %copy-start.1 = (f32[2,256,10,64]{1,3,2,0:T(8,128)S(1)}, f32[2,256,10,64]{1,3,2,0:T(8,128)}, u32[]{:S(2)}) copy-start(f32[2,256,10,64]{1,3,2,0:T(8,128)} %fusion.8) | copy-start | bytes 3932164
  55.9 21.0 %collective-permute-start.6 = (bf16[656,128]{0,1:T(8,128)(2,1)}, bf16[656,128]{0,1:T(8,128)(2,1)S(1)}, u32[]{:S(2)}, u32[]{:S(2)}) collective-permute-start(bf16[656,128]{0,1:T(8,128)(2,1)} %pad_maximum_fusion.6), channel_id=1, source_target_pairs={{0,272},{16,288},{32,304},{48,320},{64,336},{80,352},{96,368},{112... | collective-permute-start | bytes 503816 | tf_op jit(solution)/shard_map/ppermute | solution.py:12
  67.6 9.3 %collective-permute-start.5 = (bf16[656,128]{0,1:T(8,128)(2,1)}, bf16[656,128]{0,1:T(8,128)(2,1)S(1)}, u32[]{:S(2)}, u32[]{:S(2)}) collective-permute-start(bf16[656,128]{0,1:T(8,128)(2,1)} %pad_maximum_fusion.6), channel_id=1, source_target_pairs={{0,144},{16,160},{32,176},{48,192},{64,208},{80,224},{96,240},{112... | collective-permute-start | bytes 503816 | tf_op jit(solution)/shard_map/ppermute | solution.py:12
  71.6 7.8 %collective-permute-start.4 = (bf16[656,128]{0,1:T(8,128)(2,1)}, bf16[656,128]{0,1:T(8,128)(2,1)S(1)}, u32[]{:S(2)}, u32[]{:S(2)}) collective-permute-start(bf16[656,128]{0,1:T(8,128)(2,1)} %pad_maximum_fusion.6), channel_id=1, source_target_pairs={{0,16},{16,32},{32,48},{48,64},{64,80},{80,96},{96,112},{112,128},... | collective-permute-start | bytes 503816 | tf_op jit(solution)/shard_map/ppermute | solution.py:12
  75.4 5.1 %collective-permute-start.7 = (bf16[656,128]{0,1:T(8,128)(2,1)}, bf16[656,128]{0,1:T(8,128)(2,1)S(1)}, u32[]{:S(2)}, u32[]{:S(2)}) collective-permute-start(bf16[656,128]{0,1:T(8,128)(2,1)} %pad_maximum_fusion.6), channel_id=1, source_target_pairs={{0,400},{16,416},{32,432},{48,448},{64,464},{80,480},{96,496},{1,4... | collective-permute-start | bytes 503816 | tf_op jit(solution)/shard_map/ppermute | solution.py:12
  76.9 2.5 %copy-start.5 = (bf16[656,128]{0,1:T(8,128)(2,1)}, bf16[656,128]{0,1:T(8,128)(2,1)S(1)}, u32[]{:S(2)}) copy-start(bf16[656,128]{0,1:T(8,128)(2,1)S(1)} %collective-permute-done.6) | copy-start | bytes 503812
  76.9 2.5 %copy-start.6 = (bf16[656,128]{0,1:T(8,128)(2,1)}, bf16[656,128]{0,1:T(8,128)(2,1)S(1)}, u32[]{:S(2)}) copy-start(bf16[656,128]{0,1:T(8,128)(2,1)S(1)} %collective-permute-done.5) | copy-start | bytes 503812
  79.4 0.7 copy-start.7
  83.6 1.9 %copy-start = (bf16[640,2560]{0,1:T(8,128)(2,1)S(1)}, bf16[640,2560]{0,1:T(8,128)(2,1)}, u32[]{:S(2)}) copy-start(bf16[640,2560]{0,1:T(8,128)(2,1)} %copy.66) | copy-start | bytes 9830404
  83.8 1.8 %copy-start.11 = (f32[640]{0:T(1024)S(1)}, f32[640]{0:T(1024)}, u32[]{:S(2)}) copy-start(f32[640]{0:T(1024)} %param.22) | copy-start | bytes 7684
Sparse Core Ops, SparseCore 0:
  89.8 53.3 reduce-scatter.1

commit v16 on v14

--- a/solution.py
+++ b/solution.py
@@ -185,7 +185,11 @@
         jnp.concatenate([jnp.ones((head_count, 1), jnp.float32), block_decay[:, :-1]], axis=1),
         axis=1,
     )
-    reach_term = jnp.einsum("ctn,hpn->cthp", c_wide, incoming, precision=highest)
+    incoming_high = incoming.astype(jnp.bfloat16)
+    incoming_low = (incoming - incoming_high.astype(jnp.float32)).astype(jnp.bfloat16)
+    reach_term = jnp.einsum(
+        "ctn,hpn->cthp", c_vals, incoming_high, preferred_element_type=jnp.float32
+    ) + jnp.einsum("ctn,hpn->cthp", c_vals, incoming_low, preferred_element_type=jnp.float32)
     result = (
         result + reach_term * jnp.transpose(entry_gain * prefix[:, :, None], (1, 2, 0))[..., None]
     )

time: 154 us -> 154 us (level)
  no operation moved by 1% of the time
where the time goes in v16:
time: 154 us; the launch traced here: 153 us
  waiting for transfers between devices  64 us (42%)
  starting transfers between devices  34.3 us (22%)
  other arithmetic  17.3 us (11%)
  local copies, waits for them, and re-layouts  14.5 us (9%)
  between operations  13.8 us (9%)
  matrix products  8.94 us (6%)
    reduce_scatter x1, waiting for transfers between devices, local(): lax.psum_scatter(payload, 'tensor', scatter_dimension=0, tiled=True)[0]  53.6 us
    ppermute x8, starting transfers between devices, from_behind(): return lax.ppermute(block, axis, route)  34.3 us
    ppermute x8, waiting for transfers between devices, from_behind(): return lax.ppermute(block, axis, route)  10.4 us
    optimization_barrier x2, local copies, waits for them, and re-layouts, pass_state(): sent, passengers = lax.optimization_barrier((sent, passengers))  5.86 us
  transfers between devices with their start and end apart: 9, of which 5 were waited for; matrix products, arithmetic and copies ran while one was open for 11% of the time, Pallas kernels for 0%

profile of v16, /device:TPU:6, one launch (start us, length us, event | category | flops | bytes accessed | tf_op | source)
XLA Modules:
  0.0 152.8 jit_solution(5548350436376870305)
XLA Ops:
  6.5 0.8 slice.178
  7.3 0.7 fusion.94
  8.1 0.7 slice.177
  8.9 0.2 copy.59
  9.1 3.4 %collective-permute-start = (bf16[3,1024]{0,1:T(8,128)(2,1)S(1)}, bf16[3,1024]{0,1:T(8,128)(2,1)S(1)}, u32[]{:S(2)}, u32[]{:S(2)}) collective-permute-start(bf16[3,1024]{0,1:T(8,128)(2,1)S(1)} %copy.59), channel_id=1, source_target_pairs={{0,16},{16,32},{32,48},{48,64},{64,80},{80,96},{96,112},{112,128},... | collective-permute-start | bytes 18440 | tf_op jit(solution)/shard_map/ppermute | solution.py:12
  12.5 0.7 exponential_negate_fusion
  13.2 0.8 slice_convert_fusion.4
  14.0 0.9 convert_reduce_fusion.3
  14.9 0.8 broadcast_multiply_fusion.1
  15.8 0.3 fusion.30
  16.1 0.2 slice_reduce_fusion
  16.3 0.8 compare_and_fusion
  17.1 0.2 slice_reduce_fusion.2
  17.3 0.1 slice.183
  17.4 0.3 copy.61
  17.6 1.4 collective-permute-done
  19.0 0.6 slice.181
  19.6 0.8 pad_maximum_fusion.9
  20.4 0.2 slice_reduce_fusion.1
  20.6 0.1 fusion.91
  20.8 0.1 slice_compare_fusion.2
  21.3 0.1 copy.65
  21.4 0.8 multiply_convert_fusion.7
  22.2 1.7 %multiply_convert_fusion.5 = bf16[512,640]{0,1:T(8,128)(2,1)S(1)} fusion(bf16[512,640]{0,1:T(8,128)(2,1)S(1)} %copy.61, bf16[3,640]{0,1:T(8,128)(2,1)S(1)} %slice.237, f32[640]{0:T(1024)S(1)} %get-tuple-element.19, f32[640]{0:T(1024)S(1)} %get-tuple-element.20, f32[640]{0:T(1024)S(1)} %get-tuple-element.18, f32[640]{0:T(1024)S(1)} %get-tuple-element.17, ...), kind=kLoop, calls=%fused_computation.29 | loop fusion | flops 9502720 | bytes 1326848 | tf_op jit(solution)/shard_map/convert_element_type | solution.py:27
  23.9 0.2 reshape.275
  24.1 0.1 multiply_bitcast_fusion
  24.1 0.8 fusion.14
  24.9 0.8 fusion.92
  25.8 0.2 copy.66
  25.9 0.2 copy.67
  26.2 0.7 pad_maximum_fusion.3
  26.9 5.5 %collective-permute-start.1 = (bf16[656,128]{0,1:T(8,128)(2,1)}, bf16[656,128]{0,1:T(8,128)(2,1)S(1)}, u32[]{:S(2)}, u32[]{:S(2)}) collective-permute-start(bf16[656,128]{0,1:T(8,128)(2,1)} %pad_maximum_fusion.3), channel_id=1, source_target_pairs={{0,16},{16,32},{32,48},{48,64},{64,80},{80,96},{96,112},{112,128},... | collective-permute-start | bytes 503816 | tf_op jit(solution)/shard_map/ppermute | solution.py:12
  32.4 0.3 copy.68
  32.6 0.3 convert_multiply_fusion
  33.0 5.6 %copy.69 = bf16[640,2560]{0,1:T(8,128)(2,1)} copy(bf16[640,2560]{1,0:T(8,128)(2,1)} %param.23) | data formatting | bytes 6553600 | tf_op jit(solution)/shard_map/optimization_barrier | solution.py:57
  38.6 0.2 fusion.95
  39.0 2.2 %collective-permute-start.2 = (bf16[656,128]{0,1:T(8,128)(2,1)S(1)}, bf16[656,128]{0,1:T(8,128)(2,1)S(1)}, u32[]{:S(2)}, u32[]{:S(2)}) collective-permute-start(bf16[656,128]{0,1:T(8,128)(2,1)S(1)} %pad_maximum_fusion.4), channel_id=1, source_target_pairs={{0,32},{16,48},{32,64},{48,80},{64,96},{80,112},{96,128},{112,144}... | collective-permute-start | bytes 503816 | tf_op jit(solution)/shard_map/ppermute | solution.py:12
  41.2 2.8 %fusion.9 = f32[2,256,10,64]{1,3,2,0:T(8,128)} fusion(f32[10,2,256]{2,0,1:T(8,128)S(1)} %get-tuple-element.48, f32[10,2,256]{2,0,1:T(8,128)S(1)} %fusion.30, f32[2,256,256]{2,1,0:T(8,128)S(1)} %fusion.95, pred[2,256,256]{2,1,0:T(8,128)(4,1)S(1)} %copy-done.8, bf16[2,256,10,64]{1,0,3,2:T(2,128)(2,1)S(1)} %reshape.275), kind=kOutput, calls=%fused_computation.18 | convolution fusion | flops 175636480 | bytes 2662400 | tf_op jit(solution)/shard_map/hcts,cshp->cthp/dot_general | solution.py:174
  44.0 4.0 %collective-permute-done.2 = bf16[656,128]{0,1:T(8,128)(2,1)S(1)} collective-permute-done((bf16[656,128]{0,1:T(8,128)(2,1)S(1)}, bf16[656,128]{0,1:T(8,128)(2,1)S(1)}, u32[]{:S(2)}, u32[]{:S(2)}) %collective-permute-start.2) | collective-permute-done | bytes 167968 | tf_op jit(solution)/shard_map/ppermute | solution.py:12
  48.4 3.5 %collective-permute-start.3 = (bf16[656,128]{0,1:T(8,128)(2,1)S(1)}, bf16[656,128]{0,1:T(8,128)(2,1)S(1)}, u32[]{:S(2)}, u32[]{:S(2)}) collective-permute-start(bf16[656,128]{0,1:T(8,128)(2,1)S(1)} %pad_maximum_fusion.5), channel_id=1, source_target_pairs={{0,64},{16,80},{32,96},{48,112},{64,128},{80,144},{96,160},{112,17... | collective-permute-start | bytes 503816 | tf_op jit(solution)/shard_map/ppermute | solution.py:12
  52.1 2.9 %collective-permute-done.3 = bf16[656,128]{0,1:T(8,128)(2,1)S(1)} collective-permute-done((bf16[656,128]{0,1:T(8,128)(2,1)S(1)}, bf16[656,128]{0,1:T(8,128)(2,1)S(1)}, u32[]{:S(2)}, u32[]{:S(2)}) %collective-permute-start.3) | collective-permute-done | bytes 167968 | tf_op jit(solution)/shard_map/ppermute | solution.py:12
  55.0 0.1 add_convert_fusion
  55.2 0.7 pad_maximum_fusion.6
  55.9 11.7 %collective-permute-start.6 = (bf16[656,128]{0,1:T(8,128)(2,1)}, bf16[656,128]{0,1:T(8,128)(2,1)S(1)}, u32[]{:S(2)}, u32[]{:S(2)}) collective-permute-start(bf16[656,128]{0,1:T(8,128)(2,1)} %pad_maximum_fusion.6), channel_id=1, source_target_pairs={{0,272},{16,288},{32,304},{48,320},{64,336},{80,352},{96,368},{112... | collective-permute-start | bytes 503816 | tf_op jit(solution)/shard_map/ppermute | solution.py:12
  67.6 4.1 %collective-permute-start.5 = (bf16[656,128]{0,1:T(8,128)(2,1)}, bf16[656,128]{0,1:T(8,128)(2,1)S(1)}, u32[]{:S(2)}, u32[]{:S(2)}) collective-permute-start(bf16[656,128]{0,1:T(8,128)(2,1)} %pad_maximum_fusion.6), channel_id=1, source_target_pairs={{0,144},{16,160},{32,176},{48,192},{64,208},{80,224},{96,240},{112... | collective-permute-start | bytes 503816 | tf_op jit(solution)/shard_map/ppermute | solution.py:12
  71.7 1.9 %collective-permute-start.4 = (bf16[656,128]{0,1:T(8,128)(2,1)}, bf16[656,128]{0,1:T(8,128)(2,1)S(1)}, u32[]{:S(2)}, u32[]{:S(2)}) collective-permute-start(bf16[656,128]{0,1:T(8,128)(2,1)} %pad_maximum_fusion.6), channel_id=1, source_target_pairs={{0,16},{16,32},{32,48},{48,64},{64,80},{80,96},{96,112},{112,128},... | collective-permute-start | bytes 503816 | tf_op jit(solution)/shard_map/ppermute | solution.py:12
  73.6 1.8 %fusion.11 = f32[2,256,10,64]{1,3,2,0:T(8,128)S(1)} fusion(f32[2,256,10,64]{1,3,2,0:T(8,128)S(1)} %copy-done.1, bf16[2,256,128,1]{2,1,3,0:T(8,128)(2,1)S(1)} %bitcast.97, f32[10]{0:T(128)S(1)} %copy-done.10, f32[2,256,10]{1,2,0:T(8,128)S(1)} %get-tuple-element.22, f32[1,10,64,128]{3,2,1,0:T(8,128)} %get-tuple-element.41, ...), kind=kOutput, calls=%fused_computation.20 | convolution fusion | flops 504954880 | bytes 3756072 | tf_op jit(solution)/shard_map/ctn,chpn->cthp/dot_general | solution.py:166
  75.4 2.0 %collective-permute-start.7 = (bf16[656,128]{0,1:T(8,128)(2,1)}, bf16[656,128]{0,1:T(8,128)(2,1)}, u32[]{:S(2)}, u32[]{:S(2)}) collective-permute-start(bf16[656,128]{0,1:T(8,128)(2,1)} %pad_maximum_fusion.6), channel_id=1, source_target_pairs={{0,400},{16,416},{32,432},{48,448},{64,464},{80,480},{96,496},{1,4... | collective-permute-start | bytes 503816 | tf_op jit(solution)/shard_map/ppermute | solution.py:12
  77.4 2.0 %collective-permute-done.4 = bf16[656,128]{0,1:T(8,128)(2,1)S(1)} collective-permute-done((bf16[656,128]{0,1:T(8,128)(2,1)}, bf16[656,128]{0,1:T(8,128)(2,1)S(1)}, u32[]{:S(2)}, u32[]{:S(2)}) %collective-permute-start.4) | collective-permute-done | bytes 167968 | tf_op jit(solution)/shard_map/ppermute | solution.py:12
  79.5 0.7 copy-done.7
  80.5 1.3 subtract_convert_fusion
  81.8 0.2 copy.73
  82.0 0.2 copy.72
  82.2 0.3 fusion.96
  82.5 0.3 fusion.13
  82.9 1.0 copy.74
  83.9 0.1 copy.80
  84.0 0.4 multiply_reduce_fusion
  84.4 1.4 copy-done
  85.8 2.4 %convert_bitcast_fusion = bf16[8,512,320]{1,2,0:T(8,128)(2,1)S(1)} fusion(bf16[8,320,640]{2,1,0:T(8,128)(2,1)S(1)} %bitcast.95, f32[640]{0:T(1024)S(1)} %copy-done.11, f32[512,640]{0,1:T(8,128)S(1)} %bitcast.93, f32[512,640]{0,1:T(8,128)S(1)} %convert_multiply_fusion), kind=kOutput, calls=%fused_computation.3 | convolution fusion | flops 1680015360 | bytes 8522240 | tf_op jit(solution)/shard_map/tc,gkc->gtk/dot_general | solution.py:202
  88.2 1.7 %pad_maximum_fusion = bf16[8,512,321]{1,2,0:T(8,128)(2,1)} fusion(bf16[8,512,1]{1,2,0:T(2,128)(2,1)S(1)} %broadcast_in_dim.187, bf16[8,512,320]{1,2,0:T(8,128)(2,1)S(1)} %convert_bitcast_fusion), kind=kLoop, calls=%fused_computation.1 | loop fusion | flops 5259264 | bytes 5259264 | tf_op jit(solution)/shard_map/concatenate | solution.py:211
  90.0 53.6 %reduce-scatter.2.cloned.1.call-done = bf16[1,512,321]{1,2,0:T(8,128)(2,1)} async-done(((bf16[8,512,321]{1,2,0:T(8,128)(2,1)}), bf16[1,512,321]{1,2,0:T(8,128)(2,1)}) %reduce-scatter.2.cloned.1.call-update) | async-done | bytes 328720 | tf_op jit(solution)/shard_map/reduce_scatter | solution.py:212
  143.5 0.7 fusion.62
  144.2 1.8 %multiply_convert_fusion.6 = bf16[512,320]{0,1:T(8,128)(2,1)} fusion(bf16[512,321]{0,1:T(8,128)(2,1)} %bitcast.107, f32[512]{0:T(512)S(1)} %bitcast.108), kind=kLoop, calls=%fused_computation.38 | loop fusion | flops 491520 | bytes 657408 | tf_op jit(solution)/shard_map/convert_element_type | solution.py:215
  (80 shorter events, 2.1 us)
Async XLA Ops:
  6.5 14.3 %copy-start.9 = (s32[512]{0:T(512)S(1)}, s32[512]{0:T(512)}, u32[]{:S(2)}) copy-start(s32[512]{0:T(512)} %param.16) | copy-start | bytes 6148
  6.5 10.8 %copy-start.2 = (bf16[512,640]{1,0:T(8,128)(2,1)S(1)}, bf16[512,640]{1,0:T(8,128)(2,1)}, u32[]{:S(2)}) copy-start(bf16[512,640]{1,0:T(8,128)(2,1)} %param.12) | copy-start | bytes 1966084
  6.5 137.0 %reduce-scatter.2.cloned.1.call-start = ((), (), s32[]{:S(2)}) async-start(), calls=%async_computation.1 | async-start | bytes 3022848 | tf_op jit(solution)/shard_map/reduce_scatter | solution.py:212
  8.9 12.5 %copy-start.4 = (bf16[512,256]{1,0:T(8,128)(2,1)S(1)}, bf16[512,256]{1,0:T(8,128)(2,1)}, u32[]{:S(2)}) copy-start(bf16[512,256]{1,0:T(8,128)(2,1)} %param.13) | copy-start | bytes 786436
  9.1 9.9 %collective-permute-start = (bf16[3,1024]{0,1:T(8,128)(2,1)S(1)}, bf16[3,1024]{0,1:T(8,128)(2,1)S(1)}, u32[]{:S(2)}, u32[]{:S(2)}) collective-permute-start(bf16[3,1024]{0,1:T(8,128)(2,1)S(1)} %copy.59), channel_id=1, source_target_pairs={{0,16},{16,32},{32,48},{48,64},{64,80},{80,96},{96,112},{112,128},... | collective-permute-start | bytes 18440 | tf_op jit(solution)/shard_map/ppermute | solution.py:12
  25.8 6.6 %copy-start.3 = (bf16[512,640]{1,0:T(8,128)(2,1)S(1)}, bf16[512,640]{1,0:T(8,128)(2,1)}, u32[]{:S(2)}) copy-start(bf16[512,640]{1,0:T(8,128)(2,1)} %param.14) | copy-start | bytes 1966084
  26.9 12.0 %collective-permute-start.1 = (bf16[656,128]{0,1:T(8,128)(2,1)}, bf16[656,128]{0,1:T(8,128)(2,1)S(1)}, u32[]{:S(2)}, u32[]{:S(2)}) collective-permute-start(bf16[656,128]{0,1:T(8,128)(2,1)} %pad_maximum_fusion.3), channel_id=1, source_target_pairs={{0,16},{16,32},{32,48},{48,64},{64,80},{80,96},{96,112},{112,128},... | collective-permute-start | bytes 503816 | tf_op jit(solution)/shard_map/ppermute | solution.py:12
  38.6 2.6 %copy-start.8 = (pred[2,256,256]{2,1,0:T(8,128)(4,1)S(1)}, pred[2,256,256]{2,1,0:T(8,128)(4,1)}, u32[]{:S(2)}) copy-start(pred[2,256,256]{2,1,0:T(8,128)(4,1)} %compare_and_fusion) | copy-start | bytes 393220
  39.0 9.1 %collective-permute-start.2 = (bf16[656,128]{0,1:T(8,128)(2,1)S(1)}, bf16[656,128]{0,1:T(8,128)(2,1)S(1)}, u32[]{:S(2)}, u32[]{:S(2)}) collective-permute-start(bf16[656,128]{0,1:T(8,128)(2,1)S(1)} %pad_maximum_fusion.4), channel_id=1, source_target_pairs={{0,32},{16,48},{32,64},{48,80},{64,96},{80,112},{96,128},{112,144}... | collective-permute-start | bytes 503816 | tf_op jit(solution)/shard_map/ppermute | solution.py:12
  48.2 25.4 %copy-start.10 = (f32[10]{0:T(128)S(1)}, f32[10]{0:T(128)}, u32[]{:S(2)}) copy-start(f32[10]{0:T(128)} %param.21) | copy-start | bytes 124
  48.4 6.7 %collective-permute-start.3 = (bf16[656,128]{0,1:T(8,128)(2,1)S(1)}, bf16[656,128]{0,1:T(8,128)(2,1)S(1)}, u32[]{:S(2)}, u32[]{:S(2)}) collective-permute-start(bf16[656,128]{0,1:T(8,128)(2,1)S(1)} %pad_maximum_fusion.5), channel_id=1, source_target_pairs={{0,64},{16,80},{32,96},{48,112},{64,128},{80,144},{96,160},{112,17... | collective-permute-start | bytes 503816 | tf_op jit(solution)/shard_map/ppermute | solution.py:12
  52.1 21.5 %copy-start.1 = (f32[2,256,10,64]{1,3,2,0:T(8,128)S(1)}, f32[2,256,10,64]{1,3,2,0:T(8,128)}, u32[]{:S(2)}) copy-start(f32[2,256,10,64]{1,3,2,0:T(8,128)} %fusion.9) | copy-start | bytes 3932164
  55.9 21.5 %collective-permute-start.6 = (bf16[656,128]{0,1:T(8,128)(2,1)}, bf16[656,128]{0,1:T(8,128)(2,1)S(1)}, u32[]{:S(2)}, u32[]{:S(2)}) collective-permute-start(bf16[656,128]{0,1:T(8,128)(2,1)} %pad_maximum_fusion.6), channel_id=1, source_target_pairs={{0,272},{16,288},{32,304},{48,320},{64,336},{80,352},{96,368},{112... | collective-permute-start | bytes 503816 | tf_op jit(solution)/shard_map/ppermute | solution.py:12
  67.6 9.8 %collective-permute-start.5 = (bf16[656,128]{0,1:T(8,128)(2,1)}, bf16[656,128]{0,1:T(8,128)(2,1)S(1)}, u32[]{:S(2)}, u32[]{:S(2)}) collective-permute-start(bf16[656,128]{0,1:T(8,128)(2,1)} %pad_maximum_fusion.6), channel_id=1, source_target_pairs={{0,144},{16,160},{32,176},{48,192},{64,208},{80,224},{96,240},{112... | collective-permute-start | bytes 503816 | tf_op jit(solution)/shard_map/ppermute | solution.py:12
  71.7 7.8 %collective-permute-start.4 = (bf16[656,128]{0,1:T(8,128)(2,1)}, bf16[656,128]{0,1:T(8,128)(2,1)S(1)}, u32[]{:S(2)}, u32[]{:S(2)}) collective-permute-start(bf16[656,128]{0,1:T(8,128)(2,1)} %pad_maximum_fusion.6), channel_id=1, source_target_pairs={{0,16},{16,32},{32,48},{48,64},{64,80},{80,96},{96,112},{112,128},... | collective-permute-start | bytes 503816 | tf_op jit(solution)/shard_map/ppermute | solution.py:12
  75.4 5.1 %collective-permute-start.7 = (bf16[656,128]{0,1:T(8,128)(2,1)}, bf16[656,128]{0,1:T(8,128)(2,1)}, u32[]{:S(2)}, u32[]{:S(2)}) collective-permute-start(bf16[656,128]{0,1:T(8,128)(2,1)} %pad_maximum_fusion.6), channel_id=1, source_target_pairs={{0,400},{16,416},{32,432},{48,448},{64,464},{80,480},{96,496},{1,4... | collective-permute-start | bytes 503816 | tf_op jit(solution)/shard_map/ppermute | solution.py:12
  77.4 2.1 %copy-start.5 = (bf16[656,128]{0,1:T(8,128)(2,1)}, bf16[656,128]{0,1:T(8,128)(2,1)S(1)}, u32[]{:S(2)}) copy-start(bf16[656,128]{0,1:T(8,128)(2,1)S(1)} %collective-permute-done.6) | copy-start | bytes 503812
  77.4 2.1 %copy-start.6 = (bf16[656,128]{0,1:T(8,128)(2,1)}, bf16[656,128]{0,1:T(8,128)(2,1)S(1)}, u32[]{:S(2)}) copy-start(bf16[656,128]{0,1:T(8,128)(2,1)S(1)} %collective-permute-done.5) | copy-start | bytes 503812
  79.4 0.7 copy-start.7
  83.9 1.9 %copy-start = (bf16[640,2560]{0,1:T(8,128)(2,1)S(1)}, bf16[640,2560]{0,1:T(8,128)(2,1)}, u32[]{:S(2)}) copy-start(bf16[640,2560]{0,1:T(8,128)(2,1)} %copy.69) | copy-start | bytes 9830404
  84.0 1.8 %copy-start.11 = (f32[640]{0:T(1024)S(1)}, f32[640]{0:T(1024)}, u32[]{:S(2)}) copy-start(f32[640]{0:T(1024)} %param.22) | copy-start | bytes 7684
Sparse Core Ops, SparseCore 0:
  90.1 53.4 reduce-scatter.1
